TPU v7x, 32 devices: a whole 2x2x4 slice. The times are simulated.
32 devices in a mesh: doc: 8 (over y, x, core), term: 4 (over z).
Axes of the slice: x: 2, y: 2, z: 4, core: 2. Of those that a mesh axis runs over, the one named last changes fastest.
Arguments:
- tiles: bfloat16 [8, 4, 512, 128, 128], P('doc', 'term'), as said below
- tile_rows: int32 [8, 4, 512], P('doc', 'term'), may hold values from 0 to 63, as said below
- tile_cols: int32 [8, 4, 512], P('doc', 'term'), may hold values from 0 to 63
- tile_count: int32 [8, 4], P('doc', 'term'), may hold values from 64 to 512, as said below
- start_block: bfloat16 [4, 8192, 64], P('term', 'doc'), may hold values from -6 to 6
- doc_cluster: int32 [8, 8192], P('doc', 'term'), may hold values from 0 to 63, as said below
- term_cluster: int32 [4, 8192], P('term', 'doc'), may hold values from 0 to 63, as said below
Outputs:
- doc_distance: float32 [8, 8192, 64], P('doc', 'term')
- term_distance: float32 [4, 8192, 64], P('term', 'doc')
Inputs may be any that keep to these rules, and one draw needn't show every extreme that they name: `tile_rows`: the first 64 slots of every device name every row tile of its block at least once; other slots may repeat a position, and repeated tiles add. `tile_cols`: the first 64 slots of every device name each column tile of its block exactly once. `tile_count`: in every draw some device uses all 512 slots; slots at or beyond a device's count are unused. `doc_cluster`: every co-cluster holds at least one document. `term_cluster`: every co-cluster holds at least one term. `tiles`: entries are positive.
All inputs are finite; a program needn't handle non-finite values.
Results may differ from a plain program's by a relative error of at most 0.0009.
Values may be sent and summed in bfloat16 or wider, within the bound.
No kernel may reach another device: no remote copies, remote signals or barrier semaphores. Data moves between devices by JAX's collectives and lax.ppermute only.
A program may use at most 128 MiB of HBM per device.

v0:
```python
import jax
import jax.numpy as jnp
from jax import lax
from jax.sharding import PartitionSpec as P

CLUSTERS = 64
ITERS = 2
DOC_TILES = 64
TERM_TILES = 64


def tile_width(total):
    return min(64, total)


def masked_turns(count, width):
    return (count + width - 1) // width


def degree_pass(local_tiles, row_ids_all, col_ids_all, count):
    width = tile_width(local_tiles.shape[0])
    edge = local_tiles.shape[1]
    ones_vector = jnp.ones((edge,), jnp.bfloat16)

    def degree_turn(index, carry):
        row_total, col_total = carry
        first = index * width
        block = lax.dynamic_slice_in_dim(local_tiles, first, width, 0)
        row_ids = lax.dynamic_slice_in_dim(row_ids_all, first, width, 0)
        col_ids = lax.dynamic_slice_in_dim(col_ids_all, first, width, 0)
        live = (first + jnp.arange(width, dtype=jnp.int32) < count).astype(jnp.float32)
        row_part = (
            jnp.einsum("tij,j->ti", block, ones_vector, preferred_element_type=jnp.float32)
            * live[:, None]
        )
        col_part = (
            jnp.einsum("tij,i->tj", block, ones_vector, preferred_element_type=jnp.float32)
            * live[:, None]
        )
        return (
            row_total + jax.ops.segment_sum(row_part, row_ids, num_segments=DOC_TILES),
            col_total + jax.ops.segment_sum(col_part, col_ids, num_segments=TERM_TILES),
        )

    initial = (
        jnp.zeros((DOC_TILES, edge), jnp.float32),
        jnp.zeros((TERM_TILES, edge), jnp.float32),
    )
    row_total, col_total = lax.fori_loop(0, masked_turns(count, width), degree_turn, initial)
    return (row_total.reshape(-1), col_total.reshape(-1))


def left_pass(local_tiles, row_ids_all, col_ids_all, count, term_block):
    width = tile_width(local_tiles.shape[0])
    edge = local_tiles.shape[1]
    columns = term_block.shape[1]
    table = term_block.reshape(TERM_TILES, edge, columns)

    def left_turn(index, total):
        first = index * width
        block = lax.dynamic_slice_in_dim(local_tiles, first, width, 0)
        row_ids = lax.dynamic_slice_in_dim(row_ids_all, first, width, 0)
        col_ids = lax.dynamic_slice_in_dim(col_ids_all, first, width, 0)
        live = first + jnp.arange(width, dtype=jnp.int32) < count
        pieces = jnp.take(table, col_ids, axis=0)
        pieces = jnp.where(live[:, None, None], pieces, jnp.zeros_like(pieces))
        product = jnp.einsum("tij,tjk->tik", block, pieces, preferred_element_type=jnp.float32)
        return total + jax.ops.segment_sum(product, row_ids, num_segments=DOC_TILES)

    initial = jnp.zeros((DOC_TILES, edge, columns), jnp.float32)
    total = lax.fori_loop(0, masked_turns(count, width), left_turn, initial)
    return total.reshape(DOC_TILES * edge, columns)


def right_pass(local_tiles, row_ids_all, col_ids_all, count, doc_block):
    width = tile_width(local_tiles.shape[0])
    edge = local_tiles.shape[1]
    columns = doc_block.shape[1]
    table = doc_block.reshape(DOC_TILES, edge, columns)

    def right_turn(index, total):
        first = index * width
        block = lax.dynamic_slice_in_dim(local_tiles, first, width, 0)
        row_ids = lax.dynamic_slice_in_dim(row_ids_all, first, width, 0)
        col_ids = lax.dynamic_slice_in_dim(col_ids_all, first, width, 0)
        live = first + jnp.arange(width, dtype=jnp.int32) < count
        pieces = jnp.take(table, row_ids, axis=0)
        pieces = jnp.where(live[:, None, None], pieces, jnp.zeros_like(pieces))
        product = jnp.einsum("tij,tik->tjk", block, pieces, preferred_element_type=jnp.float32)
        return total + jax.ops.segment_sum(product, col_ids, num_segments=TERM_TILES)

    initial = jnp.zeros((TERM_TILES, edge, columns), jnp.float32)
    total = lax.fori_loop(0, masked_turns(count, width), right_turn, initial)
    return total.reshape(TERM_TILES * edge, columns)


def distances(embed, centers, width):
    near = jnp.dot(embed, centers.T, precision=lax.Precision.HIGHEST)
    return (
        jnp.sum(embed * embed, axis=1)[:, None]
        - 2.0 * near
        + jnp.sum(centers * centers, axis=1)[None, :]
    ) / width


def per_device(tiles, tile_rows, tile_cols, tile_count, start_block, doc_cluster, term_cluster):
    local_tiles = tiles[0, 0]
    row_ids_all = tile_rows[0, 0]
    col_ids_all = tile_cols[0, 0]
    count = tile_count[0, 0]
    start_rows = start_block[0]
    width_k = start_rows.shape[1]
    doc_labels = doc_cluster[0]
    term_labels = term_cluster[0]
    own_docs = doc_labels.shape[0]
    doc_offset = lax.axis_index("term") * own_docs
    clusters = jnp.arange(CLUSTERS, dtype=jnp.int32)
    doc_onehot = (doc_labels[:, None] == clusters[None, :]).astype(jnp.float32)
    term_onehot = (term_labels[:, None] == clusters[None, :]).astype(jnp.float32)
    row_part, col_part = degree_pass(local_tiles, row_ids_all, col_ids_all, count)
    weights = start_rows
    basis = None
    for step in range(ITERS):
        term_block = lax.all_gather(weights, "doc", axis=0, tiled=True)
        summed_part = left_pass(local_tiles, row_ids_all, col_ids_all, count, term_block)
        summed_all, degree_all = lax.psum((summed_part, row_part), "term")
        doc_block = (summed_all / degree_all[:, None]).astype(jnp.bfloat16)
        summed_own = lax.dynamic_slice_in_dim(summed_all, doc_offset, own_docs, 0)
        degree_own = lax.dynamic_slice_in_dim(degree_all, doc_offset, own_docs, 0)
        right_part = right_pass(local_tiles, row_ids_all, col_ids_all, count, doc_block)
        right_own, term_degree = (
            lax.psum_scatter(right_part, "doc", scatter_dimension=0, tiled=True),
            lax.psum_scatter(col_part, "doc", scatter_dimension=0, tiled=True),
        )
        root = jnp.sqrt(term_degree)
        raw = right_own / root[:, None]
        previous = root[:, None] * start_rows.astype(jnp.float32) if step == 0 else basis
        gram_part = jnp.dot(raw.T, raw, precision=lax.Precision.HIGHEST)
        along_part = jnp.dot(root, raw, precision=lax.Precision.HIGHEST)
        energy_part = jnp.sum(previous * raw, axis=0)
        volume_part = jnp.sum(term_degree)
        gram_matrix, along, energy, volume = lax.psum(
            (gram_part, along_part, energy_part, volume_part), ("doc", "term")
        )
        lower = jnp.linalg.cholesky(gram_matrix - jnp.outer(along, along) / volume)
        projected = raw - jnp.outer(root, along) / volume
        basis = jax.scipy.linalg.solve_triangular(lower, projected.T, lower=True).T
        weights = (basis / root[:, None]).astype(jnp.bfloat16)
    scale = jnp.sqrt(volume)
    column_scale = scale * lax.rsqrt(energy)
    doc_embed = summed_own / degree_own[:, None] * column_scale[None, :]
    term_embed = scale * basis / root[:, None]
    center_part = jnp.dot(doc_onehot.T, doc_embed, precision=lax.Precision.HIGHEST) + jnp.dot(
        term_onehot.T, term_embed, precision=lax.Precision.HIGHEST
    )
    count_part = jnp.sum(doc_onehot, axis=0) + jnp.sum(term_onehot, axis=0)
    center_sums, counts = lax.psum((center_part, count_part), ("doc", "term"))
    centers = center_sums / counts[:, None]
    doc_distance = distances(doc_embed, centers, width_k)
    term_distance = distances(term_embed, centers, width_k)
    return (doc_distance[None], term_distance[None])


def solution(mesh):
    placed = (
        P("doc", "term", None, None, None),
        P("doc", "term", None),
        P("doc", "term", None),
        P("doc", "term"),
        P("term", "doc", None),
        P("doc", "term"),
        P("term", "doc"),
    )
    return jax.shard_map(
        per_device,
        mesh=mesh,
        in_specs=placed,
        out_specs=(P("doc", "term", None), P("term", "doc", None)),
        check_vma=False,
    )
```

profile of v0, /device:TPU:0, one launch (start us, length us, event | category | flops | bytes accessed | tf_op | source)
XLA Modules:
  0.0 1025.3 jit_solution(10123105832899033675)
XLA Ops:
  8.6 27.5 %all-gather.6.cloned.1.call-done = bf16[1,8192,64]{1,2,0:T(8,128)(2,1)} async-done(((bf16[1,1024,64]{1,2,0:T(8,128)(2,1)}), bf16[1,8192,64]{1,2,0:T(8,128)(2,1)}) %all-gather.6.cloned.1.call-update) | async-done | bytes 1048592 | tf_op jit(solution)/shard_map/all_gather | solution.py:124
  39.2 134.7 %while.52 = (s32[]{:T(128)}, f32[64,128,64]{1,2,0:T(8,128)S(1)}, s32[]{:T(128)}, s32[512]{0:T(512)S(1)}, bf16[512,128,128]{2,1,0:T(8,128)(2,1)}, /*index=5*/s32[...) while((s32[]{:T(128)}, f32[64,128,64]{1,2,0:T(8,128)S(1)}, ...), condition=%wide.region_2.0_spmd, body=%wide.region_0.3_spmd.sunk | while | flops 135792128 | bytes 14686391 | solution.py:71
  49.0 7.0 scatter_fusion
  65.8 7.0 scatter_fusion
  82.7 7.0 scatter_fusion
  99.5 7.0 scatter_fusion
  116.3 7.0 scatter_fusion
  133.2 7.0 scatter_fusion
  150.0 7.0 scatter_fusion
  166.9 7.0 scatter_fusion
  175.4 56.9 %while.53 = (s32[]{:T(128)}, f32[64,128]{1,0:T(8,128)S(1)}, f32[64,128]{1,0:T(8,128)S(1)}, s32[]{:T(128)}, s32[512]{0:T(512)S(1)}, /*index=5*/bf16[512,128,128]{...) while((s32[]{:T(128)}, f32[64,128]{1,0:T(8,128)S(1)}, ...), condition=%wide.region_7.9_spmd, body=%wide.region_4.8_spmd.sunk | while | flops 4227270 | bytes 4393403 | solution.py:49
  232.3 16.9 %psum.84 = f32[8192]{0:T(1024)S(1)} all-reduce(f32[8192]{0:T(1024)S(1)} %bitcast.98), channel_id=1, replica_groups=mesh['doc'=8,'term'=4] {'term'}, use_global_device_ids=true, to_apply=%region_8.10 | all-reduce | flops 8192 | bytes 65536 | tf_op jit(solution)/shard_map/psum | solution.py:126
  249.2 12.3 %all-reduce.7.cloned.1.call-done = f32[8192,64]{0,1:T(8,128)} async-done(((f32[8192,64]{0,1:T(8,128)}), f32[8192,64]{0,1:T(8,128)}) %all-reduce.7.cloned.1.call-update) | async-done | bytes 2097168 | tf_op jit(solution)/shard_map/psum | solution.py:126
  265.3 127.8 %while.54 = (s32[]{:T(128)}, f32[64,128,64]{1,2,0:T(8,128)S(1)}, s32[]{:T(128)}, s32[512]{0:T(512)S(1)}, bf16[512,128,128]{2,1,0:T(8,128)(2,1)}, /*index=5*/s32[...) while((s32[]{:T(128)}, f32[64,128,64]{1,2,0:T(8,128)S(1)}, ...), condition=%wide.region_11.13_spmd, body=%wide.region_9.12_spmd.sunk | while | flops 135792128 | bytes 14686391 | solution.py:93
  274.3 7.0 scatter_fusion.1
  290.3 7.0 scatter_fusion.1
  306.2 7.0 scatter_fusion.1
  322.2 7.0 scatter_fusion.1
  338.2 7.0 scatter_fusion.1
  354.1 7.0 scatter_fusion.1
  370.1 7.0 scatter_fusion.1
  386.1 7.0 scatter_fusion.1
  396.5 22.6 %all-reduce = f32[8192]{0:T(1024)S(1)} all-reduce(f32[8192]{0:T(1024)S(1)} %bitcast.97), channel_id=4, replica_groups=mesh['doc'=8,'term'=4] {'doc'}, use_global_device_ids=true, to_apply=%region_13.15.clone | all-reduce | flops 8192 | bytes 65536
  419.6 14.7 %reduce-scatter.3.cloned.1.call-done = f32[1024,64]{0,1:T(8,128)} async-done(((f32[8192,64]{0,1:T(8,128)}), f32[1024,64]{0,1:T(8,128)}) %reduce-scatter.3.cloned.1.call-update) | async-done | bytes 262160 | tf_op jit(solution)/shard_map/reduce_scatter | solution.py:132
  437.1 39.9 %all-reduce.3 = (f32[]{:T(128)}, f32[64]{0:T(128)S(1)}, f32[64,64]{0,1:T(8,128)S(1)}) all-reduce(f32[]{:T(128)} %get-tuple-element.408, f32[64]{0:T(128)S(1)} %convolution_bitcast_fusion.2, f32[64,64]{0,1:T(8,128)S(1)} %fusion.84), channel_id=1, replica_groups=mesh['doc'=8,'term'=4] {'doc','term'}, use_global_device_ids=true, to_apply=%region_17.19 | all-reduce | flops 4161 | bytes 33288 | tf_op jit(solution)/shard_map/psum | solution.py:142
  492.4 24.3 %all-gather.4.cloned.1.call-done = bf16[8192,64]{0,1:T(8,128)(2,1)} async-done(((bf16[1024,64]{0,1:T(8,128)(2,1)}), bf16[8192,64]{0,1:T(8,128)(2,1)}) %all-gather.4.cloned.1.call-update) | async-done | bytes 1048592 | tf_op jit(solution)/shard_map/all_gather | solution.py:124
  519.7 134.9 %while.55 = (s32[]{:T(128)}, f32[64,128,64]{1,2,0:T(8,128)S(1)}, s32[]{:T(128)}, s32[512]{0:T(512)S(1)}, bf16[512,128,128]{2,1,0:T(8,128)(2,1)}, /*index=5*/s32[...) while((s32[]{:T(128)}, f32[64,128,64]{1,2,0:T(8,128)S(1)}, ...), condition=%wide.region_22.26_spmd, body=%wide.region_20.25_spmd.sunk | while | flops 135792128 | bytes 14686391 | solution.py:71
  529.7 7.0 scatter_fusion.2
  546.5 7.0 scatter_fusion.2
  563.3 7.0 scatter_fusion.2
  580.2 7.0 scatter_fusion.2
  597.0 7.0 scatter_fusion.2
  613.8 7.0 scatter_fusion.2
  630.7 7.0 scatter_fusion.2
  647.5 7.0 scatter_fusion.2
  656.0 85.6 %all-reduce.9.cloned.1.call-done = f32[8192,64]{0,1:T(8,128)} async-done(((f32[8192,64]{0,1:T(8,128)}), f32[8192,64]{0,1:T(8,128)}) %all-reduce.9.cloned.1.call-update) | async-done | bytes 2097168 | tf_op jit(solution)/shard_map/psum | solution.py:126
  745.4 128.2 %while.56 = (s32[]{:T(128)}, f32[64,128,64]{1,2,0:T(8,128)S(1)}, s32[]{:T(128)}, s32[512]{0:T(512)S(1)}, bf16[512,128,128]{2,1,0:T(8,128)(2,1)}, /*index=5*/s32[...) while((s32[]{:T(128)}, f32[64,128,64]{1,2,0:T(8,128)S(1)}, ...), condition=%wide.region_26.30_spmd, body=%wide.region_24.29_spmd.sunk | while | flops 135792128 | bytes 14686391 | solution.py:93
  754.4 7.0 scatter_fusion.3
  770.4 7.0 scatter_fusion.3
  786.4 7.0 scatter_fusion.3
  802.5 7.0 scatter_fusion.3
  818.5 7.0 scatter_fusion.3
  834.5 7.0 scatter_fusion.3
  850.5 7.0 scatter_fusion.3
  866.5 7.0 scatter_fusion.3
  876.7 38.1 %reduce-scatter.5.cloned.1.call-done = f32[1024,64]{0,1:T(8,128)} async-done(((f32[8192,64]{0,1:T(8,128)}), f32[1024,64]{0,1:T(8,128)}) %reduce-scatter.5.cloned.1.call-update) | async-done | bytes 262160 | tf_op jit(solution)/shard_map/reduce_scatter | solution.py:132
  918.8 39.7 %all-reduce.2 = (f32[64]{0:T(128)S(1)}, f32[64]{0:T(128)S(1)}, f32[64,64]{0,1:T(8,128)S(1)}) all-reduce(f32[64]{0:T(128)S(1)} %multiply_reduce_fusion.2, f32[64]{0:T(128)S(1)} %convolution_bitcast_fusion.1, f32[64,64]{0,1:T(8,128)S(1)} %fusion.85), channel_id=1, replica_groups=mesh['doc'=8,'term'=4] {'doc','term'}, use_global_device_ids=true, to_apply=%region_29.33 | all-reduce | flops 4224 | bytes 33792 | tf_op jit(solution)/shard_map/psum | solution.py:142
  974.1 41.3 %all-reduce.1 = (f32[64,64]{1,0:T(8,128)S(1)}, f32[64]{0:T(128)S(1)}) all-reduce(f32[64,64]{1,0:T(8,128)S(1)} %convolution_add_fusion, f32[64]{0:T(128)S(1)} %add.197), channel_id=1, replica_groups=mesh['doc'=8,'term'=4] {'doc','term'}, use_global_device_ids=true, to_apply=%region_33.37 | all-reduce | flops 4160 | bytes 33280 | tf_op jit(solution)/shard_map/psum | solution.py:157
  (296 shorter events, 420.2 us)
Async XLA Ops:
  7.2 29.0 %all-gather.6.cloned.1.call-start = ((), (), s32[]{:S(2)}) async-start(), calls=%async_computation.7 | async-start | bytes 1179648 | tf_op jit(solution)/shard_map/all_gather | solution.py:124
  7.9 253.6 %all-reduce.7.cloned.1.call-start = ((), (), s32[]{:S(2)}) async-start(), calls=%async_computation.2 | async-start | bytes 4194304 | tf_op jit(solution)/shard_map/psum | solution.py:126
  8.6 30.5 %copy-start.3 = (s32[1,1,512]{2,1,0:T(1,128)S(1)}, s32[1,1,512]{2,1,0:T(1,128)}, u32[]{:S(2)}) copy-start(s32[1,1,512]{2,1,0:T(1,128)} %param.23) | copy-start | bytes 6148
  8.6 30.5 %copy-start.4 = (s32[1,1,512]{2,1,0:T(1,128)S(1)}, s32[1,1,512]{2,1,0:T(1,128)}, u32[]{:S(2)}) copy-start(s32[1,1,512]{2,1,0:T(1,128)} %param.24) | copy-start | bytes 6148
  175.3 259.0 %reduce-scatter.3.cloned.1.call-start = ((), (), s32[]{:S(2)}) async-start(), calls=%async_computation.3 | async-start | bytes 2359296 | tf_op jit(solution)/shard_map/reduce_scatter | solution.py:132
  394.6 0.7 copy-start.7
  394.6 122.0 %all-gather.4.cloned.1.call-start = ((), (), s32[]{:S(2)}) async-start(), calls=%async_computation.4 | async-start | bytes 1179648 | tf_op jit(solution)/shard_map/all_gather | solution.py:124
  434.4 56.1 %copy-start.6 = (f32[1024,64]{0,1:T(8,128)S(1)}, f32[1024,64]{0,1:T(8,128)}, u32[]{:S(2)}) copy-start(f32[1024,64]{0,1:T(8,128)} %reduce-scatter.3.cloned.1.call-done) | copy-start | bytes 786436
  492.3 249.3 %all-reduce.9.cloned.1.call-start = ((), (), s32[]{:S(2)}) async-start(), calls=%async_computation.5 | async-start | bytes 4194304 | tf_op jit(solution)/shard_map/psum | solution.py:126
  656.0 258.8 %reduce-scatter.5.cloned.1.call-start = ((), (), s32[]{:S(2)}) async-start(), calls=%async_computation.6 | async-start | bytes 2359296 | tf_op jit(solution)/shard_map/reduce_scatter | solution.py:132
  875.0 0.7 copy-start.2
  875.0 0.8 copy-start.5
  914.8 57.3 %copy-start.1 = (f32[1024,64]{0,1:T(8,128)S(1)}, f32[1024,64]{0,1:T(8,128)}, u32[]{:S(2)}) copy-start(f32[1024,64]{0,1:T(8,128)} %reduce-scatter.5.cloned.1.call-done) | copy-start | bytes 786436
  917.5 55.7 %copy-start = (f32[8192,64]{0,1:T(8,128)S(1)}, f32[8192,64]{0,1:T(8,128)}, u32[]{:S(2)}) copy-start(f32[8192,64]{0,1:T(8,128)} %all-reduce.9.cloned.1.call-done) | copy-start | bytes 6291460
Sparse Core Ops, SparseCore 0:
  9.9 26.1 all-gather.5
  175.4 86.0 all-reduce.6
  394.7 39.5 reduce-scatter.2
  492.4 24.1 all-gather.3
  656.1 85.4 all-reduce.8
  875.1 39.5 reduce-scatter.4
where the time goes:
time: 1030 us
  other arithmetic  302 us (29%)
  waiting for transfers between devices  203 us (20%)
  matrix products  201 us (20%)
  blocking collectives  160 us (16%)
  local copies, waits for them, and re-layouts  140 us (14%)
  between operations  16.4 us (2%)
    scatter-add x16, other arithmetic, left_turn(): return total + jax.ops.segment_sum(product, row_ids, num_segments=DOC_TILES)  112 us
    scatter-add x16, other arithmetic, right_turn(): jax.ops.segment_sum(product, col_ids, num_segments=TERM_TILES)  112 us
    psum x2, waiting for transfers between devices, per_device(): summed_all, degree_all = lax.psum((summed_part, row_part), 'term')  97.9 us
    dot_general x16, matrix products, left_turn(): jnp.einsum('tij,tjk->tik', block, pieces, preferred_element_type=jnp.floa...  84.7 us
    psum x2, blocking collectives, per_device(): lax.psum((gram_part, along_part, energy_part, volume_part), ('doc', 'term'))  79.6 us
    dot_general x16, matrix products, right_turn(): jnp.einsum('tij,tik->tjk', block, pieces, preferred_element_type=jnp.floa...  70.9 us
    gather x16, local copies, waits for them, and re-layouts, right_turn(): pieces = jnp.take(table, row_ids, axis=0)  59.5 us
    gather x16, local copies, waits for them, and re-layouts, left_turn(): pieces = jnp.take(table, col_ids, axis=0)  59.2 us
  transfers between devices with their start and end apart: 6, of which 6 were waited for; matrix products, arithmetic and copies ran while one was open for 6% of the time, Pallas kernels for 0%

commit v1 on v0

v1 whole, which is shorter than its diff:
```python
import functools

import jax
import jax.numpy as jnp
from jax import lax
from jax.experimental import pallas as pl
from jax.experimental.pallas import tpu as pltpu
from jax.sharding import PartitionSpec as P

CLUSTERS = 64
ITERS = 2
CHUNK = 32
DEG_ROWS = 8

HIGH = lax.Precision.HIGHEST
NT_DIMS = (((1,), (1,)), ((), ()))


def tile_kernel(transpose_tile, with_degree, shard_tiles_in, shard_tiles_out, rows_ref, cols_ref, cnt_ref, tiles_ref, side_ref, out_ref):
    step = pl.program_id(0)
    chunk = tiles_ref.shape[0]
    width = side_ref.shape[1]

    @pl.when(step == 0)
    def _():
        out_ref[...] = jnp.zeros_like(out_ref)

    base = step * chunk
    live = jnp.clip(cnt_ref[0] - base, 0, chunk)
    ones = jnp.ones((DEG_ROWS, tiles_ref.shape[2]), jnp.bfloat16)

    def body(j, carry):
        slot = base + j
        if transpose_tile:
            src, dst = cols_ref[slot], rows_ref[slot]
        else:
            src, dst = rows_ref[slot], cols_ref[slot]
        tile = tiles_ref[j]
        piece = side_ref[src]
        if transpose_tile:
            prod = lax.dot_general(piece, tile, NT_DIMS, preferred_element_type=jnp.float32)
        else:
            prod = jnp.dot(piece, tile, preferred_element_type=jnp.float32)
        out_ref[dst, pl.ds(0, width), :] += prod
        if with_degree:
            if transpose_tile:
                deg = lax.dot_general(ones, tile, NT_DIMS, preferred_element_type=jnp.float32)
            else:
                deg = jnp.dot(ones, tile, preferred_element_type=jnp.float32)
            out_ref[dst, pl.ds(width, DEG_ROWS), :] += deg
        return carry

    lax.fori_loop(0, live, body, 0)


def tile_pass(tiles, rows, cols, count, side, transpose_tile, with_degree):
    slots, edge, _ = tiles.shape
    n_tiles, width, _ = side.shape
    chunk = min(CHUNK, slots)
    steps = slots // chunk
    out_rows = width + (DEG_ROWS if with_degree else 0)
    kernel = functools.partial(tile_kernel, transpose_tile, with_degree, None, None)

    def tile_map(i, rows_ref, cols_ref, cnt_ref):
        return (jnp.minimum(i, jnp.maximum(cnt_ref[0] - 1, 0) // chunk), 0, 0)

    def whole_map(i, rows_ref, cols_ref, cnt_ref):
        return (0, 0, 0)

    flops = 2 * slots * edge * edge * out_rows
    cost = pl.CostEstimate(
        flops=flops,
        transcendentals=0,
        bytes_accessed=tiles.size * 2 + side.size * 2 + n_tiles * out_rows * edge * 4,
    )
    return pl.pallas_call(
        kernel,
        out_shape=jax.ShapeDtypeStruct((n_tiles, out_rows, edge), jnp.float32),
        grid_spec=pltpu.PrefetchScalarGridSpec(
            num_scalar_prefetch=3,
            grid=(steps,),
            in_specs=[
                pl.BlockSpec((chunk, edge, edge), tile_map),
                pl.BlockSpec((n_tiles, width, edge), whole_map),
            ],
            out_specs=pl.BlockSpec((n_tiles, out_rows, edge), whole_map),
        ),
        compiler_params=pltpu.CompilerParams(dimension_semantics=("arbitrary",)),
        cost_estimate=cost,
    )(rows, cols, count, tiles, side)


def per_device(tiles, tile_rows, tile_cols, tile_count, start_block, doc_cluster, term_cluster):
    local_tiles = tiles[0, 0]
    rows = tile_rows[0, 0]
    cols = tile_cols[0, 0]
    count = tile_count[0, 0].reshape(1)
    edge = local_tiles.shape[1]
    start_rows = start_block[0]
    width_k = start_rows.shape[1]
    term_tiles_own = start_rows.shape[0] // edge
    start_t = start_rows.reshape(term_tiles_own, edge, width_k).transpose(0, 2, 1)
    doc_labels = doc_cluster[0].reshape(-1, edge)
    term_labels = term_cluster[0].reshape(-1, edge)
    clusters = jnp.arange(CLUSTERS, dtype=jnp.int32)

    weights = start_t
    basis = None
    doc_degree = None
    term_degree = None
    root = None
    summed_own = None
    energy = None
    volume = None
    for step in range(ITERS):
        first = step == 0
        w_all = lax.all_gather(weights, "doc", axis=0, tiled=True)
        left = tile_pass(local_tiles, rows, cols, count, w_all, True, first)
        left_own = lax.psum_scatter(left, "term", scatter_dimension=0, tiled=True)
        summed_own = left_own[:, :width_k, :]
        if first:
            doc_degree = left_own[:, width_k, :]
        quotient = (summed_own / doc_degree[:, None, :]).astype(jnp.bfloat16)
        q_all = lax.all_gather(quotient, "term", axis=0, tiled=True)
        right = tile_pass(local_tiles, rows, cols, count, q_all, False, first)
        right_own = lax.psum_scatter(right, "doc", scatter_dimension=0, tiled=True)
        if first:
            term_degree = right_own[:, width_k, :]
            root = jnp.sqrt(term_degree)
        raw = right_own[:, :width_k, :] / root[:, None, :]
        previous = root[:, None, :] * start_t.astype(jnp.float32) if first else basis
        gram_part = jnp.einsum("tki,tli->kl", raw, raw, precision=HIGH)
        along_part = jnp.einsum("tki,ti->k", raw, root, precision=HIGH)
        energy_part = jnp.sum(previous * raw, axis=(0, 2))
        volume_part = jnp.sum(term_degree)
        gram_matrix, along, energy, volume = lax.psum(
            (gram_part, along_part, energy_part, volume_part), ("doc", "term")
        )
        lower = jnp.linalg.cholesky(gram_matrix - jnp.outer(along, along) / volume)
        projected = raw - root[:, None, :] * (along / volume)[None, :, None]
        flat = projected.transpose(1, 0, 2).reshape(width_k, -1)
        solved = jax.scipy.linalg.solve_triangular(lower, flat, lower=True)
        basis = solved.reshape(width_k, term_tiles_own, edge).transpose(1, 0, 2)
        weights = (basis / root[:, None, :]).astype(jnp.bfloat16)

    scale = jnp.sqrt(volume)
    column_scale = scale * lax.rsqrt(energy)
    doc_embed = summed_own / doc_degree[:, None, :] * column_scale[None, :, None]
    term_embed = scale * basis / root[:, None, :]
    doc_onehot = (doc_labels[:, :, None] == clusters).astype(jnp.float32)
    term_onehot = (term_labels[:, :, None] == clusters).astype(jnp.float32)
    center_part = jnp.einsum("tki,tij->kj", doc_embed, doc_onehot, precision=HIGH) + jnp.einsum(
        "tki,tij->kj", term_embed, term_onehot, precision=HIGH
    )
    count_part = jnp.sum(doc_onehot, axis=(0, 1)) + jnp.sum(term_onehot, axis=(0, 1))
    center_sums, counts = lax.psum((center_part, count_part), ("doc", "term"))
    centers = center_sums / counts[None, :]
    center_norm = jnp.sum(centers * centers, axis=0)

    def distances(embed):
        near = jnp.einsum("tki,kj->tij", embed, centers, precision=HIGH)
        norm = jnp.sum(embed * embed, axis=1)
        dist = (norm[:, :, None] - 2.0 * near + center_norm[None, None, :]) / width_k
        return dist.reshape(-1, CLUSTERS)

    return (distances(doc_embed)[None], distances(term_embed)[None])


def solution(mesh):
    placed = (
        P("doc", "term", None, None, None),
        P("doc", "term", None),
        P("doc", "term", None),
        P("doc", "term"),
        P("term", "doc", None),
        P("doc", "term"),
        P("term", "doc"),
    )
    return jax.shard_map(
        per_device,
        mesh=mesh,
        in_specs=placed,
        out_specs=(P("doc", "term", None), P("term", "doc", None)),
        check_vma=False,
    )
```

time: 1030 us -> 812 us (0.79)
  waiting for transfers between devices: 203 us -> 496 us
  other arithmetic: 302 us -> 34.5 us
  matrix products: 201 us -> 10.1 us
  local copies, waits for them, and re-layouts: 140 us -> 4.7 us
  Pallas kernels: 0 us -> 86.3 us
    reduce_scatter x2 -> x4, waiting for transfers between devices: 52.8 us -> 390 us  [the longest x2 206 us: per_device(): left_own = lax.psum_scatter(left, 'term', scatter_dimension=0, tiled=True)]
    scatter-add x48 -> x0, other arithmetic: 240 us -> none  [the longest x16 112 us: left_turn(): return total + jax.ops.segment_sum(product, row_ids, num_segments=DOC_TILES)]
    dot_general x56 -> x8, matrix products: 199 us -> 7.29 us  [the longest x2 2.88 us: per_device(): gram_part = jnp.einsum('tki,tli->kl', raw, raw, precision=HIGH)]
    gather x32 -> x0, local copies, waits for them, and re-layouts: 119 us -> none  [the longest x16 59.5 us: right_turn(): pieces = jnp.take(table, row_ids, axis=0)]
    psum x2 -> x0, waiting for transfers between devices: 97.9 us -> none  [per_device(): summed_all, degree_all = lax.psum((summed_part, row_part), 'term')]
    pallas_call x0 -> x4, Pallas kernels: none -> 86.3 us  [tile_pass(): pl.pallas_call(kernel, out_shape=jax.ShapeDtypeStruct((n_tiles, out_rows,...]
    all_gather x2 -> x4, waiting for transfers between devices: 51.8 us -> 107 us  [the longest x2 55.1 us: per_device(): q_all = lax.all_gather(quotient, 'term', axis=0, tiled=True)]
    psum x2 -> x3, blocking collectives: 79.6 us -> 120 us  [per_device(): lax.psum((gram_part, along_part, energy_part, volume_part), ('doc', 'term'))]
  transfers between devices with their start and end apart: 6 -> 8, of which waited for: 6 -> 8; matrix products, arithmetic and copies ran while one was open for 6% -> 0% of each run, Pallas kernels for 0% -> 0%
where the time goes in v1:
time: 812 us; the launch traced here: 808 us
  waiting for transfers between devices  496 us (61%)
  blocking collectives  160 us (20%)
  Pallas kernels  86.3 us (11%)
  other arithmetic  34.5 us (4%)
  between operations  15.6 us (2%)
  matrix products  10.1 us (1%)
    reduce_scatter x2, waiting for transfers between devices, per_device(): left_own = lax.psum_scatter(left, 'term', scatter_dimension=0, tiled=True)  206 us
    reduce_scatter x2, waiting for transfers between devices, per_device(): right_own = lax.psum_scatter(right, 'doc', scatter_dimension=0, tiled=True)  184 us
    psum x3, blocking collectives, per_device(): lax.psum((gram_part, along_part, energy_part, volume_part), ('doc', 'term'))  120 us
    pallas_call x4, Pallas kernels, tile_pass(): pl.pallas_call(kernel, out_shape=jax.ShapeDtypeStruct((n_tiles, out_rows,...  86.3 us
    all_gather x2, waiting for transfers between devices, per_device(): q_all = lax.all_gather(quotient, 'term', axis=0, tiled=True)  55.1 us
    all_gather x2, waiting for transfers between devices, per_device(): w_all = lax.all_gather(weights, 'doc', axis=0, tiled=True)  51.5 us
    psum x1, blocking collectives, per_device(): center_sums, counts = lax.psum((center_part, count_part), ('doc', 'term'))  39.7 us
  transfers between devices with their start and end apart: 8, of which 8 were waited for; matrix products, arithmetic and copies ran while one was open for 0% of the time, Pallas kernels for 0%

profile of v1, /device:TPU:0, one launch (start us, length us, event | category | flops | bytes accessed | tf_op | source)
XLA Modules:
  0.0 808.1 jit_solution(1323986266510681473)
XLA Ops:
  7.2 0.9 copy.55
  8.1 0.7 copy.29
  9.5 27.1 %all-gather.5.cloned.1.call-done.side_ref = bf16[64,64,128]{2,1,0:T(8,128)(2,1)} async-done(((bf16[8,64,128]{2,1,0:T(8,128)(2,1)}), bf16[64,64,128]{2,1,0:T(8,128)(2,1)}) %all-gather.5.cloned.1.call-update) | async-done | bytes 1048592 | tf_op jit(solution)/shard_map/all_gather | solution.py:117
  36.7 22.9 %shard_map.86 = f32[64,72,128]{2,1,0:T(8,128)} custom-call(s32[512]{0:T(512)} %bitcast.143, s32[512]{0:T(512)} %bitcast.147, s32[1]{0:T(128)} %bitcast.118.cnt_ref, bf16[512,128,128]{2,1,0:T(8,128)(2,1)} %bitcast.122, bf16[64,64,128]{2,1,0:T(8,128)(2,1)} %all-gather.5.cloned.1.call-done.side_ref), custom_call_target="tpu_custom_call" | custom-call | flops 1207959552 | bytes 20185088 | tf_op jit(solution)/shard_map/pallas_call | solution.py:76
  59.7 106.1 %reduce-scatter.5.cloned.1.call-done = f32[16,72,128]{2,1,0:T(8,128)} async-done(((f32[64,72,128]{2,1,0:T(8,128)}), f32[16,72,128]{2,1,0:T(8,128)}) %reduce-scatter.5.cloned.1.call-update) | async-done | bytes 589840 | tf_op jit(solution)/shard_map/reduce_scatter | solution.py:119
  165.8 0.8 slice.25
  166.7 1.8 fusion.8
  168.5 27.5 %all-gather.7.cloned.1.call-done.side_ref = bf16[64,64,128]{2,1,0:T(8,128)(2,1)} async-done(((bf16[16,64,128]{2,1,0:T(8,128)(2,1)}), bf16[64,64,128]{2,1,0:T(8,128)(2,1)}) %all-gather.7.cloned.1.call-update) | async-done | bytes 1048592 | tf_op jit(solution)/shard_map/all_gather | solution.py:124
  196.1 20.9 %shard_map.87 = f32[64,72,128]{2,1,0:T(8,128)} custom-call(s32[512]{0:T(512)} %bitcast.144, s32[512]{0:T(512)} %bitcast.148, s32[1]{0:T(128)} %bitcast.119.cnt_ref, bf16[512,128,128]{2,1,0:T(8,128)(2,1)} %bitcast.123, bf16[64,64,128]{2,1,0:T(8,128)(2,1)} %all-gather.7.cloned.1.call-done.side_ref), custom_call_target="tpu_custom_call" | custom-call | flops 1207959552 | bytes 20185088 | tf_op jit(solution)/shard_map/pallas_call | solution.py:76
  217.1 94.0 %reduce-scatter.7.cloned.1.call-done = f32[8,72,128]{2,1,0:T(8,128)} async-done(((f32[64,72,128]{2,1,0:T(8,128)}), f32[8,72,128]{2,1,0:T(8,128)}) %reduce-scatter.7.cloned.1.call-update) | async-done | bytes 294928 | tf_op jit(solution)/shard_map/reduce_scatter | solution.py:126
  311.0 1.4 slice_reduce_fusion
  312.4 1.4 convolution_bitcast_fusion.4
  313.8 1.2 convolution_bitcast_fusion.6
  315.0 39.8 %all-reduce.2 = (f32[64]{0:T(128)S(1)}, f32[]{:T(128)}, f32[64,64]{0,1:T(8,128)S(1)}) all-reduce(f32[64]{0:T(128)S(1)} %convolution_bitcast_fusion.6, f32[]{:T(128)} %get-tuple-element.13, f32[64,64]{0,1:T(8,128)S(1)} %convolution_bitcast_fusion.4), channel_id=1, replica_groups=mesh['doc'=8,'term'=4] {'doc','term'}, use_global_device_ids=true, to_apply=%region_3.0 | all-reduce | flops 4161 | bytes 33288 | tf_op jit(solution)/shard_map/psum | solution.py:136
  354.8 0.6 broadcast_divide_fusion.4
  355.5 0.7 divide_subtract_fusion.1
  356.2 0.7 fusion.31
  357.0 5.8 cholesky.44
  362.8 0.6 compare_reduce_fusion.1
  363.5 0.7 fusion.24
  364.1 4.9 custom-call.6
  369.0 1.4 convolution_bitcast_fusion
  370.5 0.7 fusion.18
  371.2 24.3 %all-gather.9.cloned.1.call-done.side_ref = bf16[64,64,128]{2,1,0:T(8,128)(2,1)} async-done(((bf16[8,64,128]{2,1,0:T(8,128)(2,1)}), bf16[64,64,128]{2,1,0:T(8,128)(2,1)}) %all-gather.9.cloned.1.call-update) | async-done | bytes 1048592 | tf_op jit(solution)/shard_map/all_gather | solution.py:117
  395.6 22.2 %shard_map.88 = f32[64,64,128]{2,1,0:T(8,128)} custom-call(s32[512]{0:T(512)} %bitcast.145, s32[512]{0:T(512)} %bitcast.149, s32[1]{0:T(128)} %bitcast.120.cnt_ref, bf16[512,128,128]{2,1,0:T(8,128)(2,1)} %bitcast.124, bf16[64,64,128]{2,1,0:T(8,128)(2,1)} %all-gather.9.cloned.1.call-done.side_ref), custom_call_target="tpu_custom_call" | custom-call | flops 1073741824 | bytes 19922944 | tf_op jit(solution)/shard_map/pallas_call | solution.py:76
  417.8 99.9 %reduce-scatter.9.cloned.1.call-done = f32[16,64,128]{2,1,0:T(8,128)} async-done(((f32[64,64,128]{2,1,0:T(8,128)}), f32[16,64,128]{2,1,0:T(8,128)}) %reduce-scatter.9.cloned.1.call-update) | async-done | bytes 524304 | tf_op jit(solution)/shard_map/reduce_scatter | solution.py:119
  517.7 1.8 fusion.36
  519.6 27.6 %all-gather.11.cloned.1.call-done.side_ref = bf16[64,64,128]{2,1,0:T(8,128)(2,1)} async-done(((bf16[16,64,128]{2,1,0:T(8,128)(2,1)}), bf16[64,64,128]{2,1,0:T(8,128)(2,1)}) %all-gather.11.cloned.1.call-update) | async-done | bytes 1048592 | tf_op jit(solution)/shard_map/all_gather | solution.py:124
  547.2 20.3 %shard_map.89 = f32[64,64,128]{2,1,0:T(8,128)} custom-call(s32[512]{0:T(512)} %bitcast.146, s32[512]{0:T(512)} %bitcast.150, s32[1]{0:T(128)} %bitcast.121.cnt_ref, bf16[512,128,128]{2,1,0:T(8,128)(2,1)} %bitcast.125, bf16[64,64,128]{2,1,0:T(8,128)(2,1)} %all-gather.11.cloned.1.call-done.side_ref), custom_call_target="tpu_custom_call" | custom-call | flops 1073741824 | bytes 19922944 | tf_op jit(solution)/shard_map/pallas_call | solution.py:76
  568.5 89.6 %reduce-scatter.11.cloned.1.call-done = f32[8,64,128]{2,1,0:T(8,128)} async-done(((f32[64,64,128]{2,1,0:T(8,128)}), f32[8,64,128]{2,1,0:T(8,128)}) %reduce-scatter.11.cloned.1.call-update) | async-done | bytes 262160 | tf_op jit(solution)/shard_map/reduce_scatter | solution.py:126
  658.1 1.5 convolution_bitcast_fusion.3
  659.6 1.2 convolution_bitcast_fusion.5
  660.8 39.7 %all-reduce.1 = (f32[64]{0:T(128)S(1)}, f32[64,64]{0,1:T(8,128)S(1)}) all-reduce(f32[64]{0:T(128)S(1)} %convolution_bitcast_fusion.5, f32[64,64]{0,1:T(8,128)S(1)} %convolution_bitcast_fusion.3), channel_id=1, replica_groups=mesh['doc'=8,'term'=4] {'doc','term'}, use_global_device_ids=true, to_apply=%region_14.0 | all-reduce | flops 4160 | bytes 33280 | tf_op jit(solution)/shard_map/psum | solution.py:136
  700.5 0.6 broadcast_divide_fusion.3
  701.2 0.7 divide_subtract_fusion
  702.0 0.7 fusion.29
  702.7 5.8 cholesky.55
  708.6 0.6 compare_reduce_fusion
  709.2 0.7 fusion.25
  709.9 4.9 custom-call.7
  714.8 1.4 fusion.5
  716.6 41.0 %psum.62 = f32[64]{0:T(128)S(1)} all-reduce(f32[64]{0:T(128)S(1)} %get-tuple-element.5), channel_id=1, replica_groups=mesh['doc'=8,'term'=4] {'doc','term'}, use_global_device_ids=true, to_apply=%region_11.0 | all-reduce | flops 64 | bytes 512 | tf_op jit(solution)/shard_map/psum | solution.py:136
  757.6 0.5 fusion.7
  758.1 39.7 %all-reduce = (f32[64,64]{1,0:T(8,128)S(1)}, f32[64]{0:T(128)S(1)}) all-reduce(f32[64,64]{1,0:T(8,128)S(1)} %fusion.7, f32[64]{0:T(128)S(1)} %add.57), channel_id=1, replica_groups=mesh['doc'=8,'term'=4] {'doc','term'}, use_global_device_ids=true, to_apply=%region_15.0 | all-reduce | flops 4160 | bytes 33280 | tf_op jit(solution)/shard_map/psum | solution.py:156
  797.8 0.4 fusion.6
  798.4 0.7 broadcast_in_dim_reshape.7
  799.3 0.7 fusion.2
  800.4 0.9 broadcast_in_dim_reshape.6
  (38 shorter events, 2.0 us)
Async XLA Ops:
  7.2 29.5 %all-gather.5.cloned.1.call-start = ((), (), s32[]{:S(2)}) async-start(), calls=%async_computation.4 | async-start | bytes 1179648 | tf_op jit(solution)/shard_map/all_gather | solution.py:117
  8.8 157.0 %reduce-scatter.5.cloned.1.call-start = ((), (), s32[]{:S(2)}) async-start(), calls=%async_computation.5 | async-start | bytes 2949120 | tf_op jit(solution)/shard_map/reduce_scatter | solution.py:119
  59.6 136.4 %all-gather.7.cloned.1.call-start = ((), (), s32[]{:S(2)}) async-start(), calls=%async_computation.6 | async-start | bytes 1310720 | tf_op jit(solution)/shard_map/all_gather | solution.py:124
  168.5 142.5 %reduce-scatter.7.cloned.1.call-start = ((), (), s32[]{:S(2)}) async-start(), calls=%async_computation.7 | async-start | bytes 2654208 | tf_op jit(solution)/shard_map/reduce_scatter | solution.py:126
  217.0 178.5 %all-gather.9.cloned.1.call-start = ((), (), s32[]{:S(2)}) async-start(), calls=%async_computation.8 | async-start | bytes 1179648 | tf_op jit(solution)/shard_map/all_gather | solution.py:117
  371.2 146.5 %reduce-scatter.9.cloned.1.call-start = ((), (), s32[]{:S(2)}) async-start(), calls=%async_computation.9 | async-start | bytes 2621440 | tf_op jit(solution)/shard_map/reduce_scatter | solution.py:119
  417.8 129.4 %all-gather.11.cloned.1.call-start = ((), (), s32[]{:S(2)}) async-start(), calls=%async_computation.10 | async-start | bytes 1310720 | tf_op jit(solution)/shard_map/all_gather | solution.py:124
  519.5 138.6 %reduce-scatter.11.cloned.1.call-start = ((), (), s32[]{:S(2)}) async-start(), calls=%async_computation.11 | async-start | bytes 2359296 | tf_op jit(solution)/shard_map/reduce_scatter | solution.py:126
  547.2 20.3 %copy-start.3 = (s32[1,1024]{1,0:T(1,128)S(1)}, s32[1,1024]{1,0:T(1,128)}, u32[]{:S(2)}) copy-start(s32[1,1024]{1,0:T(1,128)} %param.16) | copy-start | bytes 12292
  547.2 20.5 %copy-start.2 = (s32[1,2048]{1,0:T(1,128)S(1)}, s32[1,2048]{1,0:T(1,128)}, u32[]{:S(2)}) copy-start(s32[1,2048]{1,0:T(1,128)} %param.15) | copy-start | bytes 24580
  568.5 189.1 %copy-start = (f32[16,64,128]{2,1,0:T(8,128)S(1)}, f32[16,64,128]{2,1,0:T(8,128)}, u32[]{:S(2)}) copy-start(f32[16,64,128]{2,1,0:T(8,128)} %reduce-scatter.9.cloned.1.call-done) | copy-start | bytes 1572868
  658.1 58.3 %copy-start.1 = (f32[8,64,128]{2,1,0:T(8,128)S(1)}, f32[8,64,128]{2,1,0:T(8,128)}, u32[]{:S(2)}) copy-start(f32[8,64,128]{2,1,0:T(8,128)} %reduce-scatter.11.cloned.1.call-done) | copy-start | bytes 786436
Sparse Core Ops, SparseCore 0:
  10.5 26.1 all-gather.4
  59.8 106.0 reduce-scatter.4
  168.6 27.4 all-gather.6
  217.1 93.8 reduce-scatter.6
  371.3 24.2 all-gather.8
  417.9 99.7 reduce-scatter.8
  519.9 27.2 all-gather.10
  567.6 90.4 reduce-scatter.10

commit v2 on v1

--- a/solution.py
+++ b/solution.py
@@ -9,14 +9,15 @@
 
 CLUSTERS = 64
 ITERS = 2
-CHUNK = 32
+CHUNK = 64
+GROUP = 4
 DEG_ROWS = 8
 
 HIGH = lax.Precision.HIGHEST
 NT_DIMS = (((1,), (1,)), ((), ()))
 
 
-def tile_kernel(transpose_tile, with_degree, shard_tiles_in, shard_tiles_out, rows_ref, cols_ref, cnt_ref, tiles_ref, side_ref, out_ref):
+def tile_kernel(transpose_tile, with_degree, group, rows_ref, cols_ref, cnt_ref, tiles_ref, side_ref, out_ref):
     step = pl.program_id(0)
     chunk = tiles_ref.shape[0]
     width = side_ref.shape[1]
@@ -25,32 +26,37 @@
     def _():
         out_ref[...] = jnp.zeros_like(out_ref)
 
+    count = cnt_ref[0]
     base = step * chunk
-    live = jnp.clip(cnt_ref[0] - base, 0, chunk)
+    live = jnp.clip(count - base, 0, chunk)
     ones = jnp.ones((DEG_ROWS, tiles_ref.shape[2]), jnp.bfloat16)
 
-    def body(j, carry):
-        slot = base + j
+    def product(lhs, tile):
         if transpose_tile:
-            src, dst = cols_ref[slot], rows_ref[slot]
-        else:
-            src, dst = rows_ref[slot], cols_ref[slot]
-        tile = tiles_ref[j]
-        piece = side_ref[src]
-        if transpose_tile:
-            prod = lax.dot_general(piece, tile, NT_DIMS, preferred_element_type=jnp.float32)
-        else:
-            prod = jnp.dot(piece, tile, preferred_element_type=jnp.float32)
-        out_ref[dst, pl.ds(0, width), :] += prod
-        if with_degree:
+            return lax.dot_general(lhs, tile, NT_DIMS, preferred_element_type=jnp.float32)
+        return jnp.dot(lhs, tile, preferred_element_type=jnp.float32)
+
+    def body(g, carry):
+        results = []
+        for u in range(group):
+            j = g * group + u
+            slot = base + j
             if transpose_tile:
-                deg = lax.dot_general(ones, tile, NT_DIMS, preferred_element_type=jnp.float32)
+                src, dst = cols_ref[slot], rows_ref[slot]
             else:
-                deg = jnp.dot(ones, tile, preferred_element_type=jnp.float32)
-            out_ref[dst, pl.ds(width, DEG_ROWS), :] += deg
+                src, dst = rows_ref[slot], cols_ref[slot]
+            tile = tiles_ref[j]
+            keep = slot < count
+            prod = jnp.where(keep, product(side_ref[src], tile), 0.0)
+            deg = jnp.where(keep, product(ones, tile), 0.0) if with_degree else None
+            results.append((dst, prod, deg))
+        for dst, prod, deg in results:
+            out_ref[dst, pl.ds(0, width), :] += prod
+            if with_degree:
+                out_ref[dst, pl.ds(width, DEG_ROWS), :] += deg
         return carry
 
-    lax.fori_loop(0, live, body, 0)
+    lax.fori_loop(0, (live + group - 1) // group, body, 0)
 
 
 def tile_pass(tiles, rows, cols, count, side, transpose_tile, with_degree):
@@ -59,7 +65,7 @@
     chunk = min(CHUNK, slots)
     steps = slots // chunk
     out_rows = width + (DEG_ROWS if with_degree else 0)
-    kernel = functools.partial(tile_kernel, transpose_tile, with_degree, None, None)
+    kernel = functools.partial(tile_kernel, transpose_tile, with_degree, GROUP)
 
     def tile_map(i, rows_ref, cols_ref, cnt_ref):
         return (jnp.minimum(i, jnp.maximum(cnt_ref[0] - 1, 0) // chunk), 0, 0)
@@ -134,7 +140,7 @@
         energy_part = jnp.sum(previous * raw, axis=(0, 2))
         volume_part = jnp.sum(term_degree)
         gram_matrix, along, energy, volume = lax.psum(
-            (gram_part, along_part, energy_part, volume_part), ("doc", "term")
+            lax.psum((gram_part, along_part, energy_part, volume_part), "term"), "doc"
         )
         lower = jnp.linalg.cholesky(gram_matrix - jnp.outer(along, along) / volume)
         projected = raw - root[:, None, :] * (along / volume)[None, :, None]
@@ -153,7 +159,11 @@
         "tki,tij->kj", term_embed, term_onehot, precision=HIGH
     )
     count_part = jnp.sum(doc_onehot, axis=(0, 1)) + jnp.sum(term_onehot, axis=(0, 1))
-    center_sums, counts = lax.psum((center_part, count_part), ("doc", "term"))
+    packed = jnp.concatenate([center_part.reshape(-1), count_part])
+    gathered = lax.all_gather(packed, ("doc", "term"), axis=0, tiled=False)
+    totals = jnp.sum(gathered, axis=0)
+    center_sums = totals[: center_part.size].reshape(center_part.shape)
+    counts = totals[center_part.size :]
     centers = center_sums / counts[None, :]
     center_norm = jnp.sum(centers * centers, axis=0)
 

time: 812 us -> 691 us (0.85)
  blocking collectives: 160 us -> 106 us
  Pallas kernels: 86.3 us -> 41.6 us
  waiting for transfers between devices: 496 us -> 477 us
    unnamed x8 -> x10, waiting for transfers between devices: 0.13 us -> 126 us
    reduce_scatter x2, waiting for transfers between devices: 206 us -> 135 us  [per_device(): left_own = lax.psum_scatter(left, 'term', scatter_dimension=0, tiled=True)]
    reduce_scatter x2, waiting for transfers between devices: 184 us -> 113 us  [per_device(): right_own = lax.psum_scatter(right, 'doc', scatter_dimension=0, tiled=True)]
    psum x4 -> x6, blocking collectives: 160 us -> 106 us  [the longest x3 58.1 us: per_device(): lax.psum(lax.psum((gram_part, along_part, energy_part, volume_part), 'ter...]
    pallas_call x4, Pallas kernels: 86.3 us -> 41.6 us  [tile_pass(): pl.pallas_call(kernel, out_shape=jax.ShapeDtypeStruct((n_tiles, out_rows,...]
  transfers between devices with their start and end apart: 8 -> 9, of which waited for: 8 -> 9; matrix products, arithmetic and copies ran while one was open for 0% -> 0% of each run, Pallas kernels for 0% -> 0%
where the time goes in v2:
time: 691 us
  waiting for transfers between devices  477 us (69%)
  blocking collectives  106 us (15%)
  Pallas kernels  41.6 us (6%)
  other arithmetic  34.4 us (5%)
  between operations  15.3 us (2%)
  matrix products  9.14 us (1%)
    reduce_scatter x2, waiting for transfers between devices, per_device(): left_own = lax.psum_scatter(left, 'term', scatter_dimension=0, tiled=True)  135 us
    unnamed x10, waiting for transfers between devices  126 us
    reduce_scatter x2, waiting for transfers between devices, per_device(): right_own = lax.psum_scatter(right, 'doc', scatter_dimension=0, tiled=True)  113 us
    psum x3, blocking collectives, per_device(): lax.psum(lax.psum((gram_part, along_part, energy_part, volume_part), 'ter...  58.1 us
    all_gather x2, waiting for transfers between devices, per_device(): q_all = lax.all_gather(quotient, 'term', axis=0, tiled=True)  55.1 us
    psum x3, blocking collectives, per_device(): lax.psum((gram_part, along_part, energy_part, volume_part), 'term')  48.2 us
    all_gather x2, waiting for transfers between devices, per_device(): w_all = lax.all_gather(weights, 'doc', axis=0, tiled=True)  47 us
    pallas_call x4, Pallas kernels, tile_pass(): pl.pallas_call(kernel, out_shape=jax.ShapeDtypeStruct((n_tiles, out_rows,...  41.6 us
  transfers between devices with their start and end apart: 9, of which 9 were waited for; matrix products, arithmetic and copies ran while one was open for 0% of the time, Pallas kernels for 0%

profile of v2, /device:TPU:0, one launch (start us, length us, event | category | flops | bytes accessed | tf_op | source)
XLA Modules:
  0.0 690.8 jit_solution(7044116070311960933)
XLA Ops:
  7.2 0.9 copy.66
  8.1 0.7 copy.40
  9.5 27.1 %all-gather.6.cloned.1.call-done.side_ref = bf16[64,64,128]{2,1,0:T(8,128)(2,1)} async-done(((bf16[8,64,128]{2,1,0:T(8,128)(2,1)}), bf16[64,64,128]{2,1,0:T(8,128)(2,1)}) %all-gather.6.cloned.1.call-update) | async-done | bytes 1048592 | tf_op jit(solution)/shard_map/all_gather | solution.py:123
  36.7 11.9 %shard_map.86 = f32[64,72,128]{2,1,0:T(8,128)} custom-call(s32[512]{0:T(512)} %bitcast.143, s32[512]{0:T(512)} %bitcast.147, s32[1]{0:T(128)} %bitcast.118.cnt_ref, bf16[512,128,128]{2,1,0:T(8,128)(2,1)} %bitcast.122, bf16[64,64,128]{2,1,0:T(8,128)(2,1)} %all-gather.6.cloned.1.call-done.side_ref), custom_call_target="tpu_custom_call" | custom-call | flops 1207959552 | bytes 20185088 | tf_op jit(solution)/shard_map/pallas_call | solution.py:82
  48.7 72.4 %reduce-scatter.5.cloned.1.call-done = f32[16,72,128]{2,1,0:T(8,128)} async-done(((f32[64,72,128]{2,1,0:T(8,128)}), f32[16,72,128]{2,1,0:T(8,128)}) %reduce-scatter.5.cloned.1.call-update) | async-done | bytes 589840 | tf_op jit(solution)/shard_map/reduce_scatter | solution.py:125
  121.1 0.8 slice.41
  121.9 1.8 fusion.8
  123.8 27.5 %all-gather.8.cloned.1.call-done.side_ref = bf16[64,64,128]{2,1,0:T(8,128)(2,1)} async-done(((bf16[16,64,128]{2,1,0:T(8,128)(2,1)}), bf16[64,64,128]{2,1,0:T(8,128)(2,1)}) %all-gather.8.cloned.1.call-update) | async-done | bytes 1048592 | tf_op jit(solution)/shard_map/all_gather | solution.py:130
  151.3 10.0 %shard_map.87 = f32[64,72,128]{2,1,0:T(8,128)} custom-call(s32[512]{0:T(512)} %bitcast.144, s32[512]{0:T(512)} %bitcast.148, s32[1]{0:T(128)} %bitcast.119.cnt_ref, bf16[512,128,128]{2,1,0:T(8,128)(2,1)} %bitcast.123, bf16[64,64,128]{2,1,0:T(8,128)(2,1)} %all-gather.8.cloned.1.call-done.side_ref), custom_call_target="tpu_custom_call" | custom-call | flops 1207959552 | bytes 20185088 | tf_op jit(solution)/shard_map/pallas_call | solution.py:82
  161.4 58.8 %reduce-scatter.7.cloned.1.call-done = f32[8,72,128]{2,1,0:T(8,128)} async-done(((f32[64,72,128]{2,1,0:T(8,128)}), f32[8,72,128]{2,1,0:T(8,128)}) %reduce-scatter.7.cloned.1.call-update) | async-done | bytes 294928 | tf_op jit(solution)/shard_map/reduce_scatter | solution.py:132
  220.2 1.4 slice_reduce_fusion
  221.6 1.4 convolution_bitcast_fusion.4
  223.0 1.2 convolution_bitcast_fusion.6
  224.3 20.4 %all-reduce.4 = (f32[64]{0:T(128)S(1)}, f32[]{:T(128)}, f32[64,64]{0,1:T(8,128)S(1)}) all-reduce(f32[64]{0:T(128)S(1)} %convolution_bitcast_fusion.6, f32[]{:T(128)} %get-tuple-element.16, f32[64,64]{0,1:T(8,128)S(1)} %convolution_bitcast_fusion.4), channel_id=1, replica_groups=mesh['doc'=8,'term'=4] {'term'}, use_global_device_ids=true, to_apply=%region_4.0 | all-reduce | flops 4161 | bytes 33288 | tf_op jit(solution)/shard_map/psum | solution.py:143
  244.7 23.7 %all-reduce.2 = (f32[64]{0:T(128)S(1)}, f32[]{:T(128)}, f32[64,64]{0,1:T(8,128)S(1)}) all-reduce(f32[64]{0:T(128)S(1)} %get-tuple-element.13, f32[]{:T(128)} %get-tuple-element.14, f32[64,64]{0,1:T(8,128)S(1)} %get-tuple-element.15), channel_id=1, replica_groups=mesh['doc'=8,'term'=4] {'doc'}, use_global_device_ids=true, to_apply=%region_5.0 | all-reduce | flops 4161 | bytes 33288 | tf_op jit(solution)/shard_map/psum | solution.py:142
  268.9 0.6 divide_subtract_fusion.1
  269.6 0.6 fusion.31
  270.3 5.8 cholesky.44
  276.2 0.6 compare_reduce_fusion.1
  276.8 0.7 fusion.24
  277.5 4.9 custom-call.6
  282.9 0.7 fusion.18
  283.6 19.8 %all-gather.10.cloned.1.call-done.side_ref = bf16[64,64,128]{2,1,0:T(8,128)(2,1)} async-done(((bf16[8,64,128]{2,1,0:T(8,128)(2,1)}), bf16[64,64,128]{2,1,0:T(8,128)(2,1)}) %all-gather.10.cloned.1.call-update) | async-done | bytes 1048592 | tf_op jit(solution)/shard_map/all_gather | solution.py:123
  303.4 10.3 %shard_map.88 = f32[64,64,128]{2,1,0:T(8,128)} custom-call(s32[512]{0:T(512)} %bitcast.145, s32[512]{0:T(512)} %bitcast.149, s32[1]{0:T(128)} %bitcast.120.cnt_ref, bf16[512,128,128]{2,1,0:T(8,128)(2,1)} %bitcast.124, bf16[64,64,128]{2,1,0:T(8,128)(2,1)} %all-gather.10.cloned.1.call-done.side_ref), custom_call_target="tpu_custom_call" | custom-call | flops 1073741824 | bytes 19922944 | tf_op jit(solution)/shard_map/pallas_call | solution.py:82
  313.8 63.1 %reduce-scatter.9.cloned.1.call-done = f32[16,64,128]{2,1,0:T(8,128)} async-done(((f32[64,64,128]{2,1,0:T(8,128)}), f32[16,64,128]{2,1,0:T(8,128)}) %reduce-scatter.9.cloned.1.call-update) | async-done | bytes 524304 | tf_op jit(solution)/shard_map/reduce_scatter | solution.py:125
  376.9 1.8 fusion.36
  378.8 27.5 %all-gather.12.cloned.1.call-done.side_ref = bf16[64,64,128]{2,1,0:T(8,128)(2,1)} async-done(((bf16[16,64,128]{2,1,0:T(8,128)(2,1)}), bf16[64,64,128]{2,1,0:T(8,128)(2,1)}) %all-gather.12.cloned.1.call-update) | async-done | bytes 1048592 | tf_op jit(solution)/shard_map/all_gather | solution.py:130
  406.3 9.5 %shard_map.89 = f32[64,64,128]{2,1,0:T(8,128)} custom-call(s32[512]{0:T(512)} %bitcast.146, s32[512]{0:T(512)} %bitcast.150, s32[1]{0:T(128)} %bitcast.121.cnt_ref, bf16[512,128,128]{2,1,0:T(8,128)(2,1)} %bitcast.125, bf16[64,64,128]{2,1,0:T(8,128)(2,1)} %all-gather.12.cloned.1.call-done.side_ref), custom_call_target="tpu_custom_call" | custom-call | flops 1073741824 | bytes 19922944 | tf_op jit(solution)/shard_map/pallas_call | solution.py:82
  416.8 54.7 %reduce-scatter.11.cloned.1.call-done = f32[8,64,128]{2,1,0:T(8,128)} async-done(((f32[64,64,128]{2,1,0:T(8,128)}), f32[8,64,128]{2,1,0:T(8,128)}) %reduce-scatter.11.cloned.1.call-update) | async-done | bytes 262160 | tf_op jit(solution)/shard_map/reduce_scatter | solution.py:132
  471.5 1.5 convolution_bitcast_fusion.3
  473.0 1.2 convolution_bitcast_fusion.5
  474.2 19.4 %all-reduce.3 = (f32[64]{0:T(128)S(1)}, f32[64,64]{0,1:T(8,128)S(1)}) all-reduce(f32[64]{0:T(128)S(1)} %convolution_bitcast_fusion.5, f32[64,64]{0,1:T(8,128)S(1)} %convolution_bitcast_fusion.3), channel_id=1, replica_groups=mesh['doc'=8,'term'=4] {'term'}, use_global_device_ids=true, to_apply=%region_19.0 | all-reduce | flops 4160 | bytes 33280 | tf_op jit(solution)/shard_map/psum | solution.py:143
  493.6 22.7 %all-reduce.1 = (f32[64]{0:T(128)S(1)}, f32[64,64]{0,1:T(8,128)S(1)}) all-reduce(f32[64]{0:T(128)S(1)} %get-tuple-element.11, f32[64,64]{0,1:T(8,128)S(1)} %get-tuple-element.12), channel_id=1, replica_groups=mesh['doc'=8,'term'=4] {'doc'}, use_global_device_ids=true, to_apply=%region_20.0 | all-reduce | flops 4160 | bytes 33280 | tf_op jit(solution)/shard_map/psum | solution.py:142
  516.8 0.6 divide_subtract_fusion
  517.5 0.6 fusion.29
  518.2 5.8 cholesky.55
  524.1 0.6 compare_reduce_fusion
  524.7 0.7 fusion.25
  525.4 4.9 custom-call.7
  530.3 1.4 fusion.5
  532.1 8.4 %psum.96 = f32[64]{0:T(128)S(1)} all-reduce(f32[64]{0:T(128)S(1)} %get-tuple-element.5), channel_id=1, replica_groups=mesh['doc'=8,'term'=4] {'term'}, use_global_device_ids=true, to_apply=%region_14.0 | all-reduce | flops 64 | bytes 512 | tf_op jit(solution)/shard_map/psum | solution.py:143
  540.5 11.8 %psum.97 = f32[64]{0:T(128)S(1)} all-reduce(f32[64]{0:T(128)S(1)} %psum.96), channel_id=1, replica_groups=mesh['doc'=8,'term'=4] {'doc'}, use_global_device_ids=true, to_apply=%region_15.0 | all-reduce | flops 64 | bytes 512 | tf_op jit(solution)/shard_map/psum | solution.py:142
  553.1 0.8 copy-done
  554.0 125.5 %all-reduce.7.cloned.1.call-done = f32[133120]{0:T(1024)} async-done(((f32[133120]{0:T(1024)}), f32[133120]{0:T(1024)}) %all-reduce.7.cloned.1.call-update) | async-done | bytes 532496
  679.5 1.2 reshape.57
  681.6 0.7 broadcast_in_dim_reshape.7
  682.3 0.7 fusion.2
  683.4 0.9 broadcast_in_dim_reshape.6
  (55 shorter events, 5.0 us)
Async XLA Ops:
  7.2 29.5 %all-gather.6.cloned.1.call-start = ((), (), s32[]{:S(2)}) async-start(), calls=%async_computation.4 | async-start | bytes 1179648 | tf_op jit(solution)/shard_map/all_gather | solution.py:123
  8.8 112.2 %reduce-scatter.5.cloned.1.call-start = ((), (), s32[]{:S(2)}) async-start(), calls=%async_computation.5 | async-start | bytes 2949120 | tf_op jit(solution)/shard_map/reduce_scatter | solution.py:125
  48.6 102.7 %all-gather.8.cloned.1.call-start = ((), (), s32[]{:S(2)}) async-start(), calls=%async_computation.6 | async-start | bytes 1310720 | tf_op jit(solution)/shard_map/all_gather | solution.py:130
  123.7 96.4 %reduce-scatter.7.cloned.1.call-start = ((), (), s32[]{:S(2)}) async-start(), calls=%async_computation.7 | async-start | bytes 2654208 | tf_op jit(solution)/shard_map/reduce_scatter | solution.py:132
  161.4 142.1 %all-gather.10.cloned.1.call-start = ((), (), s32[]{:S(2)}) async-start(), calls=%async_computation.8 | async-start | bytes 1179648 | tf_op jit(solution)/shard_map/all_gather | solution.py:123
  220.2 62.2 %copy-start.5 = (f32[8,72,128]{2,1,0:T(8,128)S(1)}, f32[8,72,128]{2,1,0:T(8,128)}, u32[]{:S(2)}) copy-start(f32[8,72,128]{2,1,0:T(8,128)} %reduce-scatter.7.cloned.1.call-done) | copy-start | bytes 884740
  283.6 93.3 %reduce-scatter.9.cloned.1.call-start = ((), (), s32[]{:S(2)}) async-start(), calls=%async_computation.9 | async-start | bytes 2621440 | tf_op jit(solution)/shard_map/reduce_scatter | solution.py:125
  313.7 92.5 %all-gather.12.cloned.1.call-start = ((), (), s32[]{:S(2)}) async-start(), calls=%async_computation.10 | async-start | bytes 1310720 | tf_op jit(solution)/shard_map/all_gather | solution.py:130
  378.7 92.8 %reduce-scatter.11.cloned.1.call-start = ((), (), s32[]{:S(2)}) async-start(), calls=%async_computation.11 | async-start | bytes 2359296 | tf_op jit(solution)/shard_map/reduce_scatter | solution.py:132
  406.3 9.6 %copy-start.4 = (s32[1,1024]{1,0:T(1,128)S(1)}, s32[1,1024]{1,0:T(1,128)}, u32[]{:S(2)}) copy-start(s32[1,1024]{1,0:T(1,128)} %param.16) | copy-start | bytes 12292
  406.3 9.7 %copy-start.3 = (s32[1,2048]{1,0:T(1,128)S(1)}, s32[1,2048]{1,0:T(1,128)}, u32[]{:S(2)}) copy-start(s32[1,2048]{1,0:T(1,128)} %param.15) | copy-start | bytes 24580
  415.8 263.8 %all-reduce.7.cloned.1.call-start = ((), (), s32[]{:S(2)}) async-start(), calls=%async_computation.12 | async-start | bytes 1064960
  416.7 135.5 %copy-start.1 = (f32[16,64,128]{2,1,0:T(8,128)S(1)}, f32[16,64,128]{2,1,0:T(8,128)}, u32[]{:S(2)}) copy-start(f32[16,64,128]{2,1,0:T(8,128)} %reduce-scatter.9.cloned.1.call-done) | copy-start | bytes 1572868
  471.5 60.5 %copy-start.2 = (f32[8,64,128]{2,1,0:T(8,128)S(1)}, f32[8,64,128]{2,1,0:T(8,128)}, u32[]{:S(2)}) copy-start(f32[8,64,128]{2,1,0:T(8,128)} %reduce-scatter.11.cloned.1.call-done) | copy-start | bytes 786436
  553.1 0.8 copy-start
Sparse Core Ops, SparseCore 0:
  10.5 26.1 all-gather.5
  48.7 72.2 reduce-scatter.4
  123.9 27.4 all-gather.7
  161.5 58.6 reduce-scatter.6
  283.7 19.7 all-gather.9
  313.9 62.9 reduce-scatter.8
  379.0 27.2 all-gather.11
  415.9 55.5 reduce-scatter.10
  554.0 125.4 all-reduce.6

commit v3 on v2

--- a/solution.py
+++ b/solution.py
@@ -96,7 +96,24 @@
     )(rows, cols, count, tiles, side)
 
 
-def per_device(tiles, tile_rows, tile_cols, tile_count, start_block, doc_cluster, term_cluster):
+def scatter_sum(x, axis_name, parts):
+    pieces = x.reshape((parts, x.shape[0] // parts) + x.shape[1:])
+    return jnp.sum(lax.all_to_all(pieces, axis_name, 0, 0, tiled=False), axis=0)
+
+
+def small_sum(values):
+    flat = jnp.concatenate([jnp.reshape(v, (-1,)) for v in values])
+    flat = jnp.sum(lax.all_gather(flat, "term", axis=0, tiled=False), axis=0)
+    flat = jnp.sum(lax.all_gather(flat, "doc", axis=0, tiled=False), axis=0)
+    out, start = [], 0
+    for v in values:
+        size = int(jnp.size(v))
+        out.append(flat[start : start + size].reshape(jnp.shape(v)))
+        start += size
+    return out
+
+
+def per_device(n_doc, n_term, tiles, tile_rows, tile_cols, tile_count, start_block, doc_cluster, term_cluster):
     local_tiles = tiles[0, 0]
     rows = tile_rows[0, 0]
     cols = tile_cols[0, 0]
@@ -122,14 +139,14 @@
         first = step == 0
         w_all = lax.all_gather(weights, "doc", axis=0, tiled=True)
         left = tile_pass(local_tiles, rows, cols, count, w_all, True, first)
-        left_own = lax.psum_scatter(left, "term", scatter_dimension=0, tiled=True)
+        left_own = scatter_sum(left, "term", n_term)
         summed_own = left_own[:, :width_k, :]
         if first:
             doc_degree = left_own[:, width_k, :]
         quotient = (summed_own / doc_degree[:, None, :]).astype(jnp.bfloat16)
         q_all = lax.all_gather(quotient, "term", axis=0, tiled=True)
         right = tile_pass(local_tiles, rows, cols, count, q_all, False, first)
-        right_own = lax.psum_scatter(right, "doc", scatter_dimension=0, tiled=True)
+        right_own = scatter_sum(right, "doc", n_doc)
         if first:
             term_degree = right_own[:, width_k, :]
             root = jnp.sqrt(term_degree)
@@ -139,9 +156,7 @@
         along_part = jnp.einsum("tki,ti->k", raw, root, precision=HIGH)
         energy_part = jnp.sum(previous * raw, axis=(0, 2))
         volume_part = jnp.sum(term_degree)
-        gram_matrix, along, energy, volume = lax.psum(
-            lax.psum((gram_part, along_part, energy_part, volume_part), "term"), "doc"
-        )
+        gram_matrix, along, energy, volume = small_sum((gram_part, along_part, energy_part, volume_part))
         lower = jnp.linalg.cholesky(gram_matrix - jnp.outer(along, along) / volume)
         projected = raw - root[:, None, :] * (along / volume)[None, :, None]
         flat = projected.transpose(1, 0, 2).reshape(width_k, -1)
@@ -159,11 +174,7 @@
         "tki,tij->kj", term_embed, term_onehot, precision=HIGH
     )
     count_part = jnp.sum(doc_onehot, axis=(0, 1)) + jnp.sum(term_onehot, axis=(0, 1))
-    packed = jnp.concatenate([center_part.reshape(-1), count_part])
-    gathered = lax.all_gather(packed, ("doc", "term"), axis=0, tiled=False)
-    totals = jnp.sum(gathered, axis=0)
-    center_sums = totals[: center_part.size].reshape(center_part.shape)
-    counts = totals[center_part.size :]
+    center_sums, counts = small_sum((center_part, count_part))
     centers = center_sums / counts[None, :]
     center_norm = jnp.sum(centers * centers, axis=0)
 
@@ -187,7 +198,7 @@
         P("term", "doc"),
     )
     return jax.shard_map(
-        per_device,
+        functools.partial(per_device, mesh.shape["doc"], mesh.shape["term"]),
         mesh=mesh,
         in_specs=placed,
         out_specs=(P("doc", "term", None), P("term", "doc", None)),

time: 691 us -> 710 us (1.027)
  starting transfers between devices: 0.37 us -> 63.1 us
  blocking collectives: 106 us -> 64.5 us
  waiting for transfers between devices: 477 us -> 460 us
  local copies, waits for them, and re-layouts: 6.9 us -> 20.3 us
  Pallas kernels: 41.6 us -> 48.8 us
    reduce_scatter x4 -> x0, waiting for transfers between devices: 249 us -> none  [the longest x2 135 us: per_device(): left_own = lax.psum_scatter(left, 'term', scatter_dimension=0, tiled=True)]
    unnamed x10 -> x16, waiting for transfers between devices: 126 us -> 254 us
    psum x6 -> x0, blocking collectives: 106 us -> none  [the longest x3 58.1 us: per_device(): lax.psum(lax.psum((gram_part, along_part, energy_part, volume_part), 'ter...]
    all_to_all x0 -> x3, waiting for transfers between devices: none -> 104 us  [scatter_sum(): return jnp.sum(lax.all_to_all(pieces, axis_name, 0, 0, tiled=False), axis=0)]
    all_to_all x0 -> x1, blocking collectives: none -> 64.5 us  [scatter_sum(): return jnp.sum(lax.all_to_all(pieces, axis_name, 0, 0, tiled=False), axis=0)]
    all_to_all x0 -> x3, starting transfers between devices: none -> 62.5 us  [scatter_sum(): return jnp.sum(lax.all_to_all(pieces, axis_name, 0, 0, tiled=False), axis=0)]
    pallas_call x4, Pallas kernels: 41.6 us -> 48.8 us  [tile_pass(): pl.pallas_call(kernel, out_shape=jax.ShapeDtypeStruct((n_tiles, out_rows,...]
  transfers between devices with their start and end apart: 9 -> 13, of which waited for: 9 -> 13; matrix products, arithmetic and copies ran while one was open for 0% -> 0% of each run, Pallas kernels for 0% -> 0%
where the time goes in v3:
time: 710 us; the launch traced here: 713 us
  waiting for transfers between devices  460 us (65%)
  blocking collectives  64.5 us (9%)
  starting transfers between devices  63.1 us (9%)
  Pallas kernels  48.8 us (7%)
  other arithmetic  33.2 us (5%)
  local copies, waits for them, and re-layouts  20.3 us (3%)
  between operations  18.4 us (3%)
    unnamed x16, waiting for transfers between devices  254 us
    all_to_all x3, waiting for transfers between devices, scatter_sum(): return jnp.sum(lax.all_to_all(pieces, axis_name, 0, 0, tiled=False), axis=0)  104 us
    all_to_all x1, blocking collectives, scatter_sum(): return jnp.sum(lax.all_to_all(pieces, axis_name, 0, 0, tiled=False), axis=0)  64.5 us
    all_to_all x3, starting transfers between devices, scatter_sum(): return jnp.sum(lax.all_to_all(pieces, axis_name, 0, 0, tiled=False), axis=0)  62.5 us
    all_gather x2, waiting for transfers between devices, per_device(): w_all = lax.all_gather(weights, 'doc', axis=0, tiled=True)  51.6 us
    all_gather x2, waiting for transfers between devices, per_device(): q_all = lax.all_gather(quotient, 'term', axis=0, tiled=True)  51 us
    pallas_call x4, Pallas kernels, tile_pass(): pl.pallas_call(kernel, out_shape=jax.ShapeDtypeStruct((n_tiles, out_rows,...  48.8 us
  transfers between devices with their start and end apart: 13, of which 13 were waited for; matrix products, arithmetic and copies ran while one was open for 0% of the time, Pallas kernels for 0%

profile of v3, /device:TPU:0, one launch (start us, length us, event | category | flops | bytes accessed | tf_op | source)
XLA Modules:
  0.0 712.7 jit_solution(9987634091258611510)
XLA Ops:
  7.2 0.9 copy.75
  8.1 0.7 copy.94
  9.5 27.2 %all-gather.11.cloned.1.call-done.side_ref = bf16[64,64,128]{2,1,0:T(8,128)(2,1)} async-done(((bf16[8,64,128]{2,1,0:T(8,128)(2,1)}), bf16[64,64,128]{2,1,0:T(8,128)(2,1)}) %all-gather.11.cloned.1.call-update) | async-done | bytes 1048592 | tf_op jit(solution)/shard_map/all_gather | solution.py:140
  36.7 14.2 %shard_map.86 = f32[64,72,128]{2,1,0:T(8,128)} custom-call(s32[512]{0:T(512)} %bitcast.170, s32[512]{0:T(512)} %bitcast.174, s32[1]{0:T(128)} %bitcast.137.cnt_ref, bf16[512,128,128]{2,1,0:T(8,128)(2,1)} %bitcast.141, bf16[64,64,128]{2,1,0:T(8,128)(2,1)} %all-gather.11.cloned.1.call-done.side_ref), custom_call_target="tpu_custom_call" | custom-call | flops 1207959552 | bytes 20185088 | tf_op jit(solution)/shard_map/pallas_call | solution.py:82
  50.9 22.8 %all-to-all-start = ((f32[4,16,72,128]{3,2,1,0:T(8,128)}), f32[4,16,72,128]{3,2,1,0:T(8,128)S(1)}, u32[]{:S(2)}, u32[]{:S(2)}) async-start(f32[4,16,72,128]{3,2,1,0:T(8,128)} %bitcast.146), calls=%async_computation | async-start | bytes 4718592 | tf_op jit(solution)/shard_map/all_to_all | solution.py:101
  73.7 50.5 %all-to-all-done = f32[4,16,72,128]{3,2,1,0:T(8,128)S(1)} async-done(((f32[4,16,72,128]{3,2,1,0:T(8,128)}), f32[4,16,72,128]{3,2,1,0:T(8,128)S(1)}, u32[]{:S(2)}, u32[]{:S(2)}) %all-to-all-start) | async-done | bytes 2359328 | tf_op jit(solution)/shard_map/all_to_all | solution.py:101
  124.4 0.8 fusion.8
  125.1 25.5 %all-gather.13.cloned.1.call-done.side_ref = bf16[64,64,128]{2,1,0:T(8,128)(2,1)} async-done(((bf16[16,64,128]{2,1,0:T(8,128)(2,1)}), bf16[64,64,128]{2,1,0:T(8,128)(2,1)}) %all-gather.13.cloned.1.call-update) | async-done | bytes 1048592 | tf_op jit(solution)/shard_map/all_gather | solution.py:147
  150.6 11.7 %shard_map.87 = f32[64,72,128]{2,1,0:T(8,128)} custom-call(s32[512]{0:T(512)} %bitcast.171, s32[512]{0:T(512)} %bitcast.175, s32[1]{0:T(128)} %bitcast.138.cnt_ref, bf16[512,128,128]{2,1,0:T(8,128)(2,1)} %bitcast.142, bf16[64,64,128]{2,1,0:T(8,128)(2,1)} %all-gather.13.cloned.1.call-done.side_ref), custom_call_target="tpu_custom_call" | custom-call | flops 1207959552 | bytes 20185088 | tf_op jit(solution)/shard_map/pallas_call | solution.py:82
  162.3 20.8 %all-to-all-start.1 = ((f32[8,8,72,128]{3,2,1,0:T(8,128)}), f32[8,8,72,128]{3,2,1,0:T(8,128)S(1)}, u32[]{:S(2)}, u32[]{:S(2)}) async-start(f32[8,8,72,128]{3,2,1,0:T(8,128)} %bitcast.145), calls=%async_computation.1 | async-start | bytes 4718592 | tf_op jit(solution)/shard_map/all_to_all | solution.py:101
  184.4 28.1 %all-to-all-done.1 = f32[8,8,72,128]{3,2,1,0:T(8,128)S(1)} async-done(((f32[8,8,72,128]{3,2,1,0:T(8,128)}), f32[8,8,72,128]{3,2,1,0:T(8,128)S(1)}, u32[]{:S(2)}, u32[]{:S(2)}) %all-to-all-start.1) | async-done | bytes 2359328 | tf_op jit(solution)/shard_map/all_to_all | solution.py:101
  212.7 0.7 slice_reduce_fusion
  214.3 0.8 concatenate.9
  217.4 29.3 %all-reduce.13.cloned.1.call-done = f32[16900]{0:T(1024)} async-done(((f32[16900]{0:T(1024)}), f32[16900]{0:T(1024)}) %all-reduce.13.cloned.1.call-update) | async-done | bytes 67616
  246.7 1.0 reshape.102
  249.0 53.4 %all-reduce.15.cloned.1.call-done = f32[33800]{0:T(1024)} async-done(((f32[33800]{0:T(1024)}), f32[33800]{0:T(1024)}) %all-reduce.15.cloned.1.call-update) | async-done | bytes 135216
  302.4 1.0 reshape.103
  304.8 0.7 divide_subtract_fusion.1
  305.6 0.7 fusion.32
  306.3 5.8 cholesky.44
  312.8 0.7 fusion.25
  313.5 4.9 custom-call.6
  318.9 0.7 fusion.18
  319.6 24.4 %all-gather.15.cloned.1.call-done.side_ref = bf16[64,64,128]{2,1,0:T(8,128)(2,1)} async-done(((bf16[8,64,128]{2,1,0:T(8,128)(2,1)}), bf16[64,64,128]{2,1,0:T(8,128)(2,1)}) %all-gather.15.cloned.1.call-update) | async-done | bytes 1048592 | tf_op jit(solution)/shard_map/all_gather | solution.py:140
  344.0 12.1 %shard_map.88 = f32[64,64,128]{2,1,0:T(8,128)} custom-call(s32[512]{0:T(512)} %bitcast.172, s32[512]{0:T(512)} %bitcast.176, s32[1]{0:T(128)} %bitcast.139.cnt_ref, bf16[512,128,128]{2,1,0:T(8,128)(2,1)} %bitcast.143, bf16[64,64,128]{2,1,0:T(8,128)(2,1)} %all-gather.15.cloned.1.call-done.side_ref), custom_call_target="tpu_custom_call" | custom-call | flops 1073741824 | bytes 19922944 | tf_op jit(solution)/shard_map/pallas_call | solution.py:82
  356.1 64.5 %all_to_all.20 = f32[4,16,64,128]{3,2,1,0:T(8,128)S(1)} all-to-all(f32[4,16,64,128]{3,2,1,0:T(8,128)} %bitcast.148), channel_id=1, replica_groups=mesh['doc'=8,'term'=4] {'term'}, dimensions={0} | all-to-all | bytes 4194304 | tf_op jit(solution)/shard_map/all_to_all | solution.py:101
  420.8 0.8 fusion.38
  421.6 25.5 %all-gather.17.cloned.1.call-done.side_ref = bf16[64,64,128]{2,1,0:T(8,128)(2,1)} async-done(((bf16[16,64,128]{2,1,0:T(8,128)(2,1)}), bf16[64,64,128]{2,1,0:T(8,128)(2,1)}) %all-gather.17.cloned.1.call-update) | async-done | bytes 1048592 | tf_op jit(solution)/shard_map/all_gather | solution.py:147
  447.2 10.9 %shard_map.89 = f32[64,64,128]{2,1,0:T(8,128)} custom-call(s32[512]{0:T(512)} %bitcast.173, s32[512]{0:T(512)} %bitcast.177, s32[1]{0:T(128)} %bitcast.140.cnt_ref, bf16[512,128,128]{2,1,0:T(8,128)(2,1)} %bitcast.144, bf16[64,64,128]{2,1,0:T(8,128)(2,1)} %all-gather.17.cloned.1.call-done.side_ref), custom_call_target="tpu_custom_call" | custom-call | flops 1073741824 | bytes 19922944 | tf_op jit(solution)/shard_map/pallas_call | solution.py:82
  458.0 18.9 %all-to-all-start.3 = ((f32[8,8,64,128]{3,2,1,0:T(8,128)}), f32[8,8,64,128]{3,2,1,0:T(8,128)S(1)}, u32[]{:S(2)}, u32[]{:S(2)}) async-start(f32[8,8,64,128]{3,2,1,0:T(8,128)} %bitcast.147), calls=%async_computation.3 | async-start | bytes 4194304 | tf_op jit(solution)/shard_map/all_to_all | solution.py:101
  478.2 25.4 %all-to-all-done.3 = f32[8,8,64,128]{3,2,1,0:T(8,128)S(1)} async-done(((f32[8,8,64,128]{3,2,1,0:T(8,128)}), f32[8,8,64,128]{3,2,1,0:T(8,128)S(1)}, u32[]{:S(2)}, u32[]{:S(2)}) %all-to-all-start.3) | async-done | bytes 2097184 | tf_op jit(solution)/shard_map/all_to_all | solution.py:101
  504.6 0.8 concatenate.10
  506.7 30.3 %all-reduce.17.cloned.1.call-done = f32[16900]{0:T(1024)} async-done(((f32[16900]{0:T(1024)}), f32[16900]{0:T(1024)}) %all-reduce.17.cloned.1.call-update) | async-done | bytes 67616
  537.0 1.0 reshape.104
  539.4 53.1 %all-reduce.19.cloned.1.call-done = f32[33800]{0:T(1024)} async-done(((f32[33800]{0:T(1024)}), f32[33800]{0:T(1024)}) %all-reduce.19.cloned.1.call-update) | async-done | bytes 135216
  592.5 1.0 reshape.105
  594.8 0.7 fusion.35
  595.7 0.7 divide_subtract_fusion
  596.5 0.7 fusion.30
  597.2 5.8 cholesky.55
  604.4 4.9 custom-call.7
  611.8 34.5 %all-reduce.21.cloned.1.call-done = f32[16640]{0:T(1024)} async-done(((f32[16640]{0:T(1024)}), f32[16640]{0:T(1024)}) %all-reduce.21.cloned.1.call-update) | async-done | bytes 66576
  646.4 1.0 reshape.106
  648.6 52.8 %all-reduce.23.cloned.1.call-done = f32[33280]{0:T(1024)} async-done(((f32[33280]{0:T(1024)}), f32[33280]{0:T(1024)}) %all-reduce.23.cloned.1.call-update) | async-done | bytes 133136
  701.4 1.0 reshape.107
  703.2 0.7 broadcast_in_dim_reshape.7
  703.9 0.7 fusion.2
  705.0 0.9 broadcast_in_dim_reshape.6
  (106 shorter events, 18.3 us)
Async XLA Ops:
  7.2 29.5 %all-gather.11.cloned.1.call-start = ((), (), s32[]{:S(2)}) async-start(), calls=%async_computation.4 | async-start | bytes 1179648 | tf_op jit(solution)/shard_map/all_gather | solution.py:140
  50.9 73.3 %all-to-all-start = ((f32[4,16,72,128]{3,2,1,0:T(8,128)}), f32[4,16,72,128]{3,2,1,0:T(8,128)S(1)}, u32[]{:S(2)}, u32[]{:S(2)}) async-start(f32[4,16,72,128]{3,2,1,0:T(8,128)} %bitcast.146), calls=%async_computation | async-start | bytes 4718592 | tf_op jit(solution)/shard_map/all_to_all | solution.py:101
  73.7 76.9 %all-gather.13.cloned.1.call-start = ((), (), s32[]{:S(2)}) async-start(), calls=%async_computation.5 | async-start | bytes 1310720 | tf_op jit(solution)/shard_map/all_gather | solution.py:147
  162.3 20.9 %copy-start.9 = (u32[32]{0:T(128)S(1)}, u32[32]{0:T(128)}, u32[]{:S(2)}) copy-start(u32[32]{0:T(128)} %constant.50) | copy-start | bytes 388
  162.3 50.3 %all-to-all-start.1 = ((f32[8,8,72,128]{3,2,1,0:T(8,128)}), f32[8,8,72,128]{3,2,1,0:T(8,128)S(1)}, u32[]{:S(2)}, u32[]{:S(2)}) async-start(f32[8,8,72,128]{3,2,1,0:T(8,128)} %bitcast.145), calls=%async_computation.1 | async-start | bytes 4718592 | tf_op jit(solution)/shard_map/all_to_all | solution.py:101
  183.1 63.6 %all-reduce.13.cloned.1.call-start = ((), (), s32[]{:S(2)}) async-start(), calls=%async_computation.8 | async-start | bytes 139264
  184.4 31.8 %copy-start.8 = (u32[32]{0:T(128)S(1)}, u32[32]{0:T(128)}, u32[]{:S(2)}) copy-start(u32[32]{0:T(128)} %constant.55) | copy-start | bytes 388
  215.5 0.6 copy-start.5
  216.2 86.2 %all-reduce.15.cloned.1.call-start = ((), (), s32[]{:S(2)}) async-start(), calls=%async_computation.9 | async-start | bytes 278528
  248.2 0.7 copy-start.1
  248.9 95.1 %all-gather.15.cloned.1.call-start = ((), (), s32[]{:S(2)}) async-start(), calls=%async_computation.6 | async-start | bytes 1179648 | tf_op jit(solution)/shard_map/all_gather | solution.py:140
  319.6 127.6 %all-gather.17.cloned.1.call-start = ((), (), s32[]{:S(2)}) async-start(), calls=%async_computation.7 | async-start | bytes 1310720 | tf_op jit(solution)/shard_map/all_gather | solution.py:147
  458.0 45.6 %all-to-all-start.3 = ((f32[8,8,64,128]{3,2,1,0:T(8,128)}), f32[8,8,64,128]{3,2,1,0:T(8,128)S(1)}, u32[]{:S(2)}, u32[]{:S(2)}) async-start(f32[8,8,64,128]{3,2,1,0:T(8,128)} %bitcast.147), calls=%async_computation.3 | async-start | bytes 4194304 | tf_op jit(solution)/shard_map/all_to_all | solution.py:101
  476.9 60.1 %all-reduce.17.cloned.1.call-start = ((), (), s32[]{:S(2)}) async-start(), calls=%async_computation.10 | async-start | bytes 139264
  478.2 28.3 %copy-start.6 = (s32[1,2048]{1,0:T(1,128)S(1)}, s32[1,2048]{1,0:T(1,128)}, u32[]{:S(2)}) copy-start(s32[1,2048]{1,0:T(1,128)} %param.15) | copy-start | bytes 24580
  478.2 61.0 %copy-start.7 = (s32[1,1024]{1,0:T(1,128)S(1)}, s32[1,1024]{1,0:T(1,128)}, u32[]{:S(2)}) copy-start(s32[1,1024]{1,0:T(1,128)} %param.16) | copy-start | bytes 12292
  505.8 0.6 copy-start.4
  506.5 86.0 %all-reduce.19.cloned.1.call-start = ((), (), s32[]{:S(2)}) async-start(), calls=%async_computation.11 | async-start | bytes 278528
  538.5 0.7 copy-start
  539.2 107.2 %all-reduce.21.cloned.1.call-start = ((), (), s32[]{:S(2)}) async-start(), calls=%async_computation.12 | async-start | bytes 139264
  610.8 0.6 copy-start.3
  611.5 89.9 %all-reduce.23.cloned.1.call-start = ((), (), s32[]{:S(2)}) async-start(), calls=%async_computation.13 | async-start | bytes 270336
  647.9 0.7 copy-start.2
Sparse Core Ops, SparseCore 0:
  10.5 26.1 all-gather.10
  125.3 25.2 all-gather.12
  216.3 30.3 all-reduce.12
  250.5 51.7 all-reduce.14
  319.7 24.2 all-gather.14
  421.7 25.3 all-gather.16
  506.6 30.3 all-reduce.16
  540.7 51.7 all-reduce.18
  611.6 34.7 all-reduce.20
  650.2 51.1 all-reduce.22

commit v4 on v3

--- a/solution.py
+++ b/solution.py
@@ -101,10 +101,9 @@
     return jnp.sum(lax.all_to_all(pieces, axis_name, 0, 0, tiled=False), axis=0)
 
 
-def small_sum(values):
+def packed_psum(values):
     flat = jnp.concatenate([jnp.reshape(v, (-1,)) for v in values])
-    flat = jnp.sum(lax.all_gather(flat, "term", axis=0, tiled=False), axis=0)
-    flat = jnp.sum(lax.all_gather(flat, "doc", axis=0, tiled=False), axis=0)
+    flat = lax.psum(flat, ("doc", "term"))
     out, start = [], 0
     for v in values:
         size = int(jnp.size(v))
@@ -126,6 +125,8 @@
     doc_labels = doc_cluster[0].reshape(-1, edge)
     term_labels = term_cluster[0].reshape(-1, edge)
     clusters = jnp.arange(CLUSTERS, dtype=jnp.int32)
+    doc_onehot = (doc_labels[:, :, None] == clusters).astype(jnp.float32)
+    term_onehot = (term_labels[:, :, None] == clusters).astype(jnp.float32)
 
     weights = start_t
     basis = None
@@ -139,7 +140,7 @@
         first = step == 0
         w_all = lax.all_gather(weights, "doc", axis=0, tiled=True)
         left = tile_pass(local_tiles, rows, cols, count, w_all, True, first)
-        left_own = scatter_sum(left, "term", n_term)
+        left_own = lax.psum_scatter(left, "term", scatter_dimension=0, tiled=True)
         summed_own = left_own[:, :width_k, :]
         if first:
             doc_degree = left_own[:, width_k, :]
@@ -156,7 +157,14 @@
         along_part = jnp.einsum("tki,ti->k", raw, root, precision=HIGH)
         energy_part = jnp.sum(previous * raw, axis=(0, 2))
         volume_part = jnp.sum(term_degree)
-        gram_matrix, along, energy, volume = small_sum((gram_part, along_part, energy_part, volume_part))
+        sums = [gram_part, along_part, energy_part, volume_part]
+        if step == ITERS - 1:
+            doc_ratio = summed_own / doc_degree[:, None, :]
+            doc_part = jnp.einsum("tki,tij->kj", doc_ratio, doc_onehot, precision=HIGH)
+            term_part = jnp.einsum("tki,tij->kj", raw / root[:, None, :], term_onehot, precision=HIGH)
+            sums += [doc_part, term_part, jnp.sum(doc_onehot, axis=(0, 1)), jnp.sum(term_onehot, axis=(0, 1))]
+        sums = packed_psum(sums)
+        gram_matrix, along, energy, volume = sums[:4]
         lower = jnp.linalg.cholesky(gram_matrix - jnp.outer(along, along) / volume)
         projected = raw - root[:, None, :] * (along / volume)[None, :, None]
         flat = projected.transpose(1, 0, 2).reshape(width_k, -1)
@@ -164,18 +172,14 @@
         basis = solved.reshape(width_k, term_tiles_own, edge).transpose(1, 0, 2)
         weights = (basis / root[:, None, :]).astype(jnp.bfloat16)
 
+    doc_part, term_part, doc_count, term_count = sums[4:]
     scale = jnp.sqrt(volume)
     column_scale = scale * lax.rsqrt(energy)
     doc_embed = summed_own / doc_degree[:, None, :] * column_scale[None, :, None]
     term_embed = scale * basis / root[:, None, :]
-    doc_onehot = (doc_labels[:, :, None] == clusters).astype(jnp.float32)
-    term_onehot = (term_labels[:, :, None] == clusters).astype(jnp.float32)
-    center_part = jnp.einsum("tki,tij->kj", doc_embed, doc_onehot, precision=HIGH) + jnp.einsum(
-        "tki,tij->kj", term_embed, term_onehot, precision=HIGH
-    )
-    count_part = jnp.sum(doc_onehot, axis=(0, 1)) + jnp.sum(term_onehot, axis=(0, 1))
-    center_sums, counts = small_sum((center_part, count_part))
-    centers = center_sums / counts[None, :]
+    term_centered = term_part - jnp.outer(along / volume, term_count)
+    term_sums = scale * jax.scipy.linalg.solve_triangular(lower, term_centered, lower=True)
+    centers = (column_scale[:, None] * doc_part + term_sums) / (doc_count + term_count)[None, :]
     center_norm = jnp.sum(centers * centers, axis=0)
 
     def distances(embed):

time: 710 us -> 520 us (0.73)
  waiting for transfers between devices: 460 us -> 268 us
  blocking collectives: 64.5 us -> 140 us
  starting transfers between devices: 63.1 us -> 14.3 us
  Pallas kernels: 48.8 us -> 35.8 us
  local copies, waits for them, and re-layouts: 20.3 us -> 7.82 us
    unnamed x16 -> x6, waiting for transfers between devices: 254 us -> 0.1 us
    reduce_scatter x0 -> x2, waiting for transfers between devices: none -> 137 us  [per_device(): left_own = lax.psum_scatter(left, 'term', scatter_dimension=0, tiled=True)]
    psum x0 -> x2, blocking collectives: none -> 95.3 us  [packed_psum(): flat = lax.psum(flat, ('doc', 'term'))]
    all_to_all x3 -> x1, waiting for transfers between devices: 104 us -> 25.8 us  [scatter_sum(): return jnp.sum(lax.all_to_all(pieces, axis_name, 0, 0, tiled=False), axis=0)]
    all_to_all x3 -> x1, starting transfers between devices: 62.5 us -> 14.1 us  [scatter_sum(): return jnp.sum(lax.all_to_all(pieces, axis_name, 0, 0, tiled=False), axis=0)]
    all_to_all x1, blocking collectives: 64.5 us -> 44.7 us  [scatter_sum(): return jnp.sum(lax.all_to_all(pieces, axis_name, 0, 0, tiled=False), axis=0)]
    pallas_call x4, Pallas kernels: 48.8 us -> 35.8 us  [tile_pass(): pl.pallas_call(kernel, out_shape=jax.ShapeDtypeStruct((n_tiles, out_rows,...]
    unnamed x34 -> x7, local copies, waits for them, and re-layouts: 8.16 us -> 0.94 us
  transfers between devices with their start and end apart: 13 -> 7, of which waited for: 13 -> 7; matrix products, arithmetic and copies ran while one was open for 0% -> 0% of each run, Pallas kernels for 0% -> 0%
where the time goes in v4:
time: 520 us
  waiting for transfers between devices  268 us (52%)
  blocking collectives  140 us (27%)
  Pallas kernels  35.8 us (7%)
  other arithmetic  34.5 us (7%)
  between operations  15.6 us (3%)
  starting transfers between devices  14.3 us (3%)
  local copies, waits for them, and re-layouts  7.82 us (2%)
    reduce_scatter x2, waiting for transfers between devices, per_device(): left_own = lax.psum_scatter(left, 'term', scatter_dimension=0, tiled=True)  137 us
    psum x2, blocking collectives, packed_psum(): flat = lax.psum(flat, ('doc', 'term'))  95.3 us
    all_gather x2, waiting for transfers between devices, per_device(): q_all = lax.all_gather(quotient, 'term', axis=0, tiled=True)  55.1 us
    all_gather x2, waiting for transfers between devices, per_device(): w_all = lax.all_gather(weights, 'doc', axis=0, tiled=True)  49.8 us
    all_to_all x1, blocking collectives, scatter_sum(): return jnp.sum(lax.all_to_all(pieces, axis_name, 0, 0, tiled=False), axis=0)  44.7 us
    pallas_call x4, Pallas kernels, tile_pass(): pl.pallas_call(kernel, out_shape=jax.ShapeDtypeStruct((n_tiles, out_rows,...  35.8 us
    all_to_all x1, waiting for transfers between devices, scatter_sum(): return jnp.sum(lax.all_to_all(pieces, axis_name, 0, 0, tiled=False), axis=0)  25.8 us
    all_to_all x1, starting transfers between devices, scatter_sum(): return jnp.sum(lax.all_to_all(pieces, axis_name, 0, 0, tiled=False), axis=0)  14.1 us
  transfers between devices with their start and end apart: 7, of which 7 were waited for; matrix products, arithmetic and copies ran while one was open for 0% of the time, Pallas kernels for 0%

profile of v4, /device:TPU:0, one launch (start us, length us, event | category | flops | bytes accessed | tf_op | source)
XLA Modules:
  0.0 520.4 jit_solution(12008219852406723476)
XLA Ops:
  7.2 0.9 copy.64
  8.1 0.7 copy.82
  9.5 27.1 %all-gather.5.cloned.1.call-done.side_ref = bf16[64,64,128]{2,1,0:T(8,128)(2,1)} async-done(((bf16[8,64,128]{2,1,0:T(8,128)(2,1)}), bf16[64,64,128]{2,1,0:T(8,128)(2,1)}) %all-gather.5.cloned.1.call-update) | async-done | bytes 1048592 | tf_op jit(solution)/shard_map/all_gather | solution.py:141
  36.7 10.1 %shard_map.86 = f32[64,72,128]{2,1,0:T(8,128)} custom-call(s32[512]{0:T(512)} %bitcast.166, s32[512]{0:T(512)} %bitcast.170, s32[1]{0:T(128)} %bitcast.134.cnt_ref, bf16[512,128,128]{2,1,0:T(8,128)(2,1)} %bitcast.138, bf16[64,64,128]{2,1,0:T(8,128)(2,1)} %all-gather.5.cloned.1.call-done.side_ref), custom_call_target="tpu_custom_call" | custom-call | flops 1207959552 | bytes 20185088 | tf_op jit(solution)/shard_map/pallas_call | solution.py:82
  46.9 73.5 %reduce-scatter.3.cloned.1.call-done = f32[16,72,128]{2,1,0:T(8,128)} async-done(((f32[64,72,128]{2,1,0:T(8,128)}), f32[16,72,128]{2,1,0:T(8,128)}) %reduce-scatter.3.cloned.1.call-update) | async-done | bytes 589840 | tf_op jit(solution)/shard_map/reduce_scatter | solution.py:143
  120.3 0.8 slice.75
  121.2 1.8 fusion.9
  123.1 27.5 %all-gather.7.cloned.1.call-done.side_ref = bf16[64,64,128]{2,1,0:T(8,128)(2,1)} async-done(((bf16[16,64,128]{2,1,0:T(8,128)(2,1)}), bf16[64,64,128]{2,1,0:T(8,128)(2,1)}) %all-gather.7.cloned.1.call-update) | async-done | bytes 1048592 | tf_op jit(solution)/shard_map/all_gather | solution.py:148
  150.6 8.7 %shard_map.87 = f32[64,72,128]{2,1,0:T(8,128)} custom-call(s32[512]{0:T(512)} %bitcast.167, s32[512]{0:T(512)} %bitcast.171, s32[1]{0:T(128)} %bitcast.135.cnt_ref, bf16[512,128,128]{2,1,0:T(8,128)(2,1)} %bitcast.139, bf16[64,64,128]{2,1,0:T(8,128)(2,1)} %all-gather.7.cloned.1.call-done.side_ref), custom_call_target="tpu_custom_call" | custom-call | flops 1207959552 | bytes 20185088 | tf_op jit(solution)/shard_map/pallas_call | solution.py:82
  159.2 44.7 %all_to_all.10 = f32[8,8,72,128]{3,2,1,0:T(8,128)S(1)} all-to-all(f32[8,8,72,128]{3,2,1,0:T(8,128)} %bitcast.142), channel_id=1, replica_groups=mesh['doc'=8,'term'=4] {'doc'}, dimensions={0} | all-to-all | bytes 4718592 | tf_op jit(solution)/shard_map/all_to_all | solution.py:101
  204.1 0.6 slice_reduce_fusion
  205.1 0.4 convolution_bitcast_fusion.4
  205.6 0.6 concatenate.6
  206.3 47.7 %psum.14 = f32[4225]{0:T(1024)S(1)} all-reduce(f32[4225]{0:T(1024)S(1)} %concatenate.6), channel_id=1, replica_groups=mesh['doc'=8,'term'=4] {'doc','term'}, use_global_device_ids=true, to_apply=%region_4.0 | all-reduce | flops 4225 | bytes 33800 | tf_op jit(solution)/shard_map/psum | solution.py:106
  254.0 0.5 slice.80
  254.5 0.6 fusion.41
  255.3 0.7 divide_subtract_fusion.1
  256.1 0.7 fusion.35
  256.9 5.8 %cholesky.44 = f32[64,64]{1,0:T(8,128)S(1)} custom-call(f32[64,64]{1,0:T(8,128)S(1)} %fusion.35), custom_call_target="Cholesky" | custom-call | tf_op jit(solution)/shard_map/jit(cholesky)/cholesky | solution.py:168
  262.7 0.6 compare_reduce_fusion.1
  263.4 0.7 fusion.27
  264.0 4.9 custom-call.11
  268.9 0.5 convolution_bitcast_fusion
  269.4 0.7 fusion.18
  270.2 22.7 %all-gather.9.cloned.1.call-done.side_ref = bf16[64,64,128]{2,1,0:T(8,128)(2,1)} async-done(((bf16[8,64,128]{2,1,0:T(8,128)(2,1)}), bf16[64,64,128]{2,1,0:T(8,128)(2,1)}) %all-gather.9.cloned.1.call-update) | async-done | bytes 1048592 | tf_op jit(solution)/shard_map/all_gather | solution.py:141
  292.8 8.9 %shard_map.88 = f32[64,64,128]{2,1,0:T(8,128)} custom-call(s32[512]{0:T(512)} %bitcast.168, s32[512]{0:T(512)} %bitcast.172, s32[1]{0:T(128)} %bitcast.136.cnt_ref, bf16[512,128,128]{2,1,0:T(8,128)(2,1)} %bitcast.140, bf16[64,64,128]{2,1,0:T(8,128)(2,1)} %all-gather.9.cloned.1.call-done.side_ref), custom_call_target="tpu_custom_call" | custom-call | flops 1073741824 | bytes 19922944 | tf_op jit(solution)/shard_map/pallas_call | solution.py:82
  301.8 63.5 %reduce-scatter.5.cloned.1.call-done = f32[16,64,128]{2,1,0:T(8,128)} async-done(((f32[64,64,128]{2,1,0:T(8,128)}), f32[16,64,128]{2,1,0:T(8,128)}) %reduce-scatter.5.cloned.1.call-update) | async-done | bytes 524304 | tf_op jit(solution)/shard_map/reduce_scatter | solution.py:143
  365.3 1.8 fusion.39
  367.1 27.6 %all-gather.11.cloned.1.call-done.side_ref = bf16[64,64,128]{2,1,0:T(8,128)(2,1)} async-done(((bf16[16,64,128]{2,1,0:T(8,128)(2,1)}), bf16[64,64,128]{2,1,0:T(8,128)(2,1)}) %all-gather.11.cloned.1.call-update) | async-done | bytes 1048592 | tf_op jit(solution)/shard_map/all_gather | solution.py:148
  394.7 8.1 %shard_map.89 = f32[64,64,128]{2,1,0:T(8,128)} custom-call(s32[512]{0:T(512)} %bitcast.169, s32[512]{0:T(512)} %bitcast.173, s32[1]{0:T(128)} %bitcast.137.cnt_ref, bf16[512,128,128]{2,1,0:T(8,128)(2,1)} %bitcast.141, bf16[64,64,128]{2,1,0:T(8,128)(2,1)} %all-gather.11.cloned.1.call-done.side_ref), custom_call_target="tpu_custom_call" | custom-call | flops 1073741824 | bytes 19922944 | tf_op jit(solution)/shard_map/pallas_call | solution.py:82
  402.8 14.1 %all-to-all-start.1 = ((f32[8,8,64,128]{3,2,1,0:T(8,128)}), f32[8,8,64,128]{3,2,1,0:T(8,128)S(1)}, u32[]{:S(2)}, u32[]{:S(2)}) async-start(f32[8,8,64,128]{3,2,1,0:T(8,128)} %bitcast.143), calls=%async_computation.3 | async-start | bytes 4194304 | tf_op jit(solution)/shard_map/all_to_all | solution.py:101
  417.2 0.5 convolution_bitcast_fusion.2
  417.8 25.8 %all-to-all-done.1 = f32[8,8,64,128]{3,2,1,0:T(8,128)S(1)} async-done(((f32[8,8,64,128]{3,2,1,0:T(8,128)}), f32[8,8,64,128]{3,2,1,0:T(8,128)S(1)}, u32[]{:S(2)}, u32[]{:S(2)}) %all-to-all-start.1) | async-done | bytes 2097184 | tf_op jit(solution)/shard_map/all_to_all | solution.py:101
  445.0 0.6 concatenate.7
  445.6 47.6 %psum.15 = f32[12545]{0:T(1024)S(1)} all-reduce(f32[12545]{0:T(1024)S(1)} %concatenate.7), channel_id=1, replica_groups=mesh['doc'=8,'term'=4] {'doc','term'}, use_global_device_ids=true, to_apply=%region_12.15 | all-reduce | flops 12545 | bytes 100360 | tf_op jit(solution)/shard_map/psum | solution.py:106
  493.2 0.5 slice.81
  494.4 0.7 fusion.38
  495.5 0.7 divide_subtract_fusion
  496.3 0.7 fusion.33
  497.1 5.8 %cholesky.55 = f32[64,64]{1,0:T(8,128)S(1)} custom-call(f32[64,64]{1,0:T(8,128)S(1)} %fusion.33), custom_call_target="Cholesky" | custom-call | tf_op jit(solution)/shard_map/jit(cholesky)/cholesky | solution.py:168
  503.0 0.6 compare_reduce_fusion
  503.6 0.7 fusion.28
  504.3 4.9 custom-call.9
  509.2 0.5 fusion.5
  510.1 0.4 fusion.6
  510.7 0.7 broadcast_in_dim_reshape.7
  511.6 0.7 fusion.2
  512.7 0.9 broadcast_in_dim_reshape.6
  (52 shorter events, 4.5 us)
Async XLA Ops:
  7.2 29.5 %all-gather.5.cloned.1.call-start = ((), (), s32[]{:S(2)}) async-start(), calls=%async_computation.4 | async-start | bytes 1179648 | tf_op jit(solution)/shard_map/all_gather | solution.py:141
  8.8 111.5 %reduce-scatter.3.cloned.1.call-start = ((), (), s32[]{:S(2)}) async-start(), calls=%async_computation.5 | async-start | bytes 2949120 | tf_op jit(solution)/shard_map/reduce_scatter | solution.py:143
  46.8 103.8 %all-gather.7.cloned.1.call-start = ((), (), s32[]{:S(2)}) async-start(), calls=%async_computation.6 | async-start | bytes 1310720 | tf_op jit(solution)/shard_map/all_gather | solution.py:148
  123.0 169.8 %all-gather.9.cloned.1.call-start = ((), (), s32[]{:S(2)}) async-start(), calls=%async_computation.7 | async-start | bytes 1179648 | tf_op jit(solution)/shard_map/all_gather | solution.py:141
  270.1 95.2 %reduce-scatter.5.cloned.1.call-start = ((), (), s32[]{:S(2)}) async-start(), calls=%async_computation.8 | async-start | bytes 2621440 | tf_op jit(solution)/shard_map/reduce_scatter | solution.py:143
  301.7 93.0 %all-gather.11.cloned.1.call-start = ((), (), s32[]{:S(2)}) async-start(), calls=%async_computation.9 | async-start | bytes 1310720 | tf_op jit(solution)/shard_map/all_gather | solution.py:148
  402.8 14.1 %copy-start.2 = (s32[1,1024]{1,0:T(1,128)S(1)}, s32[1,1024]{1,0:T(1,128)}, u32[]{:S(2)}) copy-start(s32[1,1024]{1,0:T(1,128)} %param.16) | copy-start | bytes 12292
  402.8 14.2 %copy-start.1 = (s32[1,2048]{1,0:T(1,128)S(1)}, s32[1,2048]{1,0:T(1,128)}, u32[]{:S(2)}) copy-start(s32[1,2048]{1,0:T(1,128)} %param.15) | copy-start | bytes 24580
  402.8 14.4 %copy-start = (f32[16,64,128]{2,1,0:T(8,128)S(1)}, f32[16,64,128]{2,1,0:T(8,128)}, u32[]{:S(2)}) copy-start(f32[16,64,128]{2,1,0:T(8,128)} %reduce-scatter.5.cloned.1.call-done) | copy-start | bytes 1572868
  402.8 40.7 %all-to-all-start.1 = ((f32[8,8,64,128]{3,2,1,0:T(8,128)}), f32[8,8,64,128]{3,2,1,0:T(8,128)S(1)}, u32[]{:S(2)}, u32[]{:S(2)}) async-start(f32[8,8,64,128]{3,2,1,0:T(8,128)} %bitcast.143), calls=%async_computation.3 | async-start | bytes 4194304 | tf_op jit(solution)/shard_map/all_to_all | solution.py:101
Sparse Core Ops, SparseCore 0:
  10.5 26.1 all-gather.4
  46.9 73.3 reduce-scatter.2
  123.1 27.4 all-gather.6
  270.3 22.5 all-gather.8
  301.9 63.4 reduce-scatter.4
  367.4 27.2 all-gather.10

commit v5 on v4

--- a/solution.py
+++ b/solution.py
@@ -9,8 +9,8 @@
 
 CLUSTERS = 64
 ITERS = 2
-CHUNK = 64
-GROUP = 4
+CHUNK = 128
+GROUP = 8
 DEG_ROWS = 8
 
 HIGH = lax.Precision.HIGHEST
@@ -103,7 +103,7 @@
 
 def packed_psum(values):
     flat = jnp.concatenate([jnp.reshape(v, (-1,)) for v in values])
-    flat = lax.psum(flat, ("doc", "term"))
+    flat = lax.psum(lax.psum(flat, "term"), "doc")
     out, start = [], 0
     for v in values:
         size = int(jnp.size(v))

time: 520 us -> 488 us (0.938)
  waiting for transfers between devices: 268 us -> 235 us
  Pallas kernels: 35.8 us -> 60.8 us
  blocking collectives: 140 us -> 126 us
  starting transfers between devices: 14.3 us -> 3.99 us
    reduce_scatter x2, waiting for transfers between devices: 137 us -> 107 us  [per_device(): left_own = lax.psum_scatter(left, 'term', scatter_dimension=0, tiled=True)]
    pallas_call x4, Pallas kernels: 35.8 us -> 60.8 us  [tile_pass(): pl.pallas_call(kernel, out_shape=jax.ShapeDtypeStruct((n_tiles, out_rows,...]
    all_to_all x1, blocking collectives: 44.7 us -> 33.2 us  [scatter_sum(): return jnp.sum(lax.all_to_all(pieces, axis_name, 0, 0, tiled=False), axis=0)]
    all_to_all x1, starting transfers between devices: 14.1 us -> 3.74 us  [scatter_sum(): return jnp.sum(lax.all_to_all(pieces, axis_name, 0, 0, tiled=False), axis=0)]
    psum x2 -> x4, blocking collectives: 95.3 us -> 92.4 us  [packed_psum(): flat = lax.psum(lax.psum(flat, 'term'), 'doc')]
where the time goes in v5:
time: 488 us
  waiting for transfers between devices  235 us (48%)
  blocking collectives  126 us (26%)
  Pallas kernels  60.8 us (12%)
  other arithmetic  34.5 us (7%)
  between operations  15.7 us (3%)
  local copies, waits for them, and re-layouts  7.82 us (2%)
    reduce_scatter x2, waiting for transfers between devices, per_device(): left_own = lax.psum_scatter(left, 'term', scatter_dimension=0, tiled=True)  107 us
    psum x4, blocking collectives, packed_psum(): flat = lax.psum(lax.psum(flat, 'term'), 'doc')  92.4 us
    pallas_call x4, Pallas kernels, tile_pass(): pl.pallas_call(kernel, out_shape=jax.ShapeDtypeStruct((n_tiles, out_rows,...  60.8 us
    all_gather x2, waiting for transfers between devices, per_device(): q_all = lax.all_gather(quotient, 'term', axis=0, tiled=True)  55.1 us
    all_gather x2, waiting for transfers between devices, per_device(): w_all = lax.all_gather(weights, 'doc', axis=0, tiled=True)  47.1 us
    all_to_all x1, blocking collectives, scatter_sum(): return jnp.sum(lax.all_to_all(pieces, axis_name, 0, 0, tiled=False), axis=0)  33.2 us
    all_to_all x1, waiting for transfers between devices, scatter_sum(): return jnp.sum(lax.all_to_all(pieces, axis_name, 0, 0, tiled=False), axis=0)  25.8 us
    another operation x6, other arithmetic, per_device(): lower = jnp.linalg.cholesky(gram_matrix - jnp.outer(along, along) / volume)  13 us
  transfers between devices with their start and end apart: 7, of which 7 were waited for; matrix products, arithmetic and copies ran while one was open for 0% of the time, Pallas kernels for 0%

profile of v5, /device:TPU:0, one launch (start us, length us, event | category | flops | bytes accessed | tf_op | source)
XLA Modules:
  0.0 488.1 jit_solution(898778793934649922)
XLA Ops:
  7.2 0.9 copy.64
  8.1 0.7 copy.82
  9.5 27.1 %all-gather.5.cloned.1.call-done.side_ref = bf16[64,64,128]{2,1,0:T(8,128)(2,1)} async-done(((bf16[8,64,128]{2,1,0:T(8,128)(2,1)}), bf16[64,64,128]{2,1,0:T(8,128)(2,1)}) %all-gather.5.cloned.1.call-update) | async-done | bytes 1048592 | tf_op jit(solution)/shard_map/all_gather | solution.py:141
  36.7 19.0 %shard_map.86 = f32[64,72,128]{2,1,0:T(8,128)} custom-call(s32[512]{0:T(512)} %bitcast.166, s32[512]{0:T(512)} %bitcast.170, s32[1]{0:T(128)} %bitcast.134.cnt_ref, bf16[512,128,128]{2,1,0:T(8,128)(2,1)} %bitcast.138, bf16[64,64,128]{2,1,0:T(8,128)(2,1)} %all-gather.5.cloned.1.call-done.side_ref), custom_call_target="tpu_custom_call" | custom-call | flops 1207959552 | bytes 20185088 | tf_op jit(solution)/shard_map/pallas_call | solution.py:82
  55.8 57.2 %reduce-scatter.3.cloned.1.call-done = f32[16,72,128]{2,1,0:T(8,128)} async-done(((f32[64,72,128]{2,1,0:T(8,128)}), f32[16,72,128]{2,1,0:T(8,128)}) %reduce-scatter.3.cloned.1.call-update) | async-done | bytes 589840 | tf_op jit(solution)/shard_map/reduce_scatter | solution.py:143
  113.0 0.8 slice.75
  113.8 1.8 fusion.9
  115.7 27.5 %all-gather.7.cloned.1.call-done.side_ref = bf16[64,64,128]{2,1,0:T(8,128)(2,1)} async-done(((bf16[16,64,128]{2,1,0:T(8,128)(2,1)}), bf16[64,64,128]{2,1,0:T(8,128)(2,1)}) %all-gather.7.cloned.1.call-update) | async-done | bytes 1048592 | tf_op jit(solution)/shard_map/all_gather | solution.py:148
  143.2 14.2 %shard_map.87 = f32[64,72,128]{2,1,0:T(8,128)} custom-call(s32[512]{0:T(512)} %bitcast.167, s32[512]{0:T(512)} %bitcast.171, s32[1]{0:T(128)} %bitcast.135.cnt_ref, bf16[512,128,128]{2,1,0:T(8,128)(2,1)} %bitcast.139, bf16[64,64,128]{2,1,0:T(8,128)(2,1)} %all-gather.7.cloned.1.call-done.side_ref), custom_call_target="tpu_custom_call" | custom-call | flops 1207959552 | bytes 20185088 | tf_op jit(solution)/shard_map/pallas_call | solution.py:82
  157.5 33.2 %all_to_all.10 = f32[8,8,72,128]{3,2,1,0:T(8,128)S(1)} all-to-all(f32[8,8,72,128]{3,2,1,0:T(8,128)} %bitcast.142), channel_id=1, replica_groups=mesh['doc'=8,'term'=4] {'doc'}, dimensions={0} | all-to-all | bytes 4718592 | tf_op jit(solution)/shard_map/all_to_all | solution.py:101
  190.8 0.6 slice_reduce_fusion
  192.3 0.6 concatenate.6
  193.0 23.8 %psum.28 = f32[4225]{0:T(1024)S(1)} all-reduce(f32[4225]{0:T(1024)S(1)} %concatenate.6), channel_id=1, replica_groups=mesh['doc'=8,'term'=4] {'term'}, use_global_device_ids=true, to_apply=%region_4.0 | all-reduce | flops 4225 | bytes 33800 | tf_op jit(solution)/shard_map/psum | solution.py:106
  216.7 22.3 %psum.29 = f32[4225]{0:T(1024)S(1)} all-reduce(f32[4225]{0:T(1024)S(1)} %psum.28), channel_id=1, replica_groups=mesh['doc'=8,'term'=4] {'doc'}, use_global_device_ids=true, to_apply=%region_5.0 | all-reduce | flops 4225 | bytes 33800 | tf_op jit(solution)/shard_map/psum | solution.py:106
  239.1 0.5 slice.80
  239.6 0.6 fusion.41
  240.4 0.7 divide_subtract_fusion.1
  241.2 0.7 fusion.35
  241.9 5.8 %cholesky.44 = f32[64,64]{1,0:T(8,128)S(1)} custom-call(f32[64,64]{1,0:T(8,128)S(1)} %fusion.35), custom_call_target="Cholesky" | custom-call | tf_op jit(solution)/shard_map/jit(cholesky)/cholesky | solution.py:168
  247.8 0.6 compare_reduce_fusion.1
  248.5 0.7 fusion.27
  249.1 4.9 %custom-call.11 = f32[1,64,64]{1,2,0:T(8,128)S(1)} custom-call(f32[1,64,64]{2,1,0:T(8,128)S(1)} %fusion.27), custom_call_target="InvertDiagBlocksLowerTriangular" | custom-call | tf_op jit(solution)/shard_map/jit(_solve_triangular)/triangular_solve | solution.py:171
  254.0 0.5 convolution_bitcast_fusion
  254.5 0.7 fusion.18
  255.3 20.0 %all-gather.9.cloned.1.call-done.side_ref = bf16[64,64,128]{2,1,0:T(8,128)(2,1)} async-done(((bf16[8,64,128]{2,1,0:T(8,128)(2,1)}), bf16[64,64,128]{2,1,0:T(8,128)(2,1)}) %all-gather.9.cloned.1.call-update) | async-done | bytes 1048592 | tf_op jit(solution)/shard_map/all_gather | solution.py:141
  275.2 15.1 %shard_map.88 = f32[64,64,128]{2,1,0:T(8,128)} custom-call(s32[512]{0:T(512)} %bitcast.168, s32[512]{0:T(512)} %bitcast.172, s32[1]{0:T(128)} %bitcast.136.cnt_ref, bf16[512,128,128]{2,1,0:T(8,128)(2,1)} %bitcast.140, bf16[64,64,128]{2,1,0:T(8,128)(2,1)} %all-gather.9.cloned.1.call-done.side_ref), custom_call_target="tpu_custom_call" | custom-call | flops 1073741824 | bytes 19922944 | tf_op jit(solution)/shard_map/pallas_call | solution.py:82
  290.4 50.0 %reduce-scatter.5.cloned.1.call-done = f32[16,64,128]{2,1,0:T(8,128)} async-done(((f32[64,64,128]{2,1,0:T(8,128)}), f32[16,64,128]{2,1,0:T(8,128)}) %reduce-scatter.5.cloned.1.call-update) | async-done | bytes 524304 | tf_op jit(solution)/shard_map/reduce_scatter | solution.py:143
  340.4 1.8 fusion.39
  342.3 27.5 %all-gather.11.cloned.1.call-done.side_ref = bf16[64,64,128]{2,1,0:T(8,128)(2,1)} async-done(((bf16[16,64,128]{2,1,0:T(8,128)(2,1)}), bf16[64,64,128]{2,1,0:T(8,128)(2,1)}) %all-gather.11.cloned.1.call-update) | async-done | bytes 1048592 | tf_op jit(solution)/shard_map/all_gather | solution.py:148
  369.8 12.4 %shard_map.89 = f32[64,64,128]{2,1,0:T(8,128)} custom-call(s32[512]{0:T(512)} %bitcast.169, s32[512]{0:T(512)} %bitcast.173, s32[1]{0:T(128)} %bitcast.137.cnt_ref, bf16[512,128,128]{2,1,0:T(8,128)(2,1)} %bitcast.141, bf16[64,64,128]{2,1,0:T(8,128)(2,1)} %all-gather.11.cloned.1.call-done.side_ref), custom_call_target="tpu_custom_call" | custom-call | flops 1073741824 | bytes 19922944 | tf_op jit(solution)/shard_map/pallas_call | solution.py:82
  382.2 3.7 all-to-all-start.1
  386.2 0.5 convolution_bitcast_fusion.2
  386.8 25.8 %all-to-all-done.1 = f32[8,8,64,128]{3,2,1,0:T(8,128)S(1)} async-done(((f32[8,8,64,128]{3,2,1,0:T(8,128)}), f32[8,8,64,128]{3,2,1,0:T(8,128)S(1)}, u32[]{:S(2)}, u32[]{:S(2)}) %all-to-all-start.1) | async-done | bytes 2097184 | tf_op jit(solution)/shard_map/all_to_all | solution.py:101
  414.0 0.6 concatenate.7
  414.6 23.3 %psum.30 = f32[12545]{0:T(1024)S(1)} all-reduce(f32[12545]{0:T(1024)S(1)} %concatenate.7), channel_id=1, replica_groups=mesh['doc'=8,'term'=4] {'term'}, use_global_device_ids=true, to_apply=%region_13.0 | all-reduce | flops 12545 | bytes 100360 | tf_op jit(solution)/shard_map/psum | solution.py:106
  437.9 23.0 %psum.31 = f32[12545]{0:T(1024)S(1)} all-reduce(f32[12545]{0:T(1024)S(1)} %psum.30), channel_id=1, replica_groups=mesh['doc'=8,'term'=4] {'doc'}, use_global_device_ids=true, to_apply=%region_14.17 | all-reduce | flops 12545 | bytes 100360 | tf_op jit(solution)/shard_map/psum | solution.py:106
  460.9 0.5 slice.81
  462.1 0.7 fusion.38
  463.2 0.7 divide_subtract_fusion
  464.1 0.7 fusion.33
  464.8 5.8 %cholesky.55 = f32[64,64]{1,0:T(8,128)S(1)} custom-call(f32[64,64]{1,0:T(8,128)S(1)} %fusion.33), custom_call_target="Cholesky" | custom-call | tf_op jit(solution)/shard_map/jit(cholesky)/cholesky | solution.py:168
  470.7 0.6 compare_reduce_fusion
  471.3 0.7 fusion.28
  472.0 4.9 %custom-call.9 = f32[1,64,64]{1,2,0:T(8,128)S(1)} custom-call(f32[1,64,64]{2,1,0:T(8,128)S(1)} %fusion.28), custom_call_target="InvertDiagBlocksLowerTriangular" | custom-call | tf_op jit(solution)/shard_map/jit(_solve_triangular)/triangular_solve | solution.py:181
  476.9 0.5 fusion.5
  478.4 0.7 broadcast_in_dim_reshape.7
  479.3 0.7 fusion.2
  480.4 0.9 broadcast_in_dim_reshape.6
  (54 shorter events, 5.4 us)
Async XLA Ops:
  7.2 29.5 %all-gather.5.cloned.1.call-start = ((), (), s32[]{:S(2)}) async-start(), calls=%async_computation.4 | async-start | bytes 1179648 | tf_op jit(solution)/shard_map/all_gather | solution.py:141
  8.8 104.1 %reduce-scatter.3.cloned.1.call-start = ((), (), s32[]{:S(2)}) async-start(), calls=%async_computation.5 | async-start | bytes 2949120 | tf_op jit(solution)/shard_map/reduce_scatter | solution.py:143
  55.8 87.5 %all-gather.7.cloned.1.call-start = ((), (), s32[]{:S(2)}) async-start(), calls=%async_computation.6 | async-start | bytes 1310720 | tf_op jit(solution)/shard_map/all_gather | solution.py:148
  115.6 159.6 %all-gather.9.cloned.1.call-start = ((), (), s32[]{:S(2)}) async-start(), calls=%async_computation.7 | async-start | bytes 1179648 | tf_op jit(solution)/shard_map/all_gather | solution.py:141
  255.2 85.2 %reduce-scatter.5.cloned.1.call-start = ((), (), s32[]{:S(2)}) async-start(), calls=%async_computation.8 | async-start | bytes 2621440 | tf_op jit(solution)/shard_map/reduce_scatter | solution.py:143
  290.4 79.4 %all-gather.11.cloned.1.call-start = ((), (), s32[]{:S(2)}) async-start(), calls=%async_computation.9 | async-start | bytes 1310720 | tf_op jit(solution)/shard_map/all_gather | solution.py:148
  382.2 3.8 copy-start.2
  382.2 3.9 copy-start.1
  382.2 4.1 copy-start
  382.2 30.4 %all-to-all-start.1 = ((f32[8,8,64,128]{3,2,1,0:T(8,128)}), f32[8,8,64,128]{3,2,1,0:T(8,128)S(1)}, u32[]{:S(2)}, u32[]{:S(2)}) async-start(f32[8,8,64,128]{3,2,1,0:T(8,128)} %bitcast.143), calls=%async_computation.3 | async-start | bytes 4194304 | tf_op jit(solution)/shard_map/all_to_all | solution.py:101
Sparse Core Ops, SparseCore 0:
  10.5 26.1 all-gather.4
  55.9 57.0 reduce-scatter.2
  115.8 27.4 all-gather.6
  255.3 19.8 all-gather.8
  290.5 49.8 reduce-scatter.4
  342.5 27.2 all-gather.10

commit v6 on v5

--- a/solution.py
+++ b/solution.py
@@ -101,9 +101,20 @@
     return jnp.sum(lax.all_to_all(pieces, axis_name, 0, 0, tiled=False), axis=0)
 
 
-def packed_psum(values):
+def exchange_sum(flat, axis_name, parts):
+    copies = jnp.broadcast_to(flat, (parts,) + flat.shape)
+    return jnp.sum(lax.all_to_all(copies, axis_name, 0, 0, tiled=False), axis=0)
+
+
+def exchange_gather(x, axis_name, parts):
+    copies = jnp.broadcast_to(x, (parts,) + x.shape)
+    got = lax.all_to_all(copies, axis_name, 0, 0, tiled=False)
+    return got.reshape((parts * x.shape[0],) + x.shape[1:])
+
+
+def packed_psum(n_doc, n_term, values):
     flat = jnp.concatenate([jnp.reshape(v, (-1,)) for v in values])
-    flat = lax.psum(lax.psum(flat, "term"), "doc")
+    flat = exchange_sum(exchange_sum(flat, "term", n_term), "doc", n_doc)
     out, start = [], 0
     for v in values:
         size = int(jnp.size(v))
@@ -138,7 +149,7 @@
     volume = None
     for step in range(ITERS):
         first = step == 0
-        w_all = lax.all_gather(weights, "doc", axis=0, tiled=True)
+        w_all = exchange_gather(weights, "doc", n_doc)
         left = tile_pass(local_tiles, rows, cols, count, w_all, True, first)
         left_own = lax.psum_scatter(left, "term", scatter_dimension=0, tiled=True)
         summed_own = left_own[:, :width_k, :]
@@ -163,7 +174,7 @@
             doc_part = jnp.einsum("tki,tij->kj", doc_ratio, doc_onehot, precision=HIGH)
             term_part = jnp.einsum("tki,tij->kj", raw / root[:, None, :], term_onehot, precision=HIGH)
             sums += [doc_part, term_part, jnp.sum(doc_onehot, axis=(0, 1)), jnp.sum(term_onehot, axis=(0, 1))]
-        sums = packed_psum(sums)
+        sums = packed_psum(n_doc, n_term, sums)
         gram_matrix, along, energy, volume = sums[:4]
         lower = jnp.linalg.cholesky(gram_matrix - jnp.outer(along, along) / volume)
         projected = raw - root[:, None, :] * (along / volume)[None, :, None]

time: 488 us -> 437 us (0.90)
  waiting for transfers between devices: 235 us -> 191 us
  blocking collectives: 126 us -> 92 us
  Pallas kernels: 60.8 us -> 79.1 us
  starting transfers between devices: 3.99 us -> 10.1 us
    psum x4 -> x0, blocking collectives: 92.4 us -> none  [packed_psum(): flat = lax.psum(lax.psum(flat, 'term'), 'doc')]
    all_to_all x0 -> x5, blocking collectives: none -> 57.5 us  [the longest x4 39 us: exchange_sum(): return jnp.sum(lax.all_to_all(copies, axis_name, 0, 0, tiled=False), axis=0)]
    all_gather x2 -> x0, waiting for transfers between devices: 47.1 us -> none  [per_device(): w_all = lax.all_gather(weights, 'doc', axis=0, tiled=True)]
    pallas_call x4, Pallas kernels: 60.8 us -> 79.1 us  [tile_pass(): pl.pallas_call(kernel, out_shape=jax.ShapeDtypeStruct((n_tiles, out_rows,...]
    all_to_all x0 -> x1, waiting for transfers between devices: none -> 14.7 us  [exchange_gather(): got = lax.all_to_all(copies, axis_name, 0, 0, tiled=False)]
    reduce_scatter x2, waiting for transfers between devices: 107 us -> 95.1 us  [per_device(): left_own = lax.psum_scatter(left, 'term', scatter_dimension=0, tiled=True)]
    all_to_all x0 -> x1, starting transfers between devices: none -> 5.17 us  [exchange_gather(): got = lax.all_to_all(copies, axis_name, 0, 0, tiled=False)]
  transfers between devices with their start and end apart: 7 -> 6, of which waited for: 7 -> 6; matrix products, arithmetic and copies ran while one was open for 0% -> 0% of each run, Pallas kernels for 0% -> 0%
where the time goes in v6:
time: 437 us; the launch traced here: 436 us
  waiting for transfers between devices  191 us (44%)
  blocking collectives  92 us (21%)
  Pallas kernels  79.1 us (18%)
  other arithmetic  34.5 us (8%)
  between operations  15.4 us (4%)
  starting transfers between devices  10.1 us (2%)
  local copies, waits for them, and re-layouts  10 us (2%)
  matrix products  4.51 us (1%)
    reduce_scatter x2, waiting for transfers between devices, per_device(): left_own = lax.psum_scatter(left, 'term', scatter_dimension=0, tiled=True)  95.1 us
    pallas_call x4, Pallas kernels, tile_pass(): pl.pallas_call(kernel, out_shape=jax.ShapeDtypeStruct((n_tiles, out_rows,...  79.1 us
    all_gather x2, waiting for transfers between devices, per_device(): q_all = lax.all_gather(quotient, 'term', axis=0, tiled=True)  55.1 us
    all_to_all x4, blocking collectives, exchange_sum(): return jnp.sum(lax.all_to_all(copies, axis_name, 0, 0, tiled=False), axis=0)  39 us
    all_to_all x1, blocking collectives, scatter_sum(): return jnp.sum(lax.all_to_all(pieces, axis_name, 0, 0, tiled=False), axis=0)  34.5 us
    all_to_all x1, waiting for transfers between devices, scatter_sum(): return jnp.sum(lax.all_to_all(pieces, axis_name, 0, 0, tiled=False), axis=0)  25.8 us
    all_to_all x1, blocking collectives, exchange_gather(): got = lax.all_to_all(copies, axis_name, 0, 0, tiled=False)  18.5 us
    all_to_all x1, waiting for transfers between devices, exchange_gather(): got = lax.all_to_all(copies, axis_name, 0, 0, tiled=False)  14.7 us
  transfers between devices with their start and end apart: 6, of which 6 were waited for; matrix products, arithmetic and copies ran while one was open for 0% of the time, Pallas kernels for 0%

profile of v6, /device:TPU:0, one launch (start us, length us, event | category | flops | bytes accessed | tf_op | source)
XLA Modules:
  0.0 436.4 jit_solution(16868581276469160974)
XLA Ops:
  7.2 0.9 copy.111
  8.1 1.2 broadcast_in_dim.13
  9.4 5.2 %all-to-all-start = ((bf16[8,8,64,128]{3,2,1,0:T(8,128)(2,1)}), bf16[8,8,64,128]{3,2,1,0:T(8,128)(2,1)S(1)}, u32[]{:S(2)}, u32[]{:S(2)}) async-start(bf16[8,8,64,128]{3,2,1,0:T(8,128)(2,1)} %broadcast_in_dim.13), calls=%async_computation | async-start | bytes 2097152 | tf_op jit(solution)/shard_map/all_to_all | solution.py:111
  15.2 14.7 %all-to-all-done = bf16[8,8,64,128]{3,2,1,0:T(8,128)(2,1)S(1)} async-done(((bf16[8,8,64,128]{3,2,1,0:T(8,128)(2,1)}), bf16[8,8,64,128]{3,2,1,0:T(8,128)(2,1)S(1)}, u32[]{:S(2)}, u32[]{:S(2)}) %all-to-all-start) | async-done | bytes 1048608 | tf_op jit(solution)/shard_map/all_to_all | solution.py:111
  29.9 1.0 copy-done
  30.9 25.3 %shard_map.86 = f32[64,72,128]{2,1,0:T(8,128)} custom-call(s32[512]{0:T(512)} %bitcast.170, s32[512]{0:T(512)} %bitcast.174, s32[1]{0:T(128)} %bitcast.136.cnt_ref, bf16[512,128,128]{2,1,0:T(8,128)(2,1)} %bitcast.140, bf16[64,64,128]{2,1,0:T(8,128)(2,1)} %bitcast.146), custom_call_target="tpu_custom_call" | custom-call | flops 1207959552 | bytes 20185088 | tf_op jit(solution)/shard_map/pallas_call | solution.py:82
  56.3 51.2 %reduce-scatter.3.cloned.1.call-done = f32[16,72,128]{2,1,0:T(8,128)} async-done(((f32[64,72,128]{2,1,0:T(8,128)}), f32[16,72,128]{2,1,0:T(8,128)}) %reduce-scatter.3.cloned.1.call-update) | async-done | bytes 589840 | tf_op jit(solution)/shard_map/reduce_scatter | solution.py:154
  107.6 0.8 slice.75
  108.4 1.8 fusion.9
  110.3 27.5 %all-gather.3.cloned.1.call-done.side_ref = bf16[64,64,128]{2,1,0:T(8,128)(2,1)} async-done(((bf16[16,64,128]{2,1,0:T(8,128)(2,1)}), bf16[64,64,128]{2,1,0:T(8,128)(2,1)}) %all-gather.3.cloned.1.call-update) | async-done | bytes 1048592 | tf_op jit(solution)/shard_map/all_gather | solution.py:159
  137.8 18.4 %shard_map.87 = f32[64,72,128]{2,1,0:T(8,128)} custom-call(s32[512]{0:T(512)} %bitcast.171, s32[512]{0:T(512)} %bitcast.175, s32[1]{0:T(128)} %bitcast.137.cnt_ref, bf16[512,128,128]{2,1,0:T(8,128)(2,1)} %bitcast.141, bf16[64,64,128]{2,1,0:T(8,128)(2,1)} %all-gather.3.cloned.1.call-done.side_ref), custom_call_target="tpu_custom_call" | custom-call | flops 1207959552 | bytes 20185088 | tf_op jit(solution)/shard_map/pallas_call | solution.py:82
  156.2 34.5 %all_to_all.44 = f32[8,8,72,128]{3,2,1,0:T(8,128)S(1)} all-to-all(f32[8,8,72,128]{3,2,1,0:T(8,128)} %bitcast.144), channel_id=1, replica_groups=mesh['doc'=8,'term'=4] {'doc'}, dimensions={0} | all-to-all | bytes 4718592 | tf_op jit(solution)/shard_map/all_to_all | solution.py:101
  190.8 0.6 slice_reduce_fusion
  192.3 0.6 concatenate.6
  193.0 9.5 %all_to_all.45 = f32[4,1,4225]{2,1,0:T(1,128)S(1)} all-to-all(f32[4,1,4225]{2,1,0:T(1,128)S(1)} %broadcast_in_dim.14), channel_id=1, replica_groups=mesh['doc'=8,'term'=4] {'term'}, dimensions={0} | all-to-all | bytes 135200 | tf_op jit(solution)/shard_map/all_to_all | solution.py:106
  202.7 8.0 %all_to_all.46 = f32[8,1,4225]{2,1,0:T(1,128)S(1)} all-to-all(f32[8,1,4225]{2,1,0:T(1,128)S(1)} %broadcast_in_dim.15), channel_id=1, replica_groups=mesh['doc'=8,'term'=4] {'doc'}, dimensions={0} | all-to-all | bytes 270400 | tf_op jit(solution)/shard_map/all_to_all | solution.py:106
  210.8 0.5 slice.80
  211.3 0.6 fusion.41
  212.1 0.7 divide_subtract_fusion.1
  212.9 0.7 fusion.35
  213.7 5.8 %cholesky.44 = f32[64,64]{1,0:T(8,128)S(1)} custom-call(f32[64,64]{1,0:T(8,128)S(1)} %fusion.35), custom_call_target="Cholesky" | custom-call | tf_op jit(solution)/shard_map/jit(cholesky)/cholesky | solution.py:179
  219.6 0.6 compare_reduce_fusion.1
  220.2 0.7 fusion.27
  220.9 4.9 %custom-call.11 = f32[1,64,64]{1,2,0:T(8,128)S(1)} custom-call(f32[1,64,64]{2,1,0:T(8,128)S(1)} %fusion.27), custom_call_target="InvertDiagBlocksLowerTriangular" | custom-call | tf_op jit(solution)/shard_map/jit(_solve_triangular)/triangular_solve | solution.py:182
  225.8 0.5 convolution_bitcast_fusion
  226.5 18.5 %all_to_all.47 = bf16[8,8,64,128]{3,2,1,0:T(8,128)(2,1)} all-to-all(bf16[8,8,64,128]{3,2,1,0:T(8,128)(2,1)S(1)} %broadcast_in_dim.16), channel_id=1, replica_groups=mesh['doc'=8,'term'=4] {'doc'}, dimensions={0} | all-to-all | bytes 2097152 | tf_op jit(solution)/shard_map/all_to_all | solution.py:111
  245.0 19.7 %shard_map.88 = f32[64,64,128]{2,1,0:T(8,128)} custom-call(s32[512]{0:T(512)} %bitcast.172, s32[512]{0:T(512)} %bitcast.176, s32[1]{0:T(128)} %bitcast.138.cnt_ref, bf16[512,128,128]{2,1,0:T(8,128)(2,1)} %bitcast.142, bf16[64,64,128]{2,1,0:T(8,128)(2,1)} %bitcast.147), custom_call_target="tpu_custom_call" | custom-call | flops 1073741824 | bytes 19922944 | tf_op jit(solution)/shard_map/pallas_call | solution.py:82
  264.8 43.9 %reduce-scatter.5.cloned.1.call-done = f32[16,64,128]{2,1,0:T(8,128)} async-done(((f32[64,64,128]{2,1,0:T(8,128)}), f32[16,64,128]{2,1,0:T(8,128)}) %reduce-scatter.5.cloned.1.call-update) | async-done | bytes 524304 | tf_op jit(solution)/shard_map/reduce_scatter | solution.py:154
  308.7 1.8 fusion.39
  310.5 27.5 %all-gather.5.cloned.1.call-done.side_ref = bf16[64,64,128]{2,1,0:T(8,128)(2,1)} async-done(((bf16[16,64,128]{2,1,0:T(8,128)(2,1)}), bf16[64,64,128]{2,1,0:T(8,128)(2,1)}) %all-gather.5.cloned.1.call-update) | async-done | bytes 1048592 | tf_op jit(solution)/shard_map/all_gather | solution.py:159
  338.0 15.7 %shard_map.89 = f32[64,64,128]{2,1,0:T(8,128)} custom-call(s32[512]{0:T(512)} %bitcast.173, s32[512]{0:T(512)} %bitcast.177, s32[1]{0:T(128)} %bitcast.139.cnt_ref, bf16[512,128,128]{2,1,0:T(8,128)(2,1)} %bitcast.143, bf16[64,64,128]{2,1,0:T(8,128)(2,1)} %all-gather.5.cloned.1.call-done.side_ref), custom_call_target="tpu_custom_call" | custom-call | flops 1073741824 | bytes 19922944 | tf_op jit(solution)/shard_map/pallas_call | solution.py:82
  353.8 4.8 %all-to-all-start.5 = ((f32[8,8,64,128]{3,2,1,0:T(8,128)}), f32[8,8,64,128]{3,2,1,0:T(8,128)S(1)}, u32[]{:S(2)}, u32[]{:S(2)}) async-start(f32[8,8,64,128]{3,2,1,0:T(8,128)} %bitcast.145), calls=%async_computation.7 | async-start | bytes 4194304 | tf_op jit(solution)/shard_map/all_to_all | solution.py:101
  359.4 25.8 %all-to-all-done.5 = f32[8,8,64,128]{3,2,1,0:T(8,128)S(1)} async-done(((f32[8,8,64,128]{3,2,1,0:T(8,128)}), f32[8,8,64,128]{3,2,1,0:T(8,128)S(1)}, u32[]{:S(2)}, u32[]{:S(2)}) %all-to-all-start.5) | async-done | bytes 2097184 | tf_op jit(solution)/shard_map/all_to_all | solution.py:101
  386.6 0.6 concatenate.7
  387.4 10.4 %all_to_all.48 = f32[4,1,12545]{2,1,0:T(1,128)S(1)} all-to-all(f32[4,1,12545]{2,1,0:T(1,128)S(1)} %broadcast_in_dim.17), channel_id=1, replica_groups=mesh['doc'=8,'term'=4] {'term'}, dimensions={0} | all-to-all | bytes 401440 | tf_op jit(solution)/shard_map/all_to_all | solution.py:106
  398.2 11.1 %all_to_all.49 = f32[8,1,12545]{2,1,0:T(1,128)S(1)} all-to-all(f32[8,1,12545]{2,1,0:T(1,128)S(1)} %broadcast_in_dim.18), channel_id=1, replica_groups=mesh['doc'=8,'term'=4] {'doc'}, dimensions={0} | all-to-all | bytes 802880 | tf_op jit(solution)/shard_map/all_to_all | solution.py:106
  409.6 0.5 slice.81
  410.8 0.7 fusion.38
  411.9 0.7 divide_subtract_fusion
  412.7 0.7 fusion.33
  413.5 5.8 %cholesky.55 = f32[64,64]{1,0:T(8,128)S(1)} custom-call(f32[64,64]{1,0:T(8,128)S(1)} %fusion.33), custom_call_target="Cholesky" | custom-call | tf_op jit(solution)/shard_map/jit(cholesky)/cholesky | solution.py:179
  419.3 0.6 compare_reduce_fusion
  420.0 0.7 fusion.28
  420.6 4.9 %custom-call.9 = f32[1,64,64]{1,2,0:T(8,128)S(1)} custom-call(f32[1,64,64]{2,1,0:T(8,128)S(1)} %fusion.28), custom_call_target="InvertDiagBlocksLowerTriangular" | custom-call | tf_op jit(solution)/shard_map/jit(_solve_triangular)/triangular_solve | solution.py:192
  425.5 0.5 fusion.5
  427.1 0.7 broadcast_in_dim_reshape.7
  428.0 0.7 fusion.2
  429.0 0.9 broadcast_in_dim_reshape.6
  (63 shorter events, 7.1 us)
Async XLA Ops:
  9.4 20.6 %all-to-all-start = ((bf16[8,8,64,128]{3,2,1,0:T(8,128)(2,1)}), bf16[8,8,64,128]{3,2,1,0:T(8,128)(2,1)S(1)}, u32[]{:S(2)}, u32[]{:S(2)}) async-start(bf16[8,8,64,128]{3,2,1,0:T(8,128)(2,1)} %broadcast_in_dim.13), calls=%async_computation | async-start | bytes 2097152 | tf_op jit(solution)/shard_map/all_to_all | solution.py:111
  14.5 93.0 %reduce-scatter.3.cloned.1.call-start = ((), (), s32[]{:S(2)}) async-start(), calls=%async_computation.10 | async-start | bytes 2949120 | tf_op jit(solution)/shard_map/reduce_scatter | solution.py:154
  29.9 1.0 copy-start
  56.3 81.5 %all-gather.3.cloned.1.call-start = ((), (), s32[]{:S(2)}) async-start(), calls=%async_computation.11 | async-start | bytes 1310720 | tf_op jit(solution)/shard_map/all_gather | solution.py:159
  110.2 198.5 %reduce-scatter.5.cloned.1.call-start = ((), (), s32[]{:S(2)}) async-start(), calls=%async_computation.12 | async-start | bytes 2621440 | tf_op jit(solution)/shard_map/reduce_scatter | solution.py:154
  264.7 73.3 %all-gather.5.cloned.1.call-start = ((), (), s32[]{:S(2)}) async-start(), calls=%async_computation.13 | async-start | bytes 1310720 | tf_op jit(solution)/shard_map/all_gather | solution.py:159
  353.8 4.8 %copy-start.3 = (s32[1,1024]{1,0:T(1,128)S(1)}, s32[1,1024]{1,0:T(1,128)}, u32[]{:S(2)}) copy-start(s32[1,1024]{1,0:T(1,128)} %param.16) | copy-start | bytes 12292
  353.8 4.9 %copy-start.2 = (s32[1,2048]{1,0:T(1,128)S(1)}, s32[1,2048]{1,0:T(1,128)}, u32[]{:S(2)}) copy-start(s32[1,2048]{1,0:T(1,128)} %param.15) | copy-start | bytes 24580
  353.8 5.1 %copy-start.1 = (f32[16,64,128]{2,1,0:T(8,128)S(1)}, f32[16,64,128]{2,1,0:T(8,128)}, u32[]{:S(2)}) copy-start(f32[16,64,128]{2,1,0:T(8,128)} %reduce-scatter.5.cloned.1.call-done) | copy-start | bytes 1572868
  353.8 31.4 %all-to-all-start.5 = ((f32[8,8,64,128]{3,2,1,0:T(8,128)}), f32[8,8,64,128]{3,2,1,0:T(8,128)S(1)}, u32[]{:S(2)}, u32[]{:S(2)}) async-start(f32[8,8,64,128]{3,2,1,0:T(8,128)} %bitcast.145), calls=%async_computation.7 | async-start | bytes 4194304 | tf_op jit(solution)/shard_map/all_to_all | solution.py:101
Sparse Core Ops, SparseCore 0:
  56.4 51.1 reduce-scatter.2
  110.4 27.4 all-gather.2
  264.9 43.7 reduce-scatter.4
  310.8 27.2 all-gather.4

commit v7 on v6

--- a/solution.py
+++ b/solution.py
@@ -112,6 +112,25 @@
     return got.reshape((parts * x.shape[0],) + x.shape[1:])
 
 
+def line_scatter_sum(x, axis_name, parts):
+    me = lax.axis_index(axis_name)
+    chunks = x.reshape((parts, x.shape[0] // parts) + x.shape[1:])
+
+    def chunk(index):
+        return lax.dynamic_index_in_dim(chunks, jnp.clip(index, 0, parts - 1), 0, keepdims=False)
+
+    rightward = leftward = None
+    for s in range(1, parts):
+        send_r = chunk(parts - s + me)
+        send_l = chunk(s - parts + me)
+        if rightward is not None:
+            send_r = send_r + rightward
+            send_l = send_l + leftward
+        rightward = lax.ppermute(send_r, axis_name, [(i, i + 1) for i in range(s)])
+        leftward = lax.ppermute(send_l, axis_name, [(parts - 1 - i, parts - 2 - i) for i in range(s)])
+    return chunk(me) + rightward + leftward
+
+
 def packed_psum(n_doc, n_term, values):
     flat = jnp.concatenate([jnp.reshape(v, (-1,)) for v in values])
     flat = exchange_sum(exchange_sum(flat, "term", n_term), "doc", n_doc)
@@ -151,7 +170,7 @@
         first = step == 0
         w_all = exchange_gather(weights, "doc", n_doc)
         left = tile_pass(local_tiles, rows, cols, count, w_all, True, first)
-        left_own = lax.psum_scatter(left, "term", scatter_dimension=0, tiled=True)
+        left_own = line_scatter_sum(left, "term", n_term)
         summed_own = left_own[:, :width_k, :]
         if first:
             doc_degree = left_own[:, width_k, :]

time: 437 us -> 463 us (1.059)
  starting transfers between devices: 10.1 us -> 62.7 us
  Pallas kernels: 79.1 us -> 35.6 us
  blocking collectives: 92 us -> 105 us
  waiting for transfers between devices: 191 us -> 181 us
  other arithmetic: 34.5 us -> 40.4 us
    reduce_scatter x2 -> x0, waiting for transfers between devices: 95.1 us -> none  [per_device(): left_own = lax.psum_scatter(left, 'term', scatter_dimension=0, tiled=True)]
    ppermute x0 -> x12, waiting for transfers between devices: none -> 64.3 us  [the longest x6 37.8 us: line_scatter_sum(): rightward = lax.ppermute(send_r, axis_name, [(i, i + 1) for i in range(s)])]
    ppermute x0 -> x12, starting transfers between devices: none -> 49.2 us  [the longest x6 42.3 us: line_scatter_sum(): rightward = lax.ppermute(send_r, axis_name, [(i, i + 1) for i in range(s)])]
    pallas_call x4, Pallas kernels: 79.1 us -> 35.6 us  [tile_pass(): pl.pallas_call(kernel, out_shape=jax.ShapeDtypeStruct((n_tiles, out_rows,...]
    all_gather x2, waiting for transfers between devices: 55.1 us -> 75.9 us  [per_device(): q_all = lax.all_gather(quotient, 'term', axis=0, tiled=True)]
    all_to_all x4, blocking collectives: 39 us -> 47.9 us  [exchange_sum(): return jnp.sum(lax.all_to_all(copies, axis_name, 0, 0, tiled=False), axis=0)]
    add x0 -> x7, other arithmetic: none -> 7.73 us  [the longest x4 4.57 us: line_scatter_sum(): send_r = send_r + rightward]
  transfers between devices with their start and end apart: 6 -> 16, of which waited for: 6 -> 12; matrix products, arithmetic and copies ran while one was open for 0% -> 1% of each run, Pallas kernels for 0% -> 0%
where the time goes in v7:
time: 463 us; the launch traced here: 458 us
  waiting for transfers between devices  181 us (39%)
  blocking collectives  105 us (23%)
  starting transfers between devices  62.7 us (14%)
  other arithmetic  40.4 us (9%)
  Pallas kernels  35.6 us (8%)
  between operations  15.8 us (3%)
  local copies, waits for them, and re-layouts  12.9 us (3%)
    all_gather x2, waiting for transfers between devices, per_device(): q_all = lax.all_gather(quotient, 'term', axis=0, tiled=True)  75.9 us
    all_to_all x4, blocking collectives, exchange_sum(): return jnp.sum(lax.all_to_all(copies, axis_name, 0, 0, tiled=False), axis=0)  47.9 us
    ppermute x6, starting transfers between devices, line_scatter_sum(): rightward = lax.ppermute(send_r, axis_name, [(i, i + 1) for i in range(s)])  42.3 us
    all_to_all x1, blocking collectives, scatter_sum(): return jnp.sum(lax.all_to_all(pieces, axis_name, 0, 0, tiled=False), axis=0)  38.9 us
    ppermute x6, waiting for transfers between devices, line_scatter_sum(): rightward = lax.ppermute(send_r, axis_name, [(i, i + 1) for i in range(s)])  37.8 us
    pallas_call x4, Pallas kernels, tile_pass(): pl.pallas_call(kernel, out_shape=jax.ShapeDtypeStruct((n_tiles, out_rows,...  35.6 us
    ppermute x6, waiting for transfers between devices, line_scatter_sum(): lax.ppermute(send_l, axis_name, [(parts - 1 - i, parts - 2 - i) for i in...  26.5 us
    all_to_all x1, waiting for transfers between devices, scatter_sum(): return jnp.sum(lax.all_to_all(pieces, axis_name, 0, 0, tiled=False), axis=0)  25.8 us
  transfers between devices with their start and end apart: 16, of which 12 were waited for; matrix products, arithmetic and copies ran while one was open for 1% of the time, Pallas kernels for 0%

profile of v7, /device:TPU:0, one launch (start us, length us, event | category | flops | bytes accessed | tf_op | source)
XLA Modules:
  0.0 457.8 jit_solution(17868602203461719186)
XLA Ops:
  7.2 0.9 copy.111
  8.1 1.2 broadcast_in_dim.13
  9.4 5.2 %all-to-all-start = ((bf16[8,8,64,128]{3,2,1,0:T(8,128)(2,1)}), bf16[8,8,64,128]{3,2,1,0:T(8,128)(2,1)S(1)}, u32[]{:S(2)}, u32[]{:S(2)}) async-start(bf16[8,8,64,128]{3,2,1,0:T(8,128)(2,1)} %broadcast_in_dim.13), calls=%async_computation | async-start | bytes 2097152 | tf_op jit(solution)/shard_map/all_to_all | solution.py:111
  15.2 14.7 %all-to-all-done = bf16[8,8,64,128]{3,2,1,0:T(8,128)(2,1)S(1)} async-done(((bf16[8,8,64,128]{3,2,1,0:T(8,128)(2,1)}), bf16[8,8,64,128]{3,2,1,0:T(8,128)(2,1)S(1)}, u32[]{:S(2)}, u32[]{:S(2)}) %all-to-all-start) | async-done | bytes 1048608 | tf_op jit(solution)/shard_map/all_to_all | solution.py:111
  29.9 1.0 copy-done.2
  30.9 10.4 %shard_map.86 = f32[64,72,128]{2,1,0:T(8,128)} custom-call(s32[512]{0:T(512)} %bitcast.215, s32[512]{0:T(512)} %bitcast.219, s32[1]{0:T(128)} %bitcast.174.cnt_ref, bf16[512,128,128]{2,1,0:T(8,128)(2,1)} %bitcast.178, bf16[64,64,128]{2,1,0:T(8,128)(2,1)} %bitcast.194), custom_call_target="tpu_custom_call" | custom-call | flops 1207959552 | bytes 20185088 | tf_op jit(solution)/shard_map/pallas_call | solution.py:82
  41.4 2.3 dynamic-slice_bitcast_fusion.1
  43.6 13.7 %collective-permute-start = (f32[16,72,128]{2,1,0:T(8,128)}, f32[16,72,128]{2,1,0:T(8,128)}, u32[]{:S(2)}, u32[]{:S(2)}) collective-permute-start(f32[16,72,128]{2,1,0:T(8,128)} %get-tuple-element.8), channel_id=1, source_target_pairs={{0,1},{4,5},{8,9},{12,13},{16,17},{20,21},{24,25},{28,29}} | collective-permute-start | bytes 1769480 | tf_op jit(solution)/shard_map/ppermute | solution.py:129
  57.3 1.5 collective-permute-start.3
  58.8 5.4 %collective-permute-done = f32[16,72,128]{2,1,0:T(8,128)} collective-permute-done((f32[16,72,128]{2,1,0:T(8,128)}, f32[16,72,128]{2,1,0:T(8,128)}, u32[]{:S(2)}, u32[]{:S(2)}) %collective-permute-start) | collective-permute-done | bytes 589856 | tf_op jit(solution)/shard_map/ppermute | solution.py:129
  64.2 1.9 bitcast_add_fusion.2
  66.1 5.2 %collective-permute-start.1 = (f32[16,72,128]{2,1,0:T(8,128)}, f32[16,72,128]{2,1,0:T(8,128)}, u32[]{:S(2)}, u32[]{:S(2)}) collective-permute-start(f32[16,72,128]{2,1,0:T(8,128)} %bitcast_add_fusion.2), channel_id=1, source_target_pairs={{0,1},{1,2},{4,5},{5,6},{8,9},{9,10},{12,13},{13,14},{16,17},{17,1... | collective-permute-start | bytes 1769480 | tf_op jit(solution)/shard_map/ppermute | solution.py:129
  71.3 6.9 %collective-permute-done.1 = f32[16,72,128]{2,1,0:T(8,128)} collective-permute-done((f32[16,72,128]{2,1,0:T(8,128)}, f32[16,72,128]{2,1,0:T(8,128)}, u32[]{:S(2)}, u32[]{:S(2)}) %collective-permute-start.1) | collective-permute-done | bytes 589856 | tf_op jit(solution)/shard_map/ppermute | solution.py:129
  78.2 2.4 bitcast_add_fusion.3
  80.6 1.5 collective-permute-start.4
  82.1 4.2 collective-permute-start.2
  86.4 1.9 bitcast_add_fusion.1
  88.3 1.3 collective-permute-start.5
  89.6 4.4 collective-permute-done.2
  94.0 15.4 %collective-permute-done.5 = f32[16,72,128]{2,1,0:T(8,128)} collective-permute-done((f32[16,72,128]{2,1,0:T(8,128)}, f32[16,72,128]{2,1,0:T(8,128)}, u32[]{:S(2)}, u32[]{:S(2)}) %collective-permute-start.5) | collective-permute-done | bytes 589856 | tf_op jit(solution)/shard_map/ppermute | solution.py:130
  109.4 1.1 fusion.9
  111.4 38.8 %all-gather.3.cloned.1.call-done.side_ref = bf16[64,64,128]{2,1,0:T(8,128)(2,1)} async-done(((bf16[16,64,128]{2,1,0:T(8,128)(2,1)}), bf16[64,64,128]{2,1,0:T(8,128)(2,1)}) %all-gather.3.cloned.1.call-update) | async-done | bytes 1048592 | tf_op jit(solution)/shard_map/all_gather | solution.py:178
  150.2 8.6 %shard_map.87 = f32[64,72,128]{2,1,0:T(8,128)} custom-call(s32[512]{0:T(512)} %bitcast.216, s32[512]{0:T(512)} %bitcast.220, s32[1]{0:T(128)} %bitcast.175.cnt_ref, bf16[512,128,128]{2,1,0:T(8,128)(2,1)} %bitcast.179, bf16[64,64,128]{2,1,0:T(8,128)(2,1)} %all-gather.3.cloned.1.call-done.side_ref), custom_call_target="tpu_custom_call" | custom-call | flops 1207959552 | bytes 20185088 | tf_op jit(solution)/shard_map/pallas_call | solution.py:82
  158.7 38.9 %all_to_all.44 = f32[8,8,72,128]{3,2,1,0:T(8,128)S(1)} all-to-all(f32[8,8,72,128]{3,2,1,0:T(8,128)} %bitcast.192), channel_id=1, replica_groups=mesh['doc'=8,'term'=4] {'doc'}, dimensions={0} | all-to-all | bytes 4718592 | tf_op jit(solution)/shard_map/all_to_all | solution.py:101
  199.9 14.5 %all_to_all.45 = f32[4,1,4225]{2,1,0:T(1,128)S(1)} all-to-all(f32[4,1,4225]{2,1,0:T(1,128)S(1)} %broadcast_in_dim.14), channel_id=1, replica_groups=mesh['doc'=8,'term'=4] {'term'}, dimensions={0} | all-to-all | bytes 135200 | tf_op jit(solution)/shard_map/all_to_all | solution.py:106
  214.5 8.0 %all_to_all.46 = f32[8,1,4225]{2,1,0:T(1,128)S(1)} all-to-all(f32[8,1,4225]{2,1,0:T(1,128)S(1)} %broadcast_in_dim.15), channel_id=1, replica_groups=mesh['doc'=8,'term'=4] {'doc'}, dimensions={0} | all-to-all | bytes 270400 | tf_op jit(solution)/shard_map/all_to_all | solution.py:106
  225.5 5.8 %cholesky.44 = f32[64,64]{1,0:T(8,128)S(1)} custom-call(f32[64,64]{1,0:T(8,128)S(1)} %fusion.38), custom_call_target="Cholesky" | custom-call | tf_op jit(solution)/shard_map/jit(cholesky)/cholesky | solution.py:198
  232.7 4.9 %custom-call.11 = f32[1,64,64]{1,2,0:T(8,128)S(1)} custom-call(f32[1,64,64]{2,1,0:T(8,128)S(1)} %fusion.30), custom_call_target="InvertDiagBlocksLowerTriangular" | custom-call | tf_op jit(solution)/shard_map/jit(_solve_triangular)/triangular_solve | solution.py:201
  238.4 18.5 %all_to_all.47 = bf16[8,8,64,128]{3,2,1,0:T(8,128)(2,1)} all-to-all(bf16[8,8,64,128]{3,2,1,0:T(8,128)(2,1)S(1)} %broadcast_in_dim.16), channel_id=1, replica_groups=mesh['doc'=8,'term'=4] {'doc'}, dimensions={0} | all-to-all | bytes 2097152 | tf_op jit(solution)/shard_map/all_to_all | solution.py:111
  256.9 8.9 %shard_map.88 = f32[64,64,128]{2,1,0:T(8,128)} custom-call(s32[512]{0:T(512)} %bitcast.217, s32[512]{0:T(512)} %bitcast.221, s32[1]{0:T(128)} %bitcast.176.cnt_ref, bf16[512,128,128]{2,1,0:T(8,128)(2,1)} %bitcast.180, bf16[64,64,128]{2,1,0:T(8,128)(2,1)} %bitcast.195), custom_call_target="tpu_custom_call" | custom-call | flops 1073741824 | bytes 19922944 | tf_op jit(solution)/shard_map/pallas_call | solution.py:82
  265.7 1.4 dynamic-slice_bitcast_fusion.3
  267.2 9.7 %collective-permute-start.6 = (f32[16,64,128]{2,1,0:T(8,128)S(1)}, f32[16,64,128]{2,1,0:T(8,128)S(1)}, u32[]{:S(2)}, u32[]{:S(2)}) collective-permute-start(f32[16,64,128]{2,1,0:T(8,128)S(1)} %get-tuple-element.12), channel_id=1, source_target_pairs={{0,1},{4,5},{8,9},{12,13},{16,17},{20,21},{24,25},{28,29}} | collective-permute-start | bytes 1572872 | tf_op jit(solution)/shard_map/ppermute | solution.py:129
  277.6 7.9 %collective-permute-done.6 = f32[16,64,128]{2,1,0:T(8,128)S(1)} collective-permute-done((f32[16,64,128]{2,1,0:T(8,128)S(1)}, f32[16,64,128]{2,1,0:T(8,128)S(1)}, u32[]{:S(2)}, u32[]{:S(2)}) %collective-permute-start.6) | collective-permute-done | bytes 524320 | tf_op jit(solution)/shard_map/ppermute | solution.py:129
  285.6 4.4 collective-permute-start.7
  290.1 7.7 %collective-permute-done.7 = f32[16,64,128]{2,1,0:T(8,128)S(1)} collective-permute-done((f32[16,64,128]{2,1,0:T(8,128)S(1)}, f32[16,64,128]{2,1,0:T(8,128)S(1)}, u32[]{:S(2)}, u32[]{:S(2)}) %collective-permute-start.7) | collective-permute-done | bytes 524320 | tf_op jit(solution)/shard_map/ppermute | solution.py:129
  298.7 5.0 %collective-permute-start.8 = (f32[16,64,128]{2,1,0:T(8,128)S(1)}, f32[16,64,128]{2,1,0:T(8,128)S(1)}, u32[]{:S(2)}, u32[]{:S(2)}) collective-permute-start(f32[16,64,128]{2,1,0:T(8,128)S(1)} %get-tuple-element.10), channel_id=1, source_target_pairs={{0,1},{1,2},{2,3},{4,5},{5,6},{6,7},{8,9},{9,10},{10,11},{12,13},{... | collective-permute-start | bytes 1572872 | tf_op jit(solution)/shard_map/ppermute | solution.py:129
  303.8 1.3 collective-permute-start.11
  305.1 5.4 %collective-permute-done.8 = f32[16,64,128]{2,1,0:T(8,128)S(1)} collective-permute-done((f32[16,64,128]{2,1,0:T(8,128)S(1)}, f32[16,64,128]{2,1,0:T(8,128)S(1)}, u32[]{:S(2)}, u32[]{:S(2)}) %collective-permute-start.8) | collective-permute-done | bytes 524320 | tf_op jit(solution)/shard_map/ppermute | solution.py:129
  310.5 11.1 %collective-permute-done.11 = f32[16,64,128]{2,1,0:T(8,128)S(1)} collective-permute-done((f32[16,64,128]{2,1,0:T(8,128)S(1)}, f32[16,64,128]{2,1,0:T(8,128)S(1)}, u32[]{:S(2)}, u32[]{:S(2)}) %collective-permute-start.11) | collective-permute-done | bytes 524320 | tf_op jit(solution)/shard_map/ppermute | solution.py:130
  322.5 37.1 %all-gather.5.cloned.1.call-done.side_ref = bf16[64,64,128]{2,1,0:T(8,128)(2,1)} async-done(((bf16[16,64,128]{2,1,0:T(8,128)(2,1)}), bf16[64,64,128]{2,1,0:T(8,128)(2,1)}) %all-gather.5.cloned.1.call-update) | async-done | bytes 1048592 | tf_op jit(solution)/shard_map/all_gather | solution.py:178
  359.6 7.8 %shard_map.89 = f32[64,64,128]{2,1,0:T(8,128)} custom-call(s32[512]{0:T(512)} %bitcast.218, s32[512]{0:T(512)} %bitcast.222, s32[1]{0:T(128)} %bitcast.177.cnt_ref, bf16[512,128,128]{2,1,0:T(8,128)(2,1)} %bitcast.181, bf16[64,64,128]{2,1,0:T(8,128)(2,1)} %all-gather.5.cloned.1.call-done.side_ref), custom_call_target="tpu_custom_call" | custom-call | flops 1073741824 | bytes 19922944 | tf_op jit(solution)/shard_map/pallas_call | solution.py:82
  367.4 8.3 %all-to-all-start.5 = ((f32[8,8,64,128]{3,2,1,0:T(8,128)}), f32[8,8,64,128]{3,2,1,0:T(8,128)S(1)}, u32[]{:S(2)}, u32[]{:S(2)}) async-start(f32[8,8,64,128]{3,2,1,0:T(8,128)} %bitcast.193), calls=%async_computation.5 | async-start | bytes 4194304 | tf_op jit(solution)/shard_map/all_to_all | solution.py:101
  376.5 25.8 %all-to-all-done.5 = f32[8,8,64,128]{3,2,1,0:T(8,128)S(1)} async-done(((f32[8,8,64,128]{3,2,1,0:T(8,128)}), f32[8,8,64,128]{3,2,1,0:T(8,128)S(1)}, u32[]{:S(2)}, u32[]{:S(2)}) %all-to-all-start.5) | async-done | bytes 2097184 | tf_op jit(solution)/shard_map/all_to_all | solution.py:101
  404.5 14.4 %all_to_all.48 = f32[4,1,12545]{2,1,0:T(1,128)S(1)} all-to-all(f32[4,1,12545]{2,1,0:T(1,128)S(1)} %broadcast_in_dim.17), channel_id=1, replica_groups=mesh['doc'=8,'term'=4] {'term'}, dimensions={0} | all-to-all | bytes 401440 | tf_op jit(solution)/shard_map/all_to_all | solution.py:106
  419.3 11.1 %all_to_all.49 = f32[8,1,12545]{2,1,0:T(1,128)S(1)} all-to-all(f32[8,1,12545]{2,1,0:T(1,128)S(1)} %broadcast_in_dim.18), channel_id=1, replica_groups=mesh['doc'=8,'term'=4] {'doc'}, dimensions={0} | all-to-all | bytes 802880 | tf_op jit(solution)/shard_map/all_to_all | solution.py:106
  434.6 5.8 %cholesky.55 = f32[64,64]{1,0:T(8,128)S(1)} custom-call(f32[64,64]{1,0:T(8,128)S(1)} %fusion.36), custom_call_target="Cholesky" | custom-call | tf_op jit(solution)/shard_map/jit(cholesky)/cholesky | solution.py:198
  441.8 4.9 %custom-call.9 = f32[1,64,64]{1,2,0:T(8,128)S(1)} custom-call(f32[1,64,64]{2,1,0:T(8,128)S(1)} %fusion.31), custom_call_target="InvertDiagBlocksLowerTriangular" | custom-call | tf_op jit(solution)/shard_map/jit(_solve_triangular)/triangular_solve | solution.py:211
  448.7 0.9 broadcast_in_dim_reshape.6
  (92 shorter events, 22.5 us)
Async XLA Ops:
  9.4 20.6 %all-to-all-start = ((bf16[8,8,64,128]{3,2,1,0:T(8,128)(2,1)}), bf16[8,8,64,128]{3,2,1,0:T(8,128)(2,1)S(1)}, u32[]{:S(2)}, u32[]{:S(2)}) async-start(bf16[8,8,64,128]{3,2,1,0:T(8,128)(2,1)} %broadcast_in_dim.13), calls=%async_computation | async-start | bytes 2097152 | tf_op jit(solution)/shard_map/all_to_all | solution.py:111
  14.5 135.6 %all-gather.3.cloned.1.call-start = ((), (), s32[]{:S(2)}) async-start(), calls=%async_computation.8 | async-start | bytes 1310720 | tf_op jit(solution)/shard_map/all_gather | solution.py:178
  29.9 1.0 copy-start.2
  41.4 22.9 %copy-start = (f32[64,72,128]{2,1,0:T(8,128)S(1)}, f32[64,72,128]{2,1,0:T(8,128)}, u32[]{:S(2)}) copy-start(f32[64,72,128]{2,1,0:T(8,128)} %shard_map.86) | copy-start | bytes 7077892
  43.6 20.6 %collective-permute-start = (f32[16,72,128]{2,1,0:T(8,128)}, f32[16,72,128]{2,1,0:T(8,128)}, u32[]{:S(2)}, u32[]{:S(2)}) collective-permute-start(f32[16,72,128]{2,1,0:T(8,128)} %get-tuple-element.8), channel_id=1, source_target_pairs={{0,1},{4,5},{8,9},{12,13},{16,17},{20,21},{24,25},{28,29}} | collective-permute-start | bytes 1769480 | tf_op jit(solution)/shard_map/ppermute | solution.py:129
  57.3 14.0 %collective-permute-start.3 = (f32[16,72,128]{2,1,0:T(8,128)S(1)}, f32[16,72,128]{2,1,0:T(8,128)}, u32[]{:S(2)}, u32[]{:S(2)}) collective-permute-start(f32[16,72,128]{2,1,0:T(8,128)S(1)} %get-tuple-element.9), channel_id=1, source_target_pairs={{3,2},{7,6},{11,10},{15,14},{19,18},{23,22},{27,26},{31,30}} | collective-permute-start | bytes 1769480 | tf_op jit(solution)/shard_map/ppermute | solution.py:130
  66.1 12.1 %collective-permute-start.1 = (f32[16,72,128]{2,1,0:T(8,128)}, f32[16,72,128]{2,1,0:T(8,128)}, u32[]{:S(2)}, u32[]{:S(2)}) collective-permute-start(f32[16,72,128]{2,1,0:T(8,128)} %bitcast_add_fusion.2), channel_id=1, source_target_pairs={{0,1},{1,2},{4,5},{5,6},{8,9},{9,10},{12,13},{13,14},{16,17},{17,1... | collective-permute-start | bytes 1769480 | tf_op jit(solution)/shard_map/ppermute | solution.py:129
  80.6 5.7 %collective-permute-start.4 = (f32[16,72,128]{2,1,0:T(8,128)}, f32[16,72,128]{2,1,0:T(8,128)}, u32[]{:S(2)}, u32[]{:S(2)}) collective-permute-start(f32[16,72,128]{2,1,0:T(8,128)} %get-tuple-element.7), channel_id=1, source_target_pairs={{3,2},{2,1},{7,6},{6,5},{11,10},{10,9},{15,14},{14,13},{19,18},{18... | collective-permute-start | bytes 1769480 | tf_op jit(solution)/shard_map/ppermute | solution.py:130
  82.1 11.9 %collective-permute-start.2 = (f32[16,72,128]{2,1,0:T(8,128)}, f32[16,72,128]{2,1,0:T(8,128)S(1)}, u32[]{:S(2)}, u32[]{:S(2)}) collective-permute-start(f32[16,72,128]{2,1,0:T(8,128)} %get-tuple-element.6), channel_id=1, source_target_pairs={{0,1},{1,2},{2,3},{4,5},{5,6},{6,7},{8,9},{9,10},{10,11},{12,13},{... | collective-permute-start | bytes 1769480 | tf_op jit(solution)/shard_map/ppermute | solution.py:129
  88.3 21.1 %collective-permute-start.5 = (f32[16,72,128]{2,1,0:T(8,128)}, f32[16,72,128]{2,1,0:T(8,128)}, u32[]{:S(2)}, u32[]{:S(2)}) collective-permute-start(f32[16,72,128]{2,1,0:T(8,128)} %bitcast_add_fusion.1), channel_id=1, source_target_pairs={{3,2},{2,1},{1,0},{7,6},{6,5},{5,4},{11,10},{10,9},{9,8},{15,14},{... | collective-permute-start | bytes 1769480 | tf_op jit(solution)/shard_map/ppermute | solution.py:130
  111.4 248.3 %all-gather.5.cloned.1.call-start = ((), (), s32[]{:S(2)}) async-start(), calls=%async_computation.9 | async-start | bytes 1310720 | tf_op jit(solution)/shard_map/all_gather | solution.py:178
  265.7 19.8 %copy-start.1 = (f32[64,64,128]{2,1,0:T(8,128)S(1)}, f32[64,64,128]{2,1,0:T(8,128)}, u32[]{:S(2)}) copy-start(f32[64,64,128]{2,1,0:T(8,128)} %shard_map.88) | copy-start | bytes 6291460
  267.2 18.4 %collective-permute-start.6 = (f32[16,64,128]{2,1,0:T(8,128)S(1)}, f32[16,64,128]{2,1,0:T(8,128)S(1)}, u32[]{:S(2)}, u32[]{:S(2)}) collective-permute-start(f32[16,64,128]{2,1,0:T(8,128)S(1)} %get-tuple-element.12), channel_id=1, source_target_pairs={{0,1},{4,5},{8,9},{12,13},{16,17},{20,21},{24,25},{28,29}} | collective-permute-start | bytes 1572872 | tf_op jit(solution)/shard_map/ppermute | solution.py:129
  276.9 13.2 %collective-permute-start.9 = (f32[16,64,128]{2,1,0:T(8,128)S(1)}, f32[16,64,128]{2,1,0:T(8,128)S(1)}, u32[]{:S(2)}, u32[]{:S(2)}) collective-permute-start(f32[16,64,128]{2,1,0:T(8,128)S(1)} %get-tuple-element.13), channel_id=1, source_target_pairs={{3,2},{7,6},{11,10},{15,14},{19,18},{23,22},{27,26},{31,30}} | collective-permute-start | bytes 1572872 | tf_op jit(solution)/shard_map/ppermute | solution.py:130
  285.6 12.1 %collective-permute-start.7 = (f32[16,64,128]{2,1,0:T(8,128)S(1)}, f32[16,64,128]{2,1,0:T(8,128)S(1)}, u32[]{:S(2)}, u32[]{:S(2)}) collective-permute-start(f32[16,64,128]{2,1,0:T(8,128)S(1)} %bitcast_add_fusion.7), channel_id=1, source_target_pairs={{0,1},{1,2},{4,5},{5,6},{8,9},{9,10},{12,13},{13,14},{16,17},{17,1... | collective-permute-start | bytes 1572872 | tf_op jit(solution)/shard_map/ppermute | solution.py:129
  298.0 5.7 %collective-permute-start.10 = (f32[16,64,128]{2,1,0:T(8,128)S(1)}, f32[16,64,128]{2,1,0:T(8,128)S(1)}, u32[]{:S(2)}, u32[]{:S(2)}) collective-permute-start(f32[16,64,128]{2,1,0:T(8,128)S(1)} %get-tuple-element.11), channel_id=1, source_target_pairs={{3,2},{2,1},{7,6},{6,5},{11,10},{10,9},{15,14},{14,13},{19,18},{18... | collective-permute-start | bytes 1572872 | tf_op jit(solution)/shard_map/ppermute | solution.py:130
  298.7 11.8 %collective-permute-start.8 = (f32[16,64,128]{2,1,0:T(8,128)S(1)}, f32[16,64,128]{2,1,0:T(8,128)S(1)}, u32[]{:S(2)}, u32[]{:S(2)}) collective-permute-start(f32[16,64,128]{2,1,0:T(8,128)S(1)} %get-tuple-element.10), channel_id=1, source_target_pairs={{0,1},{1,2},{2,3},{4,5},{5,6},{6,7},{8,9},{9,10},{10,11},{12,13},{... | collective-permute-start | bytes 1572872 | tf_op jit(solution)/shard_map/ppermute | solution.py:129
  303.8 17.8 %collective-permute-start.11 = (f32[16,64,128]{2,1,0:T(8,128)S(1)}, f32[16,64,128]{2,1,0:T(8,128)S(1)}, u32[]{:S(2)}, u32[]{:S(2)}) collective-permute-start(f32[16,64,128]{2,1,0:T(8,128)S(1)} %bitcast_add_fusion.6), channel_id=1, source_target_pairs={{3,2},{2,1},{1,0},{7,6},{6,5},{5,4},{11,10},{10,9},{9,8},{15,14},{... | collective-permute-start | bytes 1572872 | tf_op jit(solution)/shard_map/ppermute | solution.py:130
  367.4 8.3 %copy-start.4 = (s32[1,1024]{1,0:T(1,128)S(1)}, s32[1,1024]{1,0:T(1,128)}, u32[]{:S(2)}) copy-start(s32[1,1024]{1,0:T(1,128)} %param.16) | copy-start | bytes 12292
  367.4 8.4 %copy-start.3 = (s32[1,2048]{1,0:T(1,128)S(1)}, s32[1,2048]{1,0:T(1,128)}, u32[]{:S(2)}) copy-start(s32[1,2048]{1,0:T(1,128)} %param.15) | copy-start | bytes 24580
  367.4 34.9 %all-to-all-start.5 = ((f32[8,8,64,128]{3,2,1,0:T(8,128)}), f32[8,8,64,128]{3,2,1,0:T(8,128)S(1)}, u32[]{:S(2)}, u32[]{:S(2)}) async-start(f32[8,8,64,128]{3,2,1,0:T(8,128)} %bitcast.193), calls=%async_computation.5 | async-start | bytes 4194304 | tf_op jit(solution)/shard_map/all_to_all | solution.py:101
Sparse Core Ops, SparseCore 0:
  111.5 38.6 all-gather.2
  322.6 36.9 all-gather.4

commit v8 on v6

--- a/solution.py
+++ b/solution.py
@@ -10,7 +10,7 @@
 CLUSTERS = 64
 ITERS = 2
 CHUNK = 128
-GROUP = 8
+GROUP = 16
 DEG_ROWS = 8
 
 HIGH = lax.Precision.HIGHEST
@@ -36,7 +36,7 @@
             return lax.dot_general(lhs, tile, NT_DIMS, preferred_element_type=jnp.float32)
         return jnp.dot(lhs, tile, preferred_element_type=jnp.float32)
 
-    def body(g, carry):
+    def run(g, masked):
         results = []
         for u in range(group):
             j = g * group + u
@@ -46,17 +46,28 @@
             else:
                 src, dst = rows_ref[slot], cols_ref[slot]
             tile = tiles_ref[j]
-            keep = slot < count
-            prod = jnp.where(keep, product(side_ref[src], tile), 0.0)
-            deg = jnp.where(keep, product(ones, tile), 0.0) if with_degree else None
+            prod = product(side_ref[src], tile)
+            deg = product(ones, tile) if with_degree else None
+            if masked:
+                keep = slot < count
+                prod = jnp.where(keep, prod, 0.0)
+                deg = jnp.where(keep, deg, 0.0) if with_degree else None
             results.append((dst, prod, deg))
         for dst, prod, deg in results:
             out_ref[dst, pl.ds(0, width), :] += prod
             if with_degree:
                 out_ref[dst, pl.ds(width, DEG_ROWS), :] += deg
+
+    def body(g, carry):
+        run(g, False)
         return carry
 
-    lax.fori_loop(0, (live + group - 1) // group, body, 0)
+    full = live // group
+    lax.fori_loop(0, full, body, 0)
+
+    @pl.when(full * group < live)
+    def _():
+        run(full, True)
 
 
 def tile_pass(tiles, rows, cols, count, side, transpose_tile, with_degree):

time: 437 us -> 417 us (0.954)
  Pallas kernels: 79.1 us -> 62.7 us
    pallas_call x4, Pallas kernels: 79.1 us -> 62.7 us  [tile_pass(): pl.pallas_call(kernel, out_shape=jax.ShapeDtypeStruct((n_tiles, out_rows,...]
where the time goes in v8:
time: 417 us
  waiting for transfers between devices  190 us (46%)
  blocking collectives  90.3 us (22%)
  Pallas kernels  62.7 us (15%)
  other arithmetic  34.5 us (8%)
  between operations  15.4 us (4%)
  local copies, waits for them, and re-layouts  10 us (2%)
  starting transfers between devices  9.07 us (2%)
  matrix products  4.52 us (1%)
    reduce_scatter x2, waiting for transfers between devices, per_device(): left_own = lax.psum_scatter(left, 'term', scatter_dimension=0, tiled=True)  94.4 us
    pallas_call x4, Pallas kernels, tile_pass(): pl.pallas_call(kernel, out_shape=jax.ShapeDtypeStruct((n_tiles, out_rows,...  62.7 us
    all_gather x2, waiting for transfers between devices, per_device(): q_all = lax.all_gather(quotient, 'term', axis=0, tiled=True)  55.1 us
    all_to_all x4, blocking collectives, exchange_sum(): return jnp.sum(lax.all_to_all(copies, axis_name, 0, 0, tiled=False), axis=0)  38.9 us
    all_to_all x1, blocking collectives, scatter_sum(): return jnp.sum(lax.all_to_all(pieces, axis_name, 0, 0, tiled=False), axis=0)  32.9 us
    all_to_all x1, waiting for transfers between devices, scatter_sum(): return jnp.sum(lax.all_to_all(pieces, axis_name, 0, 0, tiled=False), axis=0)  25.7 us
    all_to_all x1, blocking collectives, exchange_gather(): got = lax.all_to_all(copies, axis_name, 0, 0, tiled=False)  18.5 us
    all_to_all x1, waiting for transfers between devices, exchange_gather(): got = lax.all_to_all(copies, axis_name, 0, 0, tiled=False)  14.7 us
  transfers between devices with their start and end apart: 6, of which 6 were waited for; matrix products, arithmetic and copies ran while one was open for 0% of the time, Pallas kernels for 0%

profile of v8, /device:TPU:0, one launch (start us, length us, event | category | flops | bytes accessed | tf_op | source)
XLA Modules:
  0.0 416.5 jit_solution(5879645075722477754)
XLA Ops:
  7.2 0.9 copy.111
  8.1 1.2 broadcast_in_dim.13
  9.4 5.2 %all-to-all-start = ((bf16[8,8,64,128]{3,2,1,0:T(8,128)(2,1)}), bf16[8,8,64,128]{3,2,1,0:T(8,128)(2,1)S(1)}, u32[]{:S(2)}, u32[]{:S(2)}) async-start(bf16[8,8,64,128]{3,2,1,0:T(8,128)(2,1)} %broadcast_in_dim.13), calls=%async_computation | async-start | bytes 2097152 | tf_op jit(solution)/shard_map/all_to_all | solution.py:122
  15.2 14.7 %all-to-all-done = bf16[8,8,64,128]{3,2,1,0:T(8,128)(2,1)S(1)} async-done(((bf16[8,8,64,128]{3,2,1,0:T(8,128)(2,1)}), bf16[8,8,64,128]{3,2,1,0:T(8,128)(2,1)S(1)}, u32[]{:S(2)}, u32[]{:S(2)}) %all-to-all-start) | async-done | bytes 1048608 | tf_op jit(solution)/shard_map/all_to_all | solution.py:122
  29.9 1.0 copy-done
  30.9 20.8 %shard_map.86 = f32[64,72,128]{2,1,0:T(8,128)} custom-call(s32[512]{0:T(512)} %bitcast.170, s32[512]{0:T(512)} %bitcast.174, s32[1]{0:T(128)} %bitcast.136.cnt_ref, bf16[512,128,128]{2,1,0:T(8,128)(2,1)} %bitcast.140, bf16[64,64,128]{2,1,0:T(8,128)(2,1)} %bitcast.146), custom_call_target="tpu_custom_call" | custom-call | flops 1207959552 | bytes 20185088 | tf_op jit(solution)/shard_map/pallas_call | solution.py:93
  51.8 50.5 %reduce-scatter.3.cloned.1.call-done = f32[16,72,128]{2,1,0:T(8,128)} async-done(((f32[64,72,128]{2,1,0:T(8,128)}), f32[16,72,128]{2,1,0:T(8,128)}) %reduce-scatter.3.cloned.1.call-update) | async-done | bytes 589840 | tf_op jit(solution)/shard_map/reduce_scatter | solution.py:165
  102.3 0.8 slice.75
  103.1 1.8 fusion.9
  105.0 27.5 %all-gather.3.cloned.1.call-done.side_ref = bf16[64,64,128]{2,1,0:T(8,128)(2,1)} async-done(((bf16[16,64,128]{2,1,0:T(8,128)(2,1)}), bf16[64,64,128]{2,1,0:T(8,128)(2,1)}) %all-gather.3.cloned.1.call-update) | async-done | bytes 1048592 | tf_op jit(solution)/shard_map/all_gather | solution.py:170
  132.6 14.4 %shard_map.87 = f32[64,72,128]{2,1,0:T(8,128)} custom-call(s32[512]{0:T(512)} %bitcast.171, s32[512]{0:T(512)} %bitcast.175, s32[1]{0:T(128)} %bitcast.137.cnt_ref, bf16[512,128,128]{2,1,0:T(8,128)(2,1)} %bitcast.141, bf16[64,64,128]{2,1,0:T(8,128)(2,1)} %all-gather.3.cloned.1.call-done.side_ref), custom_call_target="tpu_custom_call" | custom-call | flops 1207959552 | bytes 20185088 | tf_op jit(solution)/shard_map/pallas_call | solution.py:93
  147.0 32.9 %all_to_all.44 = f32[8,8,72,128]{3,2,1,0:T(8,128)S(1)} all-to-all(f32[8,8,72,128]{3,2,1,0:T(8,128)} %bitcast.144), channel_id=1, replica_groups=mesh['doc'=8,'term'=4] {'doc'}, dimensions={0} | all-to-all | bytes 4718592 | tf_op jit(solution)/shard_map/all_to_all | solution.py:112
  180.0 0.6 slice_reduce_fusion
  181.6 0.6 concatenate.6
  182.2 9.9 %all_to_all.45 = f32[4,1,4225]{2,1,0:T(1,128)S(1)} all-to-all(f32[4,1,4225]{2,1,0:T(1,128)S(1)} %broadcast_in_dim.14), channel_id=1, replica_groups=mesh['doc'=8,'term'=4] {'term'}, dimensions={0} | all-to-all | bytes 135200 | tf_op jit(solution)/shard_map/all_to_all | solution.py:117
  192.3 8.0 %all_to_all.46 = f32[8,1,4225]{2,1,0:T(1,128)S(1)} all-to-all(f32[8,1,4225]{2,1,0:T(1,128)S(1)} %broadcast_in_dim.15), channel_id=1, replica_groups=mesh['doc'=8,'term'=4] {'doc'}, dimensions={0} | all-to-all | bytes 270400 | tf_op jit(solution)/shard_map/all_to_all | solution.py:117
  200.4 0.5 slice.80
  200.9 0.6 fusion.41
  201.7 0.7 divide_subtract_fusion.1
  202.5 0.7 fusion.35
  203.3 5.8 %cholesky.44 = f32[64,64]{1,0:T(8,128)S(1)} custom-call(f32[64,64]{1,0:T(8,128)S(1)} %fusion.35), custom_call_target="Cholesky" | custom-call | tf_op jit(solution)/shard_map/jit(cholesky)/cholesky | solution.py:190
  209.1 0.6 compare_reduce_fusion.1
  209.8 0.7 fusion.27
  210.4 4.9 %custom-call.11 = f32[1,64,64]{1,2,0:T(8,128)S(1)} custom-call(f32[1,64,64]{2,1,0:T(8,128)S(1)} %fusion.27), custom_call_target="InvertDiagBlocksLowerTriangular" | custom-call | tf_op jit(solution)/shard_map/jit(_solve_triangular)/triangular_solve | solution.py:193
  215.3 0.5 convolution_bitcast_fusion
  216.1 18.5 %all_to_all.47 = bf16[8,8,64,128]{3,2,1,0:T(8,128)(2,1)} all-to-all(bf16[8,8,64,128]{3,2,1,0:T(8,128)(2,1)S(1)} %broadcast_in_dim.16), channel_id=1, replica_groups=mesh['doc'=8,'term'=4] {'doc'}, dimensions={0} | all-to-all | bytes 2097152 | tf_op jit(solution)/shard_map/all_to_all | solution.py:122
  234.6 15.9 %shard_map.88 = f32[64,64,128]{2,1,0:T(8,128)} custom-call(s32[512]{0:T(512)} %bitcast.172, s32[512]{0:T(512)} %bitcast.176, s32[1]{0:T(128)} %bitcast.138.cnt_ref, bf16[512,128,128]{2,1,0:T(8,128)(2,1)} %bitcast.142, bf16[64,64,128]{2,1,0:T(8,128)(2,1)} %bitcast.147), custom_call_target="tpu_custom_call" | custom-call | flops 1073741824 | bytes 19922944 | tf_op jit(solution)/shard_map/pallas_call | solution.py:93
  250.6 43.9 %reduce-scatter.5.cloned.1.call-done = f32[16,64,128]{2,1,0:T(8,128)} async-done(((f32[64,64,128]{2,1,0:T(8,128)}), f32[16,64,128]{2,1,0:T(8,128)}) %reduce-scatter.5.cloned.1.call-update) | async-done | bytes 524304 | tf_op jit(solution)/shard_map/reduce_scatter | solution.py:165
  294.5 1.8 fusion.39
  296.4 27.5 %all-gather.5.cloned.1.call-done.side_ref = bf16[64,64,128]{2,1,0:T(8,128)(2,1)} async-done(((bf16[16,64,128]{2,1,0:T(8,128)(2,1)}), bf16[64,64,128]{2,1,0:T(8,128)(2,1)}) %all-gather.5.cloned.1.call-update) | async-done | bytes 1048592 | tf_op jit(solution)/shard_map/all_gather | solution.py:170
  323.9 11.5 %shard_map.89 = f32[64,64,128]{2,1,0:T(8,128)} custom-call(s32[512]{0:T(512)} %bitcast.173, s32[512]{0:T(512)} %bitcast.177, s32[1]{0:T(128)} %bitcast.139.cnt_ref, bf16[512,128,128]{2,1,0:T(8,128)(2,1)} %bitcast.143, bf16[64,64,128]{2,1,0:T(8,128)(2,1)} %all-gather.5.cloned.1.call-done.side_ref), custom_call_target="tpu_custom_call" | custom-call | flops 1073741824 | bytes 19922944 | tf_op jit(solution)/shard_map/pallas_call | solution.py:93
  335.4 3.7 all-to-all-start.5
  340.0 25.7 %all-to-all-done.5 = f32[8,8,64,128]{3,2,1,0:T(8,128)S(1)} async-done(((f32[8,8,64,128]{3,2,1,0:T(8,128)}), f32[8,8,64,128]{3,2,1,0:T(8,128)S(1)}, u32[]{:S(2)}, u32[]{:S(2)}) %all-to-all-start.5) | async-done | bytes 2097184 | tf_op jit(solution)/shard_map/all_to_all | solution.py:112
  367.1 0.6 concatenate.7
  367.9 10.0 %all_to_all.48 = f32[4,1,12545]{2,1,0:T(1,128)S(1)} all-to-all(f32[4,1,12545]{2,1,0:T(1,128)S(1)} %broadcast_in_dim.17), channel_id=1, replica_groups=mesh['doc'=8,'term'=4] {'term'}, dimensions={0} | all-to-all | bytes 401440 | tf_op jit(solution)/shard_map/all_to_all | solution.py:117
  378.3 11.1 %all_to_all.49 = f32[8,1,12545]{2,1,0:T(1,128)S(1)} all-to-all(f32[8,1,12545]{2,1,0:T(1,128)S(1)} %broadcast_in_dim.18), channel_id=1, replica_groups=mesh['doc'=8,'term'=4] {'doc'}, dimensions={0} | all-to-all | bytes 802880 | tf_op jit(solution)/shard_map/all_to_all | solution.py:117
  389.7 0.5 slice.81
  390.9 0.7 fusion.38
  392.0 0.7 divide_subtract_fusion
  392.8 0.7 fusion.33
  393.5 5.8 %cholesky.55 = f32[64,64]{1,0:T(8,128)S(1)} custom-call(f32[64,64]{1,0:T(8,128)S(1)} %fusion.33), custom_call_target="Cholesky" | custom-call | tf_op jit(solution)/shard_map/jit(cholesky)/cholesky | solution.py:190
  399.4 0.6 compare_reduce_fusion
  400.0 0.7 fusion.28
  400.7 4.9 %custom-call.9 = f32[1,64,64]{1,2,0:T(8,128)S(1)} custom-call(f32[1,64,64]{2,1,0:T(8,128)S(1)} %fusion.28), custom_call_target="InvertDiagBlocksLowerTriangular" | custom-call | tf_op jit(solution)/shard_map/jit(_solve_triangular)/triangular_solve | solution.py:203
  405.6 0.5 fusion.5
  407.2 0.7 broadcast_in_dim_reshape.7
  408.0 0.7 fusion.2
  409.1 0.9 broadcast_in_dim_reshape.6
  (63 shorter events, 7.1 us)
Async XLA Ops:
  9.4 20.6 %all-to-all-start = ((bf16[8,8,64,128]{3,2,1,0:T(8,128)(2,1)}), bf16[8,8,64,128]{3,2,1,0:T(8,128)(2,1)S(1)}, u32[]{:S(2)}, u32[]{:S(2)}) async-start(bf16[8,8,64,128]{3,2,1,0:T(8,128)(2,1)} %broadcast_in_dim.13), calls=%async_computation | async-start | bytes 2097152 | tf_op jit(solution)/shard_map/all_to_all | solution.py:122
  14.5 87.8 %reduce-scatter.3.cloned.1.call-start = ((), (), s32[]{:S(2)}) async-start(), calls=%async_computation.10 | async-start | bytes 2949120 | tf_op jit(solution)/shard_map/reduce_scatter | solution.py:165
  29.9 1.0 copy-start
  51.8 80.8 %all-gather.3.cloned.1.call-start = ((), (), s32[]{:S(2)}) async-start(), calls=%async_computation.11 | async-start | bytes 1310720 | tf_op jit(solution)/shard_map/all_gather | solution.py:170
  105.0 189.6 %reduce-scatter.5.cloned.1.call-start = ((), (), s32[]{:S(2)}) async-start(), calls=%async_computation.12 | async-start | bytes 2621440 | tf_op jit(solution)/shard_map/reduce_scatter | solution.py:165
  250.6 73.3 %all-gather.5.cloned.1.call-start = ((), (), s32[]{:S(2)}) async-start(), calls=%async_computation.13 | async-start | bytes 1310720 | tf_op jit(solution)/shard_map/all_gather | solution.py:170
  335.4 3.8 copy-start.3
  335.4 3.9 copy-start.2
  335.4 4.1 copy-start.1
  335.4 30.3 %all-to-all-start.5 = ((f32[8,8,64,128]{3,2,1,0:T(8,128)}), f32[8,8,64,128]{3,2,1,0:T(8,128)S(1)}, u32[]{:S(2)}, u32[]{:S(2)}) async-start(f32[8,8,64,128]{3,2,1,0:T(8,128)} %bitcast.145), calls=%async_computation.7 | async-start | bytes 4194304 | tf_op jit(solution)/shard_map/all_to_all | solution.py:112
Sparse Core Ops, SparseCore 0:
  51.9 50.3 reduce-scatter.2
  105.1 27.4 all-gather.2
  250.7 43.8 reduce-scatter.4
  296.6 27.2 all-gather.4

commit v9 on v8

--- a/solution.py
+++ b/solution.py
@@ -167,7 +167,7 @@
         if first:
             doc_degree = left_own[:, width_k, :]
         quotient = (summed_own / doc_degree[:, None, :]).astype(jnp.bfloat16)
-        q_all = lax.all_gather(quotient, "term", axis=0, tiled=True)
+        q_all = exchange_gather(quotient, "term", n_term)
         right = tile_pass(local_tiles, rows, cols, count, q_all, False, first)
         right_own = scatter_sum(right, "doc", n_doc)
         if first:

time: 417 us -> 418 us (level)
  blocking collectives: 90.3 us -> 152 us
  waiting for transfers between devices: 190 us -> 144 us
  Pallas kernels: 62.7 us -> 46.6 us
    all_to_all x1 -> x3, blocking collectives: 18.5 us -> 76.5 us  [exchange_gather(): got = lax.all_to_all(copies, axis_name, 0, 0, tiled=False)]
    all_gather x2 -> x0, waiting for transfers between devices: 55.1 us -> none  [per_device(): q_all = lax.all_gather(quotient, 'term', axis=0, tiled=True)]
    pallas_call x4, Pallas kernels: 62.7 us -> 46.6 us  [tile_pass(): pl.pallas_call(kernel, out_shape=jax.ShapeDtypeStruct((n_tiles, out_rows,...]
    reduce_scatter x2, waiting for transfers between devices: 94.4 us -> 104 us  [per_device(): left_own = lax.psum_scatter(left, 'term', scatter_dimension=0, tiled=True)]
    all_to_all x1, blocking collectives: 32.9 us -> 38.9 us  [scatter_sum(): return jnp.sum(lax.all_to_all(pieces, axis_name, 0, 0, tiled=False), axis=0)]
  transfers between devices with their start and end apart: 6 -> 4, of which waited for: 6 -> 4; matrix products, arithmetic and copies ran while one was open for 0% -> 0% of each run, Pallas kernels for 0% -> 0%
where the time goes in v9:
time: 418 us; the launch traced here: 420 us
  blocking collectives  152 us (36%)
  waiting for transfers between devices  144 us (34%)
  Pallas kernels  46.6 us (11%)
  other arithmetic  33.4 us (8%)
  between operations  15.7 us (4%)
  starting transfers between devices  12.8 us (3%)
  local copies, waits for them, and re-layouts  10.8 us (3%)
  matrix products  4.52 us (1%)
    reduce_scatter x2, waiting for transfers between devices, per_device(): left_own = lax.psum_scatter(left, 'term', scatter_dimension=0, tiled=True)  104 us
    all_to_all x3, blocking collectives, exchange_gather(): got = lax.all_to_all(copies, axis_name, 0, 0, tiled=False)  76.5 us
    pallas_call x4, Pallas kernels, tile_pass(): pl.pallas_call(kernel, out_shape=jax.ShapeDtypeStruct((n_tiles, out_rows,...  46.6 us
    all_to_all x1, blocking collectives, scatter_sum(): return jnp.sum(lax.all_to_all(pieces, axis_name, 0, 0, tiled=False), axis=0)  38.9 us
    all_to_all x4, blocking collectives, exchange_sum(): return jnp.sum(lax.all_to_all(copies, axis_name, 0, 0, tiled=False), axis=0)  36.7 us
    all_to_all x1, waiting for transfers between devices, scatter_sum(): return jnp.sum(lax.all_to_all(pieces, axis_name, 0, 0, tiled=False), axis=0)  25.8 us
    all_to_all x1, waiting for transfers between devices, exchange_gather(): got = lax.all_to_all(copies, axis_name, 0, 0, tiled=False)  14.7 us
    another operation x6, other arithmetic, per_device(): lower = jnp.linalg.cholesky(gram_matrix - jnp.outer(along, along) / volume)  13.1 us
  transfers between devices with their start and end apart: 4, of which 4 were waited for; matrix products, arithmetic and copies ran while one was open for 0% of the time, Pallas kernels for 0%

profile of v9, /device:TPU:0, one launch (start us, length us, event | category | flops | bytes accessed | tf_op | source)
XLA Modules:
  0.0 420.2 jit_solution(11556984167626987167)
XLA Ops:
  7.2 0.9 copy.111
  8.1 1.2 broadcast_in_dim.17
  9.4 5.2 %all-to-all-start = ((bf16[8,8,64,128]{3,2,1,0:T(8,128)(2,1)}), bf16[8,8,64,128]{3,2,1,0:T(8,128)(2,1)S(1)}, u32[]{:S(2)}, u32[]{:S(2)}) async-start(bf16[8,8,64,128]{3,2,1,0:T(8,128)(2,1)} %broadcast_in_dim.17), calls=%async_computation | async-start | bytes 2097152 | tf_op jit(solution)/shard_map/all_to_all | solution.py:122
  15.2 14.7 %all-to-all-done = bf16[8,8,64,128]{3,2,1,0:T(8,128)(2,1)S(1)} async-done(((bf16[8,8,64,128]{3,2,1,0:T(8,128)(2,1)}), bf16[8,8,64,128]{3,2,1,0:T(8,128)(2,1)S(1)}, u32[]{:S(2)}, u32[]{:S(2)}) %all-to-all-start) | async-done | bytes 1048608 | tf_op jit(solution)/shard_map/all_to_all | solution.py:122
  29.9 1.0 copy-done
  30.9 14.9 %shard_map.86 = f32[64,72,128]{2,1,0:T(8,128)} custom-call(s32[512]{0:T(512)} %bitcast.174, s32[512]{0:T(512)} %bitcast.178, s32[1]{0:T(128)} %bitcast.138.cnt_ref, bf16[512,128,128]{2,1,0:T(8,128)(2,1)} %bitcast.142, bf16[64,64,128]{2,1,0:T(8,128)(2,1)} %bitcast.148), custom_call_target="tpu_custom_call" | custom-call | flops 1207959552 | bytes 20185088 | tf_op jit(solution)/shard_map/pallas_call | solution.py:93
  45.9 55.8 %reduce-scatter.3.cloned.1.call-done = f32[16,72,128]{2,1,0:T(8,128)} async-done(((f32[64,72,128]{2,1,0:T(8,128)}), f32[16,72,128]{2,1,0:T(8,128)}) %reduce-scatter.3.cloned.1.call-update) | async-done | bytes 589840 | tf_op jit(solution)/shard_map/reduce_scatter | solution.py:165
  101.6 0.8 slice.75
  102.5 1.1 fusion.9
  103.8 29.0 %all_to_all.54 = bf16[4,16,64,128]{3,2,1,0:T(8,128)(2,1)} all-to-all(bf16[4,16,64,128]{3,2,1,0:T(8,128)(2,1)S(1)} %broadcast_in_dim.18), channel_id=1, replica_groups=mesh['doc'=8,'term'=4] {'term'}, dimensions={0} | all-to-all | bytes 2097152 | tf_op jit(solution)/shard_map/all_to_all | solution.py:122
  132.8 10.9 %shard_map.87 = f32[64,72,128]{2,1,0:T(8,128)} custom-call(s32[512]{0:T(512)} %bitcast.175, s32[512]{0:T(512)} %bitcast.179, s32[1]{0:T(128)} %bitcast.139.cnt_ref, bf16[512,128,128]{2,1,0:T(8,128)(2,1)} %bitcast.143, bf16[64,64,128]{2,1,0:T(8,128)(2,1)} %bitcast.150), custom_call_target="tpu_custom_call" | custom-call | flops 1207959552 | bytes 20185088 | tf_op jit(solution)/shard_map/pallas_call | solution.py:93
  143.6 38.9 %all_to_all.55 = f32[8,8,72,128]{3,2,1,0:T(8,128)S(1)} all-to-all(f32[8,8,72,128]{3,2,1,0:T(8,128)} %bitcast.146), channel_id=1, replica_groups=mesh['doc'=8,'term'=4] {'doc'}, dimensions={0} | all-to-all | bytes 4718592 | tf_op jit(solution)/shard_map/all_to_all | solution.py:112
  182.7 0.6 slice_reduce_fusion
  184.2 0.7 concatenate.6
  184.9 8.1 %all_to_all.56 = f32[4,1,4225]{2,1,0:T(1,128)S(1)} all-to-all(f32[4,1,4225]{2,1,0:T(1,128)S(1)} %broadcast_in_dim.19), channel_id=1, replica_groups=mesh['doc'=8,'term'=4] {'term'}, dimensions={0} | all-to-all | bytes 135200 | tf_op jit(solution)/shard_map/all_to_all | solution.py:117
  193.2 8.0 %all_to_all.57 = f32[8,1,4225]{2,1,0:T(1,128)S(1)} all-to-all(f32[8,1,4225]{2,1,0:T(1,128)S(1)} %broadcast_in_dim.20), channel_id=1, replica_groups=mesh['doc'=8,'term'=4] {'doc'}, dimensions={0} | all-to-all | bytes 270400 | tf_op jit(solution)/shard_map/all_to_all | solution.py:117
  201.4 0.6 slice.80
  201.9 0.7 fusion.41
  202.8 0.8 divide_subtract_fusion.1
  203.6 0.8 fusion.35
  204.4 5.8 %cholesky.44 = f32[64,64]{1,0:T(8,128)S(1)} custom-call(f32[64,64]{1,0:T(8,128)S(1)} %fusion.35), custom_call_target="Cholesky" | custom-call | tf_op jit(solution)/shard_map/jit(cholesky)/cholesky | solution.py:190
  210.3 0.7 compare_reduce_fusion.1
  211.0 0.7 fusion.27
  211.7 4.9 %custom-call.11 = f32[1,64,64]{1,2,0:T(8,128)S(1)} custom-call(f32[1,64,64]{2,1,0:T(8,128)S(1)} %fusion.27), custom_call_target="InvertDiagBlocksLowerTriangular" | custom-call | tf_op jit(solution)/shard_map/jit(_solve_triangular)/triangular_solve | solution.py:193
  216.6 0.5 convolution_bitcast_fusion
  217.4 18.5 %all_to_all.58 = bf16[8,8,64,128]{3,2,1,0:T(8,128)(2,1)} all-to-all(bf16[8,8,64,128]{3,2,1,0:T(8,128)(2,1)S(1)} %broadcast_in_dim.21), channel_id=1, replica_groups=mesh['doc'=8,'term'=4] {'doc'}, dimensions={0} | all-to-all | bytes 2097152 | tf_op jit(solution)/shard_map/all_to_all | solution.py:122
  235.9 11.8 %shard_map.88 = f32[64,64,128]{2,1,0:T(8,128)} custom-call(s32[512]{0:T(512)} %bitcast.176, s32[512]{0:T(512)} %bitcast.180, s32[1]{0:T(128)} %bitcast.140.cnt_ref, bf16[512,128,128]{2,1,0:T(8,128)(2,1)} %bitcast.144, bf16[64,64,128]{2,1,0:T(8,128)(2,1)} %bitcast.151), custom_call_target="tpu_custom_call" | custom-call | flops 1073741824 | bytes 19922944 | tf_op jit(solution)/shard_map/pallas_call | solution.py:93
  247.7 48.2 %reduce-scatter.5.cloned.1.call-done = f32[16,64,128]{2,1,0:T(8,128)} async-done(((f32[64,64,128]{2,1,0:T(8,128)}), f32[16,64,128]{2,1,0:T(8,128)}) %reduce-scatter.5.cloned.1.call-update) | async-done | bytes 524304 | tf_op jit(solution)/shard_map/reduce_scatter | solution.py:165
  295.9 1.1 fusion.39
  297.2 29.0 %all_to_all.59 = bf16[4,16,64,128]{3,2,1,0:T(8,128)(2,1)} all-to-all(bf16[4,16,64,128]{3,2,1,0:T(8,128)(2,1)S(1)} %broadcast_in_dim.22), channel_id=1, replica_groups=mesh['doc'=8,'term'=4] {'term'}, dimensions={0} | all-to-all | bytes 2097152 | tf_op jit(solution)/shard_map/all_to_all | solution.py:122
  326.3 9.0 %shard_map.89 = f32[64,64,128]{2,1,0:T(8,128)} custom-call(s32[512]{0:T(512)} %bitcast.177, s32[512]{0:T(512)} %bitcast.181, s32[1]{0:T(128)} %bitcast.141.cnt_ref, bf16[512,128,128]{2,1,0:T(8,128)(2,1)} %bitcast.145, bf16[64,64,128]{2,1,0:T(8,128)(2,1)} %bitcast.149), custom_call_target="tpu_custom_call" | custom-call | flops 1073741824 | bytes 19922944 | tf_op jit(solution)/shard_map/pallas_call | solution.py:93
  335.3 7.6 %all-to-all-start.7 = ((f32[8,8,64,128]{3,2,1,0:T(8,128)}), f32[8,8,64,128]{3,2,1,0:T(8,128)S(1)}, u32[]{:S(2)}, u32[]{:S(2)}) async-start(f32[8,8,64,128]{3,2,1,0:T(8,128)} %bitcast.147), calls=%async_computation.9 | async-start | bytes 4194304 | tf_op jit(solution)/shard_map/all_to_all | solution.py:112
  343.7 25.8 %all-to-all-done.7 = f32[8,8,64,128]{3,2,1,0:T(8,128)S(1)} async-done(((f32[8,8,64,128]{3,2,1,0:T(8,128)}), f32[8,8,64,128]{3,2,1,0:T(8,128)S(1)}, u32[]{:S(2)}, u32[]{:S(2)}) %all-to-all-start.7) | async-done | bytes 2097184 | tf_op jit(solution)/shard_map/all_to_all | solution.py:112
  370.9 0.7 concatenate.7
  371.8 9.2 %all_to_all.60 = f32[4,1,12545]{2,1,0:T(1,128)S(1)} all-to-all(f32[4,1,12545]{2,1,0:T(1,128)S(1)} %broadcast_in_dim.23), channel_id=1, replica_groups=mesh['doc'=8,'term'=4] {'term'}, dimensions={0} | all-to-all | bytes 401440 | tf_op jit(solution)/shard_map/all_to_all | solution.py:117
  381.4 11.4 %all_to_all.61 = f32[8,1,12545]{2,1,0:T(1,128)S(1)} all-to-all(f32[8,1,12545]{2,1,0:T(1,128)S(1)} %broadcast_in_dim.24), channel_id=1, replica_groups=mesh['doc'=8,'term'=4] {'doc'}, dimensions={0} | all-to-all | bytes 802880 | tf_op jit(solution)/shard_map/all_to_all | solution.py:117
  393.0 0.5 slice.81
  394.2 0.7 fusion.38
  395.3 0.7 divide_subtract_fusion
  396.2 0.7 fusion.33
  396.9 5.8 %cholesky.55 = f32[64,64]{1,0:T(8,128)S(1)} custom-call(f32[64,64]{1,0:T(8,128)S(1)} %fusion.33), custom_call_target="Cholesky" | custom-call | tf_op jit(solution)/shard_map/jit(cholesky)/cholesky | solution.py:190
  402.8 0.6 compare_reduce_fusion
  403.4 0.7 fusion.28
  404.1 4.9 %custom-call.9 = f32[1,64,64]{1,2,0:T(8,128)S(1)} custom-call(f32[1,64,64]{2,1,0:T(8,128)S(1)} %fusion.28), custom_call_target="InvertDiagBlocksLowerTriangular" | custom-call | tf_op jit(solution)/shard_map/jit(_solve_triangular)/triangular_solve | solution.py:203
  409.0 0.5 fusion.5
  410.5 0.7 broadcast_in_dim_reshape.7
  411.4 0.7 fusion.2
  412.5 0.9 broadcast_in_dim_reshape.6
  (61 shorter events, 7.5 us)
Async XLA Ops:
  9.4 20.6 %all-to-all-start = ((bf16[8,8,64,128]{3,2,1,0:T(8,128)(2,1)}), bf16[8,8,64,128]{3,2,1,0:T(8,128)(2,1)S(1)}, u32[]{:S(2)}, u32[]{:S(2)}) async-start(bf16[8,8,64,128]{3,2,1,0:T(8,128)(2,1)} %broadcast_in_dim.17), calls=%async_computation | async-start | bytes 2097152 | tf_op jit(solution)/shard_map/all_to_all | solution.py:122
  14.5 87.1 %reduce-scatter.3.cloned.1.call-start = ((), (), s32[]{:S(2)}) async-start(), calls=%async_computation.12 | async-start | bytes 2949120 | tf_op jit(solution)/shard_map/reduce_scatter | solution.py:165
  29.9 1.0 copy-start
  45.8 250.1 %reduce-scatter.5.cloned.1.call-start = ((), (), s32[]{:S(2)}) async-start(), calls=%async_computation.13 | async-start | bytes 2621440 | tf_op jit(solution)/shard_map/reduce_scatter | solution.py:165
  335.3 7.6 %copy-start.3 = (s32[1,1024]{1,0:T(1,128)S(1)}, s32[1,1024]{1,0:T(1,128)}, u32[]{:S(2)}) copy-start(s32[1,1024]{1,0:T(1,128)} %param.16) | copy-start | bytes 12292
  335.3 7.7 %copy-start.2 = (s32[1,2048]{1,0:T(1,128)S(1)}, s32[1,2048]{1,0:T(1,128)}, u32[]{:S(2)}) copy-start(s32[1,2048]{1,0:T(1,128)} %param.15) | copy-start | bytes 24580
  335.3 7.9 %copy-start.1 = (f32[16,64,128]{2,1,0:T(8,128)S(1)}, f32[16,64,128]{2,1,0:T(8,128)}, u32[]{:S(2)}) copy-start(f32[16,64,128]{2,1,0:T(8,128)} %reduce-scatter.5.cloned.1.call-done) | copy-start | bytes 1572868
  335.3 34.2 %all-to-all-start.7 = ((f32[8,8,64,128]{3,2,1,0:T(8,128)}), f32[8,8,64,128]{3,2,1,0:T(8,128)S(1)}, u32[]{:S(2)}, u32[]{:S(2)}) async-start(f32[8,8,64,128]{3,2,1,0:T(8,128)} %bitcast.147), calls=%async_computation.9 | async-start | bytes 4194304 | tf_op jit(solution)/shard_map/all_to_all | solution.py:112
Sparse Core Ops, SparseCore 0:
  45.9 55.6 reduce-scatter.2
  247.8 48.0 reduce-scatter.4

commit v10 on v8

--- a/solution.py
+++ b/solution.py
@@ -29,7 +29,6 @@
     count = cnt_ref[0]
     base = step * chunk
     live = jnp.clip(count - base, 0, chunk)
-    ones = jnp.ones((DEG_ROWS, tiles_ref.shape[2]), jnp.bfloat16)
 
     def product(lhs, tile):
         if transpose_tile:
@@ -47,16 +46,11 @@
                 src, dst = rows_ref[slot], cols_ref[slot]
             tile = tiles_ref[j]
             prod = product(side_ref[src], tile)
-            deg = product(ones, tile) if with_degree else None
             if masked:
-                keep = slot < count
-                prod = jnp.where(keep, prod, 0.0)
-                deg = jnp.where(keep, deg, 0.0) if with_degree else None
-            results.append((dst, prod, deg))
-        for dst, prod, deg in results:
-            out_ref[dst, pl.ds(0, width), :] += prod
-            if with_degree:
-                out_ref[dst, pl.ds(width, DEG_ROWS), :] += deg
+                prod = jnp.where(slot < count, prod, 0.0)
+            results.append((dst, prod))
+        for dst, prod in results:
+            out_ref[dst] += prod
 
     def body(g, carry):
         run(g, False)
@@ -75,7 +69,9 @@
     n_tiles, width, _ = side.shape
     chunk = min(CHUNK, slots)
     steps = slots // chunk
-    out_rows = width + (DEG_ROWS if with_degree else 0)
+    if with_degree:
+        side = jnp.concatenate([side, jnp.ones((n_tiles, DEG_ROWS, edge), side.dtype)], axis=1)
+    out_rows = side.shape[1]
     kernel = functools.partial(tile_kernel, transpose_tile, with_degree, GROUP)
 
     def tile_map(i, rows_ref, cols_ref, cnt_ref):
@@ -98,7 +94,7 @@
             grid=(steps,),
             in_specs=[
                 pl.BlockSpec((chunk, edge, edge), tile_map),
-                pl.BlockSpec((n_tiles, width, edge), whole_map),
+                pl.BlockSpec((n_tiles, out_rows, edge), whole_map),
             ],
             out_specs=pl.BlockSpec((n_tiles, out_rows, edge), whole_map),
         ),

time: 417 us -> 417 us (level)
  Pallas kernels: 62.7 us -> 29.2 us
  waiting for transfers between devices: 190 us -> 207 us
  blocking collectives: 90.3 us -> 103 us
    pallas_call x4, Pallas kernels: 62.7 us -> 29.2 us  [tile_pass(): pl.pallas_call(kernel, out_shape=jax.ShapeDtypeStruct((n_tiles, out_rows,...]
    reduce_scatter x2, waiting for transfers between devices: 94.4 us -> 112 us  [per_device(): left_own = lax.psum_scatter(left, 'term', scatter_dimension=0, tiled=True)]
    all_to_all x4, blocking collectives: 38.9 us -> 47.9 us  [exchange_sum(): return jnp.sum(lax.all_to_all(copies, axis_name, 0, 0, tiled=False), axis=0)]
where the time goes in v10:
time: 417 us
  waiting for transfers between devices  207 us (50%)
  blocking collectives  103 us (25%)
  other arithmetic  34.5 us (8%)
  Pallas kernels  29.2 us (7%)
  between operations  15.4 us (4%)
  local copies, waits for them, and re-layouts  12.5 us (3%)
  starting transfers between devices  11.4 us (3%)
  matrix products  4.53 us (1%)
    reduce_scatter x2, waiting for transfers between devices, per_device(): left_own = lax.psum_scatter(left, 'term', scatter_dimension=0, tiled=True)  112 us
    all_gather x2, waiting for transfers between devices, per_device(): q_all = lax.all_gather(quotient, 'term', axis=0, tiled=True)  55 us
    all_to_all x4, blocking collectives, exchange_sum(): return jnp.sum(lax.all_to_all(copies, axis_name, 0, 0, tiled=False), axis=0)  47.9 us
    all_to_all x1, blocking collectives, scatter_sum(): return jnp.sum(lax.all_to_all(pieces, axis_name, 0, 0, tiled=False), axis=0)  36.1 us
    pallas_call x4, Pallas kernels, tile_pass(): pl.pallas_call(kernel, out_shape=jax.ShapeDtypeStruct((n_tiles, out_rows,...  29.2 us
    all_to_all x1, waiting for transfers between devices, scatter_sum(): return jnp.sum(lax.all_to_all(pieces, axis_name, 0, 0, tiled=False), axis=0)  25.8 us
    all_to_all x1, blocking collectives, exchange_gather(): got = lax.all_to_all(copies, axis_name, 0, 0, tiled=False)  18.5 us
    all_to_all x1, waiting for transfers between devices, exchange_gather(): got = lax.all_to_all(copies, axis_name, 0, 0, tiled=False)  14.7 us
  transfers between devices with their start and end apart: 6, of which 6 were waited for; matrix products, arithmetic and copies ran while one was open for 0% of the time, Pallas kernels for 0%

profile of v10, /device:TPU:0, one launch (start us, length us, event | category | flops | bytes accessed | tf_op | source)
XLA Modules:
  0.0 417.4 jit_solution(8780389258896837623)
XLA Ops:
  7.2 0.9 copy.111
  8.1 1.2 broadcast_in_dim.13
  9.4 5.2 %all-to-all-start = ((bf16[8,8,64,128]{3,2,1,0:T(8,128)(2,1)}), bf16[8,8,64,128]{3,2,1,0:T(8,128)(2,1)S(1)}, u32[]{:S(2)}, u32[]{:S(2)}) async-start(bf16[8,8,64,128]{3,2,1,0:T(8,128)(2,1)} %broadcast_in_dim.13), calls=%async_computation | async-start | bytes 2097152 | tf_op jit(solution)/shard_map/all_to_all | solution.py:118
  15.2 14.7 %all-to-all-done = bf16[8,8,64,128]{3,2,1,0:T(8,128)(2,1)S(1)} async-done(((bf16[8,8,64,128]{3,2,1,0:T(8,128)(2,1)}), bf16[8,8,64,128]{3,2,1,0:T(8,128)(2,1)S(1)}, u32[]{:S(2)}, u32[]{:S(2)}) %all-to-all-start) | async-done | bytes 1048608 | tf_op jit(solution)/shard_map/all_to_all | solution.py:118
  29.9 1.1 concatenate.12.side_ref
  31.0 8.0 %shard_map.86 = f32[64,72,128]{2,1,0:T(8,128)} custom-call(s32[512]{0:T(512)} %bitcast.170, s32[512]{0:T(512)} %bitcast.174, s32[1]{0:T(128)} %bitcast.136.cnt_ref, bf16[512,128,128]{2,1,0:T(8,128)(2,1)} %bitcast.140, bf16[64,72,128]{2,1,0:T(8,128)(2,1)} %concatenate.12.side_ref), custom_call_target="tpu_custom_call" | custom-call | flops 1207959552 | bytes 20316160 | tf_op jit(solution)/shard_map/pallas_call | solution.py:89
  39.1 59.3 %reduce-scatter.3.cloned.1.call-done = f32[16,72,128]{2,1,0:T(8,128)} async-done(((f32[64,72,128]{2,1,0:T(8,128)}), f32[16,72,128]{2,1,0:T(8,128)}) %reduce-scatter.3.cloned.1.call-update) | async-done | bytes 589840 | tf_op jit(solution)/shard_map/reduce_scatter | solution.py:161
  98.4 0.8 slice.75
  99.2 1.8 fusion.9
  101.1 27.5 %all-gather.3.cloned.1.call-done = bf16[64,64,128]{2,1,0:T(8,128)(2,1)} async-done(((bf16[16,64,128]{2,1,0:T(8,128)(2,1)}), bf16[64,64,128]{2,1,0:T(8,128)(2,1)}) %all-gather.3.cloned.1.call-update) | async-done | bytes 1048592 | tf_op jit(solution)/shard_map/all_gather | solution.py:166
  128.6 2.3 concatenate.13.side_ref
  131.0 7.1 %shard_map.87 = f32[64,72,128]{2,1,0:T(8,128)} custom-call(s32[512]{0:T(512)} %bitcast.171, s32[512]{0:T(512)} %bitcast.175, s32[1]{0:T(128)} %bitcast.137.cnt_ref, bf16[512,128,128]{2,1,0:T(8,128)(2,1)} %bitcast.141, bf16[64,72,128]{2,1,0:T(8,128)(2,1)} %concatenate.13.side_ref), custom_call_target="tpu_custom_call" | custom-call | flops 1207959552 | bytes 20316160 | tf_op jit(solution)/shard_map/pallas_call | solution.py:89
  138.0 36.1 %all_to_all.44 = f32[8,8,72,128]{3,2,1,0:T(8,128)S(1)} all-to-all(f32[8,8,72,128]{3,2,1,0:T(8,128)} %bitcast.144), channel_id=1, replica_groups=mesh['doc'=8,'term'=4] {'doc'}, dimensions={0} | all-to-all | bytes 4718592 | tf_op jit(solution)/shard_map/all_to_all | solution.py:108
  174.3 0.6 slice_reduce_fusion
  175.8 0.6 concatenate.14
  176.5 14.2 %all_to_all.45 = f32[4,1,4225]{2,1,0:T(1,128)S(1)} all-to-all(f32[4,1,4225]{2,1,0:T(1,128)S(1)} %broadcast_in_dim.14), channel_id=1, replica_groups=mesh['doc'=8,'term'=4] {'term'}, dimensions={0} | all-to-all | bytes 135200 | tf_op jit(solution)/shard_map/all_to_all | solution.py:113
  190.9 8.0 %all_to_all.46 = f32[8,1,4225]{2,1,0:T(1,128)S(1)} all-to-all(f32[8,1,4225]{2,1,0:T(1,128)S(1)} %broadcast_in_dim.15), channel_id=1, replica_groups=mesh['doc'=8,'term'=4] {'doc'}, dimensions={0} | all-to-all | bytes 270400 | tf_op jit(solution)/shard_map/all_to_all | solution.py:113
  199.0 0.5 slice.80
  199.5 0.6 fusion.41
  200.3 0.7 divide_subtract_fusion.1
  201.1 0.7 fusion.35
  201.9 5.8 %cholesky.44 = f32[64,64]{1,0:T(8,128)S(1)} custom-call(f32[64,64]{1,0:T(8,128)S(1)} %fusion.35), custom_call_target="Cholesky" | custom-call | tf_op jit(solution)/shard_map/jit(cholesky)/cholesky | solution.py:186
  207.8 0.6 compare_reduce_fusion.1
  208.4 0.7 fusion.27
  209.1 4.9 %custom-call.11 = f32[1,64,64]{1,2,0:T(8,128)S(1)} custom-call(f32[1,64,64]{2,1,0:T(8,128)S(1)} %fusion.27), custom_call_target="InvertDiagBlocksLowerTriangular" | custom-call | tf_op jit(solution)/shard_map/jit(_solve_triangular)/triangular_solve | solution.py:189
  214.0 0.5 convolution_bitcast_fusion
  214.7 18.5 %all_to_all.47 = bf16[8,8,64,128]{3,2,1,0:T(8,128)(2,1)} all-to-all(bf16[8,8,64,128]{3,2,1,0:T(8,128)(2,1)S(1)} %broadcast_in_dim.16), channel_id=1, replica_groups=mesh['doc'=8,'term'=4] {'doc'}, dimensions={0} | all-to-all | bytes 2097152 | tf_op jit(solution)/shard_map/all_to_all | solution.py:118
  233.2 7.6 %shard_map.88 = f32[64,64,128]{2,1,0:T(8,128)} custom-call(s32[512]{0:T(512)} %bitcast.172, s32[512]{0:T(512)} %bitcast.176, s32[1]{0:T(128)} %bitcast.138.cnt_ref, bf16[512,128,128]{2,1,0:T(8,128)(2,1)} %bitcast.142, bf16[64,64,128]{2,1,0:T(8,128)(2,1)} %bitcast.146), custom_call_target="tpu_custom_call" | custom-call | flops 1073741824 | bytes 19922944 | tf_op jit(solution)/shard_map/pallas_call | solution.py:89
  240.9 52.5 %reduce-scatter.5.cloned.1.call-done = f32[16,64,128]{2,1,0:T(8,128)} async-done(((f32[64,64,128]{2,1,0:T(8,128)}), f32[16,64,128]{2,1,0:T(8,128)}) %reduce-scatter.5.cloned.1.call-update) | async-done | bytes 524304 | tf_op jit(solution)/shard_map/reduce_scatter | solution.py:161
  293.4 1.8 fusion.39
  295.2 27.5 %all-gather.5.cloned.1.call-done.side_ref = bf16[64,64,128]{2,1,0:T(8,128)(2,1)} async-done(((bf16[16,64,128]{2,1,0:T(8,128)(2,1)}), bf16[64,64,128]{2,1,0:T(8,128)(2,1)}) %all-gather.5.cloned.1.call-update) | async-done | bytes 1048592 | tf_op jit(solution)/shard_map/all_gather | solution.py:166
  322.8 6.5 %shard_map.89 = f32[64,64,128]{2,1,0:T(8,128)} custom-call(s32[512]{0:T(512)} %bitcast.173, s32[512]{0:T(512)} %bitcast.177, s32[1]{0:T(128)} %bitcast.139.cnt_ref, bf16[512,128,128]{2,1,0:T(8,128)(2,1)} %bitcast.143, bf16[64,64,128]{2,1,0:T(8,128)(2,1)} %all-gather.5.cloned.1.call-done.side_ref), custom_call_target="tpu_custom_call" | custom-call | flops 1073741824 | bytes 19922944 | tf_op jit(solution)/shard_map/pallas_call | solution.py:89
  329.3 6.0 %all-to-all-start.5 = ((f32[8,8,64,128]{3,2,1,0:T(8,128)}), f32[8,8,64,128]{3,2,1,0:T(8,128)S(1)}, u32[]{:S(2)}, u32[]{:S(2)}) async-start(f32[8,8,64,128]{3,2,1,0:T(8,128)} %bitcast.145), calls=%async_computation.7 | async-start | bytes 4194304 | tf_op jit(solution)/shard_map/all_to_all | solution.py:108
  336.2 25.8 %all-to-all-done.5 = f32[8,8,64,128]{3,2,1,0:T(8,128)S(1)} async-done(((f32[8,8,64,128]{3,2,1,0:T(8,128)}), f32[8,8,64,128]{3,2,1,0:T(8,128)S(1)}, u32[]{:S(2)}, u32[]{:S(2)}) %all-to-all-start.5) | async-done | bytes 2097184 | tf_op jit(solution)/shard_map/all_to_all | solution.py:108
  363.4 0.6 concatenate.15
  364.2 14.6 %all_to_all.48 = f32[4,1,12545]{2,1,0:T(1,128)S(1)} all-to-all(f32[4,1,12545]{2,1,0:T(1,128)S(1)} %broadcast_in_dim.17), channel_id=1, replica_groups=mesh['doc'=8,'term'=4] {'term'}, dimensions={0} | all-to-all | bytes 401440 | tf_op jit(solution)/shard_map/all_to_all | solution.py:113
  379.2 11.1 %all_to_all.49 = f32[8,1,12545]{2,1,0:T(1,128)S(1)} all-to-all(f32[8,1,12545]{2,1,0:T(1,128)S(1)} %broadcast_in_dim.18), channel_id=1, replica_groups=mesh['doc'=8,'term'=4] {'doc'}, dimensions={0} | all-to-all | bytes 802880 | tf_op jit(solution)/shard_map/all_to_all | solution.py:113
  390.6 0.5 slice.81
  391.8 0.7 fusion.38
  392.9 0.7 divide_subtract_fusion
  393.7 0.7 fusion.33
  394.4 5.8 %cholesky.55 = f32[64,64]{1,0:T(8,128)S(1)} custom-call(f32[64,64]{1,0:T(8,128)S(1)} %fusion.33), custom_call_target="Cholesky" | custom-call | tf_op jit(solution)/shard_map/jit(cholesky)/cholesky | solution.py:186
  400.3 0.6 compare_reduce_fusion
  401.0 0.7 fusion.28
  401.6 4.9 %custom-call.9 = f32[1,64,64]{1,2,0:T(8,128)S(1)} custom-call(f32[1,64,64]{2,1,0:T(8,128)S(1)} %fusion.28), custom_call_target="InvertDiagBlocksLowerTriangular" | custom-call | tf_op jit(solution)/shard_map/jit(_solve_triangular)/triangular_solve | solution.py:199
  408.1 0.7 broadcast_in_dim_reshape.7
  409.0 0.7 fusion.2
  410.0 0.9 broadcast_in_dim_reshape.6
  (63 shorter events, 7.6 us)
Async XLA Ops:
  9.4 20.6 %all-to-all-start = ((bf16[8,8,64,128]{3,2,1,0:T(8,128)(2,1)}), bf16[8,8,64,128]{3,2,1,0:T(8,128)(2,1)S(1)}, u32[]{:S(2)}, u32[]{:S(2)}) async-start(bf16[8,8,64,128]{3,2,1,0:T(8,128)(2,1)} %broadcast_in_dim.13), calls=%async_computation | async-start | bytes 2097152 | tf_op jit(solution)/shard_map/all_to_all | solution.py:118
  14.5 83.9 %reduce-scatter.3.cloned.1.call-start = ((), (), s32[]{:S(2)}) async-start(), calls=%async_computation.10 | async-start | bytes 2949120 | tf_op jit(solution)/shard_map/reduce_scatter | solution.py:161
  39.0 89.6 %all-gather.3.cloned.1.call-start = ((), (), s32[]{:S(2)}) async-start(), calls=%async_computation.11 | async-start | bytes 1310720 | tf_op jit(solution)/shard_map/all_gather | solution.py:166
  101.1 192.3 %reduce-scatter.5.cloned.1.call-start = ((), (), s32[]{:S(2)}) async-start(), calls=%async_computation.12 | async-start | bytes 2621440 | tf_op jit(solution)/shard_map/reduce_scatter | solution.py:161
  240.9 81.9 %all-gather.5.cloned.1.call-start = ((), (), s32[]{:S(2)}) async-start(), calls=%async_computation.13 | async-start | bytes 1310720 | tf_op jit(solution)/shard_map/all_gather | solution.py:166
  329.3 6.0 %copy-start.2 = (s32[1,1024]{1,0:T(1,128)S(1)}, s32[1,1024]{1,0:T(1,128)}, u32[]{:S(2)}) copy-start(s32[1,1024]{1,0:T(1,128)} %param.16) | copy-start | bytes 12292
  329.3 6.2 %copy-start.1 = (s32[1,2048]{1,0:T(1,128)S(1)}, s32[1,2048]{1,0:T(1,128)}, u32[]{:S(2)}) copy-start(s32[1,2048]{1,0:T(1,128)} %param.15) | copy-start | bytes 24580
  329.3 6.3 %copy-start = (f32[16,64,128]{2,1,0:T(8,128)S(1)}, f32[16,64,128]{2,1,0:T(8,128)}, u32[]{:S(2)}) copy-start(f32[16,64,128]{2,1,0:T(8,128)} %reduce-scatter.5.cloned.1.call-done) | copy-start | bytes 1572868
  329.3 32.7 %all-to-all-start.5 = ((f32[8,8,64,128]{3,2,1,0:T(8,128)}), f32[8,8,64,128]{3,2,1,0:T(8,128)S(1)}, u32[]{:S(2)}, u32[]{:S(2)}) async-start(f32[8,8,64,128]{3,2,1,0:T(8,128)} %bitcast.145), calls=%async_computation.7 | async-start | bytes 4194304 | tf_op jit(solution)/shard_map/all_to_all | solution.py:108
Sparse Core Ops, SparseCore 0:
  39.2 59.1 reduce-scatter.2
  101.2 27.4 all-gather.2
  241.0 52.3 reduce-scatter.4
  295.5 27.2 all-gather.4

commit v11 on v10

--- a/solution.py
+++ b/solution.py
@@ -17,7 +17,7 @@
 NT_DIMS = (((1,), (1,)), ((), ()))
 
 
-def tile_kernel(transpose_tile, with_degree, group, rows_ref, cols_ref, cnt_ref, tiles_ref, side_ref, out_ref):
+def tile_kernel(transpose_tile, with_degree, group, split, rows_ref, cols_ref, cnt_ref, tiles_ref, side_ref, out_ref, rest_ref):
     step = pl.program_id(0)
     chunk = tiles_ref.shape[0]
     width = side_ref.shape[1]
@@ -25,6 +25,7 @@
     @pl.when(step == 0)
     def _():
         out_ref[...] = jnp.zeros_like(out_ref)
+        rest_ref[...] = jnp.zeros_like(rest_ref)
 
     count = cnt_ref[0]
     base = step * chunk
@@ -50,7 +51,8 @@
                 prod = jnp.where(slot < count, prod, 0.0)
             results.append((dst, prod))
         for dst, prod in results:
-            out_ref[dst] += prod
+            out_ref[dst] += prod[:split]
+            rest_ref[dst] += prod[split:]
 
     def body(g, carry):
         run(g, False)
@@ -64,7 +66,7 @@
         run(full, True)
 
 
-def tile_pass(tiles, rows, cols, count, side, transpose_tile, with_degree):
+def tile_pass(tiles, rows, cols, count, side, transpose_tile, with_degree, split):
     slots, edge, _ = tiles.shape
     n_tiles, width, _ = side.shape
     chunk = min(CHUNK, slots)
@@ -72,7 +74,7 @@
     if with_degree:
         side = jnp.concatenate([side, jnp.ones((n_tiles, DEG_ROWS, edge), side.dtype)], axis=1)
     out_rows = side.shape[1]
-    kernel = functools.partial(tile_kernel, transpose_tile, with_degree, GROUP)
+    kernel = functools.partial(tile_kernel, transpose_tile, with_degree, GROUP, split)
 
     def tile_map(i, rows_ref, cols_ref, cnt_ref):
         return (jnp.minimum(i, jnp.maximum(cnt_ref[0] - 1, 0) // chunk), 0, 0)
@@ -88,7 +90,10 @@
     )
     return pl.pallas_call(
         kernel,
-        out_shape=jax.ShapeDtypeStruct((n_tiles, out_rows, edge), jnp.float32),
+        out_shape=(
+            jax.ShapeDtypeStruct((n_tiles, split, edge), jnp.float32),
+            jax.ShapeDtypeStruct((n_tiles, out_rows - split, edge), jnp.float32),
+        ),
         grid_spec=pltpu.PrefetchScalarGridSpec(
             num_scalar_prefetch=3,
             grid=(steps,),
@@ -96,7 +101,10 @@
                 pl.BlockSpec((chunk, edge, edge), tile_map),
                 pl.BlockSpec((n_tiles, out_rows, edge), whole_map),
             ],
-            out_specs=pl.BlockSpec((n_tiles, out_rows, edge), whole_map),
+            out_specs=(
+                pl.BlockSpec((n_tiles, split, edge), whole_map),
+                pl.BlockSpec((n_tiles, out_rows - split, edge), whole_map),
+            ),
         ),
         compiler_params=pltpu.CompilerParams(dimension_semantics=("arbitrary",)),
         cost_estimate=cost,
@@ -117,6 +125,18 @@
     copies = jnp.broadcast_to(x, (parts,) + x.shape)
     got = lax.all_to_all(copies, axis_name, 0, 0, tiled=False)
     return got.reshape((parts * x.shape[0],) + x.shape[1:])
+
+
+def split_scatter_sum(offloaded, exchanged, axis_name, parts):
+    first = lax.psum_scatter(offloaded, axis_name, scatter_dimension=0, tiled=True)
+    second = scatter_sum(exchanged, axis_name, parts)
+    return jnp.concatenate([first, second], axis=1)
+
+
+def split_gather(x, axis_name, parts, offloaded_rows):
+    first = lax.all_gather(x[:, :offloaded_rows], axis_name, axis=0, tiled=True)
+    second = exchange_gather(x[:, offloaded_rows:], axis_name, parts)
+    return jnp.concatenate([first, second], axis=1)
 
 
 def packed_psum(n_doc, n_term, values):
@@ -156,16 +176,16 @@
     volume = None
     for step in range(ITERS):
         first = step == 0
-        w_all = exchange_gather(weights, "doc", n_doc)
-        left = tile_pass(local_tiles, rows, cols, count, w_all, True, first)
-        left_own = lax.psum_scatter(left, "term", scatter_dimension=0, tiled=True)
+        w_all = split_gather(weights, "doc", n_doc, 24)
+        left = tile_pass(local_tiles, rows, cols, count, w_all, True, first, 40)
+        left_own = split_scatter_sum(*left, "term", n_term)
         summed_own = left_own[:, :width_k, :]
         if first:
             doc_degree = left_own[:, width_k, :]
         quotient = (summed_own / doc_degree[:, None, :]).astype(jnp.bfloat16)
-        q_all = lax.all_gather(quotient, "term", axis=0, tiled=True)
-        right = tile_pass(local_tiles, rows, cols, count, q_all, False, first)
-        right_own = scatter_sum(right, "doc", n_doc)
+        q_all = split_gather(quotient, "term", n_term, 32)
+        right = tile_pass(local_tiles, rows, cols, count, q_all, False, first, 24)
+        right_own = split_scatter_sum(*right, "doc", n_doc)
         if first:
             term_degree = right_own[:, width_k, :]
             root = jnp.sqrt(term_degree)

time: 417 us -> 438 us (1.050); the launches traced: 417 us -> 444 us
  waiting for transfers between devices: 207 us -> 84 us
  blocking collectives: 103 us -> 211 us
  starting transfers between devices: 11.4 us -> 33.7 us
  Pallas kernels: 29.2 us -> 41.7 us
    all_gather x0 -> x4, blocking collectives: none -> 80.4 us  [split_gather(): first = lax.all_gather(x[:, :offloaded_rows], axis_name, axis=0, tiled=True)]
    reduce_scatter x2 -> x4, waiting for transfers between devices: 112 us -> 45.6 us  [split_scatter_sum(): lax.psum_scatter(offloaded, axis_name, scatter_dimension=0, tiled=True)]
    all_gather x2 -> x0, waiting for transfers between devices: 55 us -> none  [per_device(): q_all = lax.all_gather(quotient, 'term', axis=0, tiled=True)]
    all_to_all x1 -> x2, blocking collectives: 36.1 us -> 89.2 us  [scatter_sum(): return jnp.sum(lax.all_to_all(pieces, axis_name, 0, 0, tiled=False), axis=0)]
    all_to_all x1 -> x0, blocking collectives: 18.5 us -> none  [exchange_gather(): got = lax.all_to_all(copies, axis_name, 0, 0, tiled=False)]
    all_to_all x1 -> x4, waiting for transfers between devices: 14.7 us -> 0.01 us  [exchange_gather(): got = lax.all_to_all(copies, axis_name, 0, 0, tiled=False)]
    pallas_call x4, Pallas kernels: 29.2 us -> 41.7 us  [tile_pass(): pl.pallas_call(kernel, out_shape=(jax.ShapeDtypeStruct((n_tiles, split, e...]
    all_to_all x1 -> x2, starting transfers between devices: 6.03 us -> 17.9 us  [scatter_sum(): return jnp.sum(lax.all_to_all(pieces, axis_name, 0, 0, tiled=False), axis=0)]
  transfers between devices with their start and end apart: 6 -> 10, of which waited for: 6 -> 6; matrix products, arithmetic and copies ran while one was open for 0% -> 0% of each run, Pallas kernels for 0% -> 0%
where the time goes in v11:
time: 438 us; the launch traced here: 444 us
  blocking collectives  211 us (48%)
  waiting for transfers between devices  84 us (19%)
  Pallas kernels  41.7 us (10%)
  other arithmetic  38.8 us (9%)
  starting transfers between devices  33.7 us (8%)
  between operations  15.5 us (4%)
  local copies, waits for them, and re-layouts  10.6 us (2%)
  matrix products  8.26 us (2%)
    all_to_all x2, blocking collectives, scatter_sum(): return jnp.sum(lax.all_to_all(pieces, axis_name, 0, 0, tiled=False), axis=0)  89.2 us
    all_gather x4, blocking collectives, split_gather(): first = lax.all_gather(x[:, :offloaded_rows], axis_name, axis=0, tiled=True)  80.4 us
    reduce_scatter x4, waiting for transfers between devices, split_scatter_sum(): lax.psum_scatter(offloaded, axis_name, scatter_dimension=0, tiled=True)  45.6 us
    pallas_call x4, Pallas kernels, tile_pass(): pl.pallas_call(kernel, out_shape=(jax.ShapeDtypeStruct((n_tiles, split, e...  41.7 us
    all_to_all x4, blocking collectives, exchange_sum(): return jnp.sum(lax.all_to_all(copies, axis_name, 0, 0, tiled=False), axis=0)  41.2 us
    all_to_all x2, waiting for transfers between devices, scatter_sum(): return jnp.sum(lax.all_to_all(pieces, axis_name, 0, 0, tiled=False), axis=0)  37.7 us
    all_to_all x2, starting transfers between devices, scatter_sum(): return jnp.sum(lax.all_to_all(pieces, axis_name, 0, 0, tiled=False), axis=0)  17.9 us
    all_to_all x4, starting transfers between devices, exchange_gather(): got = lax.all_to_all(copies, axis_name, 0, 0, tiled=False)  15.7 us
  transfers between devices with their start and end apart: 10, of which 6 were waited for; matrix products, arithmetic and copies ran while one was open for 0% of the time, Pallas kernels for 0%

profile of v11, /device:TPU:0, one launch (start us, length us, event | category | flops | bytes accessed | tf_op | source)
XLA Modules:
  0.0 443.6 jit_solution(2873815362830322387)
XLA Ops:
  7.2 0.9 copy.114
  8.1 0.9 broadcast_in_dim.17
  9.1 5.2 %all-to-all-start = ((bf16[8,8,40,128]{3,2,1,0:T(8,128)(2,1)}), bf16[8,8,40,128]{3,2,1,0:T(8,128)(2,1)S(1)}, u32[]{:S(2)}, u32[]{:S(2)}) async-start(bf16[8,8,40,128]{3,2,1,0:T(8,128)(2,1)} %broadcast_in_dim.17), calls=%async_computation | async-start | bytes 1310720 | tf_op jit(solution)/shard_map/all_to_all | solution.py:126
  15.0 14.4 %all_gather.12 = bf16[64,24,128]{2,1,0:T(8,128)(2,1)S(1)} all-gather(bf16[8,24,128]{2,1,0:T(8,128)(2,1)S(1)} %slice.106), channel_id=1, replica_groups=mesh['doc'=8,'term'=4] {'doc'}, dimensions={0}, use_global_device_ids=true | all-gather | bytes 442368 | tf_op jit(solution)/shard_map/all_gather | solution.py:137
  29.4 1.3 maximum_maximum_fusion.side_ref
  30.7 11.9 %shard_map.86 = (f32[64,40,128]{2,1,0:T(8,128)}, f32[64,32,128]{2,1,0:T(8,128)}) custom-call(s32[512]{0:T(512)} %bitcast.174, s32[512]{0:T(512)} %bitcast.178, s32[1]{0:T(128)} %bitcast.135.cnt_ref, bf16[512,128,128]{2,1,0:T(8,128)(2,1)} %bitcast.139, bf16[64,72,128]{2,1,0:T(8,128)(2,1)} %maximum_maximum_fusion.side_ref), custom_call_target="tpu_custom_call" | custom-call | flops 1207959552 | bytes 20316160 | tf_op jit(solution)/shard_map/pallas_call | solution.py:91
  42.6 49.9 %all_to_all.64 = f32[4,16,32,128]{3,2,1,0:T(8,128)S(1)} all-to-all(f32[4,16,32,128]{3,2,1,0:T(8,128)} %bitcast.151), channel_id=1, replica_groups=mesh['doc'=8,'term'=4] {'term'}, dimensions={0} | all-to-all | bytes 2097152 | tf_op jit(solution)/shard_map/all_to_all | solution.py:116
  92.6 1.2 reduce-scatter.5.cloned.1.call-done
  93.8 1.0 fusion.10
  94.9 0.9 broadcast_in_dim.18
  95.8 3.5 all-to-all-start.2
  99.2 25.8 %all_gather.13 = bf16[64,32,128]{2,1,0:T(8,128)(2,1)S(1)} all-gather(bf16[16,32,128]{2,1,0:T(8,128)(2,1)S(1)} %get-tuple-element.22), channel_id=1, replica_groups=mesh['doc'=8,'term'=4] {'term'}, dimensions={0}, use_global_device_ids=true | all-gather | bytes 655360 | tf_op jit(solution)/shard_map/all_gather | solution.py:137
  125.0 1.3 maximum_maximum_fusion.1.side_ref
  126.3 9.7 %shard_map.87 = (f32[64,24,128]{2,1,0:T(8,128)}, f32[64,48,128]{2,1,0:T(8,128)}) custom-call(s32[512]{0:T(512)} %bitcast.175, s32[512]{0:T(512)} %bitcast.179, s32[1]{0:T(128)} %bitcast.136.cnt_ref, bf16[512,128,128]{2,1,0:T(8,128)(2,1)} %bitcast.140, bf16[64,72,128]{2,1,0:T(8,128)(2,1)} %maximum_maximum_fusion.1.side_ref), custom_call_target="tpu_custom_call" | custom-call | flops 1207959552 | bytes 20316160 | tf_op jit(solution)/shard_map/pallas_call | solution.py:91
  136.0 8.8 %all-to-all-start.3 = ((f32[8,8,48,128]{3,2,1,0:T(8,128)}), f32[8,8,48,128]{3,2,1,0:T(8,128)S(1)}, u32[]{:S(2)}, u32[]{:S(2)}) async-start(f32[8,8,48,128]{3,2,1,0:T(8,128)} %bitcast.147), calls=%async_computation.5 | async-start | bytes 3145728 | tf_op jit(solution)/shard_map/all_to_all | solution.py:116
  145.6 20.3 %all-to-all-done.3 = f32[8,8,48,128]{3,2,1,0:T(8,128)S(1)} async-done(((f32[8,8,48,128]{3,2,1,0:T(8,128)}), f32[8,8,48,128]{3,2,1,0:T(8,128)S(1)}, u32[]{:S(2)}, u32[]{:S(2)}) %all-to-all-start.3) | async-done | bytes 1572896 | tf_op jit(solution)/shard_map/all_to_all | solution.py:116
  166.6 22.4 %reduce-scatter.7.cloned.1.call-done = f32[8,24,128]{2,1,0:T(8,128)} async-done(((f32[64,24,128]{2,1,0:T(8,128)}), f32[8,24,128]{2,1,0:T(8,128)}) %reduce-scatter.7.cloned.1.call-update) | async-done | bytes 98320 | tf_op jit(solution)/shard_map/reduce_scatter | solution.py:131
  189.0 1.4 convolution_bitcast_fusion.4
  190.5 1.0 multiply_reduce_fusion.2
  191.5 1.2 convolution_bitcast_fusion.6
  193.4 10.2 %all_to_all.65 = f32[4,1,4225]{2,1,0:T(1,128)S(1)} all-to-all(f32[4,1,4225]{2,1,0:T(1,128)S(1)} %broadcast_in_dim.19), channel_id=1, replica_groups=mesh['doc'=8,'term'=4] {'term'}, dimensions={0} | all-to-all | bytes 135200 | tf_op jit(solution)/shard_map/all_to_all | solution.py:121
  203.7 8.1 %all_to_all.66 = f32[8,1,4225]{2,1,0:T(1,128)S(1)} all-to-all(f32[8,1,4225]{2,1,0:T(1,128)S(1)} %broadcast_in_dim.20), channel_id=1, replica_groups=mesh['doc'=8,'term'=4] {'doc'}, dimensions={0} | all-to-all | bytes 270400 | tf_op jit(solution)/shard_map/all_to_all | solution.py:121
  214.9 5.8 %cholesky.44 = f32[64,64]{1,0:T(8,128)S(1)} custom-call(f32[64,64]{1,0:T(8,128)S(1)} %fusion.37), custom_call_target="Cholesky" | custom-call | tf_op jit(solution)/shard_map/jit(cholesky)/cholesky | solution.py:206
  222.1 4.9 %custom-call.11 = f32[1,64,64]{1,2,0:T(8,128)S(1)} custom-call(f32[1,64,64]{2,1,0:T(8,128)S(1)} %fusion.29), custom_call_target="InvertDiagBlocksLowerTriangular" | custom-call | tf_op jit(solution)/shard_map/jit(_solve_triangular)/triangular_solve | solution.py:209
  227.5 0.9 broadcast_in_dim.21
  228.4 3.5 all-to-all-start.6
  232.0 15.0 %all_gather.14 = bf16[64,24,128]{2,1,0:T(8,128)(2,1)S(1)} all-gather(bf16[8,24,128]{2,1,0:T(8,128)(2,1)S(1)} %slice.115), channel_id=1, replica_groups=mesh['doc'=8,'term'=4] {'doc'}, dimensions={0}, use_global_device_ids=true | all-gather | bytes 442368 | tf_op jit(solution)/shard_map/all_gather | solution.py:137
  247.1 1.2 pad_maximum_fusion.side_ref
  248.2 11.3 %shard_map.88 = (f32[64,40,128]{2,1,0:T(8,128)}, f32[64,24,128]{2,1,0:T(8,128)}) custom-call(s32[512]{0:T(512)} %bitcast.176, s32[512]{0:T(512)} %bitcast.180, s32[1]{0:T(128)} %bitcast.137.cnt_ref, bf16[512,128,128]{2,1,0:T(8,128)(2,1)} %bitcast.141, bf16[64,64,128]{2,1,0:T(8,128)(2,1)} %pad_maximum_fusion.side_ref), custom_call_target="tpu_custom_call" | custom-call | flops 1073741824 | bytes 19922944 | tf_op jit(solution)/shard_map/pallas_call | solution.py:91
  259.6 39.3 %all_to_all.67 = f32[4,16,24,128]{3,2,1,0:T(8,128)S(1)} all-to-all(f32[4,16,24,128]{3,2,1,0:T(8,128)} %bitcast.152), channel_id=1, replica_groups=mesh['doc'=8,'term'=4] {'term'}, dimensions={0} | all-to-all | bytes 1572864 | tf_op jit(solution)/shard_map/all_to_all | solution.py:116
  299.0 4.1 reduce-scatter.9.cloned.1.call-done
  303.1 1.0 fusion.46
  304.1 0.9 broadcast_in_dim.22
  305.0 3.5 all-to-all-start.8
  308.5 25.3 %all_gather.15 = bf16[64,32,128]{2,1,0:T(8,128)(2,1)S(1)} all-gather(bf16[16,32,128]{2,1,0:T(8,128)(2,1)S(1)} %get-tuple-element.20), channel_id=1, replica_groups=mesh['doc'=8,'term'=4] {'term'}, dimensions={0}, use_global_device_ids=true | all-gather | bytes 655360 | tf_op jit(solution)/shard_map/all_gather | solution.py:137
  333.8 1.1 pad_maximum_fusion.1.side_ref
  334.9 8.7 %shard_map.89 = (f32[64,24,128]{2,1,0:T(8,128)}, f32[64,40,128]{2,1,0:T(8,128)}) custom-call(s32[512]{0:T(512)} %bitcast.177, s32[512]{0:T(512)} %bitcast.181, s32[1]{0:T(128)} %bitcast.138.cnt_ref, bf16[512,128,128]{2,1,0:T(8,128)(2,1)} %bitcast.142, bf16[64,64,128]{2,1,0:T(8,128)(2,1)} %pad_maximum_fusion.1.side_ref), custom_call_target="tpu_custom_call" | custom-call | flops 1073741824 | bytes 19922944 | tf_op jit(solution)/shard_map/pallas_call | solution.py:91
  343.7 9.1 %all-to-all-start.9 = ((f32[8,8,40,128]{3,2,1,0:T(8,128)}), f32[8,8,40,128]{3,2,1,0:T(8,128)S(1)}, u32[]{:S(2)}, u32[]{:S(2)}) async-start(f32[8,8,40,128]{3,2,1,0:T(8,128)} %bitcast.148), calls=%async_computation.13 | async-start | bytes 2621440 | tf_op jit(solution)/shard_map/all_to_all | solution.py:116
  353.6 17.4 %all-to-all-done.9 = f32[8,8,40,128]{3,2,1,0:T(8,128)S(1)} async-done(((f32[8,8,40,128]{3,2,1,0:T(8,128)}), f32[8,8,40,128]{3,2,1,0:T(8,128)S(1)}, u32[]{:S(2)}, u32[]{:S(2)}) %all-to-all-start.9) | async-done | bytes 1310752 | tf_op jit(solution)/shard_map/all_to_all | solution.py:116
  371.1 18.0 %reduce-scatter.11.cloned.1.call-done = f32[8,24,128]{2,1,0:T(8,128)} async-done(((f32[64,24,128]{2,1,0:T(8,128)}), f32[8,24,128]{2,1,0:T(8,128)}) %reduce-scatter.11.cloned.1.call-update) | async-done | bytes 98320 | tf_op jit(solution)/shard_map/reduce_scatter | solution.py:131
  389.1 1.2 convolution_bitcast_fusion.1
  390.4 1.3 convolution_bitcast_fusion.3
  393.1 11.9 %all_to_all.68 = f32[4,1,12545]{2,1,0:T(1,128)S(1)} all-to-all(f32[4,1,12545]{2,1,0:T(1,128)S(1)} %broadcast_in_dim.23), channel_id=1, replica_groups=mesh['doc'=8,'term'=4] {'term'}, dimensions={0} | all-to-all | bytes 401440 | tf_op jit(solution)/shard_map/all_to_all | solution.py:121
  405.3 11.1 %all_to_all.69 = f32[8,1,12545]{2,1,0:T(1,128)S(1)} all-to-all(f32[8,1,12545]{2,1,0:T(1,128)S(1)} %broadcast_in_dim.24), channel_id=1, replica_groups=mesh['doc'=8,'term'=4] {'doc'}, dimensions={0} | all-to-all | bytes 802880 | tf_op jit(solution)/shard_map/all_to_all | solution.py:121
  420.7 5.8 %cholesky.55 = f32[64,64]{1,0:T(8,128)S(1)} custom-call(f32[64,64]{1,0:T(8,128)S(1)} %fusion.35), custom_call_target="Cholesky" | custom-call | tf_op jit(solution)/shard_map/jit(cholesky)/cholesky | solution.py:206
  427.9 4.9 %custom-call.9 = f32[1,64,64]{1,2,0:T(8,128)S(1)} custom-call(f32[1,64,64]{2,1,0:T(8,128)S(1)} %fusion.30), custom_call_target="InvertDiagBlocksLowerTriangular" | custom-call | tf_op jit(solution)/shard_map/jit(_solve_triangular)/triangular_solve | solution.py:219
  434.3 0.9 broadcast_in_dim_reshape.6
  436.3 0.7 broadcast_in_dim_reshape.7
  (93 shorter events, 17.8 us)
Async XLA Ops:
  9.1 20.3 %all-to-all-start = ((bf16[8,8,40,128]{3,2,1,0:T(8,128)(2,1)}), bf16[8,8,40,128]{3,2,1,0:T(8,128)(2,1)S(1)}, u32[]{:S(2)}, u32[]{:S(2)}) async-start(bf16[8,8,40,128]{3,2,1,0:T(8,128)(2,1)} %broadcast_in_dim.17), calls=%async_computation | async-start | bytes 1310720 | tf_op jit(solution)/shard_map/all_to_all | solution.py:126
  14.2 79.6 %reduce-scatter.5.cloned.1.call-start = ((), (), s32[]{:S(2)}) async-start(), calls=%async_computation.16 | async-start | bytes 1638400 | tf_op jit(solution)/shard_map/reduce_scatter | solution.py:131
  95.8 29.2 %all-to-all-start.2 = ((bf16[4,16,32,128]{3,2,1,0:T(8,128)(2,1)}), bf16[4,16,32,128]{3,2,1,0:T(8,128)(2,1)S(1)}, u32[]{:S(2)}, u32[]{:S(2)}) async-start(bf16[4,16,32,128]{3,2,1,0:T(8,128)(2,1)} %broadcast_in_dim.18), calls=%async_computation.3 | async-start | bytes 1048576 | tf_op jit(solution)/shard_map/all_to_all | solution.py:126
  136.0 29.9 %all-to-all-start.3 = ((f32[8,8,48,128]{3,2,1,0:T(8,128)}), f32[8,8,48,128]{3,2,1,0:T(8,128)S(1)}, u32[]{:S(2)}, u32[]{:S(2)}) async-start(f32[8,8,48,128]{3,2,1,0:T(8,128)} %bitcast.147), calls=%async_computation.5 | async-start | bytes 3145728 | tf_op jit(solution)/shard_map/all_to_all | solution.py:116
  144.9 44.1 %reduce-scatter.7.cloned.1.call-start = ((), (), s32[]{:S(2)}) async-start(), calls=%async_computation.17 | async-start | bytes 884736 | tf_op jit(solution)/shard_map/reduce_scatter | solution.py:131
  189.0 38.0 %copy-start.2 = (f32[8,24,128]{2,1,0:T(8,128)S(1)}, f32[8,24,128]{2,1,0:T(8,128)}, u32[]{:S(2)}) copy-start(f32[8,24,128]{2,1,0:T(8,128)} %reduce-scatter.7.cloned.1.call-done) | copy-start | bytes 294916
  228.4 18.6 %all-to-all-start.6 = ((bf16[8,8,40,128]{3,2,1,0:T(8,128)(2,1)}), bf16[8,8,40,128]{3,2,1,0:T(8,128)(2,1)S(1)}, u32[]{:S(2)}, u32[]{:S(2)}) async-start(bf16[8,8,40,128]{3,2,1,0:T(8,128)(2,1)} %broadcast_in_dim.21), calls=%async_computation.8 | async-start | bytes 1310720 | tf_op jit(solution)/shard_map/all_to_all | solution.py:126
  232.0 71.1 %reduce-scatter.9.cloned.1.call-start = ((), (), s32[]{:S(2)}) async-start(), calls=%async_computation.18 | async-start | bytes 1638400 | tf_op jit(solution)/shard_map/reduce_scatter | solution.py:131
  305.0 28.8 %all-to-all-start.8 = ((bf16[4,16,32,128]{3,2,1,0:T(8,128)(2,1)}), bf16[4,16,32,128]{3,2,1,0:T(8,128)(2,1)S(1)}, u32[]{:S(2)}, u32[]{:S(2)}) async-start(bf16[4,16,32,128]{3,2,1,0:T(8,128)(2,1)} %broadcast_in_dim.22), calls=%async_computation.11 | async-start | bytes 1048576 | tf_op jit(solution)/shard_map/all_to_all | solution.py:126
  308.5 80.6 %reduce-scatter.11.cloned.1.call-start = ((), (), s32[]{:S(2)}) async-start(), calls=%async_computation.19 | async-start | bytes 884736 | tf_op jit(solution)/shard_map/reduce_scatter | solution.py:131
  343.7 9.1 %copy-start.4 = (s32[1,1024]{1,0:T(1,128)S(1)}, s32[1,1024]{1,0:T(1,128)}, u32[]{:S(2)}) copy-start(s32[1,1024]{1,0:T(1,128)} %param.16) | copy-start | bytes 12292
  343.7 9.3 %copy-start.3 = (s32[1,2048]{1,0:T(1,128)S(1)}, s32[1,2048]{1,0:T(1,128)}, u32[]{:S(2)}) copy-start(s32[1,2048]{1,0:T(1,128)} %param.15) | copy-start | bytes 24580
  343.7 9.4 %copy-start = (f32[16,40,128]{2,1,0:T(8,128)S(1)}, f32[16,40,128]{2,1,0:T(8,128)}, u32[]{:S(2)}) copy-start(f32[16,40,128]{2,1,0:T(8,128)} %reduce-scatter.9.cloned.1.call-done) | copy-start | bytes 983044
  343.7 27.3 %all-to-all-start.9 = ((f32[8,8,40,128]{3,2,1,0:T(8,128)}), f32[8,8,40,128]{3,2,1,0:T(8,128)S(1)}, u32[]{:S(2)}, u32[]{:S(2)}) async-start(f32[8,8,40,128]{3,2,1,0:T(8,128)} %bitcast.148), calls=%async_computation.13 | async-start | bytes 2621440 | tf_op jit(solution)/shard_map/all_to_all | solution.py:116
  389.1 2.7 copy-start.1
Sparse Core Ops, SparseCore 0:
  42.7 51.0 reduce-scatter.4
  148.9 40.0 reduce-scatter.6
  259.7 43.2 reduce-scatter.8
  343.8 45.1 reduce-scatter.10

commit v12 on v10

--- a/solution.py
+++ b/solution.py
@@ -45,7 +45,10 @@
             else:
                 src, dst = rows_ref[slot], cols_ref[slot]
             tile = tiles_ref[j]
-            prod = product(side_ref[src], tile)
+            lhs = side_ref[src]
+            if with_degree:
+                lhs = jnp.concatenate([lhs, jnp.ones((DEG_ROWS, lhs.shape[1]), lhs.dtype)], axis=0)
+            prod = product(lhs, tile)
             if masked:
                 prod = jnp.where(slot < count, prod, 0.0)
             results.append((dst, prod))
@@ -69,9 +72,7 @@
     n_tiles, width, _ = side.shape
     chunk = min(CHUNK, slots)
     steps = slots // chunk
-    if with_degree:
-        side = jnp.concatenate([side, jnp.ones((n_tiles, DEG_ROWS, edge), side.dtype)], axis=1)
-    out_rows = side.shape[1]
+    out_rows = width + (DEG_ROWS if with_degree else 0)
     kernel = functools.partial(tile_kernel, transpose_tile, with_degree, GROUP)
 
     def tile_map(i, rows_ref, cols_ref, cnt_ref):
@@ -94,7 +95,7 @@
             grid=(steps,),
             in_specs=[
                 pl.BlockSpec((chunk, edge, edge), tile_map),
-                pl.BlockSpec((n_tiles, out_rows, edge), whole_map),
+                pl.BlockSpec((n_tiles, width, edge), whole_map),
             ],
             out_specs=pl.BlockSpec((n_tiles, out_rows, edge), whole_map),
         ),

time: 417 us -> 413 us (level)
  Pallas kernels: 29.2 us -> 58.5 us
  waiting for transfers between devices: 207 us -> 187 us
  blocking collectives: 103 us -> 90.3 us
    pallas_call x4, Pallas kernels: 29.2 us -> 58.5 us  [tile_pass(): pl.pallas_call(kernel, out_shape=jax.ShapeDtypeStruct((n_tiles, out_rows,...]
    reduce_scatter x2, waiting for transfers between devices: 112 us -> 91.7 us  [per_device(): left_own = lax.psum_scatter(left, 'term', scatter_dimension=0, tiled=True)]
    all_to_all x4, blocking collectives: 47.9 us -> 38.4 us  [exchange_sum(): return jnp.sum(lax.all_to_all(copies, axis_name, 0, 0, tiled=False), axis=0)]
where the time goes in v12:
time: 413 us; the launch traced here: 410 us
  waiting for transfers between devices  187 us (45%)
  blocking collectives  90.3 us (22%)
  Pallas kernels  58.5 us (14%)
  other arithmetic  34.5 us (8%)
  between operations  15.4 us (4%)
  local copies, waits for them, and re-layouts  10 us (2%)
  starting transfers between devices  9.17 us (2%)
  matrix products  4.53 us (1%)
    reduce_scatter x2, waiting for transfers between devices, per_device(): left_own = lax.psum_scatter(left, 'term', scatter_dimension=0, tiled=True)  91.7 us
    pallas_call x4, Pallas kernels, tile_pass(): pl.pallas_call(kernel, out_shape=jax.ShapeDtypeStruct((n_tiles, out_rows,...  58.5 us
    all_gather x2, waiting for transfers between devices, per_device(): q_all = lax.all_gather(quotient, 'term', axis=0, tiled=True)  55.1 us
    all_to_all x4, blocking collectives, exchange_sum(): return jnp.sum(lax.all_to_all(copies, axis_name, 0, 0, tiled=False), axis=0)  38.4 us
    all_to_all x1, blocking collectives, scatter_sum(): return jnp.sum(lax.all_to_all(pieces, axis_name, 0, 0, tiled=False), axis=0)  33.4 us
    all_to_all x1, waiting for transfers between devices, scatter_sum(): return jnp.sum(lax.all_to_all(pieces, axis_name, 0, 0, tiled=False), axis=0)  25.8 us
    all_to_all x1, blocking collectives, exchange_gather(): got = lax.all_to_all(copies, axis_name, 0, 0, tiled=False)  18.5 us
    all_to_all x1, waiting for transfers between devices, exchange_gather(): got = lax.all_to_all(copies, axis_name, 0, 0, tiled=False)  14.7 us
  transfers between devices with their start and end apart: 6, of which 6 were waited for; matrix products, arithmetic and copies ran while one was open for 0% of the time, Pallas kernels for 0%

profile of v12, /device:TPU:0, one launch (start us, length us, event | category | flops | bytes accessed | tf_op | source)
XLA Modules:
  0.0 409.8 jit_solution(4565729712241299784)
XLA Ops:
  7.2 0.9 copy.111
  8.1 1.2 broadcast_in_dim.13
  9.4 5.2 %all-to-all-start = ((bf16[8,8,64,128]{3,2,1,0:T(8,128)(2,1)}), bf16[8,8,64,128]{3,2,1,0:T(8,128)(2,1)S(1)}, u32[]{:S(2)}, u32[]{:S(2)}) async-start(bf16[8,8,64,128]{3,2,1,0:T(8,128)(2,1)} %broadcast_in_dim.13), calls=%async_computation | async-start | bytes 2097152 | tf_op jit(solution)/shard_map/all_to_all | solution.py:119
  15.2 14.7 %all-to-all-done = bf16[8,8,64,128]{3,2,1,0:T(8,128)(2,1)S(1)} async-done(((bf16[8,8,64,128]{3,2,1,0:T(8,128)(2,1)}), bf16[8,8,64,128]{3,2,1,0:T(8,128)(2,1)S(1)}, u32[]{:S(2)}, u32[]{:S(2)}) %all-to-all-start) | async-done | bytes 1048608 | tf_op jit(solution)/shard_map/all_to_all | solution.py:119
  29.9 1.0 copy-done
  30.9 17.1 %shard_map.86 = f32[64,72,128]{2,1,0:T(8,128)} custom-call(s32[512]{0:T(512)} %bitcast.170, s32[512]{0:T(512)} %bitcast.174, s32[1]{0:T(128)} %bitcast.136.cnt_ref, bf16[512,128,128]{2,1,0:T(8,128)(2,1)} %bitcast.140, bf16[64,64,128]{2,1,0:T(8,128)(2,1)} %bitcast.146), custom_call_target="tpu_custom_call" | custom-call | flops 1207959552 | bytes 20185088 | tf_op jit(solution)/shard_map/pallas_call | solution.py:90
  48.1 48.9 %reduce-scatter.3.cloned.1.call-done = f32[16,72,128]{2,1,0:T(8,128)} async-done(((f32[64,72,128]{2,1,0:T(8,128)}), f32[16,72,128]{2,1,0:T(8,128)}) %reduce-scatter.3.cloned.1.call-update) | async-done | bytes 589840 | tf_op jit(solution)/shard_map/reduce_scatter | solution.py:162
  97.0 0.8 slice.75
  97.9 1.8 fusion.9
  99.8 27.5 %all-gather.3.cloned.1.call-done.side_ref = bf16[64,64,128]{2,1,0:T(8,128)(2,1)} async-done(((bf16[16,64,128]{2,1,0:T(8,128)(2,1)}), bf16[64,64,128]{2,1,0:T(8,128)(2,1)}) %all-gather.3.cloned.1.call-update) | async-done | bytes 1048592 | tf_op jit(solution)/shard_map/all_gather | solution.py:167
  127.3 13.2 %shard_map.87 = f32[64,72,128]{2,1,0:T(8,128)} custom-call(s32[512]{0:T(512)} %bitcast.171, s32[512]{0:T(512)} %bitcast.175, s32[1]{0:T(128)} %bitcast.137.cnt_ref, bf16[512,128,128]{2,1,0:T(8,128)(2,1)} %bitcast.141, bf16[64,64,128]{2,1,0:T(8,128)(2,1)} %all-gather.3.cloned.1.call-done.side_ref), custom_call_target="tpu_custom_call" | custom-call | flops 1207959552 | bytes 20185088 | tf_op jit(solution)/shard_map/pallas_call | solution.py:90
  140.5 33.4 %all_to_all.44 = f32[8,8,72,128]{3,2,1,0:T(8,128)S(1)} all-to-all(f32[8,8,72,128]{3,2,1,0:T(8,128)} %bitcast.144), channel_id=1, replica_groups=mesh['doc'=8,'term'=4] {'doc'}, dimensions={0} | all-to-all | bytes 4718592 | tf_op jit(solution)/shard_map/all_to_all | solution.py:109
  174.1 0.6 slice_reduce_fusion
  175.6 0.6 concatenate.6
  176.3 9.1 %all_to_all.45 = f32[4,1,4225]{2,1,0:T(1,128)S(1)} all-to-all(f32[4,1,4225]{2,1,0:T(1,128)S(1)} %broadcast_in_dim.14), channel_id=1, replica_groups=mesh['doc'=8,'term'=4] {'term'}, dimensions={0} | all-to-all | bytes 135200 | tf_op jit(solution)/shard_map/all_to_all | solution.py:114
  185.5 8.0 %all_to_all.46 = f32[8,1,4225]{2,1,0:T(1,128)S(1)} all-to-all(f32[8,1,4225]{2,1,0:T(1,128)S(1)} %broadcast_in_dim.15), channel_id=1, replica_groups=mesh['doc'=8,'term'=4] {'doc'}, dimensions={0} | all-to-all | bytes 270400 | tf_op jit(solution)/shard_map/all_to_all | solution.py:114
  193.6 0.5 slice.80
  194.2 0.6 fusion.41
  195.0 0.7 divide_subtract_fusion.1
  195.8 0.7 fusion.35
  196.5 5.8 %cholesky.44 = f32[64,64]{1,0:T(8,128)S(1)} custom-call(f32[64,64]{1,0:T(8,128)S(1)} %fusion.35), custom_call_target="Cholesky" | custom-call | tf_op jit(solution)/shard_map/jit(cholesky)/cholesky | solution.py:187
  202.4 0.6 compare_reduce_fusion.1
  203.0 0.7 fusion.27
  203.7 4.9 %custom-call.11 = f32[1,64,64]{1,2,0:T(8,128)S(1)} custom-call(f32[1,64,64]{2,1,0:T(8,128)S(1)} %fusion.27), custom_call_target="InvertDiagBlocksLowerTriangular" | custom-call | tf_op jit(solution)/shard_map/jit(_solve_triangular)/triangular_solve | solution.py:190
  208.6 0.5 convolution_bitcast_fusion
  209.4 18.5 %all_to_all.47 = bf16[8,8,64,128]{3,2,1,0:T(8,128)(2,1)} all-to-all(bf16[8,8,64,128]{3,2,1,0:T(8,128)(2,1)S(1)} %broadcast_in_dim.16), channel_id=1, replica_groups=mesh['doc'=8,'term'=4] {'doc'}, dimensions={0} | all-to-all | bytes 2097152 | tf_op jit(solution)/shard_map/all_to_all | solution.py:119
  227.8 16.4 %shard_map.88 = f32[64,64,128]{2,1,0:T(8,128)} custom-call(s32[512]{0:T(512)} %bitcast.172, s32[512]{0:T(512)} %bitcast.176, s32[1]{0:T(128)} %bitcast.138.cnt_ref, bf16[512,128,128]{2,1,0:T(8,128)(2,1)} %bitcast.142, bf16[64,64,128]{2,1,0:T(8,128)(2,1)} %bitcast.147), custom_call_target="tpu_custom_call" | custom-call | flops 1073741824 | bytes 19922944 | tf_op jit(solution)/shard_map/pallas_call | solution.py:90
  244.3 42.8 %reduce-scatter.5.cloned.1.call-done = f32[16,64,128]{2,1,0:T(8,128)} async-done(((f32[64,64,128]{2,1,0:T(8,128)}), f32[16,64,128]{2,1,0:T(8,128)}) %reduce-scatter.5.cloned.1.call-update) | async-done | bytes 524304 | tf_op jit(solution)/shard_map/reduce_scatter | solution.py:162
  287.1 1.8 fusion.39
  288.9 27.5 %all-gather.5.cloned.1.call-done.side_ref = bf16[64,64,128]{2,1,0:T(8,128)(2,1)} async-done(((bf16[16,64,128]{2,1,0:T(8,128)(2,1)}), bf16[64,64,128]{2,1,0:T(8,128)(2,1)}) %all-gather.5.cloned.1.call-update) | async-done | bytes 1048592 | tf_op jit(solution)/shard_map/all_gather | solution.py:167
  316.5 11.8 %shard_map.89 = f32[64,64,128]{2,1,0:T(8,128)} custom-call(s32[512]{0:T(512)} %bitcast.173, s32[512]{0:T(512)} %bitcast.177, s32[1]{0:T(128)} %bitcast.139.cnt_ref, bf16[512,128,128]{2,1,0:T(8,128)(2,1)} %bitcast.143, bf16[64,64,128]{2,1,0:T(8,128)(2,1)} %all-gather.5.cloned.1.call-done.side_ref), custom_call_target="tpu_custom_call" | custom-call | flops 1073741824 | bytes 19922944 | tf_op jit(solution)/shard_map/pallas_call | solution.py:90
  328.3 3.8 all-to-all-start.5
  333.0 25.8 %all-to-all-done.5 = f32[8,8,64,128]{3,2,1,0:T(8,128)S(1)} async-done(((f32[8,8,64,128]{3,2,1,0:T(8,128)}), f32[8,8,64,128]{3,2,1,0:T(8,128)S(1)}, u32[]{:S(2)}, u32[]{:S(2)}) %all-to-all-start.5) | async-done | bytes 2097184 | tf_op jit(solution)/shard_map/all_to_all | solution.py:109
  360.2 0.6 concatenate.7
  360.9 10.2 %all_to_all.48 = f32[4,1,12545]{2,1,0:T(1,128)S(1)} all-to-all(f32[4,1,12545]{2,1,0:T(1,128)S(1)} %broadcast_in_dim.17), channel_id=1, replica_groups=mesh['doc'=8,'term'=4] {'term'}, dimensions={0} | all-to-all | bytes 401440 | tf_op jit(solution)/shard_map/all_to_all | solution.py:114
  371.6 11.1 %all_to_all.49 = f32[8,1,12545]{2,1,0:T(1,128)S(1)} all-to-all(f32[8,1,12545]{2,1,0:T(1,128)S(1)} %broadcast_in_dim.18), channel_id=1, replica_groups=mesh['doc'=8,'term'=4] {'doc'}, dimensions={0} | all-to-all | bytes 802880 | tf_op jit(solution)/shard_map/all_to_all | solution.py:114
  383.0 0.5 slice.81
  384.2 0.7 fusion.38
  385.3 0.7 divide_subtract_fusion
  386.1 0.7 fusion.33
  386.8 5.8 %cholesky.55 = f32[64,64]{1,0:T(8,128)S(1)} custom-call(f32[64,64]{1,0:T(8,128)S(1)} %fusion.33), custom_call_target="Cholesky" | custom-call | tf_op jit(solution)/shard_map/jit(cholesky)/cholesky | solution.py:187
  392.7 0.6 compare_reduce_fusion
  393.3 0.7 fusion.28
  394.0 4.9 %custom-call.9 = f32[1,64,64]{1,2,0:T(8,128)S(1)} custom-call(f32[1,64,64]{2,1,0:T(8,128)S(1)} %fusion.28), custom_call_target="InvertDiagBlocksLowerTriangular" | custom-call | tf_op jit(solution)/shard_map/jit(_solve_triangular)/triangular_solve | solution.py:200
  398.9 0.5 fusion.5
  400.5 0.7 broadcast_in_dim_reshape.7
  401.3 0.7 fusion.2
  402.4 0.9 broadcast_in_dim_reshape.6
  (63 shorter events, 7.1 us)
Async XLA Ops:
  9.4 20.6 %all-to-all-start = ((bf16[8,8,64,128]{3,2,1,0:T(8,128)(2,1)}), bf16[8,8,64,128]{3,2,1,0:T(8,128)(2,1)S(1)}, u32[]{:S(2)}, u32[]{:S(2)}) async-start(bf16[8,8,64,128]{3,2,1,0:T(8,128)(2,1)} %broadcast_in_dim.13), calls=%async_computation | async-start | bytes 2097152 | tf_op jit(solution)/shard_map/all_to_all | solution.py:119
  14.5 82.5 %reduce-scatter.3.cloned.1.call-start = ((), (), s32[]{:S(2)}) async-start(), calls=%async_computation.10 | async-start | bytes 2949120 | tf_op jit(solution)/shard_map/reduce_scatter | solution.py:162
  29.9 1.0 copy-start
  48.1 79.2 %all-gather.3.cloned.1.call-start = ((), (), s32[]{:S(2)}) async-start(), calls=%async_computation.11 | async-start | bytes 1310720 | tf_op jit(solution)/shard_map/all_gather | solution.py:167
  99.7 187.4 %reduce-scatter.5.cloned.1.call-start = ((), (), s32[]{:S(2)}) async-start(), calls=%async_computation.12 | async-start | bytes 2621440 | tf_op jit(solution)/shard_map/reduce_scatter | solution.py:162
  244.3 72.2 %all-gather.5.cloned.1.call-start = ((), (), s32[]{:S(2)}) async-start(), calls=%async_computation.13 | async-start | bytes 1310720 | tf_op jit(solution)/shard_map/all_gather | solution.py:167
  328.3 3.8 copy-start.3
  328.3 4.0 copy-start.2
  328.3 4.1 %copy-start.1 = (f32[16,64,128]{2,1,0:T(8,128)S(1)}, f32[16,64,128]{2,1,0:T(8,128)}, u32[]{:S(2)}) copy-start(f32[16,64,128]{2,1,0:T(8,128)} %reduce-scatter.5.cloned.1.call-done) | copy-start | bytes 1572868
  328.3 30.5 %all-to-all-start.5 = ((f32[8,8,64,128]{3,2,1,0:T(8,128)}), f32[8,8,64,128]{3,2,1,0:T(8,128)S(1)}, u32[]{:S(2)}, u32[]{:S(2)}) async-start(f32[8,8,64,128]{3,2,1,0:T(8,128)} %bitcast.145), calls=%async_computation.7 | async-start | bytes 4194304 | tf_op jit(solution)/shard_map/all_to_all | solution.py:109
Sparse Core Ops, SparseCore 0:
  48.2 48.7 reduce-scatter.2
  99.8 27.4 all-gather.2
  244.4 42.6 reduce-scatter.4
  289.2 27.2 all-gather.4

commit v13 on v12

--- a/solution.py
+++ b/solution.py
@@ -17,7 +17,7 @@
 NT_DIMS = (((1,), (1,)), ((), ()))
 
 
-def tile_kernel(transpose_tile, with_degree, group, rows_ref, cols_ref, cnt_ref, tiles_ref, side_ref, out_ref):
+def tile_kernel(transpose_tile, with_degree, group, split, rows_ref, cols_ref, cnt_ref, tiles_ref, side_ref, out_ref, *rest):
     step = pl.program_id(0)
     chunk = tiles_ref.shape[0]
     width = side_ref.shape[1]
@@ -25,6 +25,8 @@
     @pl.when(step == 0)
     def _():
         out_ref[...] = jnp.zeros_like(out_ref)
+        for extra in rest:
+            extra[...] = jnp.zeros_like(extra)
 
     count = cnt_ref[0]
     base = step * chunk
@@ -53,7 +55,14 @@
                 prod = jnp.where(slot < count, prod, 0.0)
             results.append((dst, prod))
         for dst, prod in results:
-            out_ref[dst] += prod
+            if split is None:
+                out_ref[dst] += prod
+            else:
+                head = prod[:split]
+                if with_degree:
+                    head = jnp.concatenate([head, prod[width:]], axis=0)
+                out_ref[dst] += head
+                rest[0][dst] += prod[split:width]
 
     def body(g, carry):
         run(g, False)
@@ -67,13 +76,17 @@
         run(full, True)
 
 
-def tile_pass(tiles, rows, cols, count, side, transpose_tile, with_degree):
+def tile_pass(tiles, rows, cols, count, side, transpose_tile, with_degree, split=None):
     slots, edge, _ = tiles.shape
     n_tiles, width, _ = side.shape
     chunk = min(CHUNK, slots)
     steps = slots // chunk
     out_rows = width + (DEG_ROWS if with_degree else 0)
-    kernel = functools.partial(tile_kernel, transpose_tile, with_degree, GROUP)
+    kernel = functools.partial(tile_kernel, transpose_tile, with_degree, GROUP, split)
+    if split is None:
+        shapes = [(n_tiles, out_rows, edge)]
+    else:
+        shapes = [(n_tiles, out_rows - width + split, edge), (n_tiles, width - split, edge)]
 
     def tile_map(i, rows_ref, cols_ref, cnt_ref):
         return (jnp.minimum(i, jnp.maximum(cnt_ref[0] - 1, 0) // chunk), 0, 0)
@@ -87,9 +100,9 @@
         transcendentals=0,
         bytes_accessed=tiles.size * 2 + side.size * 2 + n_tiles * out_rows * edge * 4,
     )
-    return pl.pallas_call(
+    outs = pl.pallas_call(
         kernel,
-        out_shape=jax.ShapeDtypeStruct((n_tiles, out_rows, edge), jnp.float32),
+        out_shape=[jax.ShapeDtypeStruct(shape, jnp.float32) for shape in shapes],
         grid_spec=pltpu.PrefetchScalarGridSpec(
             num_scalar_prefetch=3,
             grid=(steps,),
@@ -97,11 +110,12 @@
                 pl.BlockSpec((chunk, edge, edge), tile_map),
                 pl.BlockSpec((n_tiles, width, edge), whole_map),
             ],
-            out_specs=pl.BlockSpec((n_tiles, out_rows, edge), whole_map),
+            out_specs=[pl.BlockSpec(shape, whole_map) for shape in shapes],
         ),
         compiler_params=pltpu.CompilerParams(dimension_semantics=("arbitrary",)),
         cost_estimate=cost,
     )(rows, cols, count, tiles, side)
+    return outs[0] if split is None else outs
 
 
 def scatter_sum(x, axis_name, parts):
@@ -158,18 +172,23 @@
     for step in range(ITERS):
         first = step == 0
         w_all = exchange_gather(weights, "doc", n_doc)
-        left = tile_pass(local_tiles, rows, cols, count, w_all, True, first)
-        left_own = lax.psum_scatter(left, "term", scatter_dimension=0, tiled=True)
-        summed_own = left_own[:, :width_k, :]
+        half = width_k // 2
+        left_a, left_b = tile_pass(local_tiles, rows, cols, count, w_all, True, first, half)
+        own_a = lax.psum_scatter(left_a, "term", scatter_dimension=0, tiled=True)
         if first:
-            doc_degree = left_own[:, width_k, :]
-        quotient = (summed_own / doc_degree[:, None, :]).astype(jnp.bfloat16)
-        q_all = lax.all_gather(quotient, "term", axis=0, tiled=True)
-        right = tile_pass(local_tiles, rows, cols, count, q_all, False, first)
-        right_own = scatter_sum(right, "doc", n_doc)
+            doc_degree = own_a[:, half, :]
+        summed_a = own_a[:, :half, :]
+        qa_all = lax.all_gather((summed_a / doc_degree[:, None, :]).astype(jnp.bfloat16), "term", axis=0, tiled=True)
+        left_b, _ = lax.optimization_barrier((left_b, qa_all))
+        summed_b = lax.psum_scatter(left_b, "term", scatter_dimension=0, tiled=True)
+        qb_all = lax.all_gather((summed_b / doc_degree[:, None, :]).astype(jnp.bfloat16), "term", axis=0, tiled=True)
+        summed_own = jnp.concatenate([summed_a, summed_b], axis=1)
+        right_a = scatter_sum(tile_pass(local_tiles, rows, cols, count, qa_all, False, first), "doc", n_doc)
+        right_b = scatter_sum(tile_pass(local_tiles, rows, cols, count, qb_all, False, False), "doc", n_doc)
         if first:
-            term_degree = right_own[:, width_k, :]
+            term_degree = right_a[:, half, :]
             root = jnp.sqrt(term_degree)
+        right_own = jnp.concatenate([right_a[:, :half, :], right_b], axis=1)
         raw = right_own[:, :width_k, :] / root[:, None, :]
         previous = root[:, None, :] * start_t.astype(jnp.float32) if first else basis
         gram_part = jnp.einsum("tki,tli->kl", raw, raw, precision=HIGH)

time: 413 us -> 411 us (level)
  waiting for transfers between devices: 187 us -> 144 us
  blocking collectives: 90.3 us -> 122 us
  starting transfers between devices: 9.17 us -> 30.2 us
  Pallas kernels: 58.5 us -> 45.3 us
    all_gather x0 -> x4, blocking collectives: none -> 65.6 us  [the longest x2 32.8 us: per_device(): lax.all_gather((summed_b / doc_degree[:, None, :]).astype(jnp.bfloat16),...]
    all_gather x2 -> x0, waiting for transfers between devices: 55.1 us -> none  [per_device(): q_all = lax.all_gather(quotient, 'term', axis=0, tiled=True)]
    all_to_all x1 -> x0, blocking collectives: 33.4 us -> none  [scatter_sum(): return jnp.sum(lax.all_to_all(pieces, axis_name, 0, 0, tiled=False), axis=0)]
    all_to_all x1 -> x4, starting transfers between devices: 3.84 us -> 24.8 us  [scatter_sum(): return jnp.sum(lax.all_to_all(pieces, axis_name, 0, 0, tiled=False), axis=0)]
    pallas_call x4 -> x6, Pallas kernels: 58.5 us -> 45.3 us  [tile_pass(): pl.pallas_call(kernel, out_shape=[jax.ShapeDtypeStruct(shape, jnp.float32...]
    reduce_scatter x2 -> x4, waiting for transfers between devices: 91.7 us -> 99.9 us  [the longest x2 74.6 us: per_device(): own_a = lax.psum_scatter(left_a, 'term', scatter_dimension=0, tiled=True)]
    all_to_all x1 -> x4, waiting for transfers between devices: 25.8 us -> 29.1 us  [scatter_sum(): return jnp.sum(lax.all_to_all(pieces, axis_name, 0, 0, tiled=False), axis=0)]
  transfers between devices with their start and end apart: 6 -> 9, of which waited for: 6 -> 7; matrix products, arithmetic and copies ran while one was open for 0% -> 1% of each run, Pallas kernels for 0% -> 7%
where the time goes in v13:
time: 411 us; the launch traced here: 407 us
  waiting for transfers between devices  144 us (35%)
  blocking collectives  122 us (30%)
  Pallas kernels  45.3 us (11%)
  other arithmetic  35.1 us (9%)
  starting transfers between devices  30.2 us (7%)
  between operations  15.4 us (4%)
  local copies, waits for them, and re-layouts  10.3 us (3%)
  matrix products  4.54 us (1%)
    reduce_scatter x2, waiting for transfers between devices, per_device(): own_a = lax.psum_scatter(left_a, 'term', scatter_dimension=0, tiled=True)  74.6 us
    pallas_call x6, Pallas kernels, tile_pass(): pl.pallas_call(kernel, out_shape=[jax.ShapeDtypeStruct(shape, jnp.float32...  45.3 us
    all_to_all x4, blocking collectives, exchange_sum(): return jnp.sum(lax.all_to_all(copies, axis_name, 0, 0, tiled=False), axis=0)  37.9 us
    all_gather x2, blocking collectives, per_device(): lax.all_gather((summed_b / doc_degree[:, None, :]).astype(jnp.bfloat16),...  32.8 us
    all_gather x2, blocking collectives, per_device(): lax.all_gather((summed_a / doc_degree[:, None, :]).astype(jnp.bfloat16),...  32.8 us
    all_to_all x4, waiting for transfers between devices, scatter_sum(): return jnp.sum(lax.all_to_all(pieces, axis_name, 0, 0, tiled=False), axis=0)  29.1 us
    reduce_scatter x2, waiting for transfers between devices, per_device(): summed_b = lax.psum_scatter(left_b, 'term', scatter_dimension=0, tiled=True)  25.4 us
    all_to_all x4, starting transfers between devices, scatter_sum(): return jnp.sum(lax.all_to_all(pieces, axis_name, 0, 0, tiled=False), axis=0)  24.8 us
  transfers between devices with their start and end apart: 9, of which 7 were waited for; matrix products, arithmetic and copies ran while one was open for 1% of the time, Pallas kernels for 7%

profile of v13, /device:TPU:0, one launch (start us, length us, event | category | flops | bytes accessed | tf_op | source)
XLA Modules:
  0.0 406.7 jit_solution(2838379443379468987)
XLA Ops:
  7.2 0.9 copy.111
  8.1 1.2 broadcast_in_dim.13
  9.4 5.2 %all-to-all-start = ((bf16[8,8,64,128]{3,2,1,0:T(8,128)(2,1)}), bf16[8,8,64,128]{3,2,1,0:T(8,128)(2,1)S(1)}, u32[]{:S(2)}, u32[]{:S(2)}) async-start(bf16[8,8,64,128]{3,2,1,0:T(8,128)(2,1)} %broadcast_in_dim.13), calls=%async_computation | async-start | bytes 2097152 | tf_op jit(solution)/shard_map/all_to_all | solution.py:133
  15.2 14.7 %all-to-all-done = bf16[8,8,64,128]{3,2,1,0:T(8,128)(2,1)S(1)} async-done(((bf16[8,8,64,128]{3,2,1,0:T(8,128)(2,1)}), bf16[8,8,64,128]{3,2,1,0:T(8,128)(2,1)S(1)}, u32[]{:S(2)}, u32[]{:S(2)}) %all-to-all-start) | async-done | bytes 1048608 | tf_op jit(solution)/shard_map/all_to_all | solution.py:133
  29.9 1.0 copy-done
  30.9 9.4 %shard_map.86 = (f32[64,40,128]{2,1,0:T(8,128)}, f32[64,32,128]{2,1,0:T(8,128)}) custom-call(s32[512]{0:T(512)} %bitcast.175, s32[512]{0:T(512)} %bitcast.181, s32[1]{0:T(128)} %bitcast.133.cnt_ref, bf16[512,128,128]{2,1,0:T(8,128)(2,1)} %bitcast.139, bf16[64,64,128]{2,1,0:T(8,128)(2,1)} %bitcast.149), custom_call_target="tpu_custom_call" | custom-call | flops 1207959552 | bytes 20185088 | tf_op jit(solution)/shard_map/pallas_call | solution.py:103
  40.4 40.0 %reduce-scatter.5.cloned.1.call-done = f32[16,40,128]{2,1,0:T(8,128)} async-done(((f32[64,40,128]{2,1,0:T(8,128)}), f32[16,40,128]{2,1,0:T(8,128)}) %reduce-scatter.5.cloned.1.call-update) | async-done | bytes 327696 | tf_op jit(solution)/shard_map/reduce_scatter | solution.py:177
  80.3 0.8 slice.75
  81.2 1.0 fusion.19
  82.2 16.4 %all_gather.12.side_ref = bf16[64,32,128]{2,1,0:T(8,128)(2,1)} all-gather(bf16[16,32,128]{2,1,0:T(8,128)(2,1)S(1)} %fusion.19), channel_id=1, replica_groups=mesh['doc'=8,'term'=4] {'term'}, dimensions={0}, use_global_device_ids=true | all-gather | bytes 655360 | tf_op jit(solution)/shard_map/all_gather | solution.py:181
  98.6 7.0 %shard_map.87 = f32[64,40,128]{2,1,0:T(8,128)} custom-call(s32[512]{0:T(512)} %bitcast.176, s32[512]{0:T(512)} %bitcast.182, s32[1]{0:T(128)} %bitcast.134.cnt_ref, bf16[512,128,128]{2,1,0:T(8,128)(2,1)} %bitcast.140, bf16[64,32,128]{2,1,0:T(8,128)(2,1)} %all_gather.12.side_ref), custom_call_target="tpu_custom_call" | custom-call | flops 671088640 | bytes 18612224 | tf_op jit(solution)/shard_map/pallas_call | solution.py:103
  105.6 6.2 %all-to-all-start.1 = ((f32[8,8,40,128]{3,2,1,0:T(8,128)}), f32[8,8,40,128]{3,2,1,0:T(8,128)S(1)}, u32[]{:S(2)}, u32[]{:S(2)}) async-start(f32[8,8,40,128]{3,2,1,0:T(8,128)} %bitcast.145), calls=%async_computation.2 | async-start | bytes 2621440 | tf_op jit(solution)/shard_map/all_to_all | solution.py:123
  111.8 12.4 %reduce-scatter.7.cloned.1.call-done = f32[16,32,128]{2,1,0:T(8,128)} async-done(((f32[64,32,128]{2,1,0:T(8,128)}), f32[16,32,128]{2,1,0:T(8,128)}) %reduce-scatter.7.cloned.1.call-update) | async-done | bytes 262160 | tf_op jit(solution)/shard_map/reduce_scatter | solution.py:183
  124.2 1.0 divide_convert_fusion.2
  125.2 16.4 %all_gather.13.side_ref = bf16[64,32,128]{2,1,0:T(8,128)(2,1)} all-gather(bf16[16,32,128]{2,1,0:T(8,128)(2,1)S(1)} %divide_convert_fusion.2), channel_id=1, replica_groups=mesh['doc'=8,'term'=4] {'term'}, dimensions={0}, use_global_device_ids=true | all-gather | bytes 655360 | tf_op jit(solution)/shard_map/all_gather | solution.py:184
  141.6 6.6 %shard_map.88 = f32[64,32,128]{2,1,0:T(8,128)} custom-call(s32[512]{0:T(512)} %bitcast.177, s32[512]{0:T(512)} %bitcast.183, s32[1]{0:T(128)} %bitcast.135.cnt_ref, bf16[512,128,128]{2,1,0:T(8,128)(2,1)} %bitcast.141, bf16[64,32,128]{2,1,0:T(8,128)(2,1)} %all_gather.13.side_ref), custom_call_target="tpu_custom_call" | custom-call | flops 536870912 | bytes 18350080 | tf_op jit(solution)/shard_map/pallas_call | solution.py:103
  148.2 6.0 %all-to-all-start.2 = ((f32[8,8,32,128]{3,2,1,0:T(8,128)}), f32[8,8,32,128]{3,2,1,0:T(8,128)S(1)}, u32[]{:S(2)}, u32[]{:S(2)}) async-start(f32[8,8,32,128]{3,2,1,0:T(8,128)} %bitcast.147), calls=%async_computation.4 | async-start | bytes 2097152 | tf_op jit(solution)/shard_map/all_to_all | solution.py:123
  155.0 14.7 %all-to-all-done.2 = f32[8,8,32,128]{3,2,1,0:T(8,128)S(1)} async-done(((f32[8,8,32,128]{3,2,1,0:T(8,128)}), f32[8,8,32,128]{3,2,1,0:T(8,128)S(1)}, u32[]{:S(2)}, u32[]{:S(2)}) %all-to-all-start.2) | async-done | bytes 1048608 | tf_op jit(solution)/shard_map/all_to_all | solution.py:123
  171.5 8.9 %all_to_all.54 = f32[4,1,4225]{2,1,0:T(1,128)S(1)} all-to-all(f32[4,1,4225]{2,1,0:T(1,128)S(1)} %broadcast_in_dim.14), channel_id=1, replica_groups=mesh['doc'=8,'term'=4] {'term'}, dimensions={0} | all-to-all | bytes 135200 | tf_op jit(solution)/shard_map/all_to_all | solution.py:128
  180.5 8.0 %all_to_all.55 = f32[8,1,4225]{2,1,0:T(1,128)S(1)} all-to-all(f32[8,1,4225]{2,1,0:T(1,128)S(1)} %broadcast_in_dim.15), channel_id=1, replica_groups=mesh['doc'=8,'term'=4] {'doc'}, dimensions={0} | all-to-all | bytes 270400 | tf_op jit(solution)/shard_map/all_to_all | solution.py:128
  190.1 0.8 divide_subtract_fusion.1
  190.9 0.8 fusion.35
  191.7 5.8 %cholesky.44 = f32[64,64]{1,0:T(8,128)S(1)} custom-call(f32[64,64]{1,0:T(8,128)S(1)} %fusion.35), custom_call_target="Cholesky" | custom-call | tf_op jit(solution)/shard_map/jit(cholesky)/cholesky | solution.py:206
  197.6 0.7 compare_reduce_fusion.1
  199.0 4.9 %custom-call.11 = f32[1,64,64]{1,2,0:T(8,128)S(1)} custom-call(f32[1,64,64]{2,1,0:T(8,128)S(1)} %fusion.27), custom_call_target="InvertDiagBlocksLowerTriangular" | custom-call | tf_op jit(solution)/shard_map/jit(_solve_triangular)/triangular_solve | solution.py:209
  204.7 18.5 %all_to_all.56 = bf16[8,8,64,128]{3,2,1,0:T(8,128)(2,1)} all-to-all(bf16[8,8,64,128]{3,2,1,0:T(8,128)(2,1)S(1)} %broadcast_in_dim.16), channel_id=1, replica_groups=mesh['doc'=8,'term'=4] {'doc'}, dimensions={0} | all-to-all | bytes 2097152 | tf_op jit(solution)/shard_map/all_to_all | solution.py:133
  223.2 9.1 %shard_map.89 = (f32[64,32,128]{2,1,0:T(8,128)}, f32[64,32,128]{2,1,0:T(8,128)}) custom-call(s32[512]{0:T(512)} %bitcast.178, s32[512]{0:T(512)} %bitcast.184, s32[1]{0:T(128)} %bitcast.136.cnt_ref, bf16[512,128,128]{2,1,0:T(8,128)(2,1)} %bitcast.142, bf16[64,64,128]{2,1,0:T(8,128)(2,1)} %bitcast.150), custom_call_target="tpu_custom_call" | custom-call | flops 1073741824 | bytes 19922944 | tf_op jit(solution)/shard_map/pallas_call | solution.py:103
  232.3 34.6 %reduce-scatter.9.cloned.1.call-done = f32[16,32,128]{2,1,0:T(8,128)} async-done(((f32[64,32,128]{2,1,0:T(8,128)}), f32[16,32,128]{2,1,0:T(8,128)}) %reduce-scatter.9.cloned.1.call-update) | async-done | bytes 262160 | tf_op jit(solution)/shard_map/reduce_scatter | solution.py:177
  266.9 1.0 divide_convert_fusion.1
  267.8 16.4 %all_gather.14.side_ref = bf16[64,32,128]{2,1,0:T(8,128)(2,1)} all-gather(bf16[16,32,128]{2,1,0:T(8,128)(2,1)S(1)} %divide_convert_fusion.1), channel_id=1, replica_groups=mesh['doc'=8,'term'=4] {'term'}, dimensions={0}, use_global_device_ids=true | all-gather | bytes 655360 | tf_op jit(solution)/shard_map/all_gather | solution.py:181
  284.3 6.7 %shard_map.90 = f32[64,32,128]{2,1,0:T(8,128)} custom-call(s32[512]{0:T(512)} %bitcast.179, s32[512]{0:T(512)} %bitcast.185, s32[1]{0:T(128)} %bitcast.137.cnt_ref, bf16[512,128,128]{2,1,0:T(8,128)(2,1)} %bitcast.143, bf16[64,32,128]{2,1,0:T(8,128)(2,1)} %all_gather.14.side_ref), custom_call_target="tpu_custom_call" | custom-call | flops 536870912 | bytes 18350080 | tf_op jit(solution)/shard_map/pallas_call | solution.py:103
  290.9 6.4 %all-to-all-start.6 = ((f32[8,8,32,128]{3,2,1,0:T(8,128)}), f32[8,8,32,128]{3,2,1,0:T(8,128)S(1)}, u32[]{:S(2)}, u32[]{:S(2)}) async-start(f32[8,8,32,128]{3,2,1,0:T(8,128)} %bitcast.148), calls=%async_computation.10 | async-start | bytes 2097152 | tf_op jit(solution)/shard_map/all_to_all | solution.py:123
  297.3 13.0 %reduce-scatter.11.cloned.1.call-done = f32[16,32,128]{2,1,0:T(8,128)} async-done(((f32[64,32,128]{2,1,0:T(8,128)}), f32[16,32,128]{2,1,0:T(8,128)}) %reduce-scatter.11.cloned.1.call-update) | async-done | bytes 262160 | tf_op jit(solution)/shard_map/reduce_scatter | solution.py:183
  310.2 1.0 divide_convert_fusion
  311.2 16.4 %all_gather.15.side_ref = bf16[64,32,128]{2,1,0:T(8,128)(2,1)} all-gather(bf16[16,32,128]{2,1,0:T(8,128)(2,1)S(1)} %divide_convert_fusion), channel_id=1, replica_groups=mesh['doc'=8,'term'=4] {'term'}, dimensions={0}, use_global_device_ids=true | all-gather | bytes 655360 | tf_op jit(solution)/shard_map/all_gather | solution.py:184
  327.6 6.6 %shard_map.91 = f32[64,32,128]{2,1,0:T(8,128)} custom-call(s32[512]{0:T(512)} %bitcast.180, s32[512]{0:T(512)} %bitcast.186, s32[1]{0:T(128)} %bitcast.138.cnt_ref, bf16[512,128,128]{2,1,0:T(8,128)(2,1)} %bitcast.144, bf16[64,32,128]{2,1,0:T(8,128)(2,1)} %all_gather.15.side_ref), custom_call_target="tpu_custom_call" | custom-call | flops 536870912 | bytes 18350080 | tf_op jit(solution)/shard_map/pallas_call | solution.py:103
  334.3 6.2 %all-to-all-start.7 = ((f32[8,8,32,128]{3,2,1,0:T(8,128)}), f32[8,8,32,128]{3,2,1,0:T(8,128)S(1)}, u32[]{:S(2)}, u32[]{:S(2)}) async-start(f32[8,8,32,128]{3,2,1,0:T(8,128)} %bitcast.146), calls=%async_computation.11 | async-start | bytes 2097152 | tf_op jit(solution)/shard_map/all_to_all | solution.py:123
  341.4 14.5 %all-to-all-done.7 = f32[8,8,32,128]{3,2,1,0:T(8,128)S(1)} async-done(((f32[8,8,32,128]{3,2,1,0:T(8,128)}), f32[8,8,32,128]{3,2,1,0:T(8,128)S(1)}, u32[]{:S(2)}, u32[]{:S(2)}) %all-to-all-start.7) | async-done | bytes 1048608 | tf_op jit(solution)/shard_map/all_to_all | solution.py:123
  357.3 0.7 concatenate.19
  358.1 9.9 %all_to_all.57 = f32[4,1,12545]{2,1,0:T(1,128)S(1)} all-to-all(f32[4,1,12545]{2,1,0:T(1,128)S(1)} %broadcast_in_dim.17), channel_id=1, replica_groups=mesh['doc'=8,'term'=4] {'term'}, dimensions={0} | all-to-all | bytes 401440 | tf_op jit(solution)/shard_map/all_to_all | solution.py:128
  368.4 11.1 %all_to_all.58 = f32[8,1,12545]{2,1,0:T(1,128)S(1)} all-to-all(f32[8,1,12545]{2,1,0:T(1,128)S(1)} %broadcast_in_dim.18), channel_id=1, replica_groups=mesh['doc'=8,'term'=4] {'doc'}, dimensions={0} | all-to-all | bytes 802880 | tf_op jit(solution)/shard_map/all_to_all | solution.py:128
  382.1 0.7 divide_subtract_fusion
  382.9 0.7 fusion.33
  383.7 5.8 %cholesky.55 = f32[64,64]{1,0:T(8,128)S(1)} custom-call(f32[64,64]{1,0:T(8,128)S(1)} %fusion.33), custom_call_target="Cholesky" | custom-call | tf_op jit(solution)/shard_map/jit(cholesky)/cholesky | solution.py:206
  390.9 4.9 %custom-call.9 = f32[1,64,64]{1,2,0:T(8,128)S(1)} custom-call(f32[1,64,64]{2,1,0:T(8,128)S(1)} %fusion.28), custom_call_target="InvertDiagBlocksLowerTriangular" | custom-call | tf_op jit(solution)/shard_map/jit(_solve_triangular)/triangular_solve | solution.py:219
  397.3 0.7 broadcast_in_dim_reshape.7
  398.2 0.7 fusion.2
  399.3 0.9 broadcast_in_dim_reshape.6
  (81 shorter events, 14.0 us)
Async XLA Ops:
  9.4 20.6 %all-to-all-start = ((bf16[8,8,64,128]{3,2,1,0:T(8,128)(2,1)}), bf16[8,8,64,128]{3,2,1,0:T(8,128)(2,1)S(1)}, u32[]{:S(2)}, u32[]{:S(2)}) async-start(bf16[8,8,64,128]{3,2,1,0:T(8,128)(2,1)} %broadcast_in_dim.13), calls=%async_computation | async-start | bytes 2097152 | tf_op jit(solution)/shard_map/all_to_all | solution.py:133
  14.5 65.8 %reduce-scatter.5.cloned.1.call-start = ((), (), s32[]{:S(2)}) async-start(), calls=%async_computation.14 | async-start | bytes 1638400 | tf_op jit(solution)/shard_map/reduce_scatter | solution.py:177
  29.9 1.0 copy-start
  40.3 83.9 %reduce-scatter.7.cloned.1.call-start = ((), (), s32[]{:S(2)}) async-start(), calls=%async_computation.15 | async-start | bytes 1310720 | tf_op jit(solution)/shard_map/reduce_scatter | solution.py:183
  105.6 42.7 %all-to-all-start.1 = ((f32[8,8,40,128]{3,2,1,0:T(8,128)}), f32[8,8,40,128]{3,2,1,0:T(8,128)S(1)}, u32[]{:S(2)}, u32[]{:S(2)}) async-start(f32[8,8,40,128]{3,2,1,0:T(8,128)} %bitcast.145), calls=%async_computation.2 | async-start | bytes 2621440 | tf_op jit(solution)/shard_map/all_to_all | solution.py:123
  148.2 21.5 %all-to-all-start.2 = ((f32[8,8,32,128]{3,2,1,0:T(8,128)}), f32[8,8,32,128]{3,2,1,0:T(8,128)S(1)}, u32[]{:S(2)}, u32[]{:S(2)}) async-start(f32[8,8,32,128]{3,2,1,0:T(8,128)} %bitcast.147), calls=%async_computation.4 | async-start | bytes 2097152 | tf_op jit(solution)/shard_map/all_to_all | solution.py:123
  154.3 112.6 %reduce-scatter.9.cloned.1.call-start = ((), (), s32[]{:S(2)}) async-start(), calls=%async_computation.16 | async-start | bytes 1310720 | tf_op jit(solution)/shard_map/reduce_scatter | solution.py:177
  232.2 78.0 %reduce-scatter.11.cloned.1.call-start = ((), (), s32[]{:S(2)}) async-start(), calls=%async_computation.17 | async-start | bytes 1310720 | tf_op jit(solution)/shard_map/reduce_scatter | solution.py:183
  290.9 43.3 %all-to-all-start.6 = ((f32[8,8,32,128]{3,2,1,0:T(8,128)}), f32[8,8,32,128]{3,2,1,0:T(8,128)S(1)}, u32[]{:S(2)}, u32[]{:S(2)}) async-start(f32[8,8,32,128]{3,2,1,0:T(8,128)} %bitcast.148), calls=%async_computation.10 | async-start | bytes 2097152 | tf_op jit(solution)/shard_map/all_to_all | solution.py:123
  334.2 6.2 %copy-start.4 = (s32[1,1024]{1,0:T(1,128)S(1)}, s32[1,1024]{1,0:T(1,128)}, u32[]{:S(2)}) copy-start(s32[1,1024]{1,0:T(1,128)} %param.16) | copy-start | bytes 12292
  334.2 6.4 %copy-start.3 = (s32[1,2048]{1,0:T(1,128)S(1)}, s32[1,2048]{1,0:T(1,128)}, u32[]{:S(2)}) copy-start(s32[1,2048]{1,0:T(1,128)} %param.15) | copy-start | bytes 24580
  334.2 6.6 %copy-start.1 = (f32[16,32,128]{2,1,0:T(8,128)S(1)}, f32[16,32,128]{2,1,0:T(8,128)}, u32[]{:S(2)}) copy-start(f32[16,32,128]{2,1,0:T(8,128)} %reduce-scatter.9.cloned.1.call-done) | copy-start | bytes 786436
  334.3 6.6 %copy-start.2 = (f32[16,32,128]{2,1,0:T(8,128)S(1)}, f32[16,32,128]{2,1,0:T(8,128)}, u32[]{:S(2)}) copy-start(f32[16,32,128]{2,1,0:T(8,128)} %reduce-scatter.11.cloned.1.call-done) | copy-start | bytes 786436
  334.3 21.6 %all-to-all-start.7 = ((f32[8,8,32,128]{3,2,1,0:T(8,128)}), f32[8,8,32,128]{3,2,1,0:T(8,128)S(1)}, u32[]{:S(2)}, u32[]{:S(2)}) async-start(f32[8,8,32,128]{3,2,1,0:T(8,128)} %bitcast.146), calls=%async_computation.11 | async-start | bytes 2097152 | tf_op jit(solution)/shard_map/all_to_all | solution.py:123
Sparse Core Ops, SparseCore 0:
  40.4 39.8 reduce-scatter.4
  98.7 25.4 reduce-scatter.6
  232.4 34.4 reduce-scatter.8
  284.4 25.8 reduce-scatter.10

commit v14 on v13

--- a/solution.py
+++ b/solution.py
@@ -179,7 +179,6 @@
             doc_degree = own_a[:, half, :]
         summed_a = own_a[:, :half, :]
         qa_all = lax.all_gather((summed_a / doc_degree[:, None, :]).astype(jnp.bfloat16), "term", axis=0, tiled=True)
-        left_b, _ = lax.optimization_barrier((left_b, qa_all))
         summed_b = lax.psum_scatter(left_b, "term", scatter_dimension=0, tiled=True)
         qb_all = lax.all_gather((summed_b / doc_degree[:, None, :]).astype(jnp.bfloat16), "term", axis=0, tiled=True)
         summed_own = jnp.concatenate([summed_a, summed_b], axis=1)

time: 411 us -> 445 us (1.083); the launches traced: 407 us -> 448 us
  waiting for transfers between devices: 144 us -> 182 us
  starting transfers between devices: 30.2 us -> 43.7 us
  Pallas kernels: 45.3 us -> 37.2 us
    reduce_scatter x2, waiting for transfers between devices: 25.4 us -> 63.1 us  [per_device(): summed_b = lax.psum_scatter(left_b, 'term', scatter_dimension=0, tiled=True)]
    all_to_all x4, starting transfers between devices: 24.8 us -> 38.4 us  [scatter_sum(): return jnp.sum(lax.all_to_all(pieces, axis_name, 0, 0, tiled=False), axis=0)]
    pallas_call x6, Pallas kernels: 45.3 us -> 37.2 us  [tile_pass(): pl.pallas_call(kernel, out_shape=[jax.ShapeDtypeStruct(shape, jnp.float32...]
  transfers between devices with their start and end apart: 9 -> 9, of which waited for: 7 -> 7; matrix products, arithmetic and copies ran while one was open for 1% -> 0% of each run, Pallas kernels for 7% -> 3%
where the time goes in v14:
time: 445 us; the launch traced here: 448 us
  waiting for transfers between devices  182 us (41%)
  blocking collectives  122 us (27%)
  starting transfers between devices  43.7 us (10%)
  Pallas kernels  37.2 us (8%)
  other arithmetic  33.4 us (8%)
  between operations  15.4 us (3%)
  local copies, waits for them, and re-layouts  10.3 us (2%)
  matrix products  4.54 us (1%)
    reduce_scatter x2, waiting for transfers between devices, per_device(): own_a = lax.psum_scatter(left_a, 'term', scatter_dimension=0, tiled=True)  70.2 us
    reduce_scatter x2, waiting for transfers between devices, per_device(): summed_b = lax.psum_scatter(left_b, 'term', scatter_dimension=0, tiled=True)  63.1 us
    all_to_all x4, starting transfers between devices, scatter_sum(): return jnp.sum(lax.all_to_all(pieces, axis_name, 0, 0, tiled=False), axis=0)  38.4 us
    pallas_call x6, Pallas kernels, tile_pass(): pl.pallas_call(kernel, out_shape=[jax.ShapeDtypeStruct(shape, jnp.float32...  37.2 us
    all_to_all x4, blocking collectives, exchange_sum(): return jnp.sum(lax.all_to_all(copies, axis_name, 0, 0, tiled=False), axis=0)  36.9 us
    all_gather x2, blocking collectives, per_device(): lax.all_gather((summed_b / doc_degree[:, None, :]).astype(jnp.bfloat16),...  33.3 us
    all_gather x2, blocking collectives, per_device(): lax.all_gather((summed_a / doc_degree[:, None, :]).astype(jnp.bfloat16),...  33.3 us
    all_to_all x4, waiting for transfers between devices, scatter_sum(): return jnp.sum(lax.all_to_all(pieces, axis_name, 0, 0, tiled=False), axis=0)  32.6 us
  transfers between devices with their start and end apart: 9, of which 7 were waited for; matrix products, arithmetic and copies ran while one was open for 0% of the time, Pallas kernels for 3%

profile of v14, /device:TPU:0, one launch (start us, length us, event | category | flops | bytes accessed | tf_op | source)
XLA Modules:
  0.0 448.3 jit_solution(14097564998447916681)
XLA Ops:
  7.2 0.9 copy.111
  8.1 1.2 broadcast_in_dim.13
  9.4 5.2 %all-to-all-start = ((bf16[8,8,64,128]{3,2,1,0:T(8,128)(2,1)}), bf16[8,8,64,128]{3,2,1,0:T(8,128)(2,1)S(1)}, u32[]{:S(2)}, u32[]{:S(2)}) async-start(bf16[8,8,64,128]{3,2,1,0:T(8,128)(2,1)} %broadcast_in_dim.13), calls=%async_computation | async-start | bytes 2097152 | tf_op jit(solution)/shard_map/all_to_all | solution.py:133
  15.2 14.7 %all-to-all-done = bf16[8,8,64,128]{3,2,1,0:T(8,128)(2,1)S(1)} async-done(((bf16[8,8,64,128]{3,2,1,0:T(8,128)(2,1)}), bf16[8,8,64,128]{3,2,1,0:T(8,128)(2,1)S(1)}, u32[]{:S(2)}, u32[]{:S(2)}) %all-to-all-start) | async-done | bytes 1048608 | tf_op jit(solution)/shard_map/all_to_all | solution.py:133
  29.9 1.0 copy-done
  30.9 7.4 %shard_map.86 = (f32[64,40,128]{2,1,0:T(8,128)}, f32[64,32,128]{2,1,0:T(8,128)}) custom-call(s32[512]{0:T(512)} %bitcast.173, s32[512]{0:T(512)} %bitcast.179, s32[1]{0:T(128)} %bitcast.133.cnt_ref, bf16[512,128,128]{2,1,0:T(8,128)(2,1)} %bitcast.139, bf16[64,64,128]{2,1,0:T(8,128)(2,1)} %bitcast.147), custom_call_target="tpu_custom_call" | custom-call | flops 1207959552 | bytes 20185088 | tf_op jit(solution)/shard_map/pallas_call | solution.py:103
  39.1 42.2 %reduce-scatter.5.cloned.1.call-done = f32[16,40,128]{2,1,0:T(8,128)} async-done(((f32[64,40,128]{2,1,0:T(8,128)}), f32[16,40,128]{2,1,0:T(8,128)}) %reduce-scatter.5.cloned.1.call-update) | async-done | bytes 327696 | tf_op jit(solution)/shard_map/reduce_scatter | solution.py:177
  81.3 0.8 slice.75
  82.1 27.4 %reduce-scatter.7.cloned.1.call-done = f32[16,32,128]{2,1,0:T(8,128)} async-done(((f32[64,32,128]{2,1,0:T(8,128)}), f32[16,32,128]{2,1,0:T(8,128)}) %reduce-scatter.7.cloned.1.call-update) | async-done | bytes 262160 | tf_op jit(solution)/shard_map/reduce_scatter | solution.py:182
  109.6 1.1 fusion.19
  110.6 16.4 %all_gather.13.side_ref = bf16[64,32,128]{2,1,0:T(8,128)(2,1)} all-gather(bf16[16,32,128]{2,1,0:T(8,128)(2,1)S(1)} %get-tuple-element.27), channel_id=1, replica_groups=mesh['doc'=8,'term'=4] {'term'}, dimensions={0}, use_global_device_ids=true | all-gather | bytes 655360 | tf_op jit(solution)/shard_map/all_gather | solution.py:183
  127.1 5.6 %shard_map.88 = f32[64,32,128]{2,1,0:T(8,128)} custom-call(s32[512]{0:T(512)} %bitcast.174, s32[512]{0:T(512)} %bitcast.180, s32[1]{0:T(128)} %bitcast.135.cnt_ref, bf16[512,128,128]{2,1,0:T(8,128)(2,1)} %bitcast.140, bf16[64,32,128]{2,1,0:T(8,128)(2,1)} %all_gather.13.side_ref), custom_call_target="tpu_custom_call" | custom-call | flops 536870912 | bytes 18350080 | tf_op jit(solution)/shard_map/pallas_call | solution.py:103
  132.6 9.1 %all-to-all-start.2 = ((f32[8,8,32,128]{3,2,1,0:T(8,128)}), f32[8,8,32,128]{3,2,1,0:T(8,128)S(1)}, u32[]{:S(2)}, u32[]{:S(2)}) async-start(f32[8,8,32,128]{3,2,1,0:T(8,128)} %bitcast.149), calls=%async_computation.4 | async-start | bytes 2097152 | tf_op jit(solution)/shard_map/all_to_all | solution.py:123
  141.8 16.8 %all_gather.12.side_ref = bf16[64,32,128]{2,1,0:T(8,128)(2,1)} all-gather(bf16[16,32,128]{2,1,0:T(8,128)(2,1)S(1)} %get-tuple-element.26), channel_id=1, replica_groups=mesh['doc'=8,'term'=4] {'term'}, dimensions={0}, use_global_device_ids=true | all-gather | bytes 655360 | tf_op jit(solution)/shard_map/all_gather | solution.py:181
  158.6 5.8 %shard_map.87 = f32[64,40,128]{2,1,0:T(8,128)} custom-call(s32[512]{0:T(512)} %bitcast.175, s32[512]{0:T(512)} %bitcast.181, s32[1]{0:T(128)} %bitcast.134.cnt_ref, bf16[512,128,128]{2,1,0:T(8,128)(2,1)} %bitcast.141, bf16[64,32,128]{2,1,0:T(8,128)(2,1)} %all_gather.12.side_ref), custom_call_target="tpu_custom_call" | custom-call | flops 671088640 | bytes 18612224 | tf_op jit(solution)/shard_map/pallas_call | solution.py:103
  164.4 10.3 %all-to-all-start.1 = ((f32[8,8,40,128]{3,2,1,0:T(8,128)}), f32[8,8,40,128]{3,2,1,0:T(8,128)S(1)}, u32[]{:S(2)}, u32[]{:S(2)}) async-start(f32[8,8,40,128]{3,2,1,0:T(8,128)} %bitcast.145), calls=%async_computation.2 | async-start | bytes 2621440 | tf_op jit(solution)/shard_map/all_to_all | solution.py:123
  174.8 18.1 %all-to-all-done.1 = f32[8,8,40,128]{3,2,1,0:T(8,128)S(1)} async-done(((f32[8,8,40,128]{3,2,1,0:T(8,128)}), f32[8,8,40,128]{3,2,1,0:T(8,128)S(1)}, u32[]{:S(2)}, u32[]{:S(2)}) %all-to-all-start.1) | async-done | bytes 1310752 | tf_op jit(solution)/shard_map/all_to_all | solution.py:123
  194.5 0.7 concatenate.16
  195.3 8.4 %all_to_all.54 = f32[4,1,4225]{2,1,0:T(1,128)S(1)} all-to-all(f32[4,1,4225]{2,1,0:T(1,128)S(1)} %broadcast_in_dim.14), channel_id=1, replica_groups=mesh['doc'=8,'term'=4] {'term'}, dimensions={0} | all-to-all | bytes 135200 | tf_op jit(solution)/shard_map/all_to_all | solution.py:128
  203.9 8.0 %all_to_all.55 = f32[8,1,4225]{2,1,0:T(1,128)S(1)} all-to-all(f32[8,1,4225]{2,1,0:T(1,128)S(1)} %broadcast_in_dim.15), channel_id=1, replica_groups=mesh['doc'=8,'term'=4] {'doc'}, dimensions={0} | all-to-all | bytes 270400 | tf_op jit(solution)/shard_map/all_to_all | solution.py:128
  213.4 0.8 divide_subtract_fusion.1
  214.3 0.8 fusion.35
  215.1 5.8 %cholesky.44 = f32[64,64]{1,0:T(8,128)S(1)} custom-call(f32[64,64]{1,0:T(8,128)S(1)} %fusion.35), custom_call_target="Cholesky" | custom-call | tf_op jit(solution)/shard_map/jit(cholesky)/cholesky | solution.py:205
  220.9 0.7 compare_reduce_fusion.1
  222.4 4.9 %custom-call.11 = f32[1,64,64]{1,2,0:T(8,128)S(1)} custom-call(f32[1,64,64]{2,1,0:T(8,128)S(1)} %fusion.27), custom_call_target="InvertDiagBlocksLowerTriangular" | custom-call | tf_op jit(solution)/shard_map/jit(_solve_triangular)/triangular_solve | solution.py:208
  228.0 18.5 %all_to_all.56 = bf16[8,8,64,128]{3,2,1,0:T(8,128)(2,1)} all-to-all(bf16[8,8,64,128]{3,2,1,0:T(8,128)(2,1)S(1)} %broadcast_in_dim.16), channel_id=1, replica_groups=mesh['doc'=8,'term'=4] {'doc'}, dimensions={0} | all-to-all | bytes 2097152 | tf_op jit(solution)/shard_map/all_to_all | solution.py:133
  246.5 7.2 %shard_map.89 = (f32[64,32,128]{2,1,0:T(8,128)}, f32[64,32,128]{2,1,0:T(8,128)}) custom-call(s32[512]{0:T(512)} %bitcast.176, s32[512]{0:T(512)} %bitcast.182, s32[1]{0:T(128)} %bitcast.136.cnt_ref, bf16[512,128,128]{2,1,0:T(8,128)(2,1)} %bitcast.142, bf16[64,64,128]{2,1,0:T(8,128)(2,1)} %bitcast.150), custom_call_target="tpu_custom_call" | custom-call | flops 1073741824 | bytes 19922944 | tf_op jit(solution)/shard_map/pallas_call | solution.py:103
  254.3 35.7 %reduce-scatter.11.cloned.1.call-done = f32[16,32,128]{2,1,0:T(8,128)} async-done(((f32[64,32,128]{2,1,0:T(8,128)}), f32[16,32,128]{2,1,0:T(8,128)}) %reduce-scatter.11.cloned.1.call-update) | async-done | bytes 262160 | tf_op jit(solution)/shard_map/reduce_scatter | solution.py:182
  290.0 28.0 %reduce-scatter.9.cloned.1.call-done = f32[16,32,128]{2,1,0:T(8,128)} async-done(((f32[64,32,128]{2,1,0:T(8,128)}), f32[16,32,128]{2,1,0:T(8,128)}) %reduce-scatter.9.cloned.1.call-update) | async-done | bytes 262160 | tf_op jit(solution)/shard_map/reduce_scatter | solution.py:177
  318.0 1.1 divide_convert_fusion.1
  319.1 16.4 %all_gather.14.side_ref = bf16[64,32,128]{2,1,0:T(8,128)(2,1)} all-gather(bf16[16,32,128]{2,1,0:T(8,128)(2,1)S(1)} %get-tuple-element.24), channel_id=1, replica_groups=mesh['doc'=8,'term'=4] {'term'}, dimensions={0}, use_global_device_ids=true | all-gather | bytes 655360 | tf_op jit(solution)/shard_map/all_gather | solution.py:181
  335.5 5.6 %shard_map.90 = f32[64,32,128]{2,1,0:T(8,128)} custom-call(s32[512]{0:T(512)} %bitcast.177, s32[512]{0:T(512)} %bitcast.183, s32[1]{0:T(128)} %bitcast.137.cnt_ref, bf16[512,128,128]{2,1,0:T(8,128)(2,1)} %bitcast.143, bf16[64,32,128]{2,1,0:T(8,128)(2,1)} %all_gather.14.side_ref), custom_call_target="tpu_custom_call" | custom-call | flops 536870912 | bytes 18350080 | tf_op jit(solution)/shard_map/pallas_call | solution.py:103
  341.1 9.1 %all-to-all-start.6 = ((f32[8,8,32,128]{3,2,1,0:T(8,128)}), f32[8,8,32,128]{3,2,1,0:T(8,128)S(1)}, u32[]{:S(2)}, u32[]{:S(2)}) async-start(f32[8,8,32,128]{3,2,1,0:T(8,128)} %bitcast.148), calls=%async_computation.10 | async-start | bytes 2097152 | tf_op jit(solution)/shard_map/all_to_all | solution.py:123
  350.2 16.8 %all_gather.15.side_ref = bf16[64,32,128]{2,1,0:T(8,128)(2,1)} all-gather(bf16[16,32,128]{2,1,0:T(8,128)(2,1)S(1)} %get-tuple-element.25), channel_id=1, replica_groups=mesh['doc'=8,'term'=4] {'term'}, dimensions={0}, use_global_device_ids=true | all-gather | bytes 655360 | tf_op jit(solution)/shard_map/all_gather | solution.py:183
  367.1 5.6 %shard_map.91 = f32[64,32,128]{2,1,0:T(8,128)} custom-call(s32[512]{0:T(512)} %bitcast.178, s32[512]{0:T(512)} %bitcast.184, s32[1]{0:T(128)} %bitcast.138.cnt_ref, bf16[512,128,128]{2,1,0:T(8,128)(2,1)} %bitcast.144, bf16[64,32,128]{2,1,0:T(8,128)(2,1)} %all_gather.15.side_ref), custom_call_target="tpu_custom_call" | custom-call | flops 536870912 | bytes 18350080 | tf_op jit(solution)/shard_map/pallas_call | solution.py:103
  372.7 9.9 %all-to-all-start.7 = ((f32[8,8,32,128]{3,2,1,0:T(8,128)}), f32[8,8,32,128]{3,2,1,0:T(8,128)S(1)}, u32[]{:S(2)}, u32[]{:S(2)}) async-start(f32[8,8,32,128]{3,2,1,0:T(8,128)} %bitcast.146), calls=%async_computation.11 | async-start | bytes 2097152 | tf_op jit(solution)/shard_map/all_to_all | solution.py:123
  383.5 14.5 %all-to-all-done.7 = f32[8,8,32,128]{3,2,1,0:T(8,128)S(1)} async-done(((f32[8,8,32,128]{3,2,1,0:T(8,128)}), f32[8,8,32,128]{3,2,1,0:T(8,128)S(1)}, u32[]{:S(2)}, u32[]{:S(2)}) %all-to-all-start.7) | async-done | bytes 1048608 | tf_op jit(solution)/shard_map/all_to_all | solution.py:123
  399.3 0.7 concatenate.19
  400.2 9.3 %all_to_all.57 = f32[4,1,12545]{2,1,0:T(1,128)S(1)} all-to-all(f32[4,1,12545]{2,1,0:T(1,128)S(1)} %broadcast_in_dim.17), channel_id=1, replica_groups=mesh['doc'=8,'term'=4] {'term'}, dimensions={0} | all-to-all | bytes 401440 | tf_op jit(solution)/shard_map/all_to_all | solution.py:128
  409.9 11.3 %all_to_all.58 = f32[8,1,12545]{2,1,0:T(1,128)S(1)} all-to-all(f32[8,1,12545]{2,1,0:T(1,128)S(1)} %broadcast_in_dim.18), channel_id=1, replica_groups=mesh['doc'=8,'term'=4] {'doc'}, dimensions={0} | all-to-all | bytes 802880 | tf_op jit(solution)/shard_map/all_to_all | solution.py:128
  422.7 0.7 fusion.38
  423.8 0.7 divide_subtract_fusion
  424.6 0.7 fusion.33
  425.3 5.8 %cholesky.55 = f32[64,64]{1,0:T(8,128)S(1)} custom-call(f32[64,64]{1,0:T(8,128)S(1)} %fusion.33), custom_call_target="Cholesky" | custom-call | tf_op jit(solution)/shard_map/jit(cholesky)/cholesky | solution.py:205
  432.5 4.9 %custom-call.9 = f32[1,64,64]{1,2,0:T(8,128)S(1)} custom-call(f32[1,64,64]{2,1,0:T(8,128)S(1)} %fusion.28), custom_call_target="InvertDiagBlocksLowerTriangular" | custom-call | tf_op jit(solution)/shard_map/jit(_solve_triangular)/triangular_solve | solution.py:218
  438.9 0.7 broadcast_in_dim_reshape.7
  439.8 0.7 fusion.2
  440.9 0.9 broadcast_in_dim_reshape.6
  (79 shorter events, 13.7 us)
Async XLA Ops:
  9.4 20.6 %all-to-all-start = ((bf16[8,8,64,128]{3,2,1,0:T(8,128)(2,1)}), bf16[8,8,64,128]{3,2,1,0:T(8,128)(2,1)S(1)}, u32[]{:S(2)}, u32[]{:S(2)}) async-start(bf16[8,8,64,128]{3,2,1,0:T(8,128)(2,1)} %broadcast_in_dim.13), calls=%async_computation | async-start | bytes 2097152 | tf_op jit(solution)/shard_map/all_to_all | solution.py:133
  14.5 66.8 %reduce-scatter.5.cloned.1.call-start = ((), (), s32[]{:S(2)}) async-start(), calls=%async_computation.14 | async-start | bytes 1638400 | tf_op jit(solution)/shard_map/reduce_scatter | solution.py:177
  29.9 1.0 copy-start
  38.4 71.2 %reduce-scatter.7.cloned.1.call-start = ((), (), s32[]{:S(2)}) async-start(), calls=%async_computation.15 | async-start | bytes 1310720 | tf_op jit(solution)/shard_map/reduce_scatter | solution.py:182
  132.6 31.8 %all-to-all-start.2 = ((f32[8,8,32,128]{3,2,1,0:T(8,128)}), f32[8,8,32,128]{3,2,1,0:T(8,128)S(1)}, u32[]{:S(2)}, u32[]{:S(2)}) async-start(f32[8,8,32,128]{3,2,1,0:T(8,128)} %bitcast.149), calls=%async_computation.4 | async-start | bytes 2097152 | tf_op jit(solution)/shard_map/all_to_all | solution.py:123
  164.4 28.5 %all-to-all-start.1 = ((f32[8,8,40,128]{3,2,1,0:T(8,128)}), f32[8,8,40,128]{3,2,1,0:T(8,128)S(1)}, u32[]{:S(2)}, u32[]{:S(2)}) async-start(f32[8,8,40,128]{3,2,1,0:T(8,128)} %bitcast.145), calls=%async_computation.2 | async-start | bytes 2621440 | tf_op jit(solution)/shard_map/all_to_all | solution.py:123
  174.7 115.3 %reduce-scatter.11.cloned.1.call-start = ((), (), s32[]{:S(2)}) async-start(), calls=%async_computation.17 | async-start | bytes 1310720 | tf_op jit(solution)/shard_map/reduce_scatter | solution.py:182
  253.7 64.2 %reduce-scatter.9.cloned.1.call-start = ((), (), s32[]{:S(2)}) async-start(), calls=%async_computation.16 | async-start | bytes 1310720 | tf_op jit(solution)/shard_map/reduce_scatter | solution.py:177
  341.1 31.6 %all-to-all-start.6 = ((f32[8,8,32,128]{3,2,1,0:T(8,128)}), f32[8,8,32,128]{3,2,1,0:T(8,128)S(1)}, u32[]{:S(2)}, u32[]{:S(2)}) async-start(f32[8,8,32,128]{3,2,1,0:T(8,128)} %bitcast.148), calls=%async_computation.10 | async-start | bytes 2097152 | tf_op jit(solution)/shard_map/all_to_all | solution.py:123
  372.7 9.9 %copy-start.4 = (s32[1,1024]{1,0:T(1,128)S(1)}, s32[1,1024]{1,0:T(1,128)}, u32[]{:S(2)}) copy-start(s32[1,1024]{1,0:T(1,128)} %param.16) | copy-start | bytes 12292
  372.7 10.0 %copy-start.3 = (s32[1,2048]{1,0:T(1,128)S(1)}, s32[1,2048]{1,0:T(1,128)}, u32[]{:S(2)}) copy-start(s32[1,2048]{1,0:T(1,128)} %param.15) | copy-start | bytes 24580
  372.7 10.2 %copy-start.1 = (f32[16,32,128]{2,1,0:T(8,128)S(1)}, f32[16,32,128]{2,1,0:T(8,128)}, u32[]{:S(2)}) copy-start(f32[16,32,128]{2,1,0:T(8,128)} %reduce-scatter.11.cloned.1.call-done) | copy-start | bytes 786436
  372.7 10.2 %copy-start.2 = (f32[16,32,128]{2,1,0:T(8,128)S(1)}, f32[16,32,128]{2,1,0:T(8,128)}, u32[]{:S(2)}) copy-start(f32[16,32,128]{2,1,0:T(8,128)} %reduce-scatter.9.cloned.1.call-done) | copy-start | bytes 786436
  372.7 25.3 %all-to-all-start.7 = ((f32[8,8,32,128]{3,2,1,0:T(8,128)}), f32[8,8,32,128]{3,2,1,0:T(8,128)S(1)}, u32[]{:S(2)}, u32[]{:S(2)}) async-start(f32[8,8,32,128]{3,2,1,0:T(8,128)} %bitcast.146), calls=%async_computation.11 | async-start | bytes 2097152 | tf_op jit(solution)/shard_map/all_to_all | solution.py:123
Sparse Core Ops, SparseCore 0:
  38.5 42.7 reduce-scatter.4
  83.6 25.9 reduce-scatter.6
  253.9 36.0 reduce-scatter.10
  292.1 25.7 reduce-scatter.8

commit v15 on v13

--- a/solution.py
+++ b/solution.py
@@ -172,7 +172,7 @@
     for step in range(ITERS):
         first = step == 0
         w_all = exchange_gather(weights, "doc", n_doc)
-        half = width_k // 2
+        half = width_k * 3 // 4
         left_a, left_b = tile_pass(local_tiles, rows, cols, count, w_all, True, first, half)
         own_a = lax.psum_scatter(left_a, "term", scatter_dimension=0, tiled=True)
         if first:

time: 411 us -> 437 us (1.063); the launches traced: 407 us -> 438 us
  Pallas kernels: 45.3 us -> 71.9 us
  waiting for transfers between devices: 144 us -> 152 us
    pallas_call x6, Pallas kernels: 45.3 us -> 71.9 us  [tile_pass(): pl.pallas_call(kernel, out_shape=[jax.ShapeDtypeStruct(shape, jnp.float32...]
    reduce_scatter x2, waiting for transfers between devices: 74.6 us -> 79.6 us  [per_device(): own_a = lax.psum_scatter(left_a, 'term', scatter_dimension=0, tiled=True)]
  transfers between devices with their start and end apart: 9 -> 9, of which waited for: 7 -> 7; matrix products, arithmetic and copies ran while one was open for 1% -> 0% of each run, Pallas kernels for 7% -> 7%
where the time goes in v15:
time: 437 us; the launch traced here: 438 us
  waiting for transfers between devices  152 us (35%)
  blocking collectives  123 us (28%)
  Pallas kernels  71.9 us (16%)
  other arithmetic  35 us (8%)
  starting transfers between devices  26.9 us (6%)
  between operations  15.4 us (4%)
  local copies, waits for them, and re-layouts  10.3 us (2%)
  matrix products  4.4 us (1%)
    reduce_scatter x2, waiting for transfers between devices, per_device(): own_a = lax.psum_scatter(left_a, 'term', scatter_dimension=0, tiled=True)  79.6 us
    pallas_call x6, Pallas kernels, tile_pass(): pl.pallas_call(kernel, out_shape=[jax.ShapeDtypeStruct(shape, jnp.float32...  71.9 us
    all_gather x2, blocking collectives, per_device(): lax.all_gather((summed_a / doc_degree[:, None, :]).astype(jnp.bfloat16),...  37.1 us
    all_to_all x4, blocking collectives, exchange_sum(): return jnp.sum(lax.all_to_all(copies, axis_name, 0, 0, tiled=False), axis=0)  36.7 us
    all_to_all x4, waiting for transfers between devices, scatter_sum(): return jnp.sum(lax.all_to_all(pieces, axis_name, 0, 0, tiled=False), axis=0)  32.6 us
    all_gather x2, blocking collectives, per_device(): lax.all_gather((summed_b / doc_degree[:, None, :]).astype(jnp.bfloat16),...  30.3 us
    reduce_scatter x2, waiting for transfers between devices, per_device(): summed_b = lax.psum_scatter(left_b, 'term', scatter_dimension=0, tiled=True)  24.9 us
    all_to_all x4, starting transfers between devices, scatter_sum(): return jnp.sum(lax.all_to_all(pieces, axis_name, 0, 0, tiled=False), axis=0)  21.6 us
  transfers between devices with their start and end apart: 9, of which 7 were waited for; matrix products, arithmetic and copies ran while one was open for 0% of the time, Pallas kernels for 7%

profile of v15, /device:TPU:0, one launch (start us, length us, event | category | flops | bytes accessed | tf_op | source)
XLA Modules:
  0.0 438.4 jit_solution(4747153124680654799)
XLA Ops:
  7.2 0.9 copy.111
  8.1 1.2 broadcast_in_dim.13
  9.4 5.2 %all-to-all-start = ((bf16[8,8,64,128]{3,2,1,0:T(8,128)(2,1)}), bf16[8,8,64,128]{3,2,1,0:T(8,128)(2,1)S(1)}, u32[]{:S(2)}, u32[]{:S(2)}) async-start(bf16[8,8,64,128]{3,2,1,0:T(8,128)(2,1)} %broadcast_in_dim.13), calls=%async_computation | async-start | bytes 2097152 | tf_op jit(solution)/shard_map/all_to_all | solution.py:133
  15.2 14.7 %all-to-all-done = bf16[8,8,64,128]{3,2,1,0:T(8,128)(2,1)S(1)} async-done(((bf16[8,8,64,128]{3,2,1,0:T(8,128)(2,1)}), bf16[8,8,64,128]{3,2,1,0:T(8,128)(2,1)S(1)}, u32[]{:S(2)}, u32[]{:S(2)}) %all-to-all-start) | async-done | bytes 1048608 | tf_op jit(solution)/shard_map/all_to_all | solution.py:133
  29.9 1.0 copy-done
  30.9 15.7 %shard_map.86 = (f32[64,56,128]{2,1,0:T(8,128)}, f32[64,16,128]{2,1,0:T(8,128)}) custom-call(s32[512]{0:T(512)} %bitcast.175, s32[512]{0:T(512)} %bitcast.181, s32[1]{0:T(128)} %bitcast.133.cnt_ref, bf16[512,128,128]{2,1,0:T(8,128)(2,1)} %bitcast.139, bf16[64,64,128]{2,1,0:T(8,128)(2,1)} %bitcast.147), custom_call_target="tpu_custom_call" | custom-call | flops 1207959552 | bytes 20185088 | tf_op jit(solution)/shard_map/pallas_call | solution.py:103
  46.7 43.5 %reduce-scatter.5.cloned.1.call-done = f32[16,56,128]{2,1,0:T(8,128)} async-done(((f32[64,56,128]{2,1,0:T(8,128)}), f32[16,56,128]{2,1,0:T(8,128)}) %reduce-scatter.5.cloned.1.call-update) | async-done | bytes 458768 | tf_op jit(solution)/shard_map/reduce_scatter | solution.py:177
  90.2 0.8 slice.75
  91.0 1.0 fusion.10
  92.1 18.6 %all_gather.12.side_ref = bf16[64,48,128]{2,1,0:T(8,128)(2,1)} all-gather(bf16[16,48,128]{2,1,0:T(8,128)(2,1)S(1)} %fusion.10), channel_id=1, replica_groups=mesh['doc'=8,'term'=4] {'term'}, dimensions={0}, use_global_device_ids=true | all-gather | bytes 983040 | tf_op jit(solution)/shard_map/all_gather | solution.py:181
  110.7 20.6 %reduce-scatter.7.cloned.1.call-done = f32[16,16,128]{2,1,0:T(8,128)} async-done(((f32[64,16,128]{2,1,0:T(8,128)}), f32[16,16,128]{2,1,0:T(8,128)}) %reduce-scatter.7.cloned.1.call-update) | async-done | bytes 131088 | tf_op jit(solution)/shard_map/reduce_scatter | solution.py:183
  131.3 0.9 divide_convert_fusion.2
  132.2 15.1 %all_gather.13.side_ref = bf16[64,16,128]{2,1,0:T(8,128)(2,1)} all-gather(bf16[16,16,128]{2,1,0:T(8,128)(2,1)S(1)} %divide_convert_fusion.2), channel_id=1, replica_groups=mesh['doc'=8,'term'=4] {'term'}, dimensions={0}, use_global_device_ids=true | all-gather | bytes 327680 | tf_op jit(solution)/shard_map/all_gather | solution.py:184
  147.4 9.6 %shard_map.88 = f32[64,16,128]{2,1,0:T(8,128)} custom-call(s32[512]{0:T(512)} %bitcast.176, s32[512]{0:T(512)} %bitcast.182, s32[1]{0:T(128)} %bitcast.135.cnt_ref, bf16[512,128,128]{2,1,0:T(8,128)(2,1)} %bitcast.140, bf16[64,16,128]{2,1,0:T(8,128)(2,1)} %all_gather.13.side_ref), custom_call_target="tpu_custom_call" | custom-call | flops 268435456 | bytes 17563648 | tf_op jit(solution)/shard_map/pallas_call | solution.py:103
  157.0 5.2 %all-to-all-start.2 = ((f32[8,8,16,128]{3,2,1,0:T(8,128)}), f32[8,8,16,128]{3,2,1,0:T(8,128)S(1)}, u32[]{:S(2)}, u32[]{:S(2)}) async-start(f32[8,8,16,128]{3,2,1,0:T(8,128)} %bitcast.150), calls=%async_computation.4 | async-start | bytes 1048576 | tf_op jit(solution)/shard_map/all_to_all | solution.py:123
  162.2 10.9 %shard_map.87 = f32[64,56,128]{2,1,0:T(8,128)} custom-call(s32[512]{0:T(512)} %bitcast.177, s32[512]{0:T(512)} %bitcast.183, s32[1]{0:T(128)} %bitcast.134.cnt_ref, bf16[512,128,128]{2,1,0:T(8,128)(2,1)} %bitcast.141, bf16[64,48,128]{2,1,0:T(8,128)(2,1)} %all_gather.12.side_ref), custom_call_target="tpu_custom_call" | custom-call | flops 939524096 | bytes 19398656 | tf_op jit(solution)/shard_map/pallas_call | solution.py:103
  173.0 5.9 %all-to-all-start.1 = ((f32[8,8,56,128]{3,2,1,0:T(8,128)}), f32[8,8,56,128]{3,2,1,0:T(8,128)S(1)}, u32[]{:S(2)}, u32[]{:S(2)}) async-start(f32[8,8,56,128]{3,2,1,0:T(8,128)} %bitcast.145), calls=%async_computation.2 | async-start | bytes 3670016 | tf_op jit(solution)/shard_map/all_to_all | solution.py:123
  179.0 23.7 %all-to-all-done.1 = f32[8,8,56,128]{3,2,1,0:T(8,128)S(1)} async-done(((f32[8,8,56,128]{3,2,1,0:T(8,128)}), f32[8,8,56,128]{3,2,1,0:T(8,128)S(1)}, u32[]{:S(2)}, u32[]{:S(2)}) %all-to-all-start.1) | async-done | bytes 1835040 | tf_op jit(solution)/shard_map/all_to_all | solution.py:123
  204.5 0.8 concatenate.16
  205.3 8.1 %all_to_all.54 = f32[4,1,4225]{2,1,0:T(1,128)S(1)} all-to-all(f32[4,1,4225]{2,1,0:T(1,128)S(1)} %broadcast_in_dim.14), channel_id=1, replica_groups=mesh['doc'=8,'term'=4] {'term'}, dimensions={0} | all-to-all | bytes 135200 | tf_op jit(solution)/shard_map/all_to_all | solution.py:128
  213.6 8.0 %all_to_all.55 = f32[8,1,4225]{2,1,0:T(1,128)S(1)} all-to-all(f32[8,1,4225]{2,1,0:T(1,128)S(1)} %broadcast_in_dim.15), channel_id=1, replica_groups=mesh['doc'=8,'term'=4] {'doc'}, dimensions={0} | all-to-all | bytes 270400 | tf_op jit(solution)/shard_map/all_to_all | solution.py:128
  223.8 0.7 fusion.35
  224.6 5.8 %cholesky.44 = f32[64,64]{1,0:T(8,128)S(1)} custom-call(f32[64,64]{1,0:T(8,128)S(1)} %fusion.35), custom_call_target="Cholesky" | custom-call | tf_op jit(solution)/shard_map/jit(cholesky)/cholesky | solution.py:206
  231.8 4.9 %custom-call.11 = f32[1,64,64]{1,2,0:T(8,128)S(1)} custom-call(f32[1,64,64]{2,1,0:T(8,128)S(1)} %fusion.27), custom_call_target="InvertDiagBlocksLowerTriangular" | custom-call | tf_op jit(solution)/shard_map/jit(_solve_triangular)/triangular_solve | solution.py:209
  237.4 18.5 %all_to_all.56 = bf16[8,8,64,128]{3,2,1,0:T(8,128)(2,1)} all-to-all(bf16[8,8,64,128]{3,2,1,0:T(8,128)(2,1)S(1)} %broadcast_in_dim.16), channel_id=1, replica_groups=mesh['doc'=8,'term'=4] {'doc'}, dimensions={0} | all-to-all | bytes 2097152 | tf_op jit(solution)/shard_map/all_to_all | solution.py:133
  255.9 15.0 %shard_map.89 = (f32[64,48,128]{2,1,0:T(8,128)}, f32[64,16,128]{2,1,0:T(8,128)}) custom-call(s32[512]{0:T(512)} %bitcast.178, s32[512]{0:T(512)} %bitcast.184, s32[1]{0:T(128)} %bitcast.136.cnt_ref, bf16[512,128,128]{2,1,0:T(8,128)(2,1)} %bitcast.142, bf16[64,64,128]{2,1,0:T(8,128)(2,1)} %bitcast.148), custom_call_target="tpu_custom_call" | custom-call | flops 1073741824 | bytes 19922944 | tf_op jit(solution)/shard_map/pallas_call | solution.py:103
  271.0 36.1 %reduce-scatter.9.cloned.1.call-done = f32[16,48,128]{2,1,0:T(8,128)} async-done(((f32[64,48,128]{2,1,0:T(8,128)}), f32[16,48,128]{2,1,0:T(8,128)}) %reduce-scatter.9.cloned.1.call-update) | async-done | bytes 393232 | tf_op jit(solution)/shard_map/reduce_scatter | solution.py:177
  307.1 1.0 divide_convert_fusion
  308.1 18.5 %all_gather.14.side_ref = bf16[64,48,128]{2,1,0:T(8,128)(2,1)} all-gather(bf16[16,48,128]{2,1,0:T(8,128)(2,1)S(1)} %divide_convert_fusion), channel_id=1, replica_groups=mesh['doc'=8,'term'=4] {'term'}, dimensions={0}, use_global_device_ids=true | all-gather | bytes 983040 | tf_op jit(solution)/shard_map/all_gather | solution.py:181
  326.7 10.9 %shard_map.90 = f32[64,48,128]{2,1,0:T(8,128)} custom-call(s32[512]{0:T(512)} %bitcast.179, s32[512]{0:T(512)} %bitcast.185, s32[1]{0:T(128)} %bitcast.137.cnt_ref, bf16[512,128,128]{2,1,0:T(8,128)(2,1)} %bitcast.143, bf16[64,48,128]{2,1,0:T(8,128)(2,1)} %all_gather.14.side_ref), custom_call_target="tpu_custom_call" | custom-call | flops 805306368 | bytes 19136512 | tf_op jit(solution)/shard_map/pallas_call | solution.py:103
  337.6 5.4 %all-to-all-start.6 = ((f32[8,8,48,128]{3,2,1,0:T(8,128)}), f32[8,8,48,128]{3,2,1,0:T(8,128)S(1)}, u32[]{:S(2)}, u32[]{:S(2)}) async-start(f32[8,8,48,128]{3,2,1,0:T(8,128)} %bitcast.146), calls=%async_computation.10 | async-start | bytes 3145728 | tf_op jit(solution)/shard_map/all_to_all | solution.py:123
  343.0 4.3 reduce-scatter.11.cloned.1.call-done
  347.3 0.9 divide_convert_fusion.1
  348.2 15.1 %all_gather.15.side_ref = bf16[64,16,128]{2,1,0:T(8,128)(2,1)} all-gather(bf16[16,16,128]{2,1,0:T(8,128)(2,1)S(1)} %divide_convert_fusion.1), channel_id=1, replica_groups=mesh['doc'=8,'term'=4] {'term'}, dimensions={0}, use_global_device_ids=true | all-gather | bytes 327680 | tf_op jit(solution)/shard_map/all_gather | solution.py:184
  363.4 9.8 %shard_map.91 = f32[64,16,128]{2,1,0:T(8,128)} custom-call(s32[512]{0:T(512)} %bitcast.180, s32[512]{0:T(512)} %bitcast.186, s32[1]{0:T(128)} %bitcast.138.cnt_ref, bf16[512,128,128]{2,1,0:T(8,128)(2,1)} %bitcast.144, bf16[64,16,128]{2,1,0:T(8,128)(2,1)} %all_gather.15.side_ref), custom_call_target="tpu_custom_call" | custom-call | flops 268435456 | bytes 17563648 | tf_op jit(solution)/shard_map/pallas_call | solution.py:103
  373.2 5.1 %all-to-all-start.7 = ((f32[8,8,16,128]{3,2,1,0:T(8,128)}), f32[8,8,16,128]{3,2,1,0:T(8,128)S(1)}, u32[]{:S(2)}, u32[]{:S(2)}) async-start(f32[8,8,16,128]{3,2,1,0:T(8,128)} %bitcast.149), calls=%async_computation.11 | async-start | bytes 1048576 | tf_op jit(solution)/shard_map/all_to_all | solution.py:123
  379.3 8.8 %all-to-all-done.7 = f32[8,8,16,128]{3,2,1,0:T(8,128)S(1)} async-done(((f32[8,8,16,128]{3,2,1,0:T(8,128)}), f32[8,8,16,128]{3,2,1,0:T(8,128)S(1)}, u32[]{:S(2)}, u32[]{:S(2)}) %all-to-all-start.7) | async-done | bytes 524320 | tf_op jit(solution)/shard_map/all_to_all | solution.py:123
  389.4 0.8 concatenate.19
  390.3 9.2 %all_to_all.57 = f32[4,1,12545]{2,1,0:T(1,128)S(1)} all-to-all(f32[4,1,12545]{2,1,0:T(1,128)S(1)} %broadcast_in_dim.17), channel_id=1, replica_groups=mesh['doc'=8,'term'=4] {'term'}, dimensions={0} | all-to-all | bytes 401440 | tf_op jit(solution)/shard_map/all_to_all | solution.py:128
  399.9 11.4 %all_to_all.58 = f32[8,1,12545]{2,1,0:T(1,128)S(1)} all-to-all(f32[8,1,12545]{2,1,0:T(1,128)S(1)} %broadcast_in_dim.18), channel_id=1, replica_groups=mesh['doc'=8,'term'=4] {'doc'}, dimensions={0} | all-to-all | bytes 802880 | tf_op jit(solution)/shard_map/all_to_all | solution.py:128
  412.8 0.7 fusion.38
  414.0 0.7 divide_subtract_fusion
  414.8 0.7 fusion.33
  415.5 5.8 %cholesky.55 = f32[64,64]{1,0:T(8,128)S(1)} custom-call(f32[64,64]{1,0:T(8,128)S(1)} %fusion.33), custom_call_target="Cholesky" | custom-call | tf_op jit(solution)/shard_map/jit(cholesky)/cholesky | solution.py:206
  422.7 4.9 %custom-call.9 = f32[1,64,64]{1,2,0:T(8,128)S(1)} custom-call(f32[1,64,64]{2,1,0:T(8,128)S(1)} %fusion.28), custom_call_target="InvertDiagBlocksLowerTriangular" | custom-call | tf_op jit(solution)/shard_map/jit(_solve_triangular)/triangular_solve | solution.py:219
  428.6 0.7 fusion.2
  429.6 0.9 broadcast_in_dim_reshape.6
  431.1 0.7 broadcast_in_dim_reshape.7
  (81 shorter events, 13.8 us)
Async XLA Ops:
  9.4 20.6 %all-to-all-start = ((bf16[8,8,64,128]{3,2,1,0:T(8,128)(2,1)}), bf16[8,8,64,128]{3,2,1,0:T(8,128)(2,1)S(1)}, u32[]{:S(2)}, u32[]{:S(2)}) async-start(bf16[8,8,64,128]{3,2,1,0:T(8,128)(2,1)} %broadcast_in_dim.13), calls=%async_computation | async-start | bytes 2097152 | tf_op jit(solution)/shard_map/all_to_all | solution.py:133
  14.5 75.7 %reduce-scatter.5.cloned.1.call-start = ((), (), s32[]{:S(2)}) async-start(), calls=%async_computation.14 | async-start | bytes 2293760 | tf_op jit(solution)/shard_map/reduce_scatter | solution.py:177
  29.9 1.0 copy-start
  46.7 84.6 %reduce-scatter.7.cloned.1.call-start = ((), (), s32[]{:S(2)}) async-start(), calls=%async_computation.15 | async-start | bytes 655360 | tf_op jit(solution)/shard_map/reduce_scatter | solution.py:183
  157.0 16.0 %all-to-all-start.2 = ((f32[8,8,16,128]{3,2,1,0:T(8,128)}), f32[8,8,16,128]{3,2,1,0:T(8,128)S(1)}, u32[]{:S(2)}, u32[]{:S(2)}) async-start(f32[8,8,16,128]{3,2,1,0:T(8,128)} %bitcast.150), calls=%async_computation.4 | async-start | bytes 1048576 | tf_op jit(solution)/shard_map/all_to_all | solution.py:123
  173.0 29.7 %all-to-all-start.1 = ((f32[8,8,56,128]{3,2,1,0:T(8,128)}), f32[8,8,56,128]{3,2,1,0:T(8,128)S(1)}, u32[]{:S(2)}, u32[]{:S(2)}) async-start(f32[8,8,56,128]{3,2,1,0:T(8,128)} %bitcast.145), calls=%async_computation.2 | async-start | bytes 3670016 | tf_op jit(solution)/shard_map/all_to_all | solution.py:123
  178.9 128.1 %reduce-scatter.9.cloned.1.call-start = ((), (), s32[]{:S(2)}) async-start(), calls=%async_computation.16 | async-start | bytes 1966080 | tf_op jit(solution)/shard_map/reduce_scatter | solution.py:177
  270.9 76.4 %reduce-scatter.11.cloned.1.call-start = ((), (), s32[]{:S(2)}) async-start(), calls=%async_computation.17 | async-start | bytes 655360 | tf_op jit(solution)/shard_map/reduce_scatter | solution.py:183
  337.6 35.6 %all-to-all-start.6 = ((f32[8,8,48,128]{3,2,1,0:T(8,128)}), f32[8,8,48,128]{3,2,1,0:T(8,128)S(1)}, u32[]{:S(2)}, u32[]{:S(2)}) async-start(f32[8,8,48,128]{3,2,1,0:T(8,128)} %bitcast.146), calls=%async_computation.10 | async-start | bytes 3145728 | tf_op jit(solution)/shard_map/all_to_all | solution.py:123
  363.4 15.0 %copy-start.4 = (s32[1,1024]{1,0:T(1,128)S(1)}, s32[1,1024]{1,0:T(1,128)}, u32[]{:S(2)}) copy-start(s32[1,1024]{1,0:T(1,128)} %param.16) | copy-start | bytes 12292
  363.4 15.1 %copy-start.3 = (s32[1,2048]{1,0:T(1,128)S(1)}, s32[1,2048]{1,0:T(1,128)}, u32[]{:S(2)}) copy-start(s32[1,2048]{1,0:T(1,128)} %param.15) | copy-start | bytes 24580
  363.4 15.2 %copy-start.1 = (f32[16,48,128]{2,1,0:T(8,128)S(1)}, f32[16,48,128]{2,1,0:T(8,128)}, u32[]{:S(2)}) copy-start(f32[16,48,128]{2,1,0:T(8,128)} %reduce-scatter.9.cloned.1.call-done) | copy-start | bytes 1179652
  363.4 15.3 %copy-start.2 = (f32[16,16,128]{2,1,0:T(8,128)S(1)}, f32[16,16,128]{2,1,0:T(8,128)}, u32[]{:S(2)}) copy-start(f32[16,16,128]{2,1,0:T(8,128)} %reduce-scatter.11.cloned.1.call-done) | copy-start | bytes 393220
  373.2 14.9 %all-to-all-start.7 = ((f32[8,8,16,128]{3,2,1,0:T(8,128)}), f32[8,8,16,128]{3,2,1,0:T(8,128)S(1)}, u32[]{:S(2)}, u32[]{:S(2)}) async-start(f32[8,8,16,128]{3,2,1,0:T(8,128)} %bitcast.149), calls=%async_computation.11 | async-start | bytes 1048576 | tf_op jit(solution)/shard_map/all_to_all | solution.py:123
Sparse Core Ops, SparseCore 0:
  46.8 43.3 reduce-scatter.4
  110.8 20.4 reduce-scatter.6
  271.1 35.9 reduce-scatter.8
  326.8 20.4 reduce-scatter.10

commit v16 on v13

--- a/solution.py
+++ b/solution.py
@@ -136,7 +136,10 @@
 
 def packed_psum(n_doc, n_term, values):
     flat = jnp.concatenate([jnp.reshape(v, (-1,)) for v in values])
-    flat = exchange_sum(exchange_sum(flat, "term", n_term), "doc", n_doc)
+    if flat.size * n_doc * n_term <= 1 << 18:
+        flat = exchange_sum(flat, ("doc", "term"), n_doc * n_term)
+    else:
+        flat = exchange_sum(exchange_sum(flat, "term", n_term), "doc", n_doc)
     out, start = [], 0
     for v in values:
         size = int(jnp.size(v))

time: 411 us -> 413 us (level); the launches traced: 407 us -> 413 us
  starting transfers between devices: 30.2 us -> 36.8 us
    all_to_all x4, starting transfers between devices: 24.8 us -> 31.5 us  [scatter_sum(): return jnp.sum(lax.all_to_all(pieces, axis_name, 0, 0, tiled=False), axis=0)]
    reduce_scatter x2, waiting for transfers between devices: 25.4 us -> 21.2 us  [per_device(): summed_b = lax.psum_scatter(left_b, 'term', scatter_dimension=0, tiled=True)]
    all_to_all x4 -> x3, blocking collectives: 37.9 us -> 37.6 us  [exchange_sum(): return jnp.sum(lax.all_to_all(copies, axis_name, 0, 0, tiled=False), axis=0)]
where the time goes in v16:
time: 413 us
  waiting for transfers between devices  142 us (34%)
  blocking collectives  122 us (30%)
  Pallas kernels  47.2 us (11%)
  starting transfers between devices  36.8 us (9%)
  other arithmetic  35.3 us (9%)
  between operations  15.4 us (4%)
  local copies, waits for them, and re-layouts  10.5 us (3%)
  matrix products  4.52 us (1%)
    reduce_scatter x2, waiting for transfers between devices, per_device(): own_a = lax.psum_scatter(left_a, 'term', scatter_dimension=0, tiled=True)  76.4 us
    pallas_call x6, Pallas kernels, tile_pass(): pl.pallas_call(kernel, out_shape=[jax.ShapeDtypeStruct(shape, jnp.float32...  47.2 us
    all_to_all x3, blocking collectives, exchange_sum(): return jnp.sum(lax.all_to_all(copies, axis_name, 0, 0, tiled=False), axis=0)  37.6 us
    all_gather x2, blocking collectives, per_device(): lax.all_gather((summed_a / doc_degree[:, None, :]).astype(jnp.bfloat16),...  32.8 us
    all_gather x2, blocking collectives, per_device(): lax.all_gather((summed_b / doc_degree[:, None, :]).astype(jnp.bfloat16),...  32.8 us
    all_to_all x4, starting transfers between devices, scatter_sum(): return jnp.sum(lax.all_to_all(pieces, axis_name, 0, 0, tiled=False), axis=0)  31.5 us
    all_to_all x4, waiting for transfers between devices, scatter_sum(): return jnp.sum(lax.all_to_all(pieces, axis_name, 0, 0, tiled=False), axis=0)  29.1 us
    reduce_scatter x2, waiting for transfers between devices, per_device(): summed_b = lax.psum_scatter(left_b, 'term', scatter_dimension=0, tiled=True)  21.2 us
  transfers between devices with their start and end apart: 9, of which 7 were waited for; matrix products, arithmetic and copies ran while one was open for 1% of the time, Pallas kernels for 7%

profile of v16, /device:TPU:0, one launch (start us, length us, event | category | flops | bytes accessed | tf_op | source)
XLA Modules:
  0.0 413.4 jit_solution(4453543939790497553)
XLA Ops:
  7.2 0.9 copy.109
  8.1 1.2 broadcast_in_dim.11
  9.4 5.2 %all-to-all-start = ((bf16[8,8,64,128]{3,2,1,0:T(8,128)(2,1)}), bf16[8,8,64,128]{3,2,1,0:T(8,128)(2,1)S(1)}, u32[]{:S(2)}, u32[]{:S(2)}) async-start(bf16[8,8,64,128]{3,2,1,0:T(8,128)(2,1)} %broadcast_in_dim.11), calls=%async_computation | async-start | bytes 2097152 | tf_op jit(solution)/shard_map/all_to_all | solution.py:133
  15.2 14.7 %all-to-all-done = bf16[8,8,64,128]{3,2,1,0:T(8,128)(2,1)S(1)} async-done(((bf16[8,8,64,128]{3,2,1,0:T(8,128)(2,1)}), bf16[8,8,64,128]{3,2,1,0:T(8,128)(2,1)S(1)}, u32[]{:S(2)}, u32[]{:S(2)}) %all-to-all-start) | async-done | bytes 1048608 | tf_op jit(solution)/shard_map/all_to_all | solution.py:133
  29.9 1.0 copy-done
  30.9 9.9 %shard_map.86 = (f32[64,40,128]{2,1,0:T(8,128)}, f32[64,32,128]{2,1,0:T(8,128)}) custom-call(s32[512]{0:T(512)} %bitcast.175, s32[512]{0:T(512)} %bitcast.181, s32[1]{0:T(128)} %bitcast.133.cnt_ref, bf16[512,128,128]{2,1,0:T(8,128)(2,1)} %bitcast.139, bf16[64,64,128]{2,1,0:T(8,128)(2,1)} %bitcast.149), custom_call_target="tpu_custom_call" | custom-call | flops 1207959552 | bytes 20185088 | tf_op jit(solution)/shard_map/pallas_call | solution.py:103
  40.8 41.1 %reduce-scatter.5.cloned.1.call-done = f32[16,40,128]{2,1,0:T(8,128)} async-done(((f32[64,40,128]{2,1,0:T(8,128)}), f32[16,40,128]{2,1,0:T(8,128)}) %reduce-scatter.5.cloned.1.call-update) | async-done | bytes 327696 | tf_op jit(solution)/shard_map/reduce_scatter | solution.py:180
  82.0 0.8 slice.75
  82.8 1.0 fusion.19
  83.8 16.4 %all_gather.12.side_ref = bf16[64,32,128]{2,1,0:T(8,128)(2,1)} all-gather(bf16[16,32,128]{2,1,0:T(8,128)(2,1)S(1)} %fusion.19), channel_id=1, replica_groups=mesh['doc'=8,'term'=4] {'term'}, dimensions={0}, use_global_device_ids=true | all-gather | bytes 655360 | tf_op jit(solution)/shard_map/all_gather | solution.py:184
  100.3 7.3 %shard_map.87 = f32[64,40,128]{2,1,0:T(8,128)} custom-call(s32[512]{0:T(512)} %bitcast.176, s32[512]{0:T(512)} %bitcast.182, s32[1]{0:T(128)} %bitcast.134.cnt_ref, bf16[512,128,128]{2,1,0:T(8,128)(2,1)} %bitcast.140, bf16[64,32,128]{2,1,0:T(8,128)(2,1)} %all_gather.12.side_ref), custom_call_target="tpu_custom_call" | custom-call | flops 671088640 | bytes 18612224 | tf_op jit(solution)/shard_map/pallas_call | solution.py:103
  107.5 8.2 %all-to-all-start.1 = ((f32[8,8,40,128]{3,2,1,0:T(8,128)}), f32[8,8,40,128]{3,2,1,0:T(8,128)S(1)}, u32[]{:S(2)}, u32[]{:S(2)}) async-start(f32[8,8,40,128]{3,2,1,0:T(8,128)} %bitcast.145), calls=%async_computation.2 | async-start | bytes 2621440 | tf_op jit(solution)/shard_map/all_to_all | solution.py:123
  115.7 10.2 %reduce-scatter.7.cloned.1.call-done = f32[16,32,128]{2,1,0:T(8,128)} async-done(((f32[64,32,128]{2,1,0:T(8,128)}), f32[16,32,128]{2,1,0:T(8,128)}) %reduce-scatter.7.cloned.1.call-update) | async-done | bytes 262160 | tf_op jit(solution)/shard_map/reduce_scatter | solution.py:186
  125.9 1.0 divide_convert_fusion.2
  126.9 16.4 %all_gather.13.side_ref = bf16[64,32,128]{2,1,0:T(8,128)(2,1)} all-gather(bf16[16,32,128]{2,1,0:T(8,128)(2,1)S(1)} %divide_convert_fusion.2), channel_id=1, replica_groups=mesh['doc'=8,'term'=4] {'term'}, dimensions={0}, use_global_device_ids=true | all-gather | bytes 655360 | tf_op jit(solution)/shard_map/all_gather | solution.py:187
  143.3 6.9 %shard_map.88 = f32[64,32,128]{2,1,0:T(8,128)} custom-call(s32[512]{0:T(512)} %bitcast.177, s32[512]{0:T(512)} %bitcast.183, s32[1]{0:T(128)} %bitcast.135.cnt_ref, bf16[512,128,128]{2,1,0:T(8,128)(2,1)} %bitcast.141, bf16[64,32,128]{2,1,0:T(8,128)(2,1)} %all_gather.13.side_ref), custom_call_target="tpu_custom_call" | custom-call | flops 536870912 | bytes 18350080 | tf_op jit(solution)/shard_map/pallas_call | solution.py:103
  150.2 7.7 %all-to-all-start.2 = ((f32[8,8,32,128]{3,2,1,0:T(8,128)}), f32[8,8,32,128]{3,2,1,0:T(8,128)S(1)}, u32[]{:S(2)}, u32[]{:S(2)}) async-start(f32[8,8,32,128]{3,2,1,0:T(8,128)} %bitcast.147), calls=%async_computation.4 | async-start | bytes 2097152 | tf_op jit(solution)/shard_map/all_to_all | solution.py:123
  158.7 14.7 %all-to-all-done.2 = f32[8,8,32,128]{3,2,1,0:T(8,128)S(1)} async-done(((f32[8,8,32,128]{3,2,1,0:T(8,128)}), f32[8,8,32,128]{3,2,1,0:T(8,128)S(1)}, u32[]{:S(2)}, u32[]{:S(2)}) %all-to-all-start.2) | async-done | bytes 1048608 | tf_op jit(solution)/shard_map/all_to_all | solution.py:123
  175.3 16.9 %all_to_all.48 = f32[32,1,4225]{2,1,0:T(1,128)S(1)} all-to-all(f32[32,1,4225]{2,1,0:T(1,128)S(1)} %broadcast_in_dim.12), channel_id=1, replica_groups=mesh['doc'=8,'term'=4] {'doc','term'}, dimensions={0} | all-to-all | bytes 1081600 | tf_op jit(solution)/shard_map/all_to_all | solution.py:128
  194.0 0.8 divide_subtract_fusion.1
  194.9 0.8 fusion.35
  195.7 5.8 %cholesky.44 = f32[64,64]{1,0:T(8,128)S(1)} custom-call(f32[64,64]{1,0:T(8,128)S(1)} %fusion.35), custom_call_target="Cholesky" | custom-call | tf_op jit(solution)/shard_map/jit(cholesky)/cholesky | solution.py:209
  201.5 0.7 compare_reduce_fusion.1
  203.0 4.9 %custom-call.11 = f32[1,64,64]{1,2,0:T(8,128)S(1)} custom-call(f32[1,64,64]{2,1,0:T(8,128)S(1)} %fusion.27), custom_call_target="InvertDiagBlocksLowerTriangular" | custom-call | tf_op jit(solution)/shard_map/jit(_solve_triangular)/triangular_solve | solution.py:212
  208.6 18.9 %all_to_all.49 = bf16[8,8,64,128]{3,2,1,0:T(8,128)(2,1)} all-to-all(bf16[8,8,64,128]{3,2,1,0:T(8,128)(2,1)S(1)} %broadcast_in_dim.13), channel_id=1, replica_groups=mesh['doc'=8,'term'=4] {'doc'}, dimensions={0} | all-to-all | bytes 2097152 | tf_op jit(solution)/shard_map/all_to_all | solution.py:133
  227.5 9.5 %shard_map.89 = (f32[64,32,128]{2,1,0:T(8,128)}, f32[64,32,128]{2,1,0:T(8,128)}) custom-call(s32[512]{0:T(512)} %bitcast.178, s32[512]{0:T(512)} %bitcast.184, s32[1]{0:T(128)} %bitcast.136.cnt_ref, bf16[512,128,128]{2,1,0:T(8,128)(2,1)} %bitcast.142, bf16[64,64,128]{2,1,0:T(8,128)(2,1)} %bitcast.150), custom_call_target="tpu_custom_call" | custom-call | flops 1073741824 | bytes 19922944 | tf_op jit(solution)/shard_map/pallas_call | solution.py:103
  237.1 35.2 %reduce-scatter.9.cloned.1.call-done = f32[16,32,128]{2,1,0:T(8,128)} async-done(((f32[64,32,128]{2,1,0:T(8,128)}), f32[16,32,128]{2,1,0:T(8,128)}) %reduce-scatter.9.cloned.1.call-update) | async-done | bytes 262160 | tf_op jit(solution)/shard_map/reduce_scatter | solution.py:180
  272.3 1.0 divide_convert_fusion.1
  273.3 16.4 %all_gather.14.side_ref = bf16[64,32,128]{2,1,0:T(8,128)(2,1)} all-gather(bf16[16,32,128]{2,1,0:T(8,128)(2,1)S(1)} %divide_convert_fusion.1), channel_id=1, replica_groups=mesh['doc'=8,'term'=4] {'term'}, dimensions={0}, use_global_device_ids=true | all-gather | bytes 655360 | tf_op jit(solution)/shard_map/all_gather | solution.py:184
  289.8 6.9 %shard_map.90 = f32[64,32,128]{2,1,0:T(8,128)} custom-call(s32[512]{0:T(512)} %bitcast.179, s32[512]{0:T(512)} %bitcast.185, s32[1]{0:T(128)} %bitcast.137.cnt_ref, bf16[512,128,128]{2,1,0:T(8,128)(2,1)} %bitcast.143, bf16[64,32,128]{2,1,0:T(8,128)(2,1)} %all_gather.14.side_ref), custom_call_target="tpu_custom_call" | custom-call | flops 536870912 | bytes 18350080 | tf_op jit(solution)/shard_map/pallas_call | solution.py:103
  296.7 7.7 %all-to-all-start.5 = ((f32[8,8,32,128]{3,2,1,0:T(8,128)}), f32[8,8,32,128]{3,2,1,0:T(8,128)S(1)}, u32[]{:S(2)}, u32[]{:S(2)}) async-start(f32[8,8,32,128]{3,2,1,0:T(8,128)} %bitcast.148), calls=%async_computation.9 | async-start | bytes 2097152 | tf_op jit(solution)/shard_map/all_to_all | solution.py:123
  304.4 11.0 %reduce-scatter.11.cloned.1.call-done = f32[16,32,128]{2,1,0:T(8,128)} async-done(((f32[64,32,128]{2,1,0:T(8,128)}), f32[16,32,128]{2,1,0:T(8,128)}) %reduce-scatter.11.cloned.1.call-update) | async-done | bytes 262160 | tf_op jit(solution)/shard_map/reduce_scatter | solution.py:186
  315.4 1.0 divide_convert_fusion
  316.4 16.4 %all_gather.15.side_ref = bf16[64,32,128]{2,1,0:T(8,128)(2,1)} all-gather(bf16[16,32,128]{2,1,0:T(8,128)(2,1)S(1)} %divide_convert_fusion), channel_id=1, replica_groups=mesh['doc'=8,'term'=4] {'term'}, dimensions={0}, use_global_device_ids=true | all-gather | bytes 655360 | tf_op jit(solution)/shard_map/all_gather | solution.py:187
  332.8 6.9 %shard_map.91 = f32[64,32,128]{2,1,0:T(8,128)} custom-call(s32[512]{0:T(512)} %bitcast.180, s32[512]{0:T(512)} %bitcast.186, s32[1]{0:T(128)} %bitcast.138.cnt_ref, bf16[512,128,128]{2,1,0:T(8,128)(2,1)} %bitcast.144, bf16[64,32,128]{2,1,0:T(8,128)(2,1)} %all_gather.15.side_ref), custom_call_target="tpu_custom_call" | custom-call | flops 536870912 | bytes 18350080 | tf_op jit(solution)/shard_map/pallas_call | solution.py:103
  339.7 7.9 %all-to-all-start.6 = ((f32[8,8,32,128]{3,2,1,0:T(8,128)}), f32[8,8,32,128]{3,2,1,0:T(8,128)S(1)}, u32[]{:S(2)}, u32[]{:S(2)}) async-start(f32[8,8,32,128]{3,2,1,0:T(8,128)} %bitcast.146), calls=%async_computation.10 | async-start | bytes 2097152 | tf_op jit(solution)/shard_map/all_to_all | solution.py:123
  348.5 14.5 %all-to-all-done.6 = f32[8,8,32,128]{3,2,1,0:T(8,128)S(1)} async-done(((f32[8,8,32,128]{3,2,1,0:T(8,128)}), f32[8,8,32,128]{3,2,1,0:T(8,128)S(1)}, u32[]{:S(2)}, u32[]{:S(2)}) %all-to-all-start.6) | async-done | bytes 1048608 | tf_op jit(solution)/shard_map/all_to_all | solution.py:123
  364.4 0.7 concatenate.19
  365.2 9.6 %all_to_all.50 = f32[4,1,12545]{2,1,0:T(1,128)S(1)} all-to-all(f32[4,1,12545]{2,1,0:T(1,128)S(1)} %broadcast_in_dim.14), channel_id=1, replica_groups=mesh['doc'=8,'term'=4] {'term'}, dimensions={0} | all-to-all | bytes 401440 | tf_op jit(solution)/shard_map/all_to_all | solution.py:128
  375.2 11.1 %all_to_all.51 = f32[8,1,12545]{2,1,0:T(1,128)S(1)} all-to-all(f32[8,1,12545]{2,1,0:T(1,128)S(1)} %broadcast_in_dim.15), channel_id=1, replica_groups=mesh['doc'=8,'term'=4] {'doc'}, dimensions={0} | all-to-all | bytes 802880 | tf_op jit(solution)/shard_map/all_to_all | solution.py:128
  387.8 0.7 fusion.38
  388.9 0.7 divide_subtract_fusion
  389.7 0.7 fusion.33
  390.5 5.8 %cholesky.55 = f32[64,64]{1,0:T(8,128)S(1)} custom-call(f32[64,64]{1,0:T(8,128)S(1)} %fusion.33), custom_call_target="Cholesky" | custom-call | tf_op jit(solution)/shard_map/jit(cholesky)/cholesky | solution.py:209
  397.6 4.9 %custom-call.9 = f32[1,64,64]{1,2,0:T(8,128)S(1)} custom-call(f32[1,64,64]{2,1,0:T(8,128)S(1)} %fusion.28), custom_call_target="InvertDiagBlocksLowerTriangular" | custom-call | tf_op jit(solution)/shard_map/jit(_solve_triangular)/triangular_solve | solution.py:222
  404.1 0.7 broadcast_in_dim_reshape.7
  405.0 0.7 fusion.2
  406.0 0.9 broadcast_in_dim_reshape.6
  (78 shorter events, 13.6 us)
Async XLA Ops:
  9.4 20.6 %all-to-all-start = ((bf16[8,8,64,128]{3,2,1,0:T(8,128)(2,1)}), bf16[8,8,64,128]{3,2,1,0:T(8,128)(2,1)S(1)}, u32[]{:S(2)}, u32[]{:S(2)}) async-start(bf16[8,8,64,128]{3,2,1,0:T(8,128)(2,1)} %broadcast_in_dim.11), calls=%async_computation | async-start | bytes 2097152 | tf_op jit(solution)/shard_map/all_to_all | solution.py:133
  14.5 67.5 %reduce-scatter.5.cloned.1.call-start = ((), (), s32[]{:S(2)}) async-start(), calls=%async_computation.13 | async-start | bytes 1638400 | tf_op jit(solution)/shard_map/reduce_scatter | solution.py:180
  29.9 1.0 copy-start
  40.8 85.1 %reduce-scatter.7.cloned.1.call-start = ((), (), s32[]{:S(2)}) async-start(), calls=%async_computation.14 | async-start | bytes 1310720 | tf_op jit(solution)/shard_map/reduce_scatter | solution.py:186
  107.5 42.6 %all-to-all-start.1 = ((f32[8,8,40,128]{3,2,1,0:T(8,128)}), f32[8,8,40,128]{3,2,1,0:T(8,128)S(1)}, u32[]{:S(2)}, u32[]{:S(2)}) async-start(f32[8,8,40,128]{3,2,1,0:T(8,128)} %bitcast.145), calls=%async_computation.2 | async-start | bytes 2621440 | tf_op jit(solution)/shard_map/all_to_all | solution.py:123
  150.2 23.1 %all-to-all-start.2 = ((f32[8,8,32,128]{3,2,1,0:T(8,128)}), f32[8,8,32,128]{3,2,1,0:T(8,128)S(1)}, u32[]{:S(2)}, u32[]{:S(2)}) async-start(f32[8,8,32,128]{3,2,1,0:T(8,128)} %bitcast.147), calls=%async_computation.4 | async-start | bytes 2097152 | tf_op jit(solution)/shard_map/all_to_all | solution.py:123
  157.9 114.4 %reduce-scatter.9.cloned.1.call-start = ((), (), s32[]{:S(2)}) async-start(), calls=%async_computation.15 | async-start | bytes 1310720 | tf_op jit(solution)/shard_map/reduce_scatter | solution.py:180
  237.1 78.3 %reduce-scatter.11.cloned.1.call-start = ((), (), s32[]{:S(2)}) async-start(), calls=%async_computation.16 | async-start | bytes 1310720 | tf_op jit(solution)/shard_map/reduce_scatter | solution.py:186
  296.7 43.0 %all-to-all-start.5 = ((f32[8,8,32,128]{3,2,1,0:T(8,128)}), f32[8,8,32,128]{3,2,1,0:T(8,128)S(1)}, u32[]{:S(2)}, u32[]{:S(2)}) async-start(f32[8,8,32,128]{3,2,1,0:T(8,128)} %bitcast.148), calls=%async_computation.9 | async-start | bytes 2097152 | tf_op jit(solution)/shard_map/all_to_all | solution.py:123
  339.7 7.9 %copy-start.4 = (s32[1,1024]{1,0:T(1,128)S(1)}, s32[1,1024]{1,0:T(1,128)}, u32[]{:S(2)}) copy-start(s32[1,1024]{1,0:T(1,128)} %param.16) | copy-start | bytes 12292
  339.7 8.0 %copy-start.3 = (s32[1,2048]{1,0:T(1,128)S(1)}, s32[1,2048]{1,0:T(1,128)}, u32[]{:S(2)}) copy-start(s32[1,2048]{1,0:T(1,128)} %param.15) | copy-start | bytes 24580
  339.7 8.3 %copy-start.1 = (f32[16,32,128]{2,1,0:T(8,128)S(1)}, f32[16,32,128]{2,1,0:T(8,128)}, u32[]{:S(2)}) copy-start(f32[16,32,128]{2,1,0:T(8,128)} %reduce-scatter.9.cloned.1.call-done) | copy-start | bytes 786436
  339.7 8.3 %copy-start.2 = (f32[16,32,128]{2,1,0:T(8,128)S(1)}, f32[16,32,128]{2,1,0:T(8,128)}, u32[]{:S(2)}) copy-start(f32[16,32,128]{2,1,0:T(8,128)} %reduce-scatter.11.cloned.1.call-done) | copy-start | bytes 786436
  339.7 23.3 %all-to-all-start.6 = ((f32[8,8,32,128]{3,2,1,0:T(8,128)}), f32[8,8,32,128]{3,2,1,0:T(8,128)S(1)}, u32[]{:S(2)}, u32[]{:S(2)}) async-start(f32[8,8,32,128]{3,2,1,0:T(8,128)} %bitcast.146), calls=%async_computation.10 | async-start | bytes 2097152 | tf_op jit(solution)/shard_map/all_to_all | solution.py:123
Sparse Core Ops, SparseCore 0:
  40.9 41.0 reduce-scatter.4
  100.4 25.4 reduce-scatter.6
  237.2 35.1 reduce-scatter.8
  289.9 25.4 reduce-scatter.10

commit v17 on v13

--- a/solution.py
+++ b/solution.py
@@ -203,7 +203,7 @@
             sums += [doc_part, term_part, jnp.sum(doc_onehot, axis=(0, 1)), jnp.sum(term_onehot, axis=(0, 1))]
         sums = packed_psum(n_doc, n_term, sums)
         gram_matrix, along, energy, volume = sums[:4]
-        lower = jnp.linalg.cholesky(gram_matrix - jnp.outer(along, along) / volume)
+        lower = jnp.linalg.cholesky(gram_matrix - jnp.outer(along, along) / volume, symmetrize_input=False)
         projected = raw - root[:, None, :] * (along / volume)[None, :, None]
         flat = projected.transpose(1, 0, 2).reshape(width_k, -1)
         solved = jax.scipy.linalg.solve_triangular(lower, flat, lower=True)

time: 411 us -> 409 us (level)
  waiting for transfers between devices: 144 us -> 152 us
  Pallas kernels: 45.3 us -> 39.3 us
    pallas_call x6, Pallas kernels: 45.3 us -> 39.3 us  [tile_pass(): pl.pallas_call(kernel, out_shape=[jax.ShapeDtypeStruct(shape, jnp.float32...]
    all_to_all x4, blocking collectives: 37.9 us -> 42 us  [exchange_sum(): return jnp.sum(lax.all_to_all(copies, axis_name, 0, 0, tiled=False), axis=0)]
  transfers between devices with their start and end apart: 9 -> 9, of which waited for: 7 -> 7; matrix products, arithmetic and copies ran while one was open for 1% -> 1% of each run, Pallas kernels for 7% -> 6%
where the time goes in v17:
time: 409 us; the launch traced here: 407 us
  waiting for transfers between devices  152 us (37%)
  blocking collectives  126 us (31%)
  Pallas kernels  39.3 us (10%)
  other arithmetic  33.6 us (8%)
  starting transfers between devices  26.2 us (6%)
  between operations  15.4 us (4%)
  local copies, waits for them, and re-layouts  10 us (2%)
  matrix products  4.53 us (1%)
    reduce_scatter x2, waiting for transfers between devices, per_device(): own_a = lax.psum_scatter(left_a, 'term', scatter_dimension=0, tiled=True)  78.4 us
    all_to_all x4, blocking collectives, exchange_sum(): return jnp.sum(lax.all_to_all(copies, axis_name, 0, 0, tiled=False), axis=0)  42 us
    pallas_call x6, Pallas kernels, tile_pass(): pl.pallas_call(kernel, out_shape=[jax.ShapeDtypeStruct(shape, jnp.float32...  39.3 us
    all_gather x2, blocking collectives, per_device(): lax.all_gather((summed_a / doc_degree[:, None, :]).astype(jnp.bfloat16),...  32.8 us
    all_gather x2, blocking collectives, per_device(): lax.all_gather((summed_b / doc_degree[:, None, :]).astype(jnp.bfloat16),...  32.8 us
    reduce_scatter x2, waiting for transfers between devices, per_device(): summed_b = lax.psum_scatter(left_b, 'term', scatter_dimension=0, tiled=True)  29.2 us
    all_to_all x4, waiting for transfers between devices, scatter_sum(): return jnp.sum(lax.all_to_all(pieces, axis_name, 0, 0, tiled=False), axis=0)  29.1 us
    all_to_all x4, starting transfers between devices, scatter_sum(): return jnp.sum(lax.all_to_all(pieces, axis_name, 0, 0, tiled=False), axis=0)  20.9 us
  transfers between devices with their start and end apart: 9, of which 7 were waited for; matrix products, arithmetic and copies ran while one was open for 1% of the time, Pallas kernels for 6%

profile of v17, /device:TPU:0, one launch (start us, length us, event | category | flops | bytes accessed | tf_op | source)
XLA Modules:
  0.0 406.7 jit_solution(15560508991318843997)
XLA Ops:
  7.2 0.9 copy.89
  8.1 1.2 broadcast_in_dim.13
  9.4 5.2 %all-to-all-start = ((bf16[8,8,64,128]{3,2,1,0:T(8,128)(2,1)}), bf16[8,8,64,128]{3,2,1,0:T(8,128)(2,1)S(1)}, u32[]{:S(2)}, u32[]{:S(2)}) async-start(bf16[8,8,64,128]{3,2,1,0:T(8,128)(2,1)} %broadcast_in_dim.13), calls=%async_computation | async-start | bytes 2097152 | tf_op jit(solution)/shard_map/all_to_all | solution.py:133
  15.2 14.7 %all-to-all-done = bf16[8,8,64,128]{3,2,1,0:T(8,128)(2,1)S(1)} async-done(((bf16[8,8,64,128]{3,2,1,0:T(8,128)(2,1)}), bf16[8,8,64,128]{3,2,1,0:T(8,128)(2,1)S(1)}, u32[]{:S(2)}, u32[]{:S(2)}) %all-to-all-start) | async-done | bytes 1048608 | tf_op jit(solution)/shard_map/all_to_all | solution.py:133
  29.9 1.0 copy-done
  30.9 7.9 %shard_map.86 = (f32[64,40,128]{2,1,0:T(8,128)}, f32[64,32,128]{2,1,0:T(8,128)}) custom-call(s32[512]{0:T(512)} %bitcast.167, s32[512]{0:T(512)} %bitcast.173, s32[1]{0:T(128)} %bitcast.125.cnt_ref, bf16[512,128,128]{2,1,0:T(8,128)(2,1)} %bitcast.131, bf16[64,64,128]{2,1,0:T(8,128)(2,1)} %bitcast.141), custom_call_target="tpu_custom_call" | custom-call | flops 1207959552 | bytes 20185088 | tf_op jit(solution)/shard_map/pallas_call | solution.py:103
  38.9 43.1 %reduce-scatter.5.cloned.1.call-done = f32[16,40,128]{2,1,0:T(8,128)} async-done(((f32[64,40,128]{2,1,0:T(8,128)}), f32[16,40,128]{2,1,0:T(8,128)}) %reduce-scatter.5.cloned.1.call-update) | async-done | bytes 327696 | tf_op jit(solution)/shard_map/reduce_scatter | solution.py:177
  82.0 0.8 slice.75
  82.9 1.0 fusion.19
  83.8 16.4 %all_gather.12.side_ref = bf16[64,32,128]{2,1,0:T(8,128)(2,1)} all-gather(bf16[16,32,128]{2,1,0:T(8,128)(2,1)S(1)} %fusion.19), channel_id=1, replica_groups=mesh['doc'=8,'term'=4] {'term'}, dimensions={0}, use_global_device_ids=true | all-gather | bytes 655360 | tf_op jit(solution)/shard_map/all_gather | solution.py:181
  100.3 6.1 %shard_map.87 = f32[64,40,128]{2,1,0:T(8,128)} custom-call(s32[512]{0:T(512)} %bitcast.168, s32[512]{0:T(512)} %bitcast.174, s32[1]{0:T(128)} %bitcast.126.cnt_ref, bf16[512,128,128]{2,1,0:T(8,128)(2,1)} %bitcast.132, bf16[64,32,128]{2,1,0:T(8,128)(2,1)} %all_gather.12.side_ref), custom_call_target="tpu_custom_call" | custom-call | flops 671088640 | bytes 18612224 | tf_op jit(solution)/shard_map/pallas_call | solution.py:103
  106.4 5.3 %all-to-all-start.1 = ((f32[8,8,40,128]{3,2,1,0:T(8,128)}), f32[8,8,40,128]{3,2,1,0:T(8,128)S(1)}, u32[]{:S(2)}, u32[]{:S(2)}) async-start(f32[8,8,40,128]{3,2,1,0:T(8,128)} %bitcast.137), calls=%async_computation.2 | async-start | bytes 2621440 | tf_op jit(solution)/shard_map/all_to_all | solution.py:123
  111.7 14.2 %reduce-scatter.7.cloned.1.call-done = f32[16,32,128]{2,1,0:T(8,128)} async-done(((f32[64,32,128]{2,1,0:T(8,128)}), f32[16,32,128]{2,1,0:T(8,128)}) %reduce-scatter.7.cloned.1.call-update) | async-done | bytes 262160 | tf_op jit(solution)/shard_map/reduce_scatter | solution.py:183
  125.9 1.0 divide_convert_fusion.2
  126.9 16.4 %all_gather.13.side_ref = bf16[64,32,128]{2,1,0:T(8,128)(2,1)} all-gather(bf16[16,32,128]{2,1,0:T(8,128)(2,1)S(1)} %divide_convert_fusion.2), channel_id=1, replica_groups=mesh['doc'=8,'term'=4] {'term'}, dimensions={0}, use_global_device_ids=true | all-gather | bytes 655360 | tf_op jit(solution)/shard_map/all_gather | solution.py:184
  143.3 5.8 %shard_map.88 = f32[64,32,128]{2,1,0:T(8,128)} custom-call(s32[512]{0:T(512)} %bitcast.169, s32[512]{0:T(512)} %bitcast.175, s32[1]{0:T(128)} %bitcast.127.cnt_ref, bf16[512,128,128]{2,1,0:T(8,128)(2,1)} %bitcast.133, bf16[64,32,128]{2,1,0:T(8,128)(2,1)} %all_gather.13.side_ref), custom_call_target="tpu_custom_call" | custom-call | flops 536870912 | bytes 18350080 | tf_op jit(solution)/shard_map/pallas_call | solution.py:103
  149.1 5.2 %all-to-all-start.2 = ((f32[8,8,32,128]{3,2,1,0:T(8,128)}), f32[8,8,32,128]{3,2,1,0:T(8,128)S(1)}, u32[]{:S(2)}, u32[]{:S(2)}) async-start(f32[8,8,32,128]{3,2,1,0:T(8,128)} %bitcast.139), calls=%async_computation.4 | async-start | bytes 2097152 | tf_op jit(solution)/shard_map/all_to_all | solution.py:123
  155.1 14.7 %all-to-all-done.2 = f32[8,8,32,128]{3,2,1,0:T(8,128)S(1)} async-done(((f32[8,8,32,128]{3,2,1,0:T(8,128)}), f32[8,8,32,128]{3,2,1,0:T(8,128)S(1)}, u32[]{:S(2)}, u32[]{:S(2)}) %all-to-all-start.2) | async-done | bytes 1048608 | tf_op jit(solution)/shard_map/all_to_all | solution.py:123
  170.7 0.7 concatenate.16
  171.5 10.9 %all_to_all.54 = f32[4,1,4225]{2,1,0:T(1,128)S(1)} all-to-all(f32[4,1,4225]{2,1,0:T(1,128)S(1)} %broadcast_in_dim.14), channel_id=1, replica_groups=mesh['doc'=8,'term'=4] {'term'}, dimensions={0} | all-to-all | bytes 135200 | tf_op jit(solution)/shard_map/all_to_all | solution.py:128
  182.6 8.0 %all_to_all.55 = f32[8,1,4225]{2,1,0:T(1,128)S(1)} all-to-all(f32[8,1,4225]{2,1,0:T(1,128)S(1)} %broadcast_in_dim.15), channel_id=1, replica_groups=mesh['doc'=8,'term'=4] {'doc'}, dimensions={0} | all-to-all | bytes 270400 | tf_op jit(solution)/shard_map/all_to_all | solution.py:128
  192.1 0.8 divide_subtract_fusion.1
  192.8 5.8 %cholesky.45 = f32[64,64]{1,0:T(8,128)S(1)} custom-call(f32[64,64]{1,0:T(8,128)S(1)} %divide_subtract_fusion.1), custom_call_target="Cholesky" | custom-call | tf_op jit(solution)/shard_map/jit(cholesky)/cholesky | solution.py:206
  198.7 0.7 compare_reduce_fusion.1
  200.1 4.9 %custom-call.11 = f32[1,64,64]{1,2,0:T(8,128)S(1)} custom-call(f32[1,64,64]{2,1,0:T(8,128)S(1)} %fusion.27), custom_call_target="InvertDiagBlocksLowerTriangular" | custom-call | tf_op jit(solution)/shard_map/jit(_solve_triangular)/triangular_solve | solution.py:209
  205.8 18.5 %all_to_all.56 = bf16[8,8,64,128]{3,2,1,0:T(8,128)(2,1)} all-to-all(bf16[8,8,64,128]{3,2,1,0:T(8,128)(2,1)S(1)} %broadcast_in_dim.16), channel_id=1, replica_groups=mesh['doc'=8,'term'=4] {'doc'}, dimensions={0} | all-to-all | bytes 2097152 | tf_op jit(solution)/shard_map/all_to_all | solution.py:133
  224.3 7.7 %shard_map.89 = (f32[64,32,128]{2,1,0:T(8,128)}, f32[64,32,128]{2,1,0:T(8,128)}) custom-call(s32[512]{0:T(512)} %bitcast.170, s32[512]{0:T(512)} %bitcast.176, s32[1]{0:T(128)} %bitcast.128.cnt_ref, bf16[512,128,128]{2,1,0:T(8,128)(2,1)} %bitcast.134, bf16[64,64,128]{2,1,0:T(8,128)(2,1)} %bitcast.142), custom_call_target="tpu_custom_call" | custom-call | flops 1073741824 | bytes 19922944 | tf_op jit(solution)/shard_map/pallas_call | solution.py:103
  232.1 35.3 %reduce-scatter.9.cloned.1.call-done = f32[16,32,128]{2,1,0:T(8,128)} async-done(((f32[64,32,128]{2,1,0:T(8,128)}), f32[16,32,128]{2,1,0:T(8,128)}) %reduce-scatter.9.cloned.1.call-update) | async-done | bytes 262160 | tf_op jit(solution)/shard_map/reduce_scatter | solution.py:177
  267.4 1.0 divide_convert_fusion.1
  268.3 16.4 %all_gather.14.side_ref = bf16[64,32,128]{2,1,0:T(8,128)(2,1)} all-gather(bf16[16,32,128]{2,1,0:T(8,128)(2,1)S(1)} %divide_convert_fusion.1), channel_id=1, replica_groups=mesh['doc'=8,'term'=4] {'term'}, dimensions={0}, use_global_device_ids=true | all-gather | bytes 655360 | tf_op jit(solution)/shard_map/all_gather | solution.py:181
  284.8 5.9 %shard_map.90 = f32[64,32,128]{2,1,0:T(8,128)} custom-call(s32[512]{0:T(512)} %bitcast.171, s32[512]{0:T(512)} %bitcast.177, s32[1]{0:T(128)} %bitcast.129.cnt_ref, bf16[512,128,128]{2,1,0:T(8,128)(2,1)} %bitcast.135, bf16[64,32,128]{2,1,0:T(8,128)(2,1)} %all_gather.14.side_ref), custom_call_target="tpu_custom_call" | custom-call | flops 536870912 | bytes 18350080 | tf_op jit(solution)/shard_map/pallas_call | solution.py:103
  290.7 5.1 %all-to-all-start.6 = ((f32[8,8,32,128]{3,2,1,0:T(8,128)}), f32[8,8,32,128]{3,2,1,0:T(8,128)S(1)}, u32[]{:S(2)}, u32[]{:S(2)}) async-start(f32[8,8,32,128]{3,2,1,0:T(8,128)} %bitcast.140), calls=%async_computation.10 | async-start | bytes 2097152 | tf_op jit(solution)/shard_map/all_to_all | solution.py:123
  295.8 15.0 %reduce-scatter.11.cloned.1.call-done = f32[16,32,128]{2,1,0:T(8,128)} async-done(((f32[64,32,128]{2,1,0:T(8,128)}), f32[16,32,128]{2,1,0:T(8,128)}) %reduce-scatter.11.cloned.1.call-update) | async-done | bytes 262160 | tf_op jit(solution)/shard_map/reduce_scatter | solution.py:183
  310.8 1.0 divide_convert_fusion
  311.8 16.4 %all_gather.15.side_ref = bf16[64,32,128]{2,1,0:T(8,128)(2,1)} all-gather(bf16[16,32,128]{2,1,0:T(8,128)(2,1)S(1)} %divide_convert_fusion), channel_id=1, replica_groups=mesh['doc'=8,'term'=4] {'term'}, dimensions={0}, use_global_device_ids=true | all-gather | bytes 655360 | tf_op jit(solution)/shard_map/all_gather | solution.py:184
  328.2 5.8 %shard_map.91 = f32[64,32,128]{2,1,0:T(8,128)} custom-call(s32[512]{0:T(512)} %bitcast.172, s32[512]{0:T(512)} %bitcast.178, s32[1]{0:T(128)} %bitcast.130.cnt_ref, bf16[512,128,128]{2,1,0:T(8,128)(2,1)} %bitcast.136, bf16[64,32,128]{2,1,0:T(8,128)(2,1)} %all_gather.15.side_ref), custom_call_target="tpu_custom_call" | custom-call | flops 536870912 | bytes 18350080 | tf_op jit(solution)/shard_map/pallas_call | solution.py:103
  334.1 5.3 %all-to-all-start.7 = ((f32[8,8,32,128]{3,2,1,0:T(8,128)}), f32[8,8,32,128]{3,2,1,0:T(8,128)S(1)}, u32[]{:S(2)}, u32[]{:S(2)}) async-start(f32[8,8,32,128]{3,2,1,0:T(8,128)} %bitcast.138), calls=%async_computation.11 | async-start | bytes 2097152 | tf_op jit(solution)/shard_map/all_to_all | solution.py:123
  340.3 14.5 %all-to-all-done.7 = f32[8,8,32,128]{3,2,1,0:T(8,128)S(1)} async-done(((f32[8,8,32,128]{3,2,1,0:T(8,128)}), f32[8,8,32,128]{3,2,1,0:T(8,128)S(1)}, u32[]{:S(2)}, u32[]{:S(2)}) %all-to-all-start.7) | async-done | bytes 1048608 | tf_op jit(solution)/shard_map/all_to_all | solution.py:123
  356.1 0.7 concatenate.19
  357.0 12.0 %all_to_all.57 = f32[4,1,12545]{2,1,0:T(1,128)S(1)} all-to-all(f32[4,1,12545]{2,1,0:T(1,128)S(1)} %broadcast_in_dim.17), channel_id=1, replica_groups=mesh['doc'=8,'term'=4] {'term'}, dimensions={0} | all-to-all | bytes 401440 | tf_op jit(solution)/shard_map/all_to_all | solution.py:128
  369.3 11.1 %all_to_all.58 = f32[8,1,12545]{2,1,0:T(1,128)S(1)} all-to-all(f32[8,1,12545]{2,1,0:T(1,128)S(1)} %broadcast_in_dim.18), channel_id=1, replica_groups=mesh['doc'=8,'term'=4] {'doc'}, dimensions={0} | all-to-all | bytes 802880 | tf_op jit(solution)/shard_map/all_to_all | solution.py:128
  381.9 0.7 fusion.36
  383.0 0.7 divide_subtract_fusion
  383.7 5.8 %cholesky.56 = f32[64,64]{1,0:T(8,128)S(1)} custom-call(f32[64,64]{1,0:T(8,128)S(1)} %divide_subtract_fusion), custom_call_target="Cholesky" | custom-call | tf_op jit(solution)/shard_map/jit(cholesky)/cholesky | solution.py:206
  390.9 4.9 %custom-call.9 = f32[1,64,64]{1,2,0:T(8,128)S(1)} custom-call(f32[1,64,64]{2,1,0:T(8,128)S(1)} %fusion.28), custom_call_target="InvertDiagBlocksLowerTriangular" | custom-call | tf_op jit(solution)/shard_map/jit(_solve_triangular)/triangular_solve | solution.py:219
  397.3 0.7 broadcast_in_dim_reshape.7
  398.2 0.7 fusion.2
  399.3 0.9 broadcast_in_dim_reshape.6
  (75 shorter events, 12.2 us)
Async XLA Ops:
  9.4 20.6 %all-to-all-start = ((bf16[8,8,64,128]{3,2,1,0:T(8,128)(2,1)}), bf16[8,8,64,128]{3,2,1,0:T(8,128)(2,1)S(1)}, u32[]{:S(2)}, u32[]{:S(2)}) async-start(bf16[8,8,64,128]{3,2,1,0:T(8,128)(2,1)} %broadcast_in_dim.13), calls=%async_computation | async-start | bytes 2097152 | tf_op jit(solution)/shard_map/all_to_all | solution.py:133
  14.5 67.5 %reduce-scatter.5.cloned.1.call-start = ((), (), s32[]{:S(2)}) async-start(), calls=%async_computation.14 | async-start | bytes 1638400 | tf_op jit(solution)/shard_map/reduce_scatter | solution.py:177
  29.9 1.0 copy-start
  38.8 87.1 %reduce-scatter.7.cloned.1.call-start = ((), (), s32[]{:S(2)}) async-start(), calls=%async_computation.15 | async-start | bytes 1310720 | tf_op jit(solution)/shard_map/reduce_scatter | solution.py:183
  106.4 42.8 %all-to-all-start.1 = ((f32[8,8,40,128]{3,2,1,0:T(8,128)}), f32[8,8,40,128]{3,2,1,0:T(8,128)S(1)}, u32[]{:S(2)}, u32[]{:S(2)}) async-start(f32[8,8,40,128]{3,2,1,0:T(8,128)} %bitcast.137), calls=%async_computation.2 | async-start | bytes 2621440 | tf_op jit(solution)/shard_map/all_to_all | solution.py:123
  149.1 20.6 %all-to-all-start.2 = ((f32[8,8,32,128]{3,2,1,0:T(8,128)}), f32[8,8,32,128]{3,2,1,0:T(8,128)S(1)}, u32[]{:S(2)}, u32[]{:S(2)}) async-start(f32[8,8,32,128]{3,2,1,0:T(8,128)} %bitcast.139), calls=%async_computation.4 | async-start | bytes 2097152 | tf_op jit(solution)/shard_map/all_to_all | solution.py:123
  154.3 113.0 %reduce-scatter.9.cloned.1.call-start = ((), (), s32[]{:S(2)}) async-start(), calls=%async_computation.16 | async-start | bytes 1310720 | tf_op jit(solution)/shard_map/reduce_scatter | solution.py:177
  232.0 78.8 %reduce-scatter.11.cloned.1.call-start = ((), (), s32[]{:S(2)}) async-start(), calls=%async_computation.17 | async-start | bytes 1310720 | tf_op jit(solution)/shard_map/reduce_scatter | solution.py:183
  290.7 43.3 %all-to-all-start.6 = ((f32[8,8,32,128]{3,2,1,0:T(8,128)}), f32[8,8,32,128]{3,2,1,0:T(8,128)S(1)}, u32[]{:S(2)}, u32[]{:S(2)}) async-start(f32[8,8,32,128]{3,2,1,0:T(8,128)} %bitcast.140), calls=%async_computation.10 | async-start | bytes 2097152 | tf_op jit(solution)/shard_map/all_to_all | solution.py:123
  334.0 5.3 %copy-start.4 = (s32[1,1024]{1,0:T(1,128)S(1)}, s32[1,1024]{1,0:T(1,128)}, u32[]{:S(2)}) copy-start(s32[1,1024]{1,0:T(1,128)} %param.16) | copy-start | bytes 12292
  334.0 5.4 %copy-start.3 = (s32[1,2048]{1,0:T(1,128)S(1)}, s32[1,2048]{1,0:T(1,128)}, u32[]{:S(2)}) copy-start(s32[1,2048]{1,0:T(1,128)} %param.15) | copy-start | bytes 24580
  334.0 5.7 %copy-start.1 = (f32[16,32,128]{2,1,0:T(8,128)S(1)}, f32[16,32,128]{2,1,0:T(8,128)}, u32[]{:S(2)}) copy-start(f32[16,32,128]{2,1,0:T(8,128)} %reduce-scatter.9.cloned.1.call-done) | copy-start | bytes 786436
  334.0 5.7 %copy-start.2 = (f32[16,32,128]{2,1,0:T(8,128)S(1)}, f32[16,32,128]{2,1,0:T(8,128)}, u32[]{:S(2)}) copy-start(f32[16,32,128]{2,1,0:T(8,128)} %reduce-scatter.11.cloned.1.call-done) | copy-start | bytes 786436
  334.1 20.7 %all-to-all-start.7 = ((f32[8,8,32,128]{3,2,1,0:T(8,128)}), f32[8,8,32,128]{3,2,1,0:T(8,128)S(1)}, u32[]{:S(2)}, u32[]{:S(2)}) async-start(f32[8,8,32,128]{3,2,1,0:T(8,128)} %bitcast.138), calls=%async_computation.11 | async-start | bytes 2097152 | tf_op jit(solution)/shard_map/all_to_all | solution.py:123
Sparse Core Ops, SparseCore 0:
  39.0 42.9 reduce-scatter.4
  100.4 25.4 reduce-scatter.6
  232.1 35.1 reduce-scatter.8
  284.9 25.8 reduce-scatter.10

commit v18 on v17

--- a/solution.py
+++ b/solution.py
@@ -10,7 +10,7 @@
 CLUSTERS = 64
 ITERS = 2
 CHUNK = 128
-GROUP = 16
+GROUP = 32
 DEG_ROWS = 8
 
 HIGH = lax.Precision.HIGHEST

time: 409 us -> 403 us (0.985)
  Pallas kernels: 39.3 us -> 72.2 us
  waiting for transfers between devices: 152 us -> 125 us
  starting transfers between devices: 26.2 us -> 19.9 us
  blocking collectives: 126 us -> 121 us
    pallas_call x6, Pallas kernels: 39.3 us -> 72.2 us  [tile_pass(): pl.pallas_call(kernel, out_shape=[jax.ShapeDtypeStruct(shape, jnp.float32...]
    reduce_scatter x2, waiting for transfers between devices: 78.4 us -> 57.3 us  [per_device(): own_a = lax.psum_scatter(left_a, 'term', scatter_dimension=0, tiled=True)]
    all_to_all x4, starting transfers between devices: 20.9 us -> 14.6 us  [scatter_sum(): return jnp.sum(lax.all_to_all(pieces, axis_name, 0, 0, tiled=False), axis=0)]
    reduce_scatter x2, waiting for transfers between devices: 29.2 us -> 23.6 us  [per_device(): summed_b = lax.psum_scatter(left_b, 'term', scatter_dimension=0, tiled=True)]
    all_to_all x4, blocking collectives: 42 us -> 36.7 us  [exchange_sum(): return jnp.sum(lax.all_to_all(copies, axis_name, 0, 0, tiled=False), axis=0)]
  transfers between devices with their start and end apart: 9 -> 9, of which waited for: 7 -> 7; matrix products, arithmetic and copies ran while one was open for 1% -> 1% of each run, Pallas kernels for 6% -> 10%
where the time goes in v18:
time: 403 us; the launch traced here: 401 us
  waiting for transfers between devices  125 us (31%)
  blocking collectives  121 us (30%)
  Pallas kernels  72.2 us (18%)
  other arithmetic  33.6 us (8%)
  starting transfers between devices  19.9 us (5%)
  between operations  15.4 us (4%)
  local copies, waits for them, and re-layouts  10 us (2%)
  matrix products  4.52 us (1%)
    pallas_call x6, Pallas kernels, tile_pass(): pl.pallas_call(kernel, out_shape=[jax.ShapeDtypeStruct(shape, jnp.float32...  72.2 us
    reduce_scatter x2, waiting for transfers between devices, per_device(): own_a = lax.psum_scatter(left_a, 'term', scatter_dimension=0, tiled=True)  57.3 us
    all_to_all x4, blocking collectives, exchange_sum(): return jnp.sum(lax.all_to_all(copies, axis_name, 0, 0, tiled=False), axis=0)  36.7 us
    all_gather x2, blocking collectives, per_device(): lax.all_gather((summed_a / doc_degree[:, None, :]).astype(jnp.bfloat16),...  32.8 us
    all_gather x2, blocking collectives, per_device(): lax.all_gather((summed_b / doc_degree[:, None, :]).astype(jnp.bfloat16),...  32.8 us
    all_to_all x4, waiting for transfers between devices, scatter_sum(): return jnp.sum(lax.all_to_all(pieces, axis_name, 0, 0, tiled=False), axis=0)  29 us
    reduce_scatter x2, waiting for transfers between devices, per_device(): summed_b = lax.psum_scatter(left_b, 'term', scatter_dimension=0, tiled=True)  23.6 us
    all_to_all x1, blocking collectives, exchange_gather(): got = lax.all_to_all(copies, axis_name, 0, 0, tiled=False)  18.5 us
  transfers between devices with their start and end apart: 9, of which 7 were waited for; matrix products, arithmetic and copies ran while one was open for 1% of the time, Pallas kernels for 10%

profile of v18, /device:TPU:0, one launch (start us, length us, event | category | flops | bytes accessed | tf_op | source)
XLA Modules:
  0.0 401.2 jit_solution(13184872759112165874)
XLA Ops:
  7.2 0.9 copy.89
  8.1 1.2 broadcast_in_dim.13
  9.4 5.2 %all-to-all-start = ((bf16[8,8,64,128]{3,2,1,0:T(8,128)(2,1)}), bf16[8,8,64,128]{3,2,1,0:T(8,128)(2,1)S(1)}, u32[]{:S(2)}, u32[]{:S(2)}) async-start(bf16[8,8,64,128]{3,2,1,0:T(8,128)(2,1)} %broadcast_in_dim.13), calls=%async_computation | async-start | bytes 2097152 | tf_op jit(solution)/shard_map/all_to_all | solution.py:133
  15.2 14.7 %all-to-all-done = bf16[8,8,64,128]{3,2,1,0:T(8,128)(2,1)S(1)} async-done(((bf16[8,8,64,128]{3,2,1,0:T(8,128)(2,1)}), bf16[8,8,64,128]{3,2,1,0:T(8,128)(2,1)S(1)}, u32[]{:S(2)}, u32[]{:S(2)}) %all-to-all-start) | async-done | bytes 1048608 | tf_op jit(solution)/shard_map/all_to_all | solution.py:133
  29.9 1.0 copy-done
  30.9 16.0 %shard_map.86 = (f32[64,40,128]{2,1,0:T(8,128)}, f32[64,32,128]{2,1,0:T(8,128)}) custom-call(s32[512]{0:T(512)} %bitcast.167, s32[512]{0:T(512)} %bitcast.173, s32[1]{0:T(128)} %bitcast.125.cnt_ref, bf16[512,128,128]{2,1,0:T(8,128)(2,1)} %bitcast.131, bf16[64,64,128]{2,1,0:T(8,128)(2,1)} %bitcast.141), custom_call_target="tpu_custom_call" | custom-call | flops 1207959552 | bytes 20185088 | tf_op jit(solution)/shard_map/pallas_call | solution.py:103
  47.0 31.7 %reduce-scatter.5.cloned.1.call-done = f32[16,40,128]{2,1,0:T(8,128)} async-done(((f32[64,40,128]{2,1,0:T(8,128)}), f32[16,40,128]{2,1,0:T(8,128)}) %reduce-scatter.5.cloned.1.call-update) | async-done | bytes 327696 | tf_op jit(solution)/shard_map/reduce_scatter | solution.py:177
  78.7 0.8 slice.75
  79.5 1.0 fusion.19
  80.5 16.4 %all_gather.12.side_ref = bf16[64,32,128]{2,1,0:T(8,128)(2,1)} all-gather(bf16[16,32,128]{2,1,0:T(8,128)(2,1)S(1)} %fusion.19), channel_id=1, replica_groups=mesh['doc'=8,'term'=4] {'term'}, dimensions={0}, use_global_device_ids=true | all-gather | bytes 655360 | tf_op jit(solution)/shard_map/all_gather | solution.py:181
  96.9 10.4 %shard_map.87 = f32[64,40,128]{2,1,0:T(8,128)} custom-call(s32[512]{0:T(512)} %bitcast.168, s32[512]{0:T(512)} %bitcast.174, s32[1]{0:T(128)} %bitcast.126.cnt_ref, bf16[512,128,128]{2,1,0:T(8,128)(2,1)} %bitcast.132, bf16[64,32,128]{2,1,0:T(8,128)(2,1)} %all_gather.12.side_ref), custom_call_target="tpu_custom_call" | custom-call | flops 671088640 | bytes 18612224 | tf_op jit(solution)/shard_map/pallas_call | solution.py:103
  107.4 3.6 all-to-all-start.1
  111.0 11.6 %reduce-scatter.7.cloned.1.call-done = f32[16,32,128]{2,1,0:T(8,128)} async-done(((f32[64,32,128]{2,1,0:T(8,128)}), f32[16,32,128]{2,1,0:T(8,128)}) %reduce-scatter.7.cloned.1.call-update) | async-done | bytes 262160 | tf_op jit(solution)/shard_map/reduce_scatter | solution.py:183
  122.6 1.0 divide_convert_fusion.2
  123.6 16.4 %all_gather.13.side_ref = bf16[64,32,128]{2,1,0:T(8,128)(2,1)} all-gather(bf16[16,32,128]{2,1,0:T(8,128)(2,1)S(1)} %divide_convert_fusion.2), channel_id=1, replica_groups=mesh['doc'=8,'term'=4] {'term'}, dimensions={0}, use_global_device_ids=true | all-gather | bytes 655360 | tf_op jit(solution)/shard_map/all_gather | solution.py:184
  140.0 10.1 %shard_map.88 = f32[64,32,128]{2,1,0:T(8,128)} custom-call(s32[512]{0:T(512)} %bitcast.169, s32[512]{0:T(512)} %bitcast.175, s32[1]{0:T(128)} %bitcast.127.cnt_ref, bf16[512,128,128]{2,1,0:T(8,128)(2,1)} %bitcast.133, bf16[64,32,128]{2,1,0:T(8,128)(2,1)} %all_gather.13.side_ref), custom_call_target="tpu_custom_call" | custom-call | flops 536870912 | bytes 18350080 | tf_op jit(solution)/shard_map/pallas_call | solution.py:103
  150.1 3.6 all-to-all-start.2
  154.4 14.6 %all-to-all-done.2 = f32[8,8,32,128]{3,2,1,0:T(8,128)S(1)} async-done(((f32[8,8,32,128]{3,2,1,0:T(8,128)}), f32[8,8,32,128]{3,2,1,0:T(8,128)S(1)}, u32[]{:S(2)}, u32[]{:S(2)}) %all-to-all-start.2) | async-done | bytes 1048608 | tf_op jit(solution)/shard_map/all_to_all | solution.py:123
  170.0 0.7 concatenate.16
  170.7 8.1 %all_to_all.54 = f32[4,1,4225]{2,1,0:T(1,128)S(1)} all-to-all(f32[4,1,4225]{2,1,0:T(1,128)S(1)} %broadcast_in_dim.14), channel_id=1, replica_groups=mesh['doc'=8,'term'=4] {'term'}, dimensions={0} | all-to-all | bytes 135200 | tf_op jit(solution)/shard_map/all_to_all | solution.py:128
  179.0 8.0 %all_to_all.55 = f32[8,1,4225]{2,1,0:T(1,128)S(1)} all-to-all(f32[8,1,4225]{2,1,0:T(1,128)S(1)} %broadcast_in_dim.15), channel_id=1, replica_groups=mesh['doc'=8,'term'=4] {'doc'}, dimensions={0} | all-to-all | bytes 270400 | tf_op jit(solution)/shard_map/all_to_all | solution.py:128
  188.5 0.8 divide_subtract_fusion.1
  189.3 5.8 %cholesky.45 = f32[64,64]{1,0:T(8,128)S(1)} custom-call(f32[64,64]{1,0:T(8,128)S(1)} %divide_subtract_fusion.1), custom_call_target="Cholesky" | custom-call | tf_op jit(solution)/shard_map/jit(cholesky)/cholesky | solution.py:206
  195.2 0.7 compare_reduce_fusion.1
  196.6 4.9 %custom-call.11 = f32[1,64,64]{1,2,0:T(8,128)S(1)} custom-call(f32[1,64,64]{2,1,0:T(8,128)S(1)} %fusion.27), custom_call_target="InvertDiagBlocksLowerTriangular" | custom-call | tf_op jit(solution)/shard_map/jit(_solve_triangular)/triangular_solve | solution.py:209
  202.3 18.5 %all_to_all.56 = bf16[8,8,64,128]{3,2,1,0:T(8,128)(2,1)} all-to-all(bf16[8,8,64,128]{3,2,1,0:T(8,128)(2,1)S(1)} %broadcast_in_dim.16), channel_id=1, replica_groups=mesh['doc'=8,'term'=4] {'doc'}, dimensions={0} | all-to-all | bytes 2097152 | tf_op jit(solution)/shard_map/all_to_all | solution.py:133
  220.7 15.5 %shard_map.89 = (f32[64,32,128]{2,1,0:T(8,128)}, f32[64,32,128]{2,1,0:T(8,128)}) custom-call(s32[512]{0:T(512)} %bitcast.170, s32[512]{0:T(512)} %bitcast.176, s32[1]{0:T(128)} %bitcast.128.cnt_ref, bf16[512,128,128]{2,1,0:T(8,128)(2,1)} %bitcast.134, bf16[64,64,128]{2,1,0:T(8,128)(2,1)} %bitcast.142), custom_call_target="tpu_custom_call" | custom-call | flops 1073741824 | bytes 19922944 | tf_op jit(solution)/shard_map/pallas_call | solution.py:103
  236.4 25.6 %reduce-scatter.9.cloned.1.call-done = f32[16,32,128]{2,1,0:T(8,128)} async-done(((f32[64,32,128]{2,1,0:T(8,128)}), f32[16,32,128]{2,1,0:T(8,128)}) %reduce-scatter.9.cloned.1.call-update) | async-done | bytes 262160 | tf_op jit(solution)/shard_map/reduce_scatter | solution.py:177
  262.0 1.0 divide_convert_fusion.1
  263.0 16.4 %all_gather.14.side_ref = bf16[64,32,128]{2,1,0:T(8,128)(2,1)} all-gather(bf16[16,32,128]{2,1,0:T(8,128)(2,1)S(1)} %divide_convert_fusion.1), channel_id=1, replica_groups=mesh['doc'=8,'term'=4] {'term'}, dimensions={0}, use_global_device_ids=true | all-gather | bytes 655360 | tf_op jit(solution)/shard_map/all_gather | solution.py:181
  279.4 10.1 %shard_map.90 = f32[64,32,128]{2,1,0:T(8,128)} custom-call(s32[512]{0:T(512)} %bitcast.171, s32[512]{0:T(512)} %bitcast.177, s32[1]{0:T(128)} %bitcast.129.cnt_ref, bf16[512,128,128]{2,1,0:T(8,128)(2,1)} %bitcast.135, bf16[64,32,128]{2,1,0:T(8,128)(2,1)} %all_gather.14.side_ref), custom_call_target="tpu_custom_call" | custom-call | flops 536870912 | bytes 18350080 | tf_op jit(solution)/shard_map/pallas_call | solution.py:103
  289.5 3.6 all-to-all-start.6
  293.1 12.0 %reduce-scatter.11.cloned.1.call-done = f32[16,32,128]{2,1,0:T(8,128)} async-done(((f32[64,32,128]{2,1,0:T(8,128)}), f32[16,32,128]{2,1,0:T(8,128)}) %reduce-scatter.11.cloned.1.call-update) | async-done | bytes 262160 | tf_op jit(solution)/shard_map/reduce_scatter | solution.py:183
  305.0 1.0 divide_convert_fusion
  306.0 16.4 %all_gather.15.side_ref = bf16[64,32,128]{2,1,0:T(8,128)(2,1)} all-gather(bf16[16,32,128]{2,1,0:T(8,128)(2,1)S(1)} %divide_convert_fusion), channel_id=1, replica_groups=mesh['doc'=8,'term'=4] {'term'}, dimensions={0}, use_global_device_ids=true | all-gather | bytes 655360 | tf_op jit(solution)/shard_map/all_gather | solution.py:184
  322.4 10.1 %shard_map.91 = f32[64,32,128]{2,1,0:T(8,128)} custom-call(s32[512]{0:T(512)} %bitcast.172, s32[512]{0:T(512)} %bitcast.178, s32[1]{0:T(128)} %bitcast.130.cnt_ref, bf16[512,128,128]{2,1,0:T(8,128)(2,1)} %bitcast.136, bf16[64,32,128]{2,1,0:T(8,128)(2,1)} %all_gather.15.side_ref), custom_call_target="tpu_custom_call" | custom-call | flops 536870912 | bytes 18350080 | tf_op jit(solution)/shard_map/pallas_call | solution.py:103
  332.5 3.9 all-to-all-start.7
  337.4 14.4 %all-to-all-done.7 = f32[8,8,32,128]{3,2,1,0:T(8,128)S(1)} async-done(((f32[8,8,32,128]{3,2,1,0:T(8,128)}), f32[8,8,32,128]{3,2,1,0:T(8,128)S(1)}, u32[]{:S(2)}, u32[]{:S(2)}) %all-to-all-start.7) | async-done | bytes 1048608 | tf_op jit(solution)/shard_map/all_to_all | solution.py:123
  353.1 0.7 concatenate.19
  354.0 9.2 %all_to_all.57 = f32[4,1,12545]{2,1,0:T(1,128)S(1)} all-to-all(f32[4,1,12545]{2,1,0:T(1,128)S(1)} %broadcast_in_dim.17), channel_id=1, replica_groups=mesh['doc'=8,'term'=4] {'term'}, dimensions={0} | all-to-all | bytes 401440 | tf_op jit(solution)/shard_map/all_to_all | solution.py:128
  363.6 11.3 %all_to_all.58 = f32[8,1,12545]{2,1,0:T(1,128)S(1)} all-to-all(f32[8,1,12545]{2,1,0:T(1,128)S(1)} %broadcast_in_dim.18), channel_id=1, replica_groups=mesh['doc'=8,'term'=4] {'doc'}, dimensions={0} | all-to-all | bytes 802880 | tf_op jit(solution)/shard_map/all_to_all | solution.py:128
  376.4 0.7 fusion.36
  377.5 0.7 divide_subtract_fusion
  378.2 5.8 %cholesky.56 = f32[64,64]{1,0:T(8,128)S(1)} custom-call(f32[64,64]{1,0:T(8,128)S(1)} %divide_subtract_fusion), custom_call_target="Cholesky" | custom-call | tf_op jit(solution)/shard_map/jit(cholesky)/cholesky | solution.py:206
  385.4 4.9 %custom-call.9 = f32[1,64,64]{1,2,0:T(8,128)S(1)} custom-call(f32[1,64,64]{2,1,0:T(8,128)S(1)} %fusion.28), custom_call_target="InvertDiagBlocksLowerTriangular" | custom-call | tf_op jit(solution)/shard_map/jit(_solve_triangular)/triangular_solve | solution.py:219
  391.8 0.7 broadcast_in_dim_reshape.7
  392.7 0.7 fusion.2
  393.8 0.9 broadcast_in_dim_reshape.6
  (75 shorter events, 12.2 us)
Async XLA Ops:
  9.4 20.6 %all-to-all-start = ((bf16[8,8,64,128]{3,2,1,0:T(8,128)(2,1)}), bf16[8,8,64,128]{3,2,1,0:T(8,128)(2,1)S(1)}, u32[]{:S(2)}, u32[]{:S(2)}) async-start(bf16[8,8,64,128]{3,2,1,0:T(8,128)(2,1)} %broadcast_in_dim.13), calls=%async_computation | async-start | bytes 2097152 | tf_op jit(solution)/shard_map/all_to_all | solution.py:133
  14.5 64.1 %reduce-scatter.5.cloned.1.call-start = ((), (), s32[]{:S(2)}) async-start(), calls=%async_computation.14 | async-start | bytes 1638400 | tf_op jit(solution)/shard_map/reduce_scatter | solution.py:177
  29.9 1.0 copy-start
  46.9 75.7 %reduce-scatter.7.cloned.1.call-start = ((), (), s32[]{:S(2)}) async-start(), calls=%async_computation.15 | async-start | bytes 1310720 | tf_op jit(solution)/shard_map/reduce_scatter | solution.py:183
  107.4 42.7 %all-to-all-start.1 = ((f32[8,8,40,128]{3,2,1,0:T(8,128)}), f32[8,8,40,128]{3,2,1,0:T(8,128)S(1)}, u32[]{:S(2)}, u32[]{:S(2)}) async-start(f32[8,8,40,128]{3,2,1,0:T(8,128)} %bitcast.137), calls=%async_computation.2 | async-start | bytes 2621440 | tf_op jit(solution)/shard_map/all_to_all | solution.py:123
  150.1 18.9 %all-to-all-start.2 = ((f32[8,8,32,128]{3,2,1,0:T(8,128)}), f32[8,8,32,128]{3,2,1,0:T(8,128)S(1)}, u32[]{:S(2)}, u32[]{:S(2)}) async-start(f32[8,8,32,128]{3,2,1,0:T(8,128)} %bitcast.139), calls=%async_computation.4 | async-start | bytes 2097152 | tf_op jit(solution)/shard_map/all_to_all | solution.py:123
  153.6 108.3 %reduce-scatter.9.cloned.1.call-start = ((), (), s32[]{:S(2)}) async-start(), calls=%async_computation.16 | async-start | bytes 1310720 | tf_op jit(solution)/shard_map/reduce_scatter | solution.py:177
  236.3 68.7 %reduce-scatter.11.cloned.1.call-start = ((), (), s32[]{:S(2)}) async-start(), calls=%async_computation.17 | async-start | bytes 1310720 | tf_op jit(solution)/shard_map/reduce_scatter | solution.py:183
  289.5 43.0 %all-to-all-start.6 = ((f32[8,8,32,128]{3,2,1,0:T(8,128)}), f32[8,8,32,128]{3,2,1,0:T(8,128)S(1)}, u32[]{:S(2)}, u32[]{:S(2)}) async-start(f32[8,8,32,128]{3,2,1,0:T(8,128)} %bitcast.140), calls=%async_computation.10 | async-start | bytes 2097152 | tf_op jit(solution)/shard_map/all_to_all | solution.py:123
  332.5 3.9 copy-start.4
  332.5 4.1 %copy-start.3 = (s32[1,2048]{1,0:T(1,128)S(1)}, s32[1,2048]{1,0:T(1,128)}, u32[]{:S(2)}) copy-start(s32[1,2048]{1,0:T(1,128)} %param.15) | copy-start | bytes 24580
  332.5 4.3 %copy-start.1 = (f32[16,32,128]{2,1,0:T(8,128)S(1)}, f32[16,32,128]{2,1,0:T(8,128)}, u32[]{:S(2)}) copy-start(f32[16,32,128]{2,1,0:T(8,128)} %reduce-scatter.9.cloned.1.call-done) | copy-start | bytes 786436
  332.5 4.3 %copy-start.2 = (f32[16,32,128]{2,1,0:T(8,128)S(1)}, f32[16,32,128]{2,1,0:T(8,128)}, u32[]{:S(2)}) copy-start(f32[16,32,128]{2,1,0:T(8,128)} %reduce-scatter.11.cloned.1.call-done) | copy-start | bytes 786436
  332.5 19.2 %all-to-all-start.7 = ((f32[8,8,32,128]{3,2,1,0:T(8,128)}), f32[8,8,32,128]{3,2,1,0:T(8,128)S(1)}, u32[]{:S(2)}, u32[]{:S(2)}) async-start(f32[8,8,32,128]{3,2,1,0:T(8,128)} %bitcast.138), calls=%async_computation.11 | async-start | bytes 2097152 | tf_op jit(solution)/shard_map/all_to_all | solution.py:123
Sparse Core Ops, SparseCore 0:
  47.0 31.5 reduce-scatter.4
  97.1 25.4 reduce-scatter.6
  236.4 25.4 reduce-scatter.8
  279.5 25.4 reduce-scatter.10

commit v19 on v18

--- a/solution.py
+++ b/solution.py
@@ -10,7 +10,7 @@
 CLUSTERS = 64
 ITERS = 2
 CHUNK = 128
-GROUP = 32
+GROUP = 64
 DEG_ROWS = 8
 
 HIGH = lax.Precision.HIGHEST

time: 403 us -> 396 us (0.983)
  Pallas kernels: 72.2 us -> 59.1 us
  waiting for transfers between devices: 125 us -> 133 us
    pallas_call x6, Pallas kernels: 72.2 us -> 59.1 us  [tile_pass(): pl.pallas_call(kernel, out_shape=[jax.ShapeDtypeStruct(shape, jnp.float32...]
    reduce_scatter x2, waiting for transfers between devices: 57.3 us -> 61.9 us  [per_device(): own_a = lax.psum_scatter(left_a, 'term', scatter_dimension=0, tiled=True)]
  transfers between devices with their start and end apart: 9 -> 9, of which waited for: 7 -> 7; matrix products, arithmetic and copies ran while one was open for 1% -> 1% of each run, Pallas kernels for 10% -> 9%
where the time goes in v19:
time: 396 us
  waiting for transfers between devices  133 us (34%)
  blocking collectives  121 us (31%)
  Pallas kernels  59.1 us (15%)
  other arithmetic  33.6 us (8%)
  starting transfers between devices  19.7 us (5%)
  between operations  15.4 us (4%)
  local copies, waits for them, and re-layouts  10 us (3%)
  matrix products  4.53 us (1%)
    reduce_scatter x2, waiting for transfers between devices, per_device(): own_a = lax.psum_scatter(left_a, 'term', scatter_dimension=0, tiled=True)  61.9 us
    pallas_call x6, Pallas kernels, tile_pass(): pl.pallas_call(kernel, out_shape=[jax.ShapeDtypeStruct(shape, jnp.float32...  59.1 us
    all_to_all x4, blocking collectives, exchange_sum(): return jnp.sum(lax.all_to_all(copies, axis_name, 0, 0, tiled=False), axis=0)  36.9 us
    all_gather x2, blocking collectives, per_device(): lax.all_gather((summed_b / doc_degree[:, None, :]).astype(jnp.bfloat16),...  32.9 us
    all_gather x2, blocking collectives, per_device(): lax.all_gather((summed_a / doc_degree[:, None, :]).astype(jnp.bfloat16),...  32.8 us
    all_to_all x4, waiting for transfers between devices, scatter_sum(): return jnp.sum(lax.all_to_all(pieces, axis_name, 0, 0, tiled=False), axis=0)  29 us
    reduce_scatter x2, waiting for transfers between devices, per_device(): summed_b = lax.psum_scatter(left_b, 'term', scatter_dimension=0, tiled=True)  27.1 us
    all_to_all x1, blocking collectives, exchange_gather(): got = lax.all_to_all(copies, axis_name, 0, 0, tiled=False)  18.5 us
  transfers between devices with their start and end apart: 9, of which 7 were waited for; matrix products, arithmetic and copies ran while one was open for 1% of the time, Pallas kernels for 9%

profile of v19, /device:TPU:0, one launch (start us, length us, event | category | flops | bytes accessed | tf_op | source)
XLA Modules:
  0.0 396.3 jit_solution(17978720513841602602)
XLA Ops:
  7.2 0.9 copy.89
  8.1 1.2 broadcast_in_dim.13
  9.4 5.2 %all-to-all-start = ((bf16[8,8,64,128]{3,2,1,0:T(8,128)(2,1)}), bf16[8,8,64,128]{3,2,1,0:T(8,128)(2,1)S(1)}, u32[]{:S(2)}, u32[]{:S(2)}) async-start(bf16[8,8,64,128]{3,2,1,0:T(8,128)(2,1)} %broadcast_in_dim.13), calls=%async_computation | async-start | bytes 2097152 | tf_op jit(solution)/shard_map/all_to_all | solution.py:133
  15.2 14.7 %all-to-all-done = bf16[8,8,64,128]{3,2,1,0:T(8,128)(2,1)S(1)} async-done(((bf16[8,8,64,128]{3,2,1,0:T(8,128)(2,1)}), bf16[8,8,64,128]{3,2,1,0:T(8,128)(2,1)S(1)}, u32[]{:S(2)}, u32[]{:S(2)}) %all-to-all-start) | async-done | bytes 1048608 | tf_op jit(solution)/shard_map/all_to_all | solution.py:133
  29.9 1.0 copy-done
  30.9 12.8 %shard_map.86 = (f32[64,40,128]{2,1,0:T(8,128)}, f32[64,32,128]{2,1,0:T(8,128)}) custom-call(s32[512]{0:T(512)} %bitcast.167, s32[512]{0:T(512)} %bitcast.173, s32[1]{0:T(128)} %bitcast.125.cnt_ref, bf16[512,128,128]{2,1,0:T(8,128)(2,1)} %bitcast.131, bf16[64,64,128]{2,1,0:T(8,128)(2,1)} %bitcast.141), custom_call_target="tpu_custom_call" | custom-call | flops 1207959552 | bytes 20185088 | tf_op jit(solution)/shard_map/pallas_call | solution.py:103
  43.8 33.4 %reduce-scatter.5.cloned.1.call-done = f32[16,40,128]{2,1,0:T(8,128)} async-done(((f32[64,40,128]{2,1,0:T(8,128)}), f32[16,40,128]{2,1,0:T(8,128)}) %reduce-scatter.5.cloned.1.call-update) | async-done | bytes 327696 | tf_op jit(solution)/shard_map/reduce_scatter | solution.py:177
  77.1 0.8 slice.75
  78.0 1.0 fusion.19
  79.0 16.4 %all_gather.12.side_ref = bf16[64,32,128]{2,1,0:T(8,128)(2,1)} all-gather(bf16[16,32,128]{2,1,0:T(8,128)(2,1)S(1)} %fusion.19), channel_id=1, replica_groups=mesh['doc'=8,'term'=4] {'term'}, dimensions={0}, use_global_device_ids=true | all-gather | bytes 655360 | tf_op jit(solution)/shard_map/all_gather | solution.py:181
  95.4 8.6 %shard_map.87 = f32[64,40,128]{2,1,0:T(8,128)} custom-call(s32[512]{0:T(512)} %bitcast.168, s32[512]{0:T(512)} %bitcast.174, s32[1]{0:T(128)} %bitcast.126.cnt_ref, bf16[512,128,128]{2,1,0:T(8,128)(2,1)} %bitcast.132, bf16[64,32,128]{2,1,0:T(8,128)(2,1)} %all_gather.12.side_ref), custom_call_target="tpu_custom_call" | custom-call | flops 671088640 | bytes 18612224 | tf_op jit(solution)/shard_map/pallas_call | solution.py:103
  104.0 3.6 all-to-all-start.1
  107.6 13.5 %reduce-scatter.7.cloned.1.call-done = f32[16,32,128]{2,1,0:T(8,128)} async-done(((f32[64,32,128]{2,1,0:T(8,128)}), f32[16,32,128]{2,1,0:T(8,128)}) %reduce-scatter.7.cloned.1.call-update) | async-done | bytes 262160 | tf_op jit(solution)/shard_map/reduce_scatter | solution.py:183
  121.0 1.0 divide_convert_fusion.2
  122.0 16.4 %all_gather.13.side_ref = bf16[64,32,128]{2,1,0:T(8,128)(2,1)} all-gather(bf16[16,32,128]{2,1,0:T(8,128)(2,1)S(1)} %divide_convert_fusion.2), channel_id=1, replica_groups=mesh['doc'=8,'term'=4] {'term'}, dimensions={0}, use_global_device_ids=true | all-gather | bytes 655360 | tf_op jit(solution)/shard_map/all_gather | solution.py:184
  138.4 8.4 %shard_map.88 = f32[64,32,128]{2,1,0:T(8,128)} custom-call(s32[512]{0:T(512)} %bitcast.169, s32[512]{0:T(512)} %bitcast.175, s32[1]{0:T(128)} %bitcast.127.cnt_ref, bf16[512,128,128]{2,1,0:T(8,128)(2,1)} %bitcast.133, bf16[64,32,128]{2,1,0:T(8,128)(2,1)} %all_gather.13.side_ref), custom_call_target="tpu_custom_call" | custom-call | flops 536870912 | bytes 18350080 | tf_op jit(solution)/shard_map/pallas_call | solution.py:103
  146.8 3.6 all-to-all-start.2
  151.1 14.6 %all-to-all-done.2 = f32[8,8,32,128]{3,2,1,0:T(8,128)S(1)} async-done(((f32[8,8,32,128]{3,2,1,0:T(8,128)}), f32[8,8,32,128]{3,2,1,0:T(8,128)S(1)}, u32[]{:S(2)}, u32[]{:S(2)}) %all-to-all-start.2) | async-done | bytes 1048608 | tf_op jit(solution)/shard_map/all_to_all | solution.py:123
  166.7 0.7 concatenate.16
  167.5 8.4 %all_to_all.54 = f32[4,1,4225]{2,1,0:T(1,128)S(1)} all-to-all(f32[4,1,4225]{2,1,0:T(1,128)S(1)} %broadcast_in_dim.14), channel_id=1, replica_groups=mesh['doc'=8,'term'=4] {'term'}, dimensions={0} | all-to-all | bytes 135200 | tf_op jit(solution)/shard_map/all_to_all | solution.py:128
  176.0 8.0 %all_to_all.55 = f32[8,1,4225]{2,1,0:T(1,128)S(1)} all-to-all(f32[8,1,4225]{2,1,0:T(1,128)S(1)} %broadcast_in_dim.15), channel_id=1, replica_groups=mesh['doc'=8,'term'=4] {'doc'}, dimensions={0} | all-to-all | bytes 270400 | tf_op jit(solution)/shard_map/all_to_all | solution.py:128
  185.5 0.8 divide_subtract_fusion.1
  186.3 5.8 %cholesky.45 = f32[64,64]{1,0:T(8,128)S(1)} custom-call(f32[64,64]{1,0:T(8,128)S(1)} %divide_subtract_fusion.1), custom_call_target="Cholesky" | custom-call | tf_op jit(solution)/shard_map/jit(cholesky)/cholesky | solution.py:206
  192.2 0.7 compare_reduce_fusion.1
  193.6 4.9 %custom-call.11 = f32[1,64,64]{1,2,0:T(8,128)S(1)} custom-call(f32[1,64,64]{2,1,0:T(8,128)S(1)} %fusion.27), custom_call_target="InvertDiagBlocksLowerTriangular" | custom-call | tf_op jit(solution)/shard_map/jit(_solve_triangular)/triangular_solve | solution.py:209
  199.3 18.5 %all_to_all.56 = bf16[8,8,64,128]{3,2,1,0:T(8,128)(2,1)} all-to-all(bf16[8,8,64,128]{3,2,1,0:T(8,128)(2,1)S(1)} %broadcast_in_dim.16), channel_id=1, replica_groups=mesh['doc'=8,'term'=4] {'doc'}, dimensions={0} | all-to-all | bytes 2097152 | tf_op jit(solution)/shard_map/all_to_all | solution.py:133
  217.7 12.6 %shard_map.89 = (f32[64,32,128]{2,1,0:T(8,128)}, f32[64,32,128]{2,1,0:T(8,128)}) custom-call(s32[512]{0:T(512)} %bitcast.170, s32[512]{0:T(512)} %bitcast.176, s32[1]{0:T(128)} %bitcast.128.cnt_ref, bf16[512,128,128]{2,1,0:T(8,128)(2,1)} %bitcast.134, bf16[64,64,128]{2,1,0:T(8,128)(2,1)} %bitcast.142), custom_call_target="tpu_custom_call" | custom-call | flops 1073741824 | bytes 19922944 | tf_op jit(solution)/shard_map/pallas_call | solution.py:103
  230.4 28.5 %reduce-scatter.9.cloned.1.call-done = f32[16,32,128]{2,1,0:T(8,128)} async-done(((f32[64,32,128]{2,1,0:T(8,128)}), f32[16,32,128]{2,1,0:T(8,128)}) %reduce-scatter.9.cloned.1.call-update) | async-done | bytes 262160 | tf_op jit(solution)/shard_map/reduce_scatter | solution.py:177
  258.9 1.0 divide_convert_fusion.1
  259.9 16.4 %all_gather.14.side_ref = bf16[64,32,128]{2,1,0:T(8,128)(2,1)} all-gather(bf16[16,32,128]{2,1,0:T(8,128)(2,1)S(1)} %divide_convert_fusion.1), channel_id=1, replica_groups=mesh['doc'=8,'term'=4] {'term'}, dimensions={0}, use_global_device_ids=true | all-gather | bytes 655360 | tf_op jit(solution)/shard_map/all_gather | solution.py:181
  276.3 8.4 %shard_map.90 = f32[64,32,128]{2,1,0:T(8,128)} custom-call(s32[512]{0:T(512)} %bitcast.171, s32[512]{0:T(512)} %bitcast.177, s32[1]{0:T(128)} %bitcast.129.cnt_ref, bf16[512,128,128]{2,1,0:T(8,128)(2,1)} %bitcast.135, bf16[64,32,128]{2,1,0:T(8,128)(2,1)} %all_gather.14.side_ref), custom_call_target="tpu_custom_call" | custom-call | flops 536870912 | bytes 18350080 | tf_op jit(solution)/shard_map/pallas_call | solution.py:103
  284.8 3.6 all-to-all-start.6
  288.3 13.6 %reduce-scatter.11.cloned.1.call-done = f32[16,32,128]{2,1,0:T(8,128)} async-done(((f32[64,32,128]{2,1,0:T(8,128)}), f32[16,32,128]{2,1,0:T(8,128)}) %reduce-scatter.11.cloned.1.call-update) | async-done | bytes 262160 | tf_op jit(solution)/shard_map/reduce_scatter | solution.py:183
  301.9 1.0 divide_convert_fusion
  302.9 16.5 %all_gather.15.side_ref = bf16[64,32,128]{2,1,0:T(8,128)(2,1)} all-gather(bf16[16,32,128]{2,1,0:T(8,128)(2,1)S(1)} %divide_convert_fusion), channel_id=1, replica_groups=mesh['doc'=8,'term'=4] {'term'}, dimensions={0}, use_global_device_ids=true | all-gather | bytes 655360 | tf_op jit(solution)/shard_map/all_gather | solution.py:184
  319.4 8.4 %shard_map.91 = f32[64,32,128]{2,1,0:T(8,128)} custom-call(s32[512]{0:T(512)} %bitcast.172, s32[512]{0:T(512)} %bitcast.178, s32[1]{0:T(128)} %bitcast.130.cnt_ref, bf16[512,128,128]{2,1,0:T(8,128)(2,1)} %bitcast.136, bf16[64,32,128]{2,1,0:T(8,128)(2,1)} %all_gather.15.side_ref), custom_call_target="tpu_custom_call" | custom-call | flops 536870912 | bytes 18350080 | tf_op jit(solution)/shard_map/pallas_call | solution.py:103
  327.8 3.7 all-to-all-start.7
  332.4 14.4 %all-to-all-done.7 = f32[8,8,32,128]{3,2,1,0:T(8,128)S(1)} async-done(((f32[8,8,32,128]{3,2,1,0:T(8,128)}), f32[8,8,32,128]{3,2,1,0:T(8,128)S(1)}, u32[]{:S(2)}, u32[]{:S(2)}) %all-to-all-start.7) | async-done | bytes 1048608 | tf_op jit(solution)/shard_map/all_to_all | solution.py:123
  348.2 0.7 concatenate.19
  349.1 9.4 %all_to_all.57 = f32[4,1,12545]{2,1,0:T(1,128)S(1)} all-to-all(f32[4,1,12545]{2,1,0:T(1,128)S(1)} %broadcast_in_dim.17), channel_id=1, replica_groups=mesh['doc'=8,'term'=4] {'term'}, dimensions={0} | all-to-all | bytes 401440 | tf_op jit(solution)/shard_map/all_to_all | solution.py:128
  358.9 11.2 %all_to_all.58 = f32[8,1,12545]{2,1,0:T(1,128)S(1)} all-to-all(f32[8,1,12545]{2,1,0:T(1,128)S(1)} %broadcast_in_dim.18), channel_id=1, replica_groups=mesh['doc'=8,'term'=4] {'doc'}, dimensions={0} | all-to-all | bytes 802880 | tf_op jit(solution)/shard_map/all_to_all | solution.py:128
  371.5 0.7 fusion.36
  372.5 0.7 divide_subtract_fusion
  373.3 5.8 %cholesky.56 = f32[64,64]{1,0:T(8,128)S(1)} custom-call(f32[64,64]{1,0:T(8,128)S(1)} %divide_subtract_fusion), custom_call_target="Cholesky" | custom-call | tf_op jit(solution)/shard_map/jit(cholesky)/cholesky | solution.py:206
  380.5 4.9 %custom-call.9 = f32[1,64,64]{1,2,0:T(8,128)S(1)} custom-call(f32[1,64,64]{2,1,0:T(8,128)S(1)} %fusion.28), custom_call_target="InvertDiagBlocksLowerTriangular" | custom-call | tf_op jit(solution)/shard_map/jit(_solve_triangular)/triangular_solve | solution.py:219
  386.9 0.7 broadcast_in_dim_reshape.7
  387.8 0.7 fusion.2
  388.8 0.9 broadcast_in_dim_reshape.6
  (75 shorter events, 12.2 us)
Async XLA Ops:
  9.4 20.6 %all-to-all-start = ((bf16[8,8,64,128]{3,2,1,0:T(8,128)(2,1)}), bf16[8,8,64,128]{3,2,1,0:T(8,128)(2,1)S(1)}, u32[]{:S(2)}, u32[]{:S(2)}) async-start(bf16[8,8,64,128]{3,2,1,0:T(8,128)(2,1)} %broadcast_in_dim.13), calls=%async_computation | async-start | bytes 2097152 | tf_op jit(solution)/shard_map/all_to_all | solution.py:133
  14.5 62.6 %reduce-scatter.5.cloned.1.call-start = ((), (), s32[]{:S(2)}) async-start(), calls=%async_computation.14 | async-start | bytes 1638400 | tf_op jit(solution)/shard_map/reduce_scatter | solution.py:177
  29.9 1.0 copy-start
  43.7 77.3 %reduce-scatter.7.cloned.1.call-start = ((), (), s32[]{:S(2)}) async-start(), calls=%async_computation.15 | async-start | bytes 1310720 | tf_op jit(solution)/shard_map/reduce_scatter | solution.py:183
  104.0 42.8 %all-to-all-start.1 = ((f32[8,8,40,128]{3,2,1,0:T(8,128)}), f32[8,8,40,128]{3,2,1,0:T(8,128)S(1)}, u32[]{:S(2)}, u32[]{:S(2)}) async-start(f32[8,8,40,128]{3,2,1,0:T(8,128)} %bitcast.137), calls=%async_computation.2 | async-start | bytes 2621440 | tf_op jit(solution)/shard_map/all_to_all | solution.py:123
  146.8 18.9 %all-to-all-start.2 = ((f32[8,8,32,128]{3,2,1,0:T(8,128)}), f32[8,8,32,128]{3,2,1,0:T(8,128)S(1)}, u32[]{:S(2)}, u32[]{:S(2)}) async-start(f32[8,8,32,128]{3,2,1,0:T(8,128)} %bitcast.139), calls=%async_computation.4 | async-start | bytes 2097152 | tf_op jit(solution)/shard_map/all_to_all | solution.py:123
  150.4 108.5 %reduce-scatter.9.cloned.1.call-start = ((), (), s32[]{:S(2)}) async-start(), calls=%async_computation.16 | async-start | bytes 1310720 | tf_op jit(solution)/shard_map/reduce_scatter | solution.py:177
  230.3 71.6 %reduce-scatter.11.cloned.1.call-start = ((), (), s32[]{:S(2)}) async-start(), calls=%async_computation.17 | async-start | bytes 1310720 | tf_op jit(solution)/shard_map/reduce_scatter | solution.py:183
  284.8 43.0 %all-to-all-start.6 = ((f32[8,8,32,128]{3,2,1,0:T(8,128)}), f32[8,8,32,128]{3,2,1,0:T(8,128)S(1)}, u32[]{:S(2)}, u32[]{:S(2)}) async-start(f32[8,8,32,128]{3,2,1,0:T(8,128)} %bitcast.140), calls=%async_computation.10 | async-start | bytes 2097152 | tf_op jit(solution)/shard_map/all_to_all | solution.py:123
  327.8 3.7 copy-start.4
  327.8 3.9 copy-start.3
  327.8 4.1 %copy-start.1 = (f32[16,32,128]{2,1,0:T(8,128)S(1)}, f32[16,32,128]{2,1,0:T(8,128)}, u32[]{:S(2)}) copy-start(f32[16,32,128]{2,1,0:T(8,128)} %reduce-scatter.9.cloned.1.call-done) | copy-start | bytes 786436
  327.8 4.1 %copy-start.2 = (f32[16,32,128]{2,1,0:T(8,128)S(1)}, f32[16,32,128]{2,1,0:T(8,128)}, u32[]{:S(2)}) copy-start(f32[16,32,128]{2,1,0:T(8,128)} %reduce-scatter.11.cloned.1.call-done) | copy-start | bytes 786436
  327.8 19.0 %all-to-all-start.7 = ((f32[8,8,32,128]{3,2,1,0:T(8,128)}), f32[8,8,32,128]{3,2,1,0:T(8,128)S(1)}, u32[]{:S(2)}, u32[]{:S(2)}) async-start(f32[8,8,32,128]{3,2,1,0:T(8,128)} %bitcast.138), calls=%async_computation.11 | async-start | bytes 2097152 | tf_op jit(solution)/shard_map/all_to_all | solution.py:123
Sparse Core Ops, SparseCore 0:
  43.8 33.2 reduce-scatter.4
  95.5 25.4 reduce-scatter.6
  230.4 28.4 reduce-scatter.8
  276.4 25.4 reduce-scatter.10

commit v20 on v19

--- a/solution.py
+++ b/solution.py
@@ -9,7 +9,7 @@
 
 CLUSTERS = 64
 ITERS = 2
-CHUNK = 128
+CHUNK = 256
 GROUP = 64
 DEG_ROWS = 8
 

time: 396 us -> 401 us (1.013); the launches traced: 396 us -> 397 us
  Pallas kernels: 59.1 us -> 44.8 us
  waiting for transfers between devices: 133 us -> 142 us
  starting transfers between devices: 19.7 us -> 25.1 us
    pallas_call x6, Pallas kernels: 59.1 us -> 44.8 us  [tile_pass(): pl.pallas_call(kernel, out_shape=[jax.ShapeDtypeStruct(shape, jnp.float32...]
    reduce_scatter x2, waiting for transfers between devices: 61.9 us -> 70.2 us  [per_device(): own_a = lax.psum_scatter(left_a, 'term', scatter_dimension=0, tiled=True)]
    all_to_all x4, starting transfers between devices: 14.4 us -> 19.8 us  [scatter_sum(): return jnp.sum(lax.all_to_all(pieces, axis_name, 0, 0, tiled=False), axis=0)]
  transfers between devices with their start and end apart: 9 -> 9, of which waited for: 7 -> 7; matrix products, arithmetic and copies ran while one was open for 1% -> 1% of each run, Pallas kernels for 9% -> 7%
where the time goes in v20:
time: 401 us; the launch traced here: 397 us
  waiting for transfers between devices  142 us (35%)
  blocking collectives  121 us (30%)
  Pallas kernels  44.8 us (11%)
  other arithmetic  33.6 us (8%)
  starting transfers between devices  25.1 us (6%)
  between operations  15.4 us (4%)
  local copies, waits for them, and re-layouts  10 us (2%)
  matrix products  4.54 us (1%)
    reduce_scatter x2, waiting for transfers between devices, per_device(): own_a = lax.psum_scatter(left_a, 'term', scatter_dimension=0, tiled=True)  70.2 us
    pallas_call x6, Pallas kernels, tile_pass(): pl.pallas_call(kernel, out_shape=[jax.ShapeDtypeStruct(shape, jnp.float32...  44.8 us
    all_to_all x4, blocking collectives, exchange_sum(): return jnp.sum(lax.all_to_all(copies, axis_name, 0, 0, tiled=False), axis=0)  37.3 us
    all_gather x2, blocking collectives, per_device(): lax.all_gather((summed_a / doc_degree[:, None, :]).astype(jnp.bfloat16),...  32.8 us
    all_gather x2, blocking collectives, per_device(): lax.all_gather((summed_b / doc_degree[:, None, :]).astype(jnp.bfloat16),...  32.8 us
    all_to_all x4, waiting for transfers between devices, scatter_sum(): return jnp.sum(lax.all_to_all(pieces, axis_name, 0, 0, tiled=False), axis=0)  29.1 us
    reduce_scatter x2, waiting for transfers between devices, per_device(): summed_b = lax.psum_scatter(left_b, 'term', scatter_dimension=0, tiled=True)  28.2 us
    all_to_all x4, starting transfers between devices, scatter_sum(): return jnp.sum(lax.all_to_all(pieces, axis_name, 0, 0, tiled=False), axis=0)  19.8 us
  transfers between devices with their start and end apart: 9, of which 7 were waited for; matrix products, arithmetic and copies ran while one was open for 1% of the time, Pallas kernels for 7%

profile of v20, /device:TPU:0, one launch (start us, length us, event | category | flops | bytes accessed | tf_op | source)
XLA Modules:
  0.0 397.1 jit_solution(5868579496147597327)
XLA Ops:
  7.2 0.9 copy.89
  8.1 1.2 broadcast_in_dim.13
  9.4 5.2 %all-to-all-start = ((bf16[8,8,64,128]{3,2,1,0:T(8,128)(2,1)}), bf16[8,8,64,128]{3,2,1,0:T(8,128)(2,1)S(1)}, u32[]{:S(2)}, u32[]{:S(2)}) async-start(bf16[8,8,64,128]{3,2,1,0:T(8,128)(2,1)} %broadcast_in_dim.13), calls=%async_computation | async-start | bytes 2097152 | tf_op jit(solution)/shard_map/all_to_all | solution.py:133
  15.2 14.7 %all-to-all-done = bf16[8,8,64,128]{3,2,1,0:T(8,128)(2,1)S(1)} async-done(((bf16[8,8,64,128]{3,2,1,0:T(8,128)(2,1)}), bf16[8,8,64,128]{3,2,1,0:T(8,128)(2,1)S(1)}, u32[]{:S(2)}, u32[]{:S(2)}) %all-to-all-start) | async-done | bytes 1048608 | tf_op jit(solution)/shard_map/all_to_all | solution.py:133
  29.9 1.0 copy-done
  30.9 9.1 %shard_map.86 = (f32[64,40,128]{2,1,0:T(8,128)}, f32[64,32,128]{2,1,0:T(8,128)}) custom-call(s32[512]{0:T(512)} %bitcast.167, s32[512]{0:T(512)} %bitcast.173, s32[1]{0:T(128)} %bitcast.125.cnt_ref, bf16[512,128,128]{2,1,0:T(8,128)(2,1)} %bitcast.131, bf16[64,64,128]{2,1,0:T(8,128)(2,1)} %bitcast.141), custom_call_target="tpu_custom_call" | custom-call | flops 1207959552 | bytes 20185088 | tf_op jit(solution)/shard_map/pallas_call | solution.py:103
  40.1 37.6 %reduce-scatter.5.cloned.1.call-done = f32[16,40,128]{2,1,0:T(8,128)} async-done(((f32[64,40,128]{2,1,0:T(8,128)}), f32[16,40,128]{2,1,0:T(8,128)}) %reduce-scatter.5.cloned.1.call-update) | async-done | bytes 327696 | tf_op jit(solution)/shard_map/reduce_scatter | solution.py:177
  77.7 0.8 slice.75
  78.6 1.0 fusion.19
  79.6 16.4 %all_gather.12.side_ref = bf16[64,32,128]{2,1,0:T(8,128)(2,1)} all-gather(bf16[16,32,128]{2,1,0:T(8,128)(2,1)S(1)} %fusion.19), channel_id=1, replica_groups=mesh['doc'=8,'term'=4] {'term'}, dimensions={0}, use_global_device_ids=true | all-gather | bytes 655360 | tf_op jit(solution)/shard_map/all_gather | solution.py:181
  96.0 6.8 %shard_map.87 = f32[64,40,128]{2,1,0:T(8,128)} custom-call(s32[512]{0:T(512)} %bitcast.168, s32[512]{0:T(512)} %bitcast.174, s32[1]{0:T(128)} %bitcast.126.cnt_ref, bf16[512,128,128]{2,1,0:T(8,128)(2,1)} %bitcast.132, bf16[64,32,128]{2,1,0:T(8,128)(2,1)} %all_gather.12.side_ref), custom_call_target="tpu_custom_call" | custom-call | flops 671088640 | bytes 18612224 | tf_op jit(solution)/shard_map/pallas_call | solution.py:103
  102.8 4.9 %all-to-all-start.1 = ((f32[8,8,40,128]{3,2,1,0:T(8,128)}), f32[8,8,40,128]{3,2,1,0:T(8,128)S(1)}, u32[]{:S(2)}, u32[]{:S(2)}) async-start(f32[8,8,40,128]{3,2,1,0:T(8,128)} %bitcast.137), calls=%async_computation.2 | async-start | bytes 2621440 | tf_op jit(solution)/shard_map/all_to_all | solution.py:123
  107.7 14.0 %reduce-scatter.7.cloned.1.call-done = f32[16,32,128]{2,1,0:T(8,128)} async-done(((f32[64,32,128]{2,1,0:T(8,128)}), f32[16,32,128]{2,1,0:T(8,128)}) %reduce-scatter.7.cloned.1.call-update) | async-done | bytes 262160 | tf_op jit(solution)/shard_map/reduce_scatter | solution.py:183
  121.7 1.0 divide_convert_fusion.2
  122.7 16.4 %all_gather.13.side_ref = bf16[64,32,128]{2,1,0:T(8,128)(2,1)} all-gather(bf16[16,32,128]{2,1,0:T(8,128)(2,1)S(1)} %divide_convert_fusion.2), channel_id=1, replica_groups=mesh['doc'=8,'term'=4] {'term'}, dimensions={0}, use_global_device_ids=true | all-gather | bytes 655360 | tf_op jit(solution)/shard_map/all_gather | solution.py:184
  139.1 6.6 %shard_map.88 = f32[64,32,128]{2,1,0:T(8,128)} custom-call(s32[512]{0:T(512)} %bitcast.169, s32[512]{0:T(512)} %bitcast.175, s32[1]{0:T(128)} %bitcast.127.cnt_ref, bf16[512,128,128]{2,1,0:T(8,128)(2,1)} %bitcast.133, bf16[64,32,128]{2,1,0:T(8,128)(2,1)} %all_gather.13.side_ref), custom_call_target="tpu_custom_call" | custom-call | flops 536870912 | bytes 18350080 | tf_op jit(solution)/shard_map/pallas_call | solution.py:103
  145.7 5.1 %all-to-all-start.2 = ((f32[8,8,32,128]{3,2,1,0:T(8,128)}), f32[8,8,32,128]{3,2,1,0:T(8,128)S(1)}, u32[]{:S(2)}, u32[]{:S(2)}) async-start(f32[8,8,32,128]{3,2,1,0:T(8,128)} %bitcast.139), calls=%async_computation.4 | async-start | bytes 2097152 | tf_op jit(solution)/shard_map/all_to_all | solution.py:123
  151.6 14.7 %all-to-all-done.2 = f32[8,8,32,128]{3,2,1,0:T(8,128)S(1)} async-done(((f32[8,8,32,128]{3,2,1,0:T(8,128)}), f32[8,8,32,128]{3,2,1,0:T(8,128)S(1)}, u32[]{:S(2)}, u32[]{:S(2)}) %all-to-all-start.2) | async-done | bytes 1048608 | tf_op jit(solution)/shard_map/all_to_all | solution.py:123
  167.2 0.7 concatenate.16
  168.0 8.4 %all_to_all.54 = f32[4,1,4225]{2,1,0:T(1,128)S(1)} all-to-all(f32[4,1,4225]{2,1,0:T(1,128)S(1)} %broadcast_in_dim.14), channel_id=1, replica_groups=mesh['doc'=8,'term'=4] {'term'}, dimensions={0} | all-to-all | bytes 135200 | tf_op jit(solution)/shard_map/all_to_all | solution.py:128
  176.6 8.0 %all_to_all.55 = f32[8,1,4225]{2,1,0:T(1,128)S(1)} all-to-all(f32[8,1,4225]{2,1,0:T(1,128)S(1)} %broadcast_in_dim.15), channel_id=1, replica_groups=mesh['doc'=8,'term'=4] {'doc'}, dimensions={0} | all-to-all | bytes 270400 | tf_op jit(solution)/shard_map/all_to_all | solution.py:128
  186.0 0.8 divide_subtract_fusion.1
  186.8 5.8 %cholesky.45 = f32[64,64]{1,0:T(8,128)S(1)} custom-call(f32[64,64]{1,0:T(8,128)S(1)} %divide_subtract_fusion.1), custom_call_target="Cholesky" | custom-call | tf_op jit(solution)/shard_map/jit(cholesky)/cholesky | solution.py:206
  192.7 0.7 compare_reduce_fusion.1
  194.1 4.9 %custom-call.11 = f32[1,64,64]{1,2,0:T(8,128)S(1)} custom-call(f32[1,64,64]{2,1,0:T(8,128)S(1)} %fusion.27), custom_call_target="InvertDiagBlocksLowerTriangular" | custom-call | tf_op jit(solution)/shard_map/jit(_solve_triangular)/triangular_solve | solution.py:209
  199.8 18.5 %all_to_all.56 = bf16[8,8,64,128]{3,2,1,0:T(8,128)(2,1)} all-to-all(bf16[8,8,64,128]{3,2,1,0:T(8,128)(2,1)S(1)} %broadcast_in_dim.16), channel_id=1, replica_groups=mesh['doc'=8,'term'=4] {'doc'}, dimensions={0} | all-to-all | bytes 2097152 | tf_op jit(solution)/shard_map/all_to_all | solution.py:133
  218.3 9.0 %shard_map.89 = (f32[64,32,128]{2,1,0:T(8,128)}, f32[64,32,128]{2,1,0:T(8,128)}) custom-call(s32[512]{0:T(512)} %bitcast.170, s32[512]{0:T(512)} %bitcast.176, s32[1]{0:T(128)} %bitcast.128.cnt_ref, bf16[512,128,128]{2,1,0:T(8,128)(2,1)} %bitcast.134, bf16[64,64,128]{2,1,0:T(8,128)(2,1)} %bitcast.142), custom_call_target="tpu_custom_call" | custom-call | flops 1073741824 | bytes 19922944 | tf_op jit(solution)/shard_map/pallas_call | solution.py:103
  227.3 32.5 %reduce-scatter.9.cloned.1.call-done = f32[16,32,128]{2,1,0:T(8,128)} async-done(((f32[64,32,128]{2,1,0:T(8,128)}), f32[16,32,128]{2,1,0:T(8,128)}) %reduce-scatter.9.cloned.1.call-update) | async-done | bytes 262160 | tf_op jit(solution)/shard_map/reduce_scatter | solution.py:177
  259.8 1.0 divide_convert_fusion.1
  260.8 16.4 %all_gather.14.side_ref = bf16[64,32,128]{2,1,0:T(8,128)(2,1)} all-gather(bf16[16,32,128]{2,1,0:T(8,128)(2,1)S(1)} %divide_convert_fusion.1), channel_id=1, replica_groups=mesh['doc'=8,'term'=4] {'term'}, dimensions={0}, use_global_device_ids=true | all-gather | bytes 655360 | tf_op jit(solution)/shard_map/all_gather | solution.py:181
  277.2 6.7 %shard_map.90 = f32[64,32,128]{2,1,0:T(8,128)} custom-call(s32[512]{0:T(512)} %bitcast.171, s32[512]{0:T(512)} %bitcast.177, s32[1]{0:T(128)} %bitcast.129.cnt_ref, bf16[512,128,128]{2,1,0:T(8,128)(2,1)} %bitcast.135, bf16[64,32,128]{2,1,0:T(8,128)(2,1)} %all_gather.14.side_ref), custom_call_target="tpu_custom_call" | custom-call | flops 536870912 | bytes 18350080 | tf_op jit(solution)/shard_map/pallas_call | solution.py:103
  283.9 4.8 %all-to-all-start.6 = ((f32[8,8,32,128]{3,2,1,0:T(8,128)}), f32[8,8,32,128]{3,2,1,0:T(8,128)S(1)}, u32[]{:S(2)}, u32[]{:S(2)}) async-start(f32[8,8,32,128]{3,2,1,0:T(8,128)} %bitcast.140), calls=%async_computation.10 | async-start | bytes 2097152 | tf_op jit(solution)/shard_map/all_to_all | solution.py:123
  288.7 14.2 %reduce-scatter.11.cloned.1.call-done = f32[16,32,128]{2,1,0:T(8,128)} async-done(((f32[64,32,128]{2,1,0:T(8,128)}), f32[16,32,128]{2,1,0:T(8,128)}) %reduce-scatter.11.cloned.1.call-update) | async-done | bytes 262160 | tf_op jit(solution)/shard_map/reduce_scatter | solution.py:183
  302.9 1.0 divide_convert_fusion
  303.9 16.4 %all_gather.15.side_ref = bf16[64,32,128]{2,1,0:T(8,128)(2,1)} all-gather(bf16[16,32,128]{2,1,0:T(8,128)(2,1)S(1)} %divide_convert_fusion), channel_id=1, replica_groups=mesh['doc'=8,'term'=4] {'term'}, dimensions={0}, use_global_device_ids=true | all-gather | bytes 655360 | tf_op jit(solution)/shard_map/all_gather | solution.py:184
  320.3 6.6 %shard_map.91 = f32[64,32,128]{2,1,0:T(8,128)} custom-call(s32[512]{0:T(512)} %bitcast.172, s32[512]{0:T(512)} %bitcast.178, s32[1]{0:T(128)} %bitcast.130.cnt_ref, bf16[512,128,128]{2,1,0:T(8,128)(2,1)} %bitcast.136, bf16[64,32,128]{2,1,0:T(8,128)(2,1)} %all_gather.15.side_ref), custom_call_target="tpu_custom_call" | custom-call | flops 536870912 | bytes 18350080 | tf_op jit(solution)/shard_map/pallas_call | solution.py:103
  326.9 5.0 %all-to-all-start.7 = ((f32[8,8,32,128]{3,2,1,0:T(8,128)}), f32[8,8,32,128]{3,2,1,0:T(8,128)S(1)}, u32[]{:S(2)}, u32[]{:S(2)}) async-start(f32[8,8,32,128]{3,2,1,0:T(8,128)} %bitcast.138), calls=%async_computation.11 | async-start | bytes 2097152 | tf_op jit(solution)/shard_map/all_to_all | solution.py:123
  332.8 14.5 %all-to-all-done.7 = f32[8,8,32,128]{3,2,1,0:T(8,128)S(1)} async-done(((f32[8,8,32,128]{3,2,1,0:T(8,128)}), f32[8,8,32,128]{3,2,1,0:T(8,128)S(1)}, u32[]{:S(2)}, u32[]{:S(2)}) %all-to-all-start.7) | async-done | bytes 1048608 | tf_op jit(solution)/shard_map/all_to_all | solution.py:123
  348.7 0.7 concatenate.19
  349.6 9.8 %all_to_all.57 = f32[4,1,12545]{2,1,0:T(1,128)S(1)} all-to-all(f32[4,1,12545]{2,1,0:T(1,128)S(1)} %broadcast_in_dim.17), channel_id=1, replica_groups=mesh['doc'=8,'term'=4] {'term'}, dimensions={0} | all-to-all | bytes 401440 | tf_op jit(solution)/shard_map/all_to_all | solution.py:128
  359.7 11.1 %all_to_all.58 = f32[8,1,12545]{2,1,0:T(1,128)S(1)} all-to-all(f32[8,1,12545]{2,1,0:T(1,128)S(1)} %broadcast_in_dim.18), channel_id=1, replica_groups=mesh['doc'=8,'term'=4] {'doc'}, dimensions={0} | all-to-all | bytes 802880 | tf_op jit(solution)/shard_map/all_to_all | solution.py:128
  372.3 0.7 fusion.36
  373.4 0.7 divide_subtract_fusion
  374.1 5.8 %cholesky.56 = f32[64,64]{1,0:T(8,128)S(1)} custom-call(f32[64,64]{1,0:T(8,128)S(1)} %divide_subtract_fusion), custom_call_target="Cholesky" | custom-call | tf_op jit(solution)/shard_map/jit(cholesky)/cholesky | solution.py:206
  381.3 4.9 %custom-call.9 = f32[1,64,64]{1,2,0:T(8,128)S(1)} custom-call(f32[1,64,64]{2,1,0:T(8,128)S(1)} %fusion.28), custom_call_target="InvertDiagBlocksLowerTriangular" | custom-call | tf_op jit(solution)/shard_map/jit(_solve_triangular)/triangular_solve | solution.py:219
  387.7 0.7 broadcast_in_dim_reshape.7
  388.6 0.7 fusion.2
  389.7 0.9 broadcast_in_dim_reshape.6
  (75 shorter events, 12.2 us)
Async XLA Ops:
  9.4 20.6 %all-to-all-start = ((bf16[8,8,64,128]{3,2,1,0:T(8,128)(2,1)}), bf16[8,8,64,128]{3,2,1,0:T(8,128)(2,1)S(1)}, u32[]{:S(2)}, u32[]{:S(2)}) async-start(bf16[8,8,64,128]{3,2,1,0:T(8,128)(2,1)} %broadcast_in_dim.13), calls=%async_computation | async-start | bytes 2097152 | tf_op jit(solution)/shard_map/all_to_all | solution.py:133
  14.5 63.2 %reduce-scatter.5.cloned.1.call-start = ((), (), s32[]{:S(2)}) async-start(), calls=%async_computation.14 | async-start | bytes 1638400 | tf_op jit(solution)/shard_map/reduce_scatter | solution.py:177
  29.9 1.0 copy-start
  40.0 81.6 %reduce-scatter.7.cloned.1.call-start = ((), (), s32[]{:S(2)}) async-start(), calls=%async_computation.15 | async-start | bytes 1310720 | tf_op jit(solution)/shard_map/reduce_scatter | solution.py:183
  102.8 42.9 %all-to-all-start.1 = ((f32[8,8,40,128]{3,2,1,0:T(8,128)}), f32[8,8,40,128]{3,2,1,0:T(8,128)S(1)}, u32[]{:S(2)}, u32[]{:S(2)}) async-start(f32[8,8,40,128]{3,2,1,0:T(8,128)} %bitcast.137), calls=%async_computation.2 | async-start | bytes 2621440 | tf_op jit(solution)/shard_map/all_to_all | solution.py:123
  145.7 20.5 %all-to-all-start.2 = ((f32[8,8,32,128]{3,2,1,0:T(8,128)}), f32[8,8,32,128]{3,2,1,0:T(8,128)S(1)}, u32[]{:S(2)}, u32[]{:S(2)}) async-start(f32[8,8,32,128]{3,2,1,0:T(8,128)} %bitcast.139), calls=%async_computation.4 | async-start | bytes 2097152 | tf_op jit(solution)/shard_map/all_to_all | solution.py:123
  150.8 109.0 %reduce-scatter.9.cloned.1.call-start = ((), (), s32[]{:S(2)}) async-start(), calls=%async_computation.16 | async-start | bytes 1310720 | tf_op jit(solution)/shard_map/reduce_scatter | solution.py:177
  227.3 75.6 %reduce-scatter.11.cloned.1.call-start = ((), (), s32[]{:S(2)}) async-start(), calls=%async_computation.17 | async-start | bytes 1310720 | tf_op jit(solution)/shard_map/reduce_scatter | solution.py:183
  283.9 43.0 %all-to-all-start.6 = ((f32[8,8,32,128]{3,2,1,0:T(8,128)}), f32[8,8,32,128]{3,2,1,0:T(8,128)S(1)}, u32[]{:S(2)}, u32[]{:S(2)}) async-start(f32[8,8,32,128]{3,2,1,0:T(8,128)} %bitcast.140), calls=%async_computation.10 | async-start | bytes 2097152 | tf_op jit(solution)/shard_map/all_to_all | solution.py:123
  326.9 5.0 %copy-start.4 = (s32[1,1024]{1,0:T(1,128)S(1)}, s32[1,1024]{1,0:T(1,128)}, u32[]{:S(2)}) copy-start(s32[1,1024]{1,0:T(1,128)} %param.16) | copy-start | bytes 12292
  326.9 5.1 %copy-start.3 = (s32[1,2048]{1,0:T(1,128)S(1)}, s32[1,2048]{1,0:T(1,128)}, u32[]{:S(2)}) copy-start(s32[1,2048]{1,0:T(1,128)} %param.15) | copy-start | bytes 24580
  326.9 5.4 %copy-start.1 = (f32[16,32,128]{2,1,0:T(8,128)S(1)}, f32[16,32,128]{2,1,0:T(8,128)}, u32[]{:S(2)}) copy-start(f32[16,32,128]{2,1,0:T(8,128)} %reduce-scatter.9.cloned.1.call-done) | copy-start | bytes 786436
  326.9 5.4 %copy-start.2 = (f32[16,32,128]{2,1,0:T(8,128)S(1)}, f32[16,32,128]{2,1,0:T(8,128)}, u32[]{:S(2)}) copy-start(f32[16,32,128]{2,1,0:T(8,128)} %reduce-scatter.11.cloned.1.call-done) | copy-start | bytes 786436
  326.9 20.4 %all-to-all-start.7 = ((f32[8,8,32,128]{3,2,1,0:T(8,128)}), f32[8,8,32,128]{3,2,1,0:T(8,128)S(1)}, u32[]{:S(2)}, u32[]{:S(2)}) async-start(f32[8,8,32,128]{3,2,1,0:T(8,128)} %bitcast.138), calls=%async_computation.11 | async-start | bytes 2097152 | tf_op jit(solution)/shard_map/all_to_all | solution.py:123
Sparse Core Ops, SparseCore 0:
  40.2 37.5 reduce-scatter.4
  96.1 25.5 reduce-scatter.6
  227.4 32.3 reduce-scatter.8
  277.4 25.4 reduce-scatter.10

commit v21 on v20

--- a/solution.py
+++ b/solution.py
@@ -9,7 +9,7 @@
 
 CLUSTERS = 64
 ITERS = 2
-CHUNK = 256
+CHUNK = 512
 GROUP = 64
 DEG_ROWS = 8
 

time: 401 us -> 412 us (1.027)
  Pallas kernels: 44.8 us -> 60.1 us
  waiting for transfers between devices: 142 us -> 137 us
    pallas_call x6, Pallas kernels: 44.8 us -> 60.1 us  [tile_pass(): pl.pallas_call(kernel, out_shape=[jax.ShapeDtypeStruct(shape, jnp.float32...]
    reduce_scatter x2, waiting for transfers between devices: 28.2 us -> 21.1 us  [per_device(): summed_b = lax.psum_scatter(left_b, 'term', scatter_dimension=0, tiled=True)]
  transfers between devices with their start and end apart: 9 -> 9, of which waited for: 7 -> 7; matrix products, arithmetic and copies ran while one was open for 1% -> 1% of each run, Pallas kernels for 7% -> 9%
where the time goes in v21:
time: 412 us; the launch traced here: 410 us
  waiting for transfers between devices  137 us (33%)
  blocking collectives  121 us (29%)
  Pallas kernels  60.1 us (15%)
  other arithmetic  33.6 us (8%)
  starting transfers between devices  28.9 us (7%)
  between operations  15.4 us (4%)
  local copies, waits for them, and re-layouts  10 us (2%)
  matrix products  4.54 us (1%)
    reduce_scatter x2, waiting for transfers between devices, per_device(): own_a = lax.psum_scatter(left_a, 'term', scatter_dimension=0, tiled=True)  71.6 us
    pallas_call x6, Pallas kernels, tile_pass(): pl.pallas_call(kernel, out_shape=[jax.ShapeDtypeStruct(shape, jnp.float32...  60.1 us
    all_to_all x4, blocking collectives, exchange_sum(): return jnp.sum(lax.all_to_all(copies, axis_name, 0, 0, tiled=False), axis=0)  36.7 us
    all_gather x2, blocking collectives, per_device(): lax.all_gather((summed_a / doc_degree[:, None, :]).astype(jnp.bfloat16),...  32.8 us
    all_gather x2, blocking collectives, per_device(): lax.all_gather((summed_b / doc_degree[:, None, :]).astype(jnp.bfloat16),...  32.8 us
    all_to_all x4, waiting for transfers between devices, scatter_sum(): return jnp.sum(lax.all_to_all(pieces, axis_name, 0, 0, tiled=False), axis=0)  29.1 us
    all_to_all x4, starting transfers between devices, scatter_sum(): return jnp.sum(lax.all_to_all(pieces, axis_name, 0, 0, tiled=False), axis=0)  23.5 us
    reduce_scatter x2, waiting for transfers between devices, per_device(): summed_b = lax.psum_scatter(left_b, 'term', scatter_dimension=0, tiled=True)  21.1 us
  transfers between devices with their start and end apart: 9, of which 7 were waited for; matrix products, arithmetic and copies ran while one was open for 1% of the time, Pallas kernels for 9%

profile of v21, /device:TPU:0, one launch (start us, length us, event | category | flops | bytes accessed | tf_op | source)
XLA Modules:
  0.0 409.9 jit_solution(4782462368586665991)
XLA Ops:
  7.2 0.9 copy.89
  8.1 1.2 broadcast_in_dim.13
  9.4 5.2 %all-to-all-start = ((bf16[8,8,64,128]{3,2,1,0:T(8,128)(2,1)}), bf16[8,8,64,128]{3,2,1,0:T(8,128)(2,1)S(1)}, u32[]{:S(2)}, u32[]{:S(2)}) async-start(bf16[8,8,64,128]{3,2,1,0:T(8,128)(2,1)} %broadcast_in_dim.13), calls=%async_computation | async-start | bytes 2097152 | tf_op jit(solution)/shard_map/all_to_all | solution.py:133
  15.2 14.7 %all-to-all-done = bf16[8,8,64,128]{3,2,1,0:T(8,128)(2,1)S(1)} async-done(((bf16[8,8,64,128]{3,2,1,0:T(8,128)(2,1)}), bf16[8,8,64,128]{3,2,1,0:T(8,128)(2,1)S(1)}, u32[]{:S(2)}, u32[]{:S(2)}) %all-to-all-start) | async-done | bytes 1048608 | tf_op jit(solution)/shard_map/all_to_all | solution.py:133
  29.9 1.0 copy-done
  30.9 11.5 %shard_map.86 = (f32[64,40,128]{2,1,0:T(8,128)}, f32[64,32,128]{2,1,0:T(8,128)}) custom-call(s32[512]{0:T(512)} %bitcast.167, s32[512]{0:T(512)} %bitcast.173, s32[1]{0:T(128)} %bitcast.125.cnt_ref, bf16[512,128,128]{2,1,0:T(8,128)(2,1)} %bitcast.131, bf16[64,64,128]{2,1,0:T(8,128)(2,1)} %bitcast.141), custom_call_target="tpu_custom_call" | custom-call | flops 1207959552 | bytes 20185088 | tf_op jit(solution)/shard_map/pallas_call | solution.py:103
  42.5 38.5 %reduce-scatter.5.cloned.1.call-done = f32[16,40,128]{2,1,0:T(8,128)} async-done(((f32[64,40,128]{2,1,0:T(8,128)}), f32[16,40,128]{2,1,0:T(8,128)}) %reduce-scatter.5.cloned.1.call-update) | async-done | bytes 327696 | tf_op jit(solution)/shard_map/reduce_scatter | solution.py:177
  81.0 0.8 slice.75
  81.9 1.0 fusion.19
  82.8 16.4 %all_gather.12.side_ref = bf16[64,32,128]{2,1,0:T(8,128)(2,1)} all-gather(bf16[16,32,128]{2,1,0:T(8,128)(2,1)S(1)} %fusion.19), channel_id=1, replica_groups=mesh['doc'=8,'term'=4] {'term'}, dimensions={0}, use_global_device_ids=true | all-gather | bytes 655360 | tf_op jit(solution)/shard_map/all_gather | solution.py:181
  99.3 9.5 %shard_map.87 = f32[64,40,128]{2,1,0:T(8,128)} custom-call(s32[512]{0:T(512)} %bitcast.168, s32[512]{0:T(512)} %bitcast.174, s32[1]{0:T(128)} %bitcast.126.cnt_ref, bf16[512,128,128]{2,1,0:T(8,128)(2,1)} %bitcast.132, bf16[64,32,128]{2,1,0:T(8,128)(2,1)} %all_gather.12.side_ref), custom_call_target="tpu_custom_call" | custom-call | flops 671088640 | bytes 18612224 | tf_op jit(solution)/shard_map/pallas_call | solution.py:103
  108.7 5.8 %all-to-all-start.1 = ((f32[8,8,40,128]{3,2,1,0:T(8,128)}), f32[8,8,40,128]{3,2,1,0:T(8,128)S(1)}, u32[]{:S(2)}, u32[]{:S(2)}) async-start(f32[8,8,40,128]{3,2,1,0:T(8,128)} %bitcast.137), calls=%async_computation.2 | async-start | bytes 2621440 | tf_op jit(solution)/shard_map/all_to_all | solution.py:123
  114.5 10.4 %reduce-scatter.7.cloned.1.call-done = f32[16,32,128]{2,1,0:T(8,128)} async-done(((f32[64,32,128]{2,1,0:T(8,128)}), f32[16,32,128]{2,1,0:T(8,128)}) %reduce-scatter.7.cloned.1.call-update) | async-done | bytes 262160 | tf_op jit(solution)/shard_map/reduce_scatter | solution.py:183
  124.9 1.0 divide_convert_fusion.2
  125.9 16.4 %all_gather.13.side_ref = bf16[64,32,128]{2,1,0:T(8,128)(2,1)} all-gather(bf16[16,32,128]{2,1,0:T(8,128)(2,1)S(1)} %divide_convert_fusion.2), channel_id=1, replica_groups=mesh['doc'=8,'term'=4] {'term'}, dimensions={0}, use_global_device_ids=true | all-gather | bytes 655360 | tf_op jit(solution)/shard_map/all_gather | solution.py:184
  142.3 9.1 %shard_map.88 = f32[64,32,128]{2,1,0:T(8,128)} custom-call(s32[512]{0:T(512)} %bitcast.169, s32[512]{0:T(512)} %bitcast.175, s32[1]{0:T(128)} %bitcast.127.cnt_ref, bf16[512,128,128]{2,1,0:T(8,128)(2,1)} %bitcast.133, bf16[64,32,128]{2,1,0:T(8,128)(2,1)} %all_gather.13.side_ref), custom_call_target="tpu_custom_call" | custom-call | flops 536870912 | bytes 18350080 | tf_op jit(solution)/shard_map/pallas_call | solution.py:103
  151.4 5.8 %all-to-all-start.2 = ((f32[8,8,32,128]{3,2,1,0:T(8,128)}), f32[8,8,32,128]{3,2,1,0:T(8,128)S(1)}, u32[]{:S(2)}, u32[]{:S(2)}) async-start(f32[8,8,32,128]{3,2,1,0:T(8,128)} %bitcast.139), calls=%async_computation.4 | async-start | bytes 2097152 | tf_op jit(solution)/shard_map/all_to_all | solution.py:123
  158.0 14.7 %all-to-all-done.2 = f32[8,8,32,128]{3,2,1,0:T(8,128)S(1)} async-done(((f32[8,8,32,128]{3,2,1,0:T(8,128)}), f32[8,8,32,128]{3,2,1,0:T(8,128)S(1)}, u32[]{:S(2)}, u32[]{:S(2)}) %all-to-all-start.2) | async-done | bytes 1048608 | tf_op jit(solution)/shard_map/all_to_all | solution.py:123
  173.6 0.7 concatenate.16
  174.4 8.1 %all_to_all.54 = f32[4,1,4225]{2,1,0:T(1,128)S(1)} all-to-all(f32[4,1,4225]{2,1,0:T(1,128)S(1)} %broadcast_in_dim.14), channel_id=1, replica_groups=mesh['doc'=8,'term'=4] {'term'}, dimensions={0} | all-to-all | bytes 135200 | tf_op jit(solution)/shard_map/all_to_all | solution.py:128
  182.7 8.0 %all_to_all.55 = f32[8,1,4225]{2,1,0:T(1,128)S(1)} all-to-all(f32[8,1,4225]{2,1,0:T(1,128)S(1)} %broadcast_in_dim.15), channel_id=1, replica_groups=mesh['doc'=8,'term'=4] {'doc'}, dimensions={0} | all-to-all | bytes 270400 | tf_op jit(solution)/shard_map/all_to_all | solution.py:128
  192.2 0.8 divide_subtract_fusion.1
  192.9 5.8 %cholesky.45 = f32[64,64]{1,0:T(8,128)S(1)} custom-call(f32[64,64]{1,0:T(8,128)S(1)} %divide_subtract_fusion.1), custom_call_target="Cholesky" | custom-call | tf_op jit(solution)/shard_map/jit(cholesky)/cholesky | solution.py:206
  198.8 0.7 compare_reduce_fusion.1
  200.3 4.9 %custom-call.11 = f32[1,64,64]{1,2,0:T(8,128)S(1)} custom-call(f32[1,64,64]{2,1,0:T(8,128)S(1)} %fusion.27), custom_call_target="InvertDiagBlocksLowerTriangular" | custom-call | tf_op jit(solution)/shard_map/jit(_solve_triangular)/triangular_solve | solution.py:209
  205.9 18.5 %all_to_all.56 = bf16[8,8,64,128]{3,2,1,0:T(8,128)(2,1)} all-to-all(bf16[8,8,64,128]{3,2,1,0:T(8,128)(2,1)S(1)} %broadcast_in_dim.16), channel_id=1, replica_groups=mesh['doc'=8,'term'=4] {'doc'}, dimensions={0} | all-to-all | bytes 2097152 | tf_op jit(solution)/shard_map/all_to_all | solution.py:133
  224.4 11.6 %shard_map.89 = (f32[64,32,128]{2,1,0:T(8,128)}, f32[64,32,128]{2,1,0:T(8,128)}) custom-call(s32[512]{0:T(512)} %bitcast.170, s32[512]{0:T(512)} %bitcast.176, s32[1]{0:T(128)} %bitcast.128.cnt_ref, bf16[512,128,128]{2,1,0:T(8,128)(2,1)} %bitcast.134, bf16[64,64,128]{2,1,0:T(8,128)(2,1)} %bitcast.142), custom_call_target="tpu_custom_call" | custom-call | flops 1073741824 | bytes 19922944 | tf_op jit(solution)/shard_map/pallas_call | solution.py:103
  236.1 33.2 %reduce-scatter.9.cloned.1.call-done = f32[16,32,128]{2,1,0:T(8,128)} async-done(((f32[64,32,128]{2,1,0:T(8,128)}), f32[16,32,128]{2,1,0:T(8,128)}) %reduce-scatter.9.cloned.1.call-update) | async-done | bytes 262160 | tf_op jit(solution)/shard_map/reduce_scatter | solution.py:177
  269.2 1.0 divide_convert_fusion.1
  270.2 16.4 %all_gather.14.side_ref = bf16[64,32,128]{2,1,0:T(8,128)(2,1)} all-gather(bf16[16,32,128]{2,1,0:T(8,128)(2,1)S(1)} %divide_convert_fusion.1), channel_id=1, replica_groups=mesh['doc'=8,'term'=4] {'term'}, dimensions={0}, use_global_device_ids=true | all-gather | bytes 655360 | tf_op jit(solution)/shard_map/all_gather | solution.py:181
  286.6 9.3 %shard_map.90 = f32[64,32,128]{2,1,0:T(8,128)} custom-call(s32[512]{0:T(512)} %bitcast.171, s32[512]{0:T(512)} %bitcast.177, s32[1]{0:T(128)} %bitcast.129.cnt_ref, bf16[512,128,128]{2,1,0:T(8,128)(2,1)} %bitcast.135, bf16[64,32,128]{2,1,0:T(8,128)(2,1)} %all_gather.14.side_ref), custom_call_target="tpu_custom_call" | custom-call | flops 536870912 | bytes 18350080 | tf_op jit(solution)/shard_map/pallas_call | solution.py:103
  295.9 6.0 %all-to-all-start.6 = ((f32[8,8,32,128]{3,2,1,0:T(8,128)}), f32[8,8,32,128]{3,2,1,0:T(8,128)S(1)}, u32[]{:S(2)}, u32[]{:S(2)}) async-start(f32[8,8,32,128]{3,2,1,0:T(8,128)} %bitcast.140), calls=%async_computation.10 | async-start | bytes 2097152 | tf_op jit(solution)/shard_map/all_to_all | solution.py:123
  302.0 10.6 %reduce-scatter.11.cloned.1.call-done = f32[16,32,128]{2,1,0:T(8,128)} async-done(((f32[64,32,128]{2,1,0:T(8,128)}), f32[16,32,128]{2,1,0:T(8,128)}) %reduce-scatter.11.cloned.1.call-update) | async-done | bytes 262160 | tf_op jit(solution)/shard_map/reduce_scatter | solution.py:183
  312.6 1.0 divide_convert_fusion
  313.6 16.4 %all_gather.15.side_ref = bf16[64,32,128]{2,1,0:T(8,128)(2,1)} all-gather(bf16[16,32,128]{2,1,0:T(8,128)(2,1)S(1)} %divide_convert_fusion), channel_id=1, replica_groups=mesh['doc'=8,'term'=4] {'term'}, dimensions={0}, use_global_device_ids=true | all-gather | bytes 655360 | tf_op jit(solution)/shard_map/all_gather | solution.py:184
  330.0 9.1 %shard_map.91 = f32[64,32,128]{2,1,0:T(8,128)} custom-call(s32[512]{0:T(512)} %bitcast.172, s32[512]{0:T(512)} %bitcast.178, s32[1]{0:T(128)} %bitcast.130.cnt_ref, bf16[512,128,128]{2,1,0:T(8,128)(2,1)} %bitcast.136, bf16[64,32,128]{2,1,0:T(8,128)(2,1)} %all_gather.15.side_ref), custom_call_target="tpu_custom_call" | custom-call | flops 536870912 | bytes 18350080 | tf_op jit(solution)/shard_map/pallas_call | solution.py:103
  339.1 5.9 %all-to-all-start.7 = ((f32[8,8,32,128]{3,2,1,0:T(8,128)}), f32[8,8,32,128]{3,2,1,0:T(8,128)S(1)}, u32[]{:S(2)}, u32[]{:S(2)}) async-start(f32[8,8,32,128]{3,2,1,0:T(8,128)} %bitcast.138), calls=%async_computation.11 | async-start | bytes 2097152 | tf_op jit(solution)/shard_map/all_to_all | solution.py:123
  346.0 14.5 %all-to-all-done.7 = f32[8,8,32,128]{3,2,1,0:T(8,128)S(1)} async-done(((f32[8,8,32,128]{3,2,1,0:T(8,128)}), f32[8,8,32,128]{3,2,1,0:T(8,128)S(1)}, u32[]{:S(2)}, u32[]{:S(2)}) %all-to-all-start.7) | async-done | bytes 1048608 | tf_op jit(solution)/shard_map/all_to_all | solution.py:123
  361.8 0.7 concatenate.19
  362.7 9.2 %all_to_all.57 = f32[4,1,12545]{2,1,0:T(1,128)S(1)} all-to-all(f32[4,1,12545]{2,1,0:T(1,128)S(1)} %broadcast_in_dim.17), channel_id=1, replica_groups=mesh['doc'=8,'term'=4] {'term'}, dimensions={0} | all-to-all | bytes 401440 | tf_op jit(solution)/shard_map/all_to_all | solution.py:128
  372.3 11.4 %all_to_all.58 = f32[8,1,12545]{2,1,0:T(1,128)S(1)} all-to-all(f32[8,1,12545]{2,1,0:T(1,128)S(1)} %broadcast_in_dim.18), channel_id=1, replica_groups=mesh['doc'=8,'term'=4] {'doc'}, dimensions={0} | all-to-all | bytes 802880 | tf_op jit(solution)/shard_map/all_to_all | solution.py:128
  385.1 0.7 fusion.36
  386.2 0.7 divide_subtract_fusion
  386.9 5.8 %cholesky.56 = f32[64,64]{1,0:T(8,128)S(1)} custom-call(f32[64,64]{1,0:T(8,128)S(1)} %divide_subtract_fusion), custom_call_target="Cholesky" | custom-call | tf_op jit(solution)/shard_map/jit(cholesky)/cholesky | solution.py:206
  394.1 4.9 %custom-call.9 = f32[1,64,64]{1,2,0:T(8,128)S(1)} custom-call(f32[1,64,64]{2,1,0:T(8,128)S(1)} %fusion.28), custom_call_target="InvertDiagBlocksLowerTriangular" | custom-call | tf_op jit(solution)/shard_map/jit(_solve_triangular)/triangular_solve | solution.py:219
  400.5 0.7 broadcast_in_dim_reshape.7
  401.4 0.7 fusion.2
  402.5 0.9 broadcast_in_dim_reshape.6
  (75 shorter events, 12.2 us)
Async XLA Ops:
  9.4 20.6 %all-to-all-start = ((bf16[8,8,64,128]{3,2,1,0:T(8,128)(2,1)}), bf16[8,8,64,128]{3,2,1,0:T(8,128)(2,1)S(1)}, u32[]{:S(2)}, u32[]{:S(2)}) async-start(bf16[8,8,64,128]{3,2,1,0:T(8,128)(2,1)} %broadcast_in_dim.13), calls=%async_computation | async-start | bytes 2097152 | tf_op jit(solution)/shard_map/all_to_all | solution.py:133
  14.5 66.5 %reduce-scatter.5.cloned.1.call-start = ((), (), s32[]{:S(2)}) async-start(), calls=%async_computation.14 | async-start | bytes 1638400 | tf_op jit(solution)/shard_map/reduce_scatter | solution.py:177
  29.9 1.0 copy-start
  42.5 82.5 %reduce-scatter.7.cloned.1.call-start = ((), (), s32[]{:S(2)}) async-start(), calls=%async_computation.15 | async-start | bytes 1310720 | tf_op jit(solution)/shard_map/reduce_scatter | solution.py:183
  108.7 42.7 %all-to-all-start.1 = ((f32[8,8,40,128]{3,2,1,0:T(8,128)}), f32[8,8,40,128]{3,2,1,0:T(8,128)S(1)}, u32[]{:S(2)}, u32[]{:S(2)}) async-start(f32[8,8,40,128]{3,2,1,0:T(8,128)} %bitcast.137), calls=%async_computation.2 | async-start | bytes 2621440 | tf_op jit(solution)/shard_map/all_to_all | solution.py:123
  151.4 21.2 %all-to-all-start.2 = ((f32[8,8,32,128]{3,2,1,0:T(8,128)}), f32[8,8,32,128]{3,2,1,0:T(8,128)S(1)}, u32[]{:S(2)}, u32[]{:S(2)}) async-start(f32[8,8,32,128]{3,2,1,0:T(8,128)} %bitcast.139), calls=%async_computation.4 | async-start | bytes 2097152 | tf_op jit(solution)/shard_map/all_to_all | solution.py:123
  157.2 112.0 %reduce-scatter.9.cloned.1.call-start = ((), (), s32[]{:S(2)}) async-start(), calls=%async_computation.16 | async-start | bytes 1310720 | tf_op jit(solution)/shard_map/reduce_scatter | solution.py:177
  236.0 76.6 %reduce-scatter.11.cloned.1.call-start = ((), (), s32[]{:S(2)}) async-start(), calls=%async_computation.17 | async-start | bytes 1310720 | tf_op jit(solution)/shard_map/reduce_scatter | solution.py:183
  295.9 43.1 %all-to-all-start.6 = ((f32[8,8,32,128]{3,2,1,0:T(8,128)}), f32[8,8,32,128]{3,2,1,0:T(8,128)S(1)}, u32[]{:S(2)}, u32[]{:S(2)}) async-start(f32[8,8,32,128]{3,2,1,0:T(8,128)} %bitcast.140), calls=%async_computation.10 | async-start | bytes 2097152 | tf_op jit(solution)/shard_map/all_to_all | solution.py:123
  339.1 6.0 %copy-start.4 = (s32[1,1024]{1,0:T(1,128)S(1)}, s32[1,1024]{1,0:T(1,128)}, u32[]{:S(2)}) copy-start(s32[1,1024]{1,0:T(1,128)} %param.16) | copy-start | bytes 12292
  339.1 6.1 %copy-start.3 = (s32[1,2048]{1,0:T(1,128)S(1)}, s32[1,2048]{1,0:T(1,128)}, u32[]{:S(2)}) copy-start(s32[1,2048]{1,0:T(1,128)} %param.15) | copy-start | bytes 24580
  339.1 6.4 %copy-start.1 = (f32[16,32,128]{2,1,0:T(8,128)S(1)}, f32[16,32,128]{2,1,0:T(8,128)}, u32[]{:S(2)}) copy-start(f32[16,32,128]{2,1,0:T(8,128)} %reduce-scatter.9.cloned.1.call-done) | copy-start | bytes 786436
  339.1 6.4 %copy-start.2 = (f32[16,32,128]{2,1,0:T(8,128)S(1)}, f32[16,32,128]{2,1,0:T(8,128)}, u32[]{:S(2)}) copy-start(f32[16,32,128]{2,1,0:T(8,128)} %reduce-scatter.11.cloned.1.call-done) | copy-start | bytes 786436
  339.1 21.4 %all-to-all-start.7 = ((f32[8,8,32,128]{3,2,1,0:T(8,128)}), f32[8,8,32,128]{3,2,1,0:T(8,128)S(1)}, u32[]{:S(2)}, u32[]{:S(2)}) async-start(f32[8,8,32,128]{3,2,1,0:T(8,128)} %bitcast.138), calls=%async_computation.11 | async-start | bytes 2097152 | tf_op jit(solution)/shard_map/all_to_all | solution.py:123
Sparse Core Ops, SparseCore 0:
  42.6 38.3 reduce-scatter.4
  99.4 25.4 reduce-scatter.6
  236.1 33.0 reduce-scatter.8
  286.7 25.8 reduce-scatter.10
